TPU v7x, 512 devices: a whole 4x4x16 slice. The times are simulated.
512 devices in a mesh: col: 4 (over x_lo, core), gx: 16 (over z), gy: 8 (over x_hi, y).
Axes of the slice: x: 4 (x_hi: 2, x_lo: 2; x = x_hi * 2 + x_lo), y: 4, z: 16, core: 2. Of those that a mesh axis runs over, the one named last changes fastest.
Arguments:
- volume: float32 [32, 8, 64, 1024], P('col', None, 'gx', 'gy'), may hold values from -6 to 6
- filters: float32 [32, 32, 3, 3, 3], P('col'), may hold values from -0.21875 to 0.21875
- upstream: float32 [32, 8, 64, 1024], P('col', None, 'gx', 'gy'), may hold values from -6 to 6
Outputs:
- response: float32 [32, 8, 64, 1024], P('col', None, 'gx', 'gy')
- input_grad: float32 [32, 8, 64, 1024], P('col', None, 'gx', 'gy')
- filter_grad: float32 [32, 32, 3, 3, 3], P('col')
All inputs are finite; a program needn't handle non-finite values.
Results may differ from a plain program's by a relative error of at most 0.0003.
Values sent between devices are 32-bit elements; how exact they have to be, the bound alone decides.
No kernel may reach another device: no remote copies, remote signals or barrier semaphores. Data moves between devices by JAX's collectives and lax.ppermute only.
A program may use at most 64 MiB of HBM per device.

v0:
```python
import jax
import jax.numpy as jnp
from jax import lax
from jax.sharding import PartitionSpec as P


def with_halo(block, sides, width):
    for axis, dim in sides:
        count = lax.axis_size(axis)
        forward = [(i, i + 1) for i in range(count - 1)]
        backward = [(target, source) for source, target in forward]
        low = lax.ppermute(
            lax.slice_in_dim(block, block.shape[dim] - width, None, axis=dim), axis, forward
        )
        high = lax.ppermute(lax.slice_in_dim(block, 0, width, axis=dim), axis, backward)
        block = jnp.concatenate([low, block, high], axis=dim)
    return block


def pad_depth(field):
    return jnp.pad(field, ((0, 0), (1, 1), (0, 0), (0, 0)))


def forward_conv(padded, weights, planes, rows_x, rows_y):
    output = jnp.zeros((weights.shape[0], planes, rows_x, rows_y), jnp.float32)
    for depth in range(3):
        for across in range(3):
            for along in range(3):
                window = padded[
                    :, depth : depth + planes, across : across + rows_x, along : along + rows_y
                ]
                output = output + jnp.einsum(
                    "oc,czxy->ozxy",
                    weights[:, :, depth, across, along],
                    window,
                    precision=lax.Precision.HIGHEST,
                )
    return output


def backward_conv(padded_up, weights, planes, rows_x, rows_y):
    output = jnp.zeros((weights.shape[1], planes, rows_x, rows_y), jnp.float32)
    for depth in range(3):
        for across in range(3):
            for along in range(3):
                window = padded_up[
                    :,
                    2 - depth : 2 - depth + planes,
                    2 - across : 2 - across + rows_x,
                    2 - along : 2 - along + rows_y,
                ]
                output = output + jnp.einsum(
                    "oc,ozxy->czxy",
                    weights[:, :, depth, across, along],
                    window,
                    precision=lax.Precision.HIGHEST,
                )
    return output


def weight_terms(cotangent, padded, planes, rows_x, rows_y):
    pieces = []
    for depth in range(3):
        for across in range(3):
            for along in range(3):
                window = padded[
                    :, depth : depth + planes, across : across + rows_x, along : along + rows_y
                ]
                pieces.append(
                    jnp.einsum("ozxy,czxy->oc", cotangent, window, precision=lax.Precision.HIGHEST)
                )
    stacked = jnp.stack(pieces, axis=-1)
    return stacked.reshape(stacked.shape[0], stacked.shape[1], 3, 3, 3)


def shards(volume, filters, upstream):
    planes, rows_x, rows_y = (volume.shape[1], volume.shape[2], volume.shape[3])
    own_inputs = volume.shape[0]
    scale = (planes * rows_x * lax.axis_size("gx") * rows_y * lax.axis_size("gy")) ** (-0.5)
    gathered = lax.all_gather(volume, "col", axis=0, tiled=True)
    padded = pad_depth(with_halo(gathered, (("gx", 2), ("gy", 3)), 1))
    response = forward_conv(padded, filters, planes, rows_x, rows_y)
    all_rows = lax.all_gather(filters, "col", axis=0, tiled=True)
    all_upstream = lax.all_gather(upstream, "col", axis=0, tiled=True)
    padded_up = pad_depth(with_halo(all_upstream, (("gx", 2), ("gy", 3)), 1))
    first = lax.axis_index("col") * own_inputs
    own_filters = lax.dynamic_slice_in_dim(all_rows, first, own_inputs, 1)
    input_grad = backward_conv(padded_up, own_filters, planes, rows_x, rows_y)
    local_grad = weight_terms(upstream, padded, planes, rows_x, rows_y)
    total_grad = lax.psum(local_grad, ("gx", "gy"))
    return (response, input_grad, total_grad * scale)


def solution(mesh):
    placed = (
        P("col", None, "gx", "gy"),
        P("col", None, None, None, None),
        P("col", None, "gx", "gy"),
    )
    return jax.shard_map(
        shards,
        mesh=mesh,
        in_specs=placed,
        out_specs=(
            P("col", None, "gx", "gy"),
            P("col", None, "gx", "gy"),
            P("col", None, None, None, None),
        ),
        check_vma=False,
    )
```

profile of v0, /device:TPU:6, one launch (start us, length us, event | category | flops | bytes accessed | tf_op | source)
XLA Modules:
  0.0 878.0 jit_solution(7384138758110080891)
XLA Ops:
  1.7 6.8 all_gather.9
  9.2 3.8 collective-permute-start
  13.0 1.3 collective-permute-start.1
  15.3 7.0 all_gather.11
  23.0 5.1 collective-permute-start.4
  28.1 1.3 collective-permute-start.5
  29.4 6.6 all_gather.10
  39.4 3.5 collective-permute-start.2
  43.9 6.0 collective-permute-start.3
  51.7 1.2 fusion.310
  53.0 2.1 copy.74
  55.1 1.9 collective-permute-start.6
  57.9 7.8 collective-permute-start.7
  65.8 1.7 fusion.208
  67.5 2.0 fusion.116
  69.5 2.0 fusion.112
  74.7 2.9 pad_maximum_fusion.9
  77.7 2.1 select_maximum_fusion.2
  80.8 2.0 copy.77
  82.8 1.9 select_maximum_fusion
  84.7 1.3 fusion.120
  95.3 1.3 fusion.83
  96.7 1.3 fusion.86
  100.4 1.2 fusion.106
  107.3 1.7 fusion.96
  110.2 1.3 fusion.114
  111.5 4.3 fusion.309
  115.8 1.8 fusion.212
  117.6 1.8 fusion.214
  119.5 1.7 fusion.216
  121.2 1.8 fusion.218
  123.0 1.8 fusion.220
  124.8 1.7 fusion.222
  126.6 1.9 fusion.224
  128.5 1.9 fusion.226
  130.4 1.8 convolution_bitcast_fusion.6
  132.1 1.9 convolution_bitcast_fusion.7
  134.0 1.9 convolution_bitcast_fusion.8
  135.9 1.8 convolution_bitcast_fusion.9
  138.3 1.8 fusion.210
  145.7 1.8 fusion.206
  148.1 1.8 fusion.204
  151.0 1.8 convolution_bitcast_fusion.10
  160.7 698.2 %psum.7 = f32[8,32,3,3,3]{1,0,4,3,2:T(8,128)} all-reduce(f32[8,32,3,3,3]{1,0,4,3,2:T(8,128)} %bitcast.738), channel_id=1, replica_groups=mesh['col'=4,'gx'=16,'gy'=8] {'gx','gy'}, use_global_device_ids=true, to_apply=%region_0.1 | all-reduce | flops 6912 | bytes 55296 | tf_op jit(solution)/shard_map/psum | solution.py:90
  858.9 1.7 broadcast_multiply_fusion
  860.6 2.3 fusion.48
  863.2 1.5 fusion.49
  865.5 1.3 fusion.47
  (214 shorter events, 60.8 us)
Async XLA Ops:
  0.6 28.7 %copy-start.65 = (f32[8,32,3,3,3]{1,0,4,3,2:T(8,128)S(1)}, f32[8,32,3,3,3]{1,0,4,3,2:T(8,128)}, u32[]{:S(2)}) copy-start(f32[8,32,3,3,3]{1,0,4,3,2:T(8,128)} %param.4) | copy-start | bytes 82948
  8.4 28.9 %copy-start.3 = (f32[32,8,4,128]{3,0,2,1:T(8,128)}, f32[32,8,4,128]{3,0,2,1:T(8,128)S(1)}, u32[]{:S(2)}) copy-start(f32[32,8,4,128]{3,0,2,1:T(8,128)S(1)} %all_gather.9) | copy-start | bytes 1572868
  9.2 27.9 %collective-permute-start = (f32[32,8,1,128]{3,0,2,1:T(8,128)S(1)}, f32[32,8,1,128]{3,0,2,1:T(8,128)S(1)}, u32[]{:S(2)}, u32[]{:S(2)}) collective-permute-start(f32[32,8,1,128]{3,0,2,1:T(8,128)S(1)} %get-tuple-element.46), channel_id=1, source_target_pairs={{0,8},{8,16},{16,24},{24,32},{32,40},{40,48},{48,56},{56,64},{64,7... | collective-permute-start | bytes 393224 | tf_op jit(solution)/shard_map/ppermute | solution.py:12
  13.0 24.3 %collective-permute-start.1 = (f32[32,8,1,128]{3,0,2,1:T(8,128)}, f32[32,8,1,128]{3,0,2,1:T(8,128)S(1)}, u32[]{:S(2)}, u32[]{:S(2)}) collective-permute-start(f32[32,8,1,128]{3,0,2,1:T(8,128)} %get-tuple-element.45), channel_id=1, source_target_pairs={{8,0},{16,8},{24,16},{32,24},{40,32},{48,40},{56,48},{64,56},{72,6... | collective-permute-start | bytes 393224 | tf_op jit(solution)/shard_map/ppermute | solution.py:15
  23.0 26.8 %collective-permute-start.4 = (f32[32,8,1,128]{3,0,2,1:T(8,128)}, f32[32,8,1,128]{3,0,2,1:T(8,128)}, u32[]{:S(2)}, u32[]{:S(2)}) collective-permute-start(f32[32,8,1,128]{3,0,2,1:T(8,128)} %get-tuple-element.41), channel_id=1, source_target_pairs={{0,8},{8,16},{16,24},{24,32},{32,40},{40,48},{48,56},{56,64},{64,7... | collective-permute-start | bytes 393224 | tf_op jit(solution)/shard_map/ppermute | solution.py:12
  28.1 22.7 %collective-permute-start.5 = (f32[32,8,1,128]{3,0,2,1:T(8,128)}, f32[32,8,1,128]{3,0,2,1:T(8,128)}, u32[]{:S(2)}, u32[]{:S(2)}) collective-permute-start(f32[32,8,1,128]{3,0,2,1:T(8,128)} %get-tuple-element.40), channel_id=1, source_target_pairs={{8,0},{16,8},{24,16},{32,24},{40,32},{48,40},{56,48},{64,56},{72,6... | collective-permute-start | bytes 393224 | tf_op jit(solution)/shard_map/ppermute | solution.py:15
  39.4 32.1 %collective-permute-start.2 = (f32[32,8,6,1]{0,1,3,2:T(8,128)}, f32[32,8,6,1]{0,1,3,2:T(8,128)}, u32[]{:S(2)}, u32[]{:S(2)}) collective-permute-start(f32[32,8,6,1]{0,1,3,2:T(8,128)} %copy.66), channel_id=1, source_target_pairs={{0,1},{1,2},{2,3},{3,4},{4,5},{5,6},{6,7},{8,9},{9,10},{10,11},{11... | collective-permute-start | bytes 18440 | tf_op jit(solution)/shard_map/ppermute | solution.py:12
  43.9 28.8 %collective-permute-start.3 = (f32[32,8,6,1]{0,1,3,2:T(8,128)}, f32[32,8,6,1]{0,1,3,2:T(8,128)}, u32[]{:S(2)}, u32[]{:S(2)}) collective-permute-start(f32[32,8,6,1]{0,1,3,2:T(8,128)} %copy.67), channel_id=1, source_target_pairs={{1,0},{2,1},{3,2},{4,3},{5,4},{6,5},{7,6},{9,8},{10,9},{11,10},{12... | collective-permute-start | bytes 18440 | tf_op jit(solution)/shard_map/ppermute | solution.py:15
  51.7 14.0 %copy-start.20 = (f32[32,8,5,128]{3,0,2,1:T(8,128)S(1)}, f32[32,8,5,128]{3,0,2,1:T(8,128)}, u32[]{:S(2)}) copy-start(f32[32,8,5,128]{3,0,2,1:T(8,128)} %copy-done.19) | copy-start | bytes 1966084
  55.1 24.7 %collective-permute-start.6 = (f32[32,8,6,1]{0,1,3,2:T(8,128)}, f32[32,8,6,1]{0,1,3,2:T(8,128)}, u32[]{:S(2)}, u32[]{:S(2)}) collective-permute-start(f32[32,8,6,1]{0,1,3,2:T(8,128)} %copy.74), channel_id=1, source_target_pairs={{0,1},{1,2},{2,3},{3,4},{4,5},{5,6},{6,7},{8,9},{9,10},{10,11},{11... | collective-permute-start | bytes 18440 | tf_op jit(solution)/shard_map/ppermute | solution.py:12
  57.9 22.9 %collective-permute-start.7 = (f32[32,8,6,1]{0,1,3,2:T(8,128)}, f32[32,8,6,1]{0,1,3,2:T(8,128)}, u32[]{:S(2)}, u32[]{:S(2)}) collective-permute-start(f32[32,8,6,1]{0,1,3,2:T(8,128)} %copy.75), channel_id=1, source_target_pairs={{1,0},{2,1},{3,2},{4,3},{5,4},{6,5},{7,6},{9,8},{10,9},{11,10},{12... | collective-permute-start | bytes 18440 | tf_op jit(solution)/shard_map/ppermute | solution.py:15
  84.7 22.6 %copy-start.1 = (f32[32,10,6,130]{3,0,2,1:T(8,128)}, f32[32,10,6,130]{3,0,2,1:T(8,128)S(1)}, u32[]{:S(2)}) copy-start(f32[32,10,6,130]{3,0,2,1:T(8,128)S(1)} %select_maximum_fusion) | copy-start | bytes 2995204
  90.6 4.7 copy-start.2
  126.6 11.2 %copy-start = (f32[8,8,4,128]{3,2,1,0:T(4,128)S(1)}, f32[8,8,4,128]{3,2,1,0:T(4,128)}, u32[]{:S(2)}) copy-start(f32[8,8,4,128]{3,2,1,0:T(4,128)} %param.5) | copy-start | bytes 393220
  126.6 11.2 %copy-start.33 = (f32[32,8,4,128]{3,0,2,1:T(8,128)S(1)}, f32[32,8,4,128]{3,0,2,1:T(8,128)}, u32[]{:S(2)}) copy-start(f32[32,8,4,128]{3,0,2,1:T(8,128)} %get-tuple-element.26) | copy-start | bytes 1572868
  128.5 9.8 %copy-start.13 = (f32[32,8,4,128]{3,0,2,1:T(8,128)S(1)}, f32[32,8,4,128]{3,0,2,1:T(8,128)}, u32[]{:S(2)}) copy-start(f32[32,8,4,128]{3,0,2,1:T(8,128)} %get-tuple-element.28) | copy-start | bytes 1572868
  130.4 9.7 %copy-start.32 = (f32[32,8,4,128]{3,0,2,1:T(8,128)S(1)}, f32[32,8,4,128]{3,0,2,1:T(8,128)}, u32[]{:S(2)}) copy-start(f32[32,8,4,128]{3,0,2,1:T(8,128)} %get-tuple-element.25) | copy-start | bytes 1572868
  132.1 8.5 copy-start.31
  134.0 7.1 copy-start.30
  135.9 5.8 copy-start.29
  137.7 4.5 copy-start.28
  138.3 4.6 copy-start.27
  143.4 4.7 copy-start.11
  144.5 6.0 copy-start.4
  145.0 5.9 copy-start.10
  145.7 7.0 copy-start.14
  147.6 5.8 copy-start.8
  148.1 5.8 copy-start.17
  150.4 4.5 copy-start.24
  151.0 4.5 copy-start.23
  858.8 4.1 copy-start.53
  858.8 4.1 copy-start.54
  858.8 4.1 copy-start.55
  858.8 4.1 copy-start.56
  858.8 4.1 copy-start.57
  858.9 4.1 copy-start.58
  858.9 4.1 copy-start.59
  858.9 4.1 copy-start.60
  858.9 4.1 copy-start.61
  858.9 4.1 copy-start.62
  858.9 4.1 copy-start.63
  858.9 4.1 copy-start.64
  865.5 4.6 copy-start.18
  865.5 4.6 copy-start.36
  865.5 4.6 copy-start.37
  865.5 4.6 copy-start.38
  865.5 4.6 copy-start.39
  865.5 4.6 copy-start.49
  (27 other events, 60.9 us)
where the time goes:
time: 893 us; the launch traced here: 878 us
  blocking collectives  719 us (81%)
  matrix products  92.9 us (10%)
  starting transfers between devices  30.7 us (3%)
  local copies, waits for them, and re-layouts  25.6 us (3%)
    psum x1, blocking collectives, shards(): total_grad = lax.psum(local_grad, ('gx', 'gy'))  698 us
    dot_general x27, matrix products, forward_conv(): jnp.einsum('oc,czxy->ozxy', weights[:, :, depth, across, along], window,...  42.3 us
    dot_general x27, matrix products, backward_conv(): jnp.einsum('oc,ozxy->czxy', weights[:, :, depth, across, along], window,...  35.7 us
  transfers between devices with their start and end apart: 8, of which 0 were waited for; matrix products, arithmetic and copies ran while one was open for 3% of the time, Pallas kernels for 0%

commit v1 on v0

--- a/solution.py
+++ b/solution.py
@@ -87,7 +87,12 @@
     own_filters = lax.dynamic_slice_in_dim(all_rows, first, own_inputs, 1)
     input_grad = backward_conv(padded_up, own_filters, planes, rows_x, rows_y)
     local_grad = weight_terms(upstream, padded, planes, rows_x, rows_y)
-    total_grad = lax.psum(local_grad, ("gx", "gy"))
+    ncol = lax.axis_size("col")
+    flat = local_grad.reshape(-1, 128)
+    slots = jnp.zeros((ncol,) + flat.shape, jnp.float32)
+    slots = lax.dynamic_update_index_in_dim(slots, flat, lax.axis_index("col"), 0)
+    summed = lax.psum(slots, ("col", "gx", "gy"))
+    total_grad = summed[lax.axis_index("col")].reshape(local_grad.shape)
     return (response, input_grad, total_grad * scale)
 
 

time: 893 us -> 660 us (0.74); the launches traced: 878 us -> 655 us
  blocking collectives: 719 us -> 20.3 us
  waiting for transfers between devices: 0.02 us -> 439 us
  matrix products: 92.9 us -> 109 us
  between operations: 1.74 us -> 15.5 us
    psum x1 -> x0, blocking collectives: 698 us -> none  [shards(): total_grad = lax.psum(local_grad, ('gx', 'gy'))]
    psum x0 -> x1, waiting for transfers between devices: none -> 439 us  [shards(): summed = lax.psum(slots, ('col', 'gx', 'gy'))]
    dot_general x27, matrix products: 14.9 us -> 30.8 us  [weight_terms(): jnp.einsum('ozxy,czxy->oc', cotangent, window, precision=lax.Precision.HI...]
  transfers between devices with their start and end apart: 8 -> 9, of which waited for: 0 -> 1; matrix products, arithmetic and copies ran while one was open for 3% -> 7% of each run, Pallas kernels for 0% -> 0%
where the time goes in v1:
time: 660 us; the launch traced here: 655 us
  waiting for transfers between devices  439 us (67%)
  matrix products  109 us (17%)
  local copies, waits for them, and re-layouts  32.7 us (5%)
  starting transfers between devices  30.9 us (5%)
  blocking collectives  20.3 us (3%)
  between operations  15.5 us (2%)
  other arithmetic  7.59 us (1%)
    psum x1, waiting for transfers between devices, shards(): summed = lax.psum(slots, ('col', 'gx', 'gy'))  439 us
    dot_general x27, matrix products, forward_conv(): jnp.einsum('oc,czxy->ozxy', weights[:, :, depth, across, along], window,...  43.3 us
    dot_general x27, matrix products, backward_conv(): jnp.einsum('oc,ozxy->czxy', weights[:, :, depth, across, along], window,...  35 us
    dot_general x27, matrix products, weight_terms(): jnp.einsum('ozxy,czxy->oc', cotangent, window, precision=lax.Precision.HI...  30.8 us
    ppermute x4, starting transfers between devices, with_halo(): lax.ppermute(lax.slice_in_dim(block, 0, width, axis=dim), axis, backward)  16.6 us
    ppermute x4, starting transfers between devices, with_halo(): lax.ppermute(lax.slice_in_dim(block, block.shape[dim] - width, None, axis...  14.3 us
  transfers between devices with their start and end apart: 9, of which 1 were waited for; matrix products, arithmetic and copies ran while one was open for 7% of the time, Pallas kernels for 0%

profile of v1, /device:TPU:6, one launch (start us, length us, event | category | flops | bytes accessed | tf_op | source)
XLA Modules:
  0.0 655.0 jit_solution(1451040845485001192)
XLA Ops:
  8.2 6.8 %all_gather.9 = f32[32,8,4,128]{3,0,2,1:T(8,128)S(1)} all-gather(f32[8,8,4,128]{3,0,2,1:T(8,128)S(1)} %copy.126), channel_id=1, replica_groups=mesh['col'=4,'gx'=16,'gy'=8] {'col'}, dimensions={0}, use_global_device_ids=true | all-gather | bytes 655360 | tf_op jit(solution)/shard_map/all_gather | solution.py:80
  15.7 3.8 collective-permute-start
  21.8 7.0 %all_gather.11 = f32[32,8,4,128]{3,0,2,1:T(8,128)S(1)} all-gather(f32[8,8,4,128]{3,0,2,1:T(8,128)S(1)} %copy.134), channel_id=1, replica_groups=mesh['col'=4,'gx'=16,'gy'=8] {'col'}, dimensions={0}, use_global_device_ids=true | all-gather | bytes 655360 | tf_op jit(solution)/shard_map/all_gather | solution.py:84
  29.5 5.1 collective-permute-start.4
  35.9 6.6 %all_gather.10 = f32[32,32,3,3,3]{1,0,4,3,2:T(8,128)S(1)} all-gather(f32[8,32,3,3,3]{1,0,4,3,2:T(8,128)S(1)} %copy-done.66), channel_id=1, replica_groups=mesh['col'=4,'gx'=16,'gy'=8] {'col'}, dimensions={0}, use_global_device_ids=true | all-gather | bytes 138240 | tf_op jit(solution)/shard_map/all_gather | solution.py:83
  46.0 3.5 collective-permute-start.2
  50.4 6.0 collective-permute-start.3
  59.5 2.1 copy.135
  61.6 1.9 collective-permute-start.6
  64.4 8.1 %collective-permute-start.7 = (f32[32,8,6,1]{0,1,3,2:T(8,128)}, f32[32,8,6,1]{0,1,3,2:T(8,128)}, u32[]{:S(2)}, u32[]{:S(2)}) collective-permute-start(f32[32,8,6,1]{0,1,3,2:T(8,128)} %copy.136), channel_id=1, source_target_pairs={{1,0},{2,1},{3,2},{4,3},{5,4},{6,5},{7,6},{9,8},{10,9},{11,10},{12... | collective-permute-start | bytes 18440 | tf_op jit(solution)/shard_map/ppermute | solution.py:15
  72.5 1.7 fusion.208
  74.2 2.0 fusion.116
  76.3 2.0 fusion.112
  81.5 2.9 pad_maximum_fusion.9
  84.4 2.1 select_maximum_fusion.2
  87.5 2.0 copy.138
  89.5 1.9 select_maximum_fusion
  91.4 1.3 fusion.120
  102.0 1.3 fusion.83
  103.3 1.3 fusion.86
  114.0 1.4 fusion.96
  116.5 1.3 fusion.114
  117.8 4.3 fusion.309
  122.1 1.8 fusion.212
  123.9 1.8 fusion.214
  125.7 1.7 fusion.216
  127.5 1.8 fusion.218
  129.3 1.8 fusion.220
  131.1 1.7 fusion.222
  132.9 1.9 fusion.224
  134.8 1.9 fusion.226
  136.7 1.8 convolution_bitcast_fusion.6
  138.5 1.9 convolution_bitcast_fusion.7
  140.3 1.9 convolution_bitcast_fusion.8
  142.2 1.8 convolution_bitcast_fusion.9
  145.2 1.8 fusion.210
  158.6 1.8 fusion.206
  161.6 1.8 fusion.204
  165.6 1.8 convolution_bitcast_fusion.10
  182.4 1.7 copy.195
  184.0 1.7 broadcast_in_dim.8
  186.4 1.4 constant_dynamic-update-slice_fusion.10
  187.9 2.0 fusion.47
  194.4 1.3 fusion.14
  199.7 2.1 fusion.48
  201.9 1.3 fusion.49
  205.8 438.8 %all-reduce.4.cloned.1.call-done = f32[4,54,128]{2,1,0:T(8,128)} async-done(((f32[4,54,128]{2,1,0:T(8,128)}), f32[4,54,128]{2,1,0:T(8,128)}) %all-reduce.4.cloned.1.call-update) | async-done | bytes 110608 | tf_op jit(solution)/shard_map/psum | solution.py:94
  646.2 1.6 copy.198
  (222 shorter events, 82.2 us)
Async XLA Ops:
  7.2 28.7 %copy-start.66 = (f32[8,32,3,3,3]{1,0,4,3,2:T(8,128)S(1)}, f32[8,32,3,3,3]{1,0,4,3,2:T(8,128)}, u32[]{:S(2)}) copy-start(f32[8,32,3,3,3]{1,0,4,3,2:T(8,128)} %param.4) | copy-start | bytes 82948
  7.2 637.4 %all-reduce.4.cloned.1.call-start = ((), (), s32[]{:S(2)}) async-start(), calls=%async_computation | async-start | bytes 229376 | tf_op jit(solution)/shard_map/psum | solution.py:94
  15.0 28.9 %copy-start.3 = (f32[32,8,4,128]{3,0,2,1:T(8,128)}, f32[32,8,4,128]{3,0,2,1:T(8,128)S(1)}, u32[]{:S(2)}) copy-start(f32[32,8,4,128]{3,0,2,1:T(8,128)S(1)} %all_gather.9) | copy-start | bytes 1572868
  15.7 27.9 %collective-permute-start = (f32[32,8,1,128]{3,0,2,1:T(8,128)S(1)}, f32[32,8,1,128]{3,0,2,1:T(8,128)S(1)}, u32[]{:S(2)}, u32[]{:S(2)}) collective-permute-start(f32[32,8,1,128]{3,0,2,1:T(8,128)S(1)} %get-tuple-element.49), channel_id=1, source_target_pairs={{0,8},{8,16},{16,24},{24,32},{32,40},{40,48},{48,56},{56,64},{64,7... | collective-permute-start | bytes 393224 | tf_op jit(solution)/shard_map/ppermute | solution.py:12
  19.5 24.3 %collective-permute-start.1 = (f32[32,8,1,128]{3,0,2,1:T(8,128)}, f32[32,8,1,128]{3,0,2,1:T(8,128)S(1)}, u32[]{:S(2)}, u32[]{:S(2)}) collective-permute-start(f32[32,8,1,128]{3,0,2,1:T(8,128)} %get-tuple-element.48), channel_id=1, source_target_pairs={{8,0},{16,8},{24,16},{32,24},{40,32},{48,40},{56,48},{64,56},{72,6... | collective-permute-start | bytes 393224 | tf_op jit(solution)/shard_map/ppermute | solution.py:15
  29.5 26.8 %collective-permute-start.4 = (f32[32,8,1,128]{3,0,2,1:T(8,128)}, f32[32,8,1,128]{3,0,2,1:T(8,128)}, u32[]{:S(2)}, u32[]{:S(2)}) collective-permute-start(f32[32,8,1,128]{3,0,2,1:T(8,128)} %get-tuple-element.44), channel_id=1, source_target_pairs={{0,8},{8,16},{16,24},{24,32},{32,40},{40,48},{48,56},{56,64},{64,7... | collective-permute-start | bytes 393224 | tf_op jit(solution)/shard_map/ppermute | solution.py:12
  34.6 22.7 %collective-permute-start.5 = (f32[32,8,1,128]{3,0,2,1:T(8,128)}, f32[32,8,1,128]{3,0,2,1:T(8,128)}, u32[]{:S(2)}, u32[]{:S(2)}) collective-permute-start(f32[32,8,1,128]{3,0,2,1:T(8,128)} %get-tuple-element.43), channel_id=1, source_target_pairs={{8,0},{16,8},{24,16},{32,24},{40,32},{48,40},{56,48},{64,56},{72,6... | collective-permute-start | bytes 393224 | tf_op jit(solution)/shard_map/ppermute | solution.py:15
  46.0 32.3 %collective-permute-start.2 = (f32[32,8,6,1]{0,1,3,2:T(8,128)}, f32[32,8,6,1]{0,1,3,2:T(8,128)}, u32[]{:S(2)}, u32[]{:S(2)}) collective-permute-start(f32[32,8,6,1]{0,1,3,2:T(8,128)} %copy.127), channel_id=1, source_target_pairs={{0,1},{1,2},{2,3},{3,4},{4,5},{5,6},{6,7},{8,9},{9,10},{10,11},{11... | collective-permute-start | bytes 18440 | tf_op jit(solution)/shard_map/ppermute | solution.py:12
  50.4 29.0 %collective-permute-start.3 = (f32[32,8,6,1]{0,1,3,2:T(8,128)}, f32[32,8,6,1]{0,1,3,2:T(8,128)}, u32[]{:S(2)}, u32[]{:S(2)}) collective-permute-start(f32[32,8,6,1]{0,1,3,2:T(8,128)} %copy.128), channel_id=1, source_target_pairs={{1,0},{2,1},{3,2},{4,3},{5,4},{6,5},{7,6},{9,8},{10,9},{11,10},{12... | collective-permute-start | bytes 18440 | tf_op jit(solution)/shard_map/ppermute | solution.py:15
  58.3 14.2 %copy-start.20 = (f32[32,8,5,128]{3,0,2,1:T(8,128)S(1)}, f32[32,8,5,128]{3,0,2,1:T(8,128)}, u32[]{:S(2)}) copy-start(f32[32,8,5,128]{3,0,2,1:T(8,128)} %copy-done.19) | copy-start | bytes 1966084
  61.6 24.9 %collective-permute-start.6 = (f32[32,8,6,1]{0,1,3,2:T(8,128)}, f32[32,8,6,1]{0,1,3,2:T(8,128)}, u32[]{:S(2)}, u32[]{:S(2)}) collective-permute-start(f32[32,8,6,1]{0,1,3,2:T(8,128)} %copy.135), channel_id=1, source_target_pairs={{0,1},{1,2},{2,3},{3,4},{4,5},{5,6},{6,7},{8,9},{9,10},{10,11},{11... | collective-permute-start | bytes 18440 | tf_op jit(solution)/shard_map/ppermute | solution.py:12
  64.4 23.1 %collective-permute-start.7 = (f32[32,8,6,1]{0,1,3,2:T(8,128)}, f32[32,8,6,1]{0,1,3,2:T(8,128)}, u32[]{:S(2)}, u32[]{:S(2)}) collective-permute-start(f32[32,8,6,1]{0,1,3,2:T(8,128)} %copy.136), channel_id=1, source_target_pairs={{1,0},{2,1},{3,2},{4,3},{5,4},{6,5},{7,6},{9,8},{10,9},{11,10},{12... | collective-permute-start | bytes 18440 | tf_op jit(solution)/shard_map/ppermute | solution.py:15
  91.4 22.5 %copy-start.1 = (f32[32,10,6,130]{3,0,2,1:T(8,128)}, f32[32,10,6,130]{3,0,2,1:T(8,128)S(1)}, u32[]{:S(2)}) copy-start(f32[32,10,6,130]{3,0,2,1:T(8,128)S(1)} %select_maximum_fusion) | copy-start | bytes 2995204
  132.9 11.2 %copy-start = (f32[8,8,4,128]{3,2,1,0:T(4,128)S(1)}, f32[8,8,4,128]{3,2,1,0:T(4,128)}, u32[]{:S(2)}) copy-start(f32[8,8,4,128]{3,2,1,0:T(4,128)} %param.5) | copy-start | bytes 393220
  132.9 11.2 %copy-start.33 = (f32[32,8,4,128]{3,0,2,1:T(8,128)S(1)}, f32[32,8,4,128]{3,0,2,1:T(8,128)}, u32[]{:S(2)}) copy-start(f32[32,8,4,128]{3,0,2,1:T(8,128)} %get-tuple-element.29) | copy-start | bytes 1572868
  134.8 10.4 %copy-start.13 = (f32[32,8,4,128]{3,0,2,1:T(8,128)S(1)}, f32[32,8,4,128]{3,0,2,1:T(8,128)}, u32[]{:S(2)}) copy-start(f32[32,8,4,128]{3,0,2,1:T(8,128)} %get-tuple-element.31) | copy-start | bytes 1572868
  136.7 10.3 %copy-start.32 = (f32[32,8,4,128]{3,0,2,1:T(8,128)S(1)}, f32[32,8,4,128]{3,0,2,1:T(8,128)}, u32[]{:S(2)}) copy-start(f32[32,8,4,128]{3,0,2,1:T(8,128)} %get-tuple-element.28) | copy-start | bytes 1572868
  138.4 9.7 %copy-start.31 = (f32[32,8,4,128]{3,0,2,1:T(8,128)S(1)}, f32[32,8,4,128]{3,0,2,1:T(8,128)}, u32[]{:S(2)}) copy-start(f32[32,8,4,128]{3,0,2,1:T(8,128)} %get-tuple-element.27) | copy-start | bytes 1572868
  140.3 8.9 %copy-start.30 = (f32[32,8,4,128]{3,0,2,1:T(8,128)S(1)}, f32[32,8,4,128]{3,0,2,1:T(8,128)}, u32[]{:S(2)}) copy-start(f32[32,8,4,128]{3,0,2,1:T(8,128)} %get-tuple-element.26) | copy-start | bytes 1572868
  142.2 8.2 %copy-start.29 = (f32[32,8,4,128]{3,0,2,1:T(8,128)S(1)}, f32[32,8,4,128]{3,0,2,1:T(8,128)}, u32[]{:S(2)}) copy-start(f32[32,8,4,128]{3,0,2,1:T(8,128)} %get-tuple-element.25) | copy-start | bytes 1572868
  144.0 7.5 %copy-start.28 = (f32[32,8,4,128]{3,0,2,1:T(8,128)S(1)}, f32[32,8,4,128]{3,0,2,1:T(8,128)}, u32[]{:S(2)}) copy-start(f32[32,8,4,128]{3,0,2,1:T(8,128)} %get-tuple-element.24) | copy-start | bytes 1572868
  145.2 7.5 %copy-start.27 = (f32[32,8,4,128]{3,0,2,1:T(8,128)S(1)}, f32[32,8,4,128]{3,0,2,1:T(8,128)}, u32[]{:S(2)}) copy-start(f32[32,8,4,128]{3,0,2,1:T(8,128)} %get-tuple-element.23) | copy-start | bytes 1572868
  147.0 6.9 %copy-start.26 = (f32[32,8,4,128]{3,0,2,1:T(8,128)S(1)}, f32[32,8,4,128]{3,0,2,1:T(8,128)}, u32[]{:S(2)}) copy-start(f32[32,8,4,128]{3,0,2,1:T(8,128)} %get-tuple-element.22) | copy-start | bytes 1572868
  148.1 6.9 %copy-start.25 = (f32[32,8,4,128]{3,0,2,1:T(8,128)S(1)}, f32[32,8,4,128]{3,0,2,1:T(8,128)}, u32[]{:S(2)}) copy-start(f32[32,8,4,128]{3,0,2,1:T(8,128)} %get-tuple-element.21) | copy-start | bytes 1572868
  150.4 7.0 %copy-start.21 = (f32[32,8,5,128]{3,0,2,1:T(8,128)S(1)}, f32[32,8,5,128]{3,0,2,1:T(8,128)}, u32[]{:S(2)}) copy-start(f32[32,8,5,128]{3,0,2,1:T(8,128)} %copy-done.19) | copy-start | bytes 1966084
  151.5 7.1 %copy-start.12 = (f32[32,8,4,128]{3,0,2,1:T(8,128)S(1)}, f32[32,8,4,128]{3,0,2,1:T(8,128)}, u32[]{:S(2)}) copy-start(f32[32,8,4,128]{3,0,2,1:T(8,128)} %get-tuple-element.39) | copy-start | bytes 1572868
  153.8 7.7 %copy-start.11 = (f32[32,8,4,128]{3,0,2,1:T(8,128)S(1)}, f32[32,8,4,128]{3,0,2,1:T(8,128)}, u32[]{:S(2)}) copy-start(f32[32,8,4,128]{3,0,2,1:T(8,128)} %get-tuple-element.32) | copy-start | bytes 1572868
  156.1 8.4 %copy-start.4 = (f32[32,8,4,128]{3,0,2,1:T(8,128)S(1)}, f32[32,8,4,128]{3,0,2,1:T(8,128)}, u32[]{:S(2)}) copy-start(f32[32,8,4,128]{3,0,2,1:T(8,128)} %copy-done.3) | copy-start | bytes 1572868
  157.5 8.2 %copy-start.10 = (f32[32,8,4,128]{3,0,2,1:T(8,128)S(1)}, f32[32,8,4,128]{3,0,2,1:T(8,128)}, u32[]{:S(2)}) copy-start(f32[32,8,4,128]{3,0,2,1:T(8,128)} %get-tuple-element.38) | copy-start | bytes 1572868
  158.6 8.8 %copy-start.14 = (f32[32,8,4,128]{3,0,2,1:T(8,128)S(1)}, f32[32,8,4,128]{3,0,2,1:T(8,128)}, u32[]{:S(2)}) copy-start(f32[32,8,4,128]{3,0,2,1:T(8,128)} %get-tuple-element.40) | copy-start | bytes 1572868
  160.4 8.2 %copy-start.8 = (f32[32,8,4,128]{3,0,2,1:T(8,128)S(1)}, f32[32,8,4,128]{3,0,2,1:T(8,128)}, u32[]{:S(2)}) copy-start(f32[32,8,4,128]{3,0,2,1:T(8,128)} %get-tuple-element.30) | copy-start | bytes 1572868
  161.6 8.2 %copy-start.17 = (f32[32,8,5,128]{3,0,2,1:T(8,128)S(1)}, f32[32,8,5,128]{3,0,2,1:T(8,128)}, u32[]{:S(2)}) copy-start(f32[32,8,5,128]{3,0,2,1:T(8,128)} %copy-done.16) | copy-start | bytes 1966084
  164.5 7.5 %copy-start.24 = (f32[32,8,4,128]{3,0,2,1:T(8,128)S(1)}, f32[32,8,4,128]{3,0,2,1:T(8,128)}, u32[]{:S(2)}) copy-start(f32[32,8,4,128]{3,0,2,1:T(8,128)} %get-tuple-element.20) | copy-start | bytes 1572868
  165.6 7.5 %copy-start.23 = (f32[32,8,4,128]{3,0,2,1:T(8,128)S(1)}, f32[32,8,4,128]{3,0,2,1:T(8,128)}, u32[]{:S(2)}) copy-start(f32[32,8,4,128]{3,0,2,1:T(8,128)} %get-tuple-element.19) | copy-start | bytes 1572868
  167.4 6.9 %copy-start.22 = (f32[32,8,4,128]{3,0,2,1:T(8,128)S(1)}, f32[32,8,4,128]{3,0,2,1:T(8,128)}, u32[]{:S(2)}) copy-start(f32[32,8,4,128]{3,0,2,1:T(8,128)} %get-tuple-element.18) | copy-start | bytes 1572868
  187.8 5.4 copy-start.18
  187.8 5.4 copy-start.36
  187.8 5.4 copy-start.37
  187.8 5.4 copy-start.38
  187.8 5.4 copy-start.39
  187.8 5.4 copy-start.40
  194.3 5.2 copy-start.41
  194.3 5.2 copy-start.42
  194.3 5.2 copy-start.43
  194.3 5.2 copy-start.44
  194.4 5.2 copy-start.55
  194.4 5.2 copy-start.56
  194.4 5.2 copy-start.57
  (28 other events, 110.1 us)
Sparse Core Ops, SparseCore 0:
  187.9 456.6 all-reduce.3

commit v2 on v0

--- a/solution.py
+++ b/solution.py
@@ -15,6 +15,17 @@
         high = lax.ppermute(lax.slice_in_dim(block, 0, width, axis=dim), axis, backward)
         block = jnp.concatenate([low, block, high], axis=dim)
     return block
+
+
+def butterfly_sum(value, axes):
+    for axis in axes:
+        count = lax.axis_size(axis)
+        step = 1
+        while step < count:
+            pairs = [(i, i ^ step) for i in range(count)]
+            value = value + lax.ppermute(value, axis, pairs)
+            step *= 2
+    return value
 
 
 def pad_depth(field):
@@ -87,7 +98,13 @@
     own_filters = lax.dynamic_slice_in_dim(all_rows, first, own_inputs, 1)
     input_grad = backward_conv(padded_up, own_filters, planes, rows_x, rows_y)
     local_grad = weight_terms(upstream, padded, planes, rows_x, rows_y)
-    total_grad = lax.psum(local_grad, ("gx", "gy"))
+    flat = local_grad.reshape(-1, 128)
+    sizes = [lax.axis_size(a) for a in ("gx", "gy")]
+    if all(n & (n - 1) == 0 for n in sizes):
+        flat = butterfly_sum(flat, ("gx", "gy"))
+    else:
+        flat = lax.psum(flat, ("gx", "gy"))
+    total_grad = flat.reshape(local_grad.shape)
     return (response, input_grad, total_grad * scale)
 
 

time: 893 us -> 257 us (0.29)
  the two profiles are of different devices: /device:TPU:6 before, /device:TPU:64 now
where the time goes in v2:
time: 257 us; the launch traced here: 252 us
  matrix products  108 us (42%)
  starting transfers between devices  72.1 us (28%)
  local copies, waits for them, and re-layouts  32.8 us (13%)
  blocking collectives  20.6 us (8%)
  waiting for transfers between devices  9.5 us (4%)
  other arithmetic  6.89 us (3%)
    ppermute x7, starting transfers between devices, butterfly_sum(): value = value + lax.ppermute(value, axis, pairs)  47 us
    dot_general x27, matrix products, forward_conv(): jnp.einsum('oc,czxy->ozxy', weights[:, :, depth, across, along], window,...  42.3 us
    dot_general x27, matrix products, backward_conv(): jnp.einsum('oc,ozxy->czxy', weights[:, :, depth, across, along], window,...  35 us
    dot_general x27, matrix products, weight_terms(): jnp.einsum('ozxy,czxy->oc', cotangent, window, precision=lax.Precision.HI...  30.8 us
    ppermute x4, starting transfers between devices, with_halo(): lax.ppermute(lax.slice_in_dim(block, block.shape[dim] - width, None, axis...  18 us
    ppermute x7, waiting for transfers between devices, butterfly_sum(): value = value + lax.ppermute(value, axis, pairs)  9.48 us
    unnamed x145, local copies, waits for them, and re-layouts  8.14 us
    all_gather x1, blocking collectives, shards(): gathered = lax.all_gather(volume, 'col', axis=0, tiled=True)  7.17 us
  transfers between devices with their start and end apart: 15, of which 5 were waited for; matrix products, arithmetic and copies ran while one was open for 18% of the time, Pallas kernels for 0%

profile of v2, /device:TPU:64, one launch (start us, length us, event | category | flops | bytes accessed | tf_op | source)
XLA Modules:
  0.0 252.1 jit_solution(1571422571538717983)
XLA Ops:
  1.7 7.2 %all_gather.9 = f32[32,8,4,128]{3,0,2,1:T(8,128)S(1)} all-gather(f32[8,8,4,128]{3,0,2,1:T(8,128)S(1)} %copy.126), channel_id=1, replica_groups=mesh['col'=4,'gx'=16,'gy'=8] {'col'}, dimensions={0}, use_global_device_ids=true | all-gather | bytes 655360 | tf_op jit(solution)/shard_map/all_gather | solution.py:91
  9.6 3.8 %collective-permute-start = (f32[32,8,1,128]{3,0,2,1:T(8,128)S(1)}, f32[32,8,1,128]{3,0,2,1:T(8,128)S(1)}, u32[]{:S(2)}, u32[]{:S(2)}) collective-permute-start(f32[32,8,1,128]{3,0,2,1:T(8,128)S(1)} %get-tuple-element.49), channel_id=1, source_target_pairs={{0,8},{8,16},{16,24},{24,32},{32,40},{40,48},{48,56},{56,64},{64,7... | collective-permute-start | bytes 393224 | tf_op jit(solution)/shard_map/ppermute | solution.py:12
  13.4 2.0 collective-permute-start.1
  16.4 6.9 %all_gather.11 = f32[32,8,4,128]{3,0,2,1:T(8,128)S(1)} all-gather(f32[8,8,4,128]{3,0,2,1:T(8,128)S(1)} %copy.134), channel_id=1, replica_groups=mesh['col'=4,'gx'=16,'gy'=8] {'col'}, dimensions={0}, use_global_device_ids=true | all-gather | bytes 655360 | tf_op jit(solution)/shard_map/all_gather | solution.py:95
  24.0 5.0 %collective-permute-start.4 = (f32[32,8,1,128]{3,0,2,1:T(8,128)S(1)}, f32[32,8,1,128]{3,0,2,1:T(8,128)}, u32[]{:S(2)}, u32[]{:S(2)}) collective-permute-start(f32[32,8,1,128]{3,0,2,1:T(8,128)S(1)} %get-tuple-element.44), channel_id=1, source_target_pairs={{0,8},{8,16},{16,24},{24,32},{32,40},{40,48},{48,56},{56,64},{64,7... | collective-permute-start | bytes 393224 | tf_op jit(solution)/shard_map/ppermute | solution.py:12
  29.0 1.9 collective-permute-start.5
  31.0 6.6 %all_gather.10 = f32[32,32,3,3,3]{1,0,4,3,2:T(8,128)S(1)} all-gather(f32[8,32,3,3,3]{1,0,4,3,2:T(8,128)S(1)} %copy-done.66), channel_id=1, replica_groups=mesh['col'=4,'gx'=16,'gy'=8] {'col'}, dimensions={0}, use_global_device_ids=true | all-gather | bytes 138240 | tf_op jit(solution)/shard_map/all_gather | solution.py:94
  40.9 2.1 copy.127
  43.0 4.1 %collective-permute-start.2 = (f32[32,8,6,1]{0,1,3,2:T(8,128)}, f32[32,8,6,1]{0,1,3,2:T(8,128)}, u32[]{:S(2)}, u32[]{:S(2)}) collective-permute-start(f32[32,8,6,1]{0,1,3,2:T(8,128)} %copy.127), channel_id=1, source_target_pairs={{0,1},{1,2},{2,3},{3,4},{4,5},{5,6},{6,7},{8,9},{9,10},{10,11},{11... | collective-permute-start | bytes 18440 | tf_op jit(solution)/shard_map/ppermute | solution.py:12
  52.4 2.1 copy.135
  54.5 5.1 %collective-permute-start.6 = (f32[32,8,6,1]{0,1,3,2:T(8,128)}, f32[32,8,6,1]{0,1,3,2:T(8,128)}, u32[]{:S(2)}, u32[]{:S(2)}) collective-permute-start(f32[32,8,6,1]{0,1,3,2:T(8,128)} %copy.135), channel_id=1, source_target_pairs={{0,1},{1,2},{2,3},{3,4},{4,5},{5,6},{6,7},{8,9},{9,10},{10,11},{11... | collective-permute-start | bytes 18440 | tf_op jit(solution)/shard_map/ppermute | solution.py:12
  60.6 1.8 collective-permute-start.7
  62.4 1.7 fusion.208
  64.1 2.0 fusion.116
  66.2 2.0 fusion.112
  71.4 2.9 %pad_maximum_fusion.9 = (f32[32,8,4,128]{3,0,2,1:T(8,128)}, f32[32,8,4,128]{3,0,2,1:T(8,128)}, f32[32,8,4,128]{3,0,2,1:T(8,128)}, f32[32,8,4,128]{3,0,2,1:T(8,12...) fusion(f32[32,8,6,128]{3,0,2,1:T(8,128)S(1)} %get-tuple-element.51, f32[32,8,6,1]{3,0,2,1:T(8,128)S(1)} %copy.129, ...), kind=kLoop, calls=%fused_computation.202 | loop fusion | flops 786432 | bytes 3944448 | tf_op jit(solution)/shard_map/concatenate | solution.py:16
  74.3 2.1 select_maximum_fusion.2
  77.5 2.0 copy.138
  79.5 1.9 select_maximum_fusion
  107.9 4.3 %fusion.309 = (f32[32,8,4,128]{3,0,2,1:T(8,128)S(1)}, f32[32,8,4,128]{3,0,2,1:T(8,128)S(1)}, f32[32,8,4,128]{3,0,2,1:T(8,128)S(1)}, f32[32,8,4,128]{3,0,2,1:T(8,...) fusion(f32[32,10,6,130]{3,0,2,1:T(8,128)S(1)} %select_maximum_f, ...), kind=kLoop, calls=%fused_computation.415 | loop fusion | bytes 18874368 | tf_op jit(solution)/shard_map/slice | solution.py:40
  112.2 1.8 fusion.212
  114.0 1.8 fusion.214
  115.8 1.7 fusion.216
  117.6 1.8 fusion.218
  119.4 1.8 fusion.220
  121.2 1.7 fusion.222
  123.0 1.9 fusion.224
  124.9 1.9 fusion.226
  126.8 1.8 convolution_bitcast_fusion.6
  128.5 1.9 convolution_bitcast_fusion.7
  130.4 1.9 convolution_bitcast_fusion.8
  132.3 1.8 convolution_bitcast_fusion.9
  135.3 1.8 fusion.210
  148.7 1.8 fusion.206
  151.7 1.8 fusion.204
  170.7 1.7 copy.195
  172.3 1.7 reshape_reshape.3
  174.2 5.2 %collective-permute-start.8 = (f32[54,128]{1,0:T(8,128)}, f32[54,128]{1,0:T(8,128)S(1)}, u32[]{:S(2)}, u32[]{:S(2)}) collective-permute-start(f32[54,128]{1,0:T(8,128)} %reshape_reshape.3), channel_id=1, source_target_pairs={{0,8},{8,0},{16,24},{24,16},{32,40},{40,32},{48,56},{56,48},{64,72... | collective-permute-start | bytes 82952 | tf_op jit(solution)/shard_map/ppermute | solution.py:26
  179.3 1.9 fusion.47
  184.9 1.9 fusion.48
  189.5 1.9 collective-permute-start.9
  192.6 3.6 %collective-permute-done.9 = f32[54,128]{1,0:T(8,128)S(1)} collective-permute-done((f32[54,128]{1,0:T(8,128)S(1)}, f32[54,128]{1,0:T(8,128)S(1)}, u32[]{:S(2)}, u32[]{:S(2)}) %collective-permute-start.9) | collective-permute-done | bytes 27680 | tf_op jit(solution)/shard_map/ppermute | solution.py:26
  196.2 9.1 %collective-permute-start.10 = (f32[54,128]{1,0:T(8,128)S(1)}, f32[54,128]{1,0:T(8,128)S(1)}, u32[]{:S(2)}, u32[]{:S(2)}) collective-permute-start(f32[54,128]{1,0:T(8,128)S(1)} %add.245), channel_id=1, source_target_pairs={{0,32},{8,40},{16,48},{24,56},{32,0},{40,8},{48,16},{56,24},{64,96... | collective-permute-start | bytes 82952 | tf_op jit(solution)/shard_map/ppermute | solution.py:26
  207.1 10.0 %collective-permute-start.11 = (f32[54,128]{1,0:T(8,128)S(1)}, f32[54,128]{1,0:T(8,128)S(1)}, u32[]{:S(2)}, u32[]{:S(2)}) collective-permute-start(f32[54,128]{1,0:T(8,128)S(1)} %add.246), channel_id=1, source_target_pairs={{0,64},{8,72},{16,80},{24,88},{32,96},{40,104},{48,112},{56,120},{... | collective-permute-start | bytes 82952 | tf_op jit(solution)/shard_map/ppermute | solution.py:26
  218.4 3.9 %collective-permute-done.11 = f32[54,128]{1,0:T(8,128)S(1)} collective-permute-done((f32[54,128]{1,0:T(8,128)S(1)}, f32[54,128]{1,0:T(8,128)S(1)}, u32[]{:S(2)}, u32[]{:S(2)}) %collective-permute-start.11) | collective-permute-done | bytes 27680 | tf_op jit(solution)/shard_map/ppermute | solution.py:26
  222.2 4.3 %collective-permute-start.12 = (f32[54,128]{1,0:T(8,128)S(1)}, f32[54,128]{1,0:T(8,128)S(1)}, u32[]{:S(2)}, u32[]{:S(2)}) collective-permute-start(f32[54,128]{1,0:T(8,128)S(1)} %add.247), channel_id=1, source_target_pairs={{0,1},{1,0},{2,3},{3,2},{4,5},{5,4},{6,7},{7,6},{8,9},{9,8},{10,11... | collective-permute-start | bytes 82952 | tf_op jit(solution)/shard_map/ppermute | solution.py:26
  228.4 7.8 %collective-permute-start.13 = (f32[54,128]{1,0:T(8,128)S(1)}, f32[54,128]{1,0:T(8,128)S(1)}, u32[]{:S(2)}, u32[]{:S(2)}) collective-permute-start(f32[54,128]{1,0:T(8,128)S(1)} %add.248), channel_id=1, source_target_pairs={{0,2},{1,3},{2,0},{3,1},{4,6},{5,7},{6,4},{7,5},{8,10},{9,11},{10,... | collective-permute-start | bytes 82952 | tf_op jit(solution)/shard_map/ppermute | solution.py:26
  238.1 8.7 %collective-permute-start.14 = (f32[54,128]{1,0:T(8,128)S(1)}, f32[54,128]{1,0:T(8,128)S(1)}, u32[]{:S(2)}, u32[]{:S(2)}) collective-permute-start(f32[54,128]{1,0:T(8,128)S(1)} %add.249), channel_id=1, source_target_pairs={{0,4},{1,5},{2,6},{3,7},{4,0},{5,1},{6,2},{7,3},{8,12},{9,13},{10,... | collective-permute-start | bytes 82952 | tf_op jit(solution)/shard_map/ppermute | solution.py:26
  (239 shorter events, 93.5 us)
Async XLA Ops:
  0.6 30.3 %copy-start.66 = (f32[8,32,3,3,3]{1,0,4,3,2:T(8,128)S(1)}, f32[8,32,3,3,3]{1,0,4,3,2:T(8,128)}, u32[]{:S(2)}) copy-start(f32[8,32,3,3,3]{1,0,4,3,2:T(8,128)} %param.4) | copy-start | bytes 82948
  8.8 30.0 %copy-start.3 = (f32[32,8,4,128]{3,0,2,1:T(8,128)}, f32[32,8,4,128]{3,0,2,1:T(8,128)S(1)}, u32[]{:S(2)}) copy-start(f32[32,8,4,128]{3,0,2,1:T(8,128)S(1)} %all_gather.9) | copy-start | bytes 1572868
  9.6 29.1 %collective-permute-start = (f32[32,8,1,128]{3,0,2,1:T(8,128)S(1)}, f32[32,8,1,128]{3,0,2,1:T(8,128)S(1)}, u32[]{:S(2)}, u32[]{:S(2)}) collective-permute-start(f32[32,8,1,128]{3,0,2,1:T(8,128)S(1)} %get-tuple-element.49), channel_id=1, source_target_pairs={{0,8},{8,16},{16,24},{24,32},{32,40},{40,48},{48,56},{56,64},{64,7... | collective-permute-start | bytes 393224 | tf_op jit(solution)/shard_map/ppermute | solution.py:12
  13.4 25.5 %collective-permute-start.1 = (f32[32,8,1,128]{3,0,2,1:T(8,128)}, f32[32,8,1,128]{3,0,2,1:T(8,128)S(1)}, u32[]{:S(2)}, u32[]{:S(2)}) collective-permute-start(f32[32,8,1,128]{3,0,2,1:T(8,128)} %get-tuple-element.48), channel_id=1, source_target_pairs={{8,0},{16,8},{24,16},{32,24},{40,32},{48,40},{56,48},{64,56},{72,6... | collective-permute-start | bytes 393224 | tf_op jit(solution)/shard_map/ppermute | solution.py:15
  24.0 25.3 %collective-permute-start.4 = (f32[32,8,1,128]{3,0,2,1:T(8,128)S(1)}, f32[32,8,1,128]{3,0,2,1:T(8,128)}, u32[]{:S(2)}, u32[]{:S(2)}) collective-permute-start(f32[32,8,1,128]{3,0,2,1:T(8,128)S(1)} %get-tuple-element.44), channel_id=1, source_target_pairs={{0,8},{8,16},{16,24},{24,32},{32,40},{40,48},{48,56},{56,64},{64,7... | collective-permute-start | bytes 393224 | tf_op jit(solution)/shard_map/ppermute | solution.py:12
  29.0 21.3 %collective-permute-start.5 = (f32[32,8,1,128]{3,0,2,1:T(8,128)}, f32[32,8,1,128]{3,0,2,1:T(8,128)}, u32[]{:S(2)}, u32[]{:S(2)}) collective-permute-start(f32[32,8,1,128]{3,0,2,1:T(8,128)} %get-tuple-element.43), channel_id=1, source_target_pairs={{8,0},{16,8},{24,16},{32,24},{40,32},{48,40},{56,48},{64,56},{72,6... | collective-permute-start | bytes 393224 | tf_op jit(solution)/shard_map/ppermute | solution.py:15
  43.0 25.2 %collective-permute-start.2 = (f32[32,8,6,1]{0,1,3,2:T(8,128)}, f32[32,8,6,1]{0,1,3,2:T(8,128)}, u32[]{:S(2)}, u32[]{:S(2)}) collective-permute-start(f32[32,8,6,1]{0,1,3,2:T(8,128)} %copy.127), channel_id=1, source_target_pairs={{0,1},{1,2},{2,3},{3,4},{4,5},{5,6},{6,7},{8,9},{9,10},{10,11},{11... | collective-permute-start | bytes 18440 | tf_op jit(solution)/shard_map/ppermute | solution.py:12
  48.0 21.3 %collective-permute-start.3 = (f32[32,8,6,1]{0,1,3,2:T(8,128)}, f32[32,8,6,1]{0,1,3,2:T(8,128)}, u32[]{:S(2)}, u32[]{:S(2)}) collective-permute-start(f32[32,8,6,1]{0,1,3,2:T(8,128)} %copy.128), channel_id=1, source_target_pairs={{1,0},{2,1},{3,2},{4,3},{5,4},{6,5},{7,6},{9,8},{10,9},{11,10},{12... | collective-permute-start | bytes 18440 | tf_op jit(solution)/shard_map/ppermute | solution.py:15
  51.2 11.2 %copy-start.21 = (f32[32,8,5,128]{3,0,2,1:T(8,128)S(1)}, f32[32,8,5,128]{3,0,2,1:T(8,128)}, u32[]{:S(2)}) copy-start(f32[32,8,5,128]{3,0,2,1:T(8,128)} %copy-done.20) | copy-start | bytes 1966084
  54.5 21.9 %collective-permute-start.6 = (f32[32,8,6,1]{0,1,3,2:T(8,128)}, f32[32,8,6,1]{0,1,3,2:T(8,128)}, u32[]{:S(2)}, u32[]{:S(2)}) collective-permute-start(f32[32,8,6,1]{0,1,3,2:T(8,128)} %copy.135), channel_id=1, source_target_pairs={{0,1},{1,2},{2,3},{3,4},{4,5},{5,6},{6,7},{8,9},{9,10},{10,11},{11... | collective-permute-start | bytes 18440 | tf_op jit(solution)/shard_map/ppermute | solution.py:12
  60.6 16.9 %collective-permute-start.7 = (f32[32,8,6,1]{0,1,3,2:T(8,128)}, f32[32,8,6,1]{0,1,3,2:T(8,128)}, u32[]{:S(2)}, u32[]{:S(2)}) collective-permute-start(f32[32,8,6,1]{0,1,3,2:T(8,128)} %copy.136), channel_id=1, source_target_pairs={{1,0},{2,1},{3,2},{4,3},{5,4},{6,5},{7,6},{9,8},{10,9},{11,10},{12... | collective-permute-start | bytes 18440 | tf_op jit(solution)/shard_map/ppermute | solution.py:15
  81.4 22.6 %copy-start.1 = (f32[32,10,6,130]{3,0,2,1:T(8,128)}, f32[32,10,6,130]{3,0,2,1:T(8,128)S(1)}, u32[]{:S(2)}) copy-start(f32[32,10,6,130]{3,0,2,1:T(8,128)S(1)} %select_maximum_fusion) | copy-start | bytes 2995204
  123.0 11.2 %copy-start = (f32[8,8,4,128]{3,2,1,0:T(4,128)S(1)}, f32[8,8,4,128]{3,2,1,0:T(4,128)}, u32[]{:S(2)}) copy-start(f32[8,8,4,128]{3,2,1,0:T(4,128)} %param.5) | copy-start | bytes 393220
  123.0 11.2 %copy-start.34 = (f32[32,8,4,128]{3,0,2,1:T(8,128)S(1)}, f32[32,8,4,128]{3,0,2,1:T(8,128)}, u32[]{:S(2)}) copy-start(f32[32,8,4,128]{3,0,2,1:T(8,128)} %get-tuple-element.29) | copy-start | bytes 1572868
  124.9 10.4 %copy-start.14 = (f32[32,8,4,128]{3,0,2,1:T(8,128)S(1)}, f32[32,8,4,128]{3,0,2,1:T(8,128)}, u32[]{:S(2)}) copy-start(f32[32,8,4,128]{3,0,2,1:T(8,128)} %get-tuple-element.31) | copy-start | bytes 1572868
  126.8 10.3 %copy-start.33 = (f32[32,8,4,128]{3,0,2,1:T(8,128)S(1)}, f32[32,8,4,128]{3,0,2,1:T(8,128)}, u32[]{:S(2)}) copy-start(f32[32,8,4,128]{3,0,2,1:T(8,128)} %get-tuple-element.28) | copy-start | bytes 1572868
  128.5 9.7 %copy-start.32 = (f32[32,8,4,128]{3,0,2,1:T(8,128)S(1)}, f32[32,8,4,128]{3,0,2,1:T(8,128)}, u32[]{:S(2)}) copy-start(f32[32,8,4,128]{3,0,2,1:T(8,128)} %get-tuple-element.27) | copy-start | bytes 1572868
  130.4 8.9 %copy-start.31 = (f32[32,8,4,128]{3,0,2,1:T(8,128)S(1)}, f32[32,8,4,128]{3,0,2,1:T(8,128)}, u32[]{:S(2)}) copy-start(f32[32,8,4,128]{3,0,2,1:T(8,128)} %get-tuple-element.26) | copy-start | bytes 1572868
  132.3 8.2 %copy-start.30 = (f32[32,8,4,128]{3,0,2,1:T(8,128)S(1)}, f32[32,8,4,128]{3,0,2,1:T(8,128)}, u32[]{:S(2)}) copy-start(f32[32,8,4,128]{3,0,2,1:T(8,128)} %get-tuple-element.25) | copy-start | bytes 1572868
  134.1 7.5 %copy-start.29 = (f32[32,8,4,128]{3,0,2,1:T(8,128)S(1)}, f32[32,8,4,128]{3,0,2,1:T(8,128)}, u32[]{:S(2)}) copy-start(f32[32,8,4,128]{3,0,2,1:T(8,128)} %get-tuple-element.24) | copy-start | bytes 1572868
  135.3 7.5 %copy-start.28 = (f32[32,8,4,128]{3,0,2,1:T(8,128)S(1)}, f32[32,8,4,128]{3,0,2,1:T(8,128)}, u32[]{:S(2)}) copy-start(f32[32,8,4,128]{3,0,2,1:T(8,128)} %get-tuple-element.23) | copy-start | bytes 1572868
  143.9 7.7 %copy-start.12 = (f32[32,8,4,128]{3,0,2,1:T(8,128)S(1)}, f32[32,8,4,128]{3,0,2,1:T(8,128)}, u32[]{:S(2)}) copy-start(f32[32,8,4,128]{3,0,2,1:T(8,128)} %get-tuple-element.32) | copy-start | bytes 1572868
  146.2 8.4 %copy-start.4 = (f32[32,8,4,128]{3,0,2,1:T(8,128)S(1)}, f32[32,8,4,128]{3,0,2,1:T(8,128)}, u32[]{:S(2)}) copy-start(f32[32,8,4,128]{3,0,2,1:T(8,128)} %copy-done.3) | copy-start | bytes 1572868
  147.6 8.2 %copy-start.15 = (f32[32,8,4,128]{3,0,2,1:T(8,128)S(1)}, f32[32,8,4,128]{3,0,2,1:T(8,128)}, u32[]{:S(2)}) copy-start(f32[32,8,4,128]{3,0,2,1:T(8,128)} %get-tuple-element.40) | copy-start | bytes 1572868
  148.7 8.1 %copy-start.10 = (f32[32,8,4,128]{3,0,2,1:T(8,128)S(1)}, f32[32,8,4,128]{3,0,2,1:T(8,128)}, u32[]{:S(2)}) copy-start(f32[32,8,4,128]{3,0,2,1:T(8,128)} %get-tuple-element.30) | copy-start | bytes 1572868
  150.5 7.5 %copy-start.18 = (f32[32,8,5,128]{3,0,2,1:T(8,128)S(1)}, f32[32,8,5,128]{3,0,2,1:T(8,128)}, u32[]{:S(2)}) copy-start(f32[32,8,5,128]{3,0,2,1:T(8,128)} %copy-done.17) | copy-start | bytes 1966084
  174.0 8.3 %copy-start.16 = (f32[32,8,4,128]{3,0,2,1:T(8,128)S(1)}, f32[32,8,4,128]{3,0,2,1:T(8,128)}, u32[]{:S(2)}) copy-start(f32[32,8,4,128]{3,0,2,1:T(8,128)} %get-tuple-element.40) | copy-start | bytes 1572868
  174.0 9.6 %copy-start.11 = (f32[32,8,4,128]{3,0,2,1:T(8,128)S(1)}, f32[32,8,4,128]{3,0,2,1:T(8,128)}, u32[]{:S(2)}) copy-start(f32[32,8,4,128]{3,0,2,1:T(8,128)} %get-tuple-element.30) | copy-start | bytes 1572868
  174.0 10.7 %copy-start.41 = (f32[8,8,4,128]{3,0,2,1:T(8,128)S(1)}, f32[8,8,4,128]{3,0,2,1:T(8,128)}, u32[]{:S(2)}) copy-start(f32[8,8,4,128]{3,0,2,1:T(8,128)} %fusion.116) | copy-start | bytes 393220
  174.0 10.8 %copy-start.42 = (f32[8,8,4,128]{3,0,2,1:T(8,128)S(1)}, f32[8,8,4,128]{3,0,2,1:T(8,128)}, u32[]{:S(2)}) copy-start(f32[8,8,4,128]{3,0,2,1:T(8,128)} %fusion.83) | copy-start | bytes 393220
  174.1 10.8 %copy-start.43 = (f32[8,8,4,128]{3,0,2,1:T(8,128)S(1)}, f32[8,8,4,128]{3,0,2,1:T(8,128)}, u32[]{:S(2)}) copy-start(f32[8,8,4,128]{3,0,2,1:T(8,128)} %fusion.86) | copy-start | bytes 393220
  174.1 10.8 %copy-start.44 = (f32[8,8,4,128]{3,0,2,1:T(8,128)S(1)}, f32[8,8,4,128]{3,0,2,1:T(8,128)}, u32[]{:S(2)}) copy-start(f32[8,8,4,128]{3,0,2,1:T(8,128)} %fusion.162) | copy-start | bytes 393220
  174.1 10.8 %copy-start.55 = (f32[8,8,4,128]{3,0,2,1:T(8,128)S(1)}, f32[8,8,4,128]{3,0,2,1:T(8,128)}, u32[]{:S(2)}) copy-start(f32[8,8,4,128]{3,0,2,1:T(8,128)} %fusion.120) | copy-start | bytes 393220
  174.1 10.8 %copy-start.56 = (f32[8,8,4,128]{3,0,2,1:T(8,128)S(1)}, f32[8,8,4,128]{3,0,2,1:T(8,128)}, u32[]{:S(2)}) copy-start(f32[8,8,4,128]{3,0,2,1:T(8,128)} %fusion.124) | copy-start | bytes 393220
  174.1 10.8 %copy-start.57 = (f32[8,8,4,128]{3,0,2,1:T(8,128)S(1)}, f32[8,8,4,128]{3,0,2,1:T(8,128)}, u32[]{:S(2)}) copy-start(f32[8,8,4,128]{3,0,2,1:T(8,128)} %fusion.118) | copy-start | bytes 393220
  174.1 10.8 %copy-start.58 = (f32[8,8,4,128]{3,0,2,1:T(8,128)S(1)}, f32[8,8,4,128]{3,0,2,1:T(8,128)}, u32[]{:S(2)}) copy-start(f32[8,8,4,128]{3,0,2,1:T(8,128)} %fusion.122) | copy-start | bytes 393220
  174.1 10.8 %copy-start.59 = (f32[8,8,4,128]{3,0,2,1:T(8,128)S(1)}, f32[8,8,4,128]{3,0,2,1:T(8,128)}, u32[]{:S(2)}) copy-start(f32[8,8,4,128]{3,0,2,1:T(8,128)} %fusion.126) | copy-start | bytes 393220
  174.1 10.8 %copy-start.60 = (f32[8,8,4,128]{3,0,2,1:T(8,128)S(1)}, f32[8,8,4,128]{3,0,2,1:T(8,128)}, u32[]{:S(2)}) copy-start(f32[8,8,4,128]{3,0,2,1:T(8,128)} %fusion.128) | copy-start | bytes 393220
  174.1 10.8 %copy-start.61 = (f32[8,8,4,128]{3,0,2,1:T(8,128)S(1)}, f32[8,8,4,128]{3,0,2,1:T(8,128)}, u32[]{:S(2)}) copy-start(f32[8,8,4,128]{3,0,2,1:T(8,128)} %fusion.130) | copy-start | bytes 393220
  174.1 10.8 %copy-start.62 = (f32[8,8,4,128]{3,0,2,1:T(8,128)S(1)}, f32[8,8,4,128]{3,0,2,1:T(8,128)}, u32[]{:S(2)}) copy-start(f32[8,8,4,128]{3,0,2,1:T(8,128)} %fusion.132) | copy-start | bytes 393220
  174.2 10.8 %copy-start.65 = (f32[8,8,4,128]{3,0,2,1:T(8,128)S(1)}, f32[8,8,4,128]{3,0,2,1:T(8,128)}, u32[]{:S(2)}) copy-start(f32[8,8,4,128]{3,0,2,1:T(8,128)} %fusion.80) | copy-start | bytes 393220
  174.2 15.3 %collective-permute-start.8 = (f32[54,128]{1,0:T(8,128)}, f32[54,128]{1,0:T(8,128)S(1)}, u32[]{:S(2)}, u32[]{:S(2)}) collective-permute-start(f32[54,128]{1,0:T(8,128)} %reshape_reshape.3), channel_id=1, source_target_pairs={{0,8},{8,0},{16,24},{24,16},{32,40},{40,32},{48,56},{56,48},{64,72... | collective-permute-start | bytes 82952 | tf_op jit(solution)/shard_map/ppermute | solution.py:26
  189.5 6.7 %collective-permute-start.9 = (f32[54,128]{1,0:T(8,128)S(1)}, f32[54,128]{1,0:T(8,128)S(1)}, u32[]{:S(2)}, u32[]{:S(2)}) collective-permute-start(f32[54,128]{1,0:T(8,128)S(1)} %add.244), channel_id=1, source_target_pairs={{0,16},{8,24},{16,0},{24,8},{32,48},{40,56},{48,32},{56,40},{64,80... | collective-permute-start | bytes 82952 | tf_op jit(solution)/shard_map/ppermute | solution.py:26
  196.2 10.9 %collective-permute-start.10 = (f32[54,128]{1,0:T(8,128)S(1)}, f32[54,128]{1,0:T(8,128)S(1)}, u32[]{:S(2)}, u32[]{:S(2)}) collective-permute-start(f32[54,128]{1,0:T(8,128)S(1)} %add.245), channel_id=1, source_target_pairs={{0,32},{8,40},{16,48},{24,56},{32,0},{40,8},{48,16},{56,24},{64,96... | collective-permute-start | bytes 82952 | tf_op jit(solution)/shard_map/ppermute | solution.py:26
  207.1 15.1 %collective-permute-start.11 = (f32[54,128]{1,0:T(8,128)S(1)}, f32[54,128]{1,0:T(8,128)S(1)}, u32[]{:S(2)}, u32[]{:S(2)}) collective-permute-start(f32[54,128]{1,0:T(8,128)S(1)} %add.246), channel_id=1, source_target_pairs={{0,64},{8,72},{16,80},{24,88},{32,96},{40,104},{48,112},{56,120},{... | collective-permute-start | bytes 82952 | tf_op jit(solution)/shard_map/ppermute | solution.py:26
  222.2 6.2 %collective-permute-start.12 = (f32[54,128]{1,0:T(8,128)S(1)}, f32[54,128]{1,0:T(8,128)S(1)}, u32[]{:S(2)}, u32[]{:S(2)}) collective-permute-start(f32[54,128]{1,0:T(8,128)S(1)} %add.247), channel_id=1, source_target_pairs={{0,1},{1,0},{2,3},{3,2},{4,5},{5,4},{6,7},{7,6},{8,9},{9,8},{10,11... | collective-permute-start | bytes 82952 | tf_op jit(solution)/shard_map/ppermute | solution.py:26
  228.4 9.7 %collective-permute-start.13 = (f32[54,128]{1,0:T(8,128)S(1)}, f32[54,128]{1,0:T(8,128)S(1)}, u32[]{:S(2)}, u32[]{:S(2)}) collective-permute-start(f32[54,128]{1,0:T(8,128)S(1)} %add.248), channel_id=1, source_target_pairs={{0,2},{1,3},{2,0},{3,1},{4,6},{5,7},{6,4},{7,5},{8,10},{9,11},{10,... | collective-permute-start | bytes 82952 | tf_op jit(solution)/shard_map/ppermute | solution.py:26
  238.1 11.3 %collective-permute-start.14 = (f32[54,128]{1,0:T(8,128)S(1)}, f32[54,128]{1,0:T(8,128)S(1)}, u32[]{:S(2)}, u32[]{:S(2)}) collective-permute-start(f32[54,128]{1,0:T(8,128)S(1)} %add.249), channel_id=1, source_target_pairs={{0,4},{1,5},{2,6},{3,7},{4,0},{5,1},{6,2},{7,3},{8,12},{9,13},{10,... | collective-permute-start | bytes 82952 | tf_op jit(solution)/shard_map/ppermute | solution.py:26
  (35 other events, 157.3 us)

commit v3 on v2

v3 whole, which is shorter than its diff:
```python
import jax
import jax.numpy as jnp
from jax import lax
from jax.sharding import PartitionSpec as P


def with_halo(block, sides, width):
    for axis, dim in sides:
        count = lax.axis_size(axis)
        forward = [(i, i + 1) for i in range(count - 1)]
        backward = [(target, source) for source, target in forward]
        low = lax.ppermute(
            lax.slice_in_dim(block, block.shape[dim] - width, None, axis=dim), axis, forward
        )
        high = lax.ppermute(lax.slice_in_dim(block, 0, width, axis=dim), axis, backward)
        block = jnp.concatenate([low, block, high], axis=dim)
    return block


def butterfly_sum(value, axes):
    for axis in axes:
        count = lax.axis_size(axis)
        step = 1
        while step < count:
            pairs = [(i, i ^ step) for i in range(count)]
            value = value + lax.ppermute(value, axis, pairs)
            step *= 2
    return value


def pad_depth(field):
    return jnp.pad(field, ((0, 0), (1, 1), (0, 0), (0, 0)))


def conv_valid(field, weights):
    return lax.conv_general_dilated(
        field[None],
        weights,
        (1, 1, 1),
        "VALID",
        dimension_numbers=("NCDHW", "OIDHW", "NCDHW"),
        precision=lax.Precision.HIGHEST,
    )[0]


def shards(volume, filters, upstream):
    planes, rows_x, rows_y = (volume.shape[1], volume.shape[2], volume.shape[3])
    own_inputs = volume.shape[0]
    scale = (planes * rows_x * lax.axis_size("gx") * rows_y * lax.axis_size("gy")) ** (-0.5)
    gathered = lax.all_gather(volume, "col", axis=0, tiled=True)
    padded = pad_depth(with_halo(gathered, (("gx", 2), ("gy", 3)), 1))
    response, filter_vjp = jax.vjp(lambda w: conv_valid(padded, w), filters)
    all_rows = lax.all_gather(filters, "col", axis=0, tiled=True)
    all_upstream = lax.all_gather(upstream, "col", axis=0, tiled=True)
    padded_up = pad_depth(with_halo(all_upstream, (("gx", 2), ("gy", 3)), 1))
    first = lax.axis_index("col") * own_inputs
    own_filters = lax.dynamic_slice_in_dim(all_rows, first, own_inputs, 1)
    turned = jnp.flip(jnp.swapaxes(own_filters, 0, 1), axis=(2, 3, 4))
    input_grad = conv_valid(padded_up, turned)
    (local_grad,) = filter_vjp(upstream)
    flat = local_grad.reshape(-1, 128)
    sizes = [lax.axis_size(a) for a in ("gx", "gy")]
    if all(n & (n - 1) == 0 for n in sizes):
        flat = butterfly_sum(flat, ("gx", "gy"))
    else:
        flat = lax.psum(flat, ("gx", "gy"))
    total_grad = flat.reshape(local_grad.shape)
    return (response, input_grad, total_grad * scale)


def solution(mesh):
    placed = (
        P("col", None, "gx", "gy"),
        P("col", None, None, None, None),
        P("col", None, "gx", "gy"),
    )
    return jax.shard_map(
        shards,
        mesh=mesh,
        in_specs=placed,
        out_specs=(
            P("col", None, "gx", "gy"),
            P("col", None, "gx", "gy"),
            P("col", None, None, None, None),
        ),
        check_vma=False,
    )
```

time: 257 us -> 431 us (1.68)
  the two profiles are of different devices: /device:TPU:64 before, /device:TPU:6 now
where the time goes in v3:
time: 431 us; the launch traced here: 424 us
  matrix products  246 us (57%)
  local copies, waits for them, and re-layouts  71.7 us (17%)
  starting transfers between devices  62.8 us (15%)
  blocking collectives  20.7 us (5%)
  waiting for transfers between devices  11.3 us (3%)
  other arithmetic  10.3 us (2%)
    conv_general_dilated x3, matrix products, conv_valid(): lax.conv_general_dilated(field[None], weights, (1, 1, 1), 'VALID', dimens...  246 us
    ppermute x7, starting transfers between devices, butterfly_sum(): value = value + lax.ppermute(value, axis, pairs)  37.7 us
    unnamed x25, local copies, waits for them, and re-layouts  24.2 us
    broadcast_in_dim x3, local copies, waits for them, and re-layouts, conv_valid(): field[None]  19 us
    ppermute x4, starting transfers between devices, with_halo(): lax.ppermute(lax.slice_in_dim(block, block.shape[dim] - width, None, axis...  14.9 us
    ppermute x4, starting transfers between devices, with_halo(): lax.ppermute(lax.slice_in_dim(block, 0, width, axis=dim), axis, backward)  10.2 us
  transfers between devices with their start and end apart: 15, of which 4 were waited for; matrix products, arithmetic and copies ran while one was open for 34% of the time, Pallas kernels for 0%

profile of v3, /device:TPU:6, one launch (start us, length us, event | category | flops | bytes accessed | tf_op | source)
XLA Modules:
  0.0 424.2 jit_solution(7687090785243209309)
XLA Ops:
  0.6 1.0 copy.25
  1.7 6.8 %all_gather.9 = f32[32,8,4,128]{3,0,2,1:T(8,128)S(1)} all-gather(f32[8,8,4,128]{3,0,2,1:T(8,128)S(1)} %copy.25), channel_id=1, replica_groups=mesh['col'=4,'gx'=16,'gy'=8] {'col'}, dimensions={0}, use_global_device_ids=true | all-gather | bytes 655360 | tf_op jit(solution)/shard_map/all_gather | solution.py:50
  8.5 3.8 collective-permute-start
  12.3 0.9 copy.34
  13.2 7.0 %all_gather.10 = f32[32,8,4,128]{3,1,2,0:T(8,128)S(1)} all-gather(f32[8,8,4,128]{3,1,2,0:T(8,128)S(1)} %copy.34), channel_id=1, replica_groups=mesh['col'=4,'gx'=16,'gy'=8] {'col'}, dimensions={0}, use_global_device_ids=true | all-gather | bytes 655360 | tf_op jit(solution)/shard_map/all_gather | solution.py:54
  20.9 1.3 collective-permute-start.5
  22.2 5.2 %collective-permute-start.4 = (f32[32,8,1,128]{3,1,2,0:T(8,128)S(1)}, f32[32,8,1,128]{3,1,2,0:T(8,128)}, u32[]{:S(2)}, u32[]{:S(2)}) collective-permute-start(f32[32,8,1,128]{3,1,2,0:T(8,128)S(1)} %get-tuple-element.16), channel_id=1, source_target_pairs={{0,8},{8,16},{16,24},{24,32},{32,40},{40,48},{48,56},{56,64},{64,7... | collective-permute-start | bytes 393224 | tf_op jit(solution)/shard_map/ppermute | solution.py:12
  27.4 1.3 collective-permute-start.1
  28.7 4.8 %copy.45 = f32[1,8,8,4,128]{1,0,4,3,2:T(1,128)} copy(f32[1,8,8,4,128]{4,3,2,1,0:T(4,128)} %bitcast.45) | data formatting | bytes 262144 | tf_op jit(solution)/shard_map/transpose(jvp())/broadcast_in_dim | solution.py:36
  33.5 6.9 %all_gather.11 = f32[32,32,3,3,3]{1,0,4,3,2:T(8,128)} all-gather(f32[8,32,3,3,3]{1,0,4,3,2:T(8,128)S(1)} %copy-done.4), channel_id=1, replica_groups=mesh['col'=4,'gx'=16,'gy'=8] {'col'}, dimensions={0}, use_global_device_ids=true | all-gather | bytes 138240 | tf_op jit(solution)/shard_map/all_gather | solution.py:53
  40.8 1.0 copy.26
  42.1 5.8 %collective-permute-start.3 = (f32[32,8,6,1]{0,1,3,2:T(8,128)S(1)}, f32[32,8,6,1]{0,1,3,2:T(8,128)S(1)}, u32[]{:S(2)}, u32[]{:S(2)}) collective-permute-start(f32[32,8,6,1]{0,1,3,2:T(8,128)S(1)} %copy.27), channel_id=1, source_target_pairs={{1,0},{2,1},{3,2},{4,3},{5,4},{6,5},{7,6},{9,8},{10,9},{11,10},{12... | collective-permute-start | bytes 18440 | tf_op jit(solution)/shard_map/ppermute | solution.py:15
  47.9 1.9 collective-permute-start.2
  51.7 5.7 %collective-permute-done.2 = f32[32,8,6,1]{0,1,3,2:T(8,128)S(1)} collective-permute-done((f32[32,8,6,1]{0,1,3,2:T(8,128)}, f32[32,8,6,1]{0,1,3,2:T(8,128)S(1)}, u32[]{:S(2)}, u32[]{:S(2)}) %collective-permute-start.2) | collective-permute-done | bytes 6176 | tf_op jit(solution)/shard_map/ppermute | solution.py:12
  57.4 1.3 copy.28
  58.7 1.2 copy.29
  59.9 3.4 fusion.23
  63.4 9.1 %copy.44 = f32[1,32,10,6,130]{1,0,4,3,2:T(1,128)} copy(f32[1,32,10,6,130]{4,1,3,2,0:T(8,128)} %get-tuple-element.9) | data formatting | bytes 1996800 | tf_op jit(solution)/shard_map/jvp()/broadcast_in_dim | solution.py:37
  72.4 159.1 %fusion.37 = f32[8,32,3,3,3]{1,0,4,3,2:T(8,128)S(1)} fusion(f32[1,32,10,6,130]{1,0,4,3,2:T(1,128)} %copy.44, f32[1,8,8,4,128]{1,0,4,3,2:T(1,128)} %copy.45), kind=kOutput, calls=%fused_computation.51 | convolution fusion | flops 339738624 | bytes 1157120 | tf_op jit(solution)/shard_map/transpose(jvp())/conv_general_dilated | solution.py:36
  231.6 1.8 copy.46
  233.4 3.0 reshape.12
  236.4 4.4 %collective-permute-start.8 = (f32[54,128]{1,0:T(8,128)}, f32[54,128]{1,0:T(8,128)}, u32[]{:S(2)}, u32[]{:S(2)}) collective-permute-start(f32[54,128]{1,0:T(8,128)} %reshape.12), channel_id=1, source_target_pairs={{0,8},{8,0},{16,24},{24,16},{32,40},{40,32},{48,56},{56,48},{64,72... | collective-permute-start | bytes 82952 | tf_op jit(solution)/shard_map/ppermute | solution.py:26
  240.8 1.2 fusion.33
  241.9 1.5 copy.35
  243.8 1.9 collective-permute-start.7
  245.7 3.9 collective-permute-start.6
  249.7 6.3 %copy.51 = f32[32,10,6,1,130]{0,3,4,2,1:T(1,128)} copy(f32[32,10,6,1,130]{4,0,2,1,3:T(8,128)S(1)} %get-tuple-element.10) | data formatting | bytes 1996800
  255.9 5.0 %pad.9.clone = f32[32,10,6,1,136]{0,3,4,2,1:T(1,128)S(1)} pad(f32[32,10,6,1,130]{0,3,4,2,1:T(1,128)} %copy.51, f32[]{:T(128)} %constant.3.clone.1), padding=0_0x0_0x0_0x0_0x0_6 | pad | bytes 2042884 | tf_op jit(solution)/shard_map/jvp()/broadcast_in_dim | solution.py:37
  262.0 7.0 %collective-permute-start.9 = (f32[54,128]{1,0:T(8,128)S(1)}, f32[54,128]{1,0:T(8,128)S(1)}, u32[]{:S(2)}, u32[]{:S(2)}) collective-permute-start(f32[54,128]{1,0:T(8,128)S(1)} %add.29), channel_id=1, source_target_pairs={{0,16},{8,24},{16,0},{24,8},{32,48},{40,56},{48,32},{56,40},{64,80... | collective-permute-start | bytes 82952 | tf_op jit(solution)/shard_map/ppermute | solution.py:26
  269.3 1.5 collective-permute-done.9
  270.9 9.1 %collective-permute-start.10 = (f32[54,128]{1,0:T(8,128)S(1)}, f32[54,128]{1,0:T(8,128)S(1)}, u32[]{:S(2)}, u32[]{:S(2)}) collective-permute-start(f32[54,128]{1,0:T(8,128)S(1)} %add.30), channel_id=1, source_target_pairs={{0,32},{8,40},{16,48},{24,56},{32,0},{40,8},{48,16},{56,24},{64,96... | collective-permute-start | bytes 82952 | tf_op jit(solution)/shard_map/ppermute | solution.py:26
  280.0 57.0 %fusion.17 = f32[8,4,8,17,8]{4,2,3,1,0:T(8,128)} fusion(f32[8,32,3,3,3]{1,0,4,3,2:T(8,128)S(1)} %copy-done.5, pred[8,17]{0,1:T(8,128)(4,1)S(1)} %copy-done.6, f32[32,10,6,8,19]{0,3,4,2,1:T(8,128)S(1)} %fusion.44), kind=kOutput, calls=%fused_computation.26 | convolution fusion | flops 361007104 | bytes 1334408 | tf_op jit(solution)/shard_map/jvp()/conv_general_dilated | solution.py:36
  336.9 1.3 copy.37
  338.2 1.2 copy.38
  339.5 8.8 %collective-permute-start.11 = (f32[54,128]{1,0:T(8,128)S(1)}, f32[54,128]{1,0:T(8,128)S(1)}, u32[]{:S(2)}, u32[]{:S(2)}) collective-permute-start(f32[54,128]{1,0:T(8,128)S(1)} %add.31), channel_id=1, source_target_pairs={{0,64},{8,72},{16,80},{24,88},{32,96},{40,104},{48,112},{56,120},{... | collective-permute-start | bytes 82952 | tf_op jit(solution)/shard_map/ppermute | solution.py:26
  348.2 3.0 fusion.10
  351.3 11.9 %copy.52 = f32[32,10,6,1,130]{0,3,4,2,1:T(1,128)} copy(f32[32,10,6,1,130]{4,1,2,0,3:T(8,128)S(1)} %fusion.10) | data formatting | bytes 1996800
  363.2 5.0 %pad.11.clone = f32[32,10,6,1,136]{0,3,4,2,1:T(1,128)S(1)} pad(f32[32,10,6,1,130]{0,3,4,2,1:T(1,128)} %copy.52, f32[]{:T(128)} %constant.3.clone.1), padding=0_0x0_0x0_0x0_0x0_6 | pad | bytes 2042884 | tf_op jit(solution)/shard_map/broadcast_in_dim | solution.py:37
  369.1 1.9 collective-permute-start.12
  371.1 30.1 %fusion.20 = f32[8,4,8,17,8]{4,2,3,1,0:T(8,128)} fusion(f32[32,10,6,1,7,2]{0,4,5,2,1,3:T(8,128)S(1)} %slice.46, f32[32,10,6,1,8,17]{0,4,5,2,1,3:T(8,128)S(1)} %copy.41, pred[8,17]{0,1:T(8,128)(4,1)S(1)} %copy-done.6, f32[32,32,3,3,3]{1,0,4,3,2:T(8,128)S(1)} %copy-done.3, s32[]{:T(128)S(6)} %select_n.3), kind=kOutput, calls=%fused_computation.27 | convolution fusion | flops 361882624 | bytes 1401996 | tf_op jit(solution)/shard_map/conv_general_dilated | solution.py:36
  401.2 3.0 copy.43
  404.5 1.4 add.33
  405.9 1.9 collective-permute-start.13
  408.5 1.8 copy.33
  410.6 2.9 collective-permute-done.13
  414.2 4.7 %collective-permute-start.14 = (f32[54,128]{1,0:T(8,128)S(1)}, f32[54,128]{1,0:T(8,128)S(1)}, u32[]{:S(2)}, u32[]{:S(2)}) collective-permute-start(f32[54,128]{1,0:T(8,128)S(1)} %add.34), channel_id=1, source_target_pairs={{0,4},{1,5},{2,6},{3,7},{4,0},{5,1},{6,2},{7,3},{8,12},{9,13},{10,... | collective-permute-start | bytes 82952 | tf_op jit(solution)/shard_map/ppermute | solution.py:26
  420.3 1.2 collective-permute-done.14
  422.4 1.6 copy.49
  (54 shorter events, 10.3 us)
Async XLA Ops:
  0.6 32.9 %copy-start.4 = (f32[8,32,3,3,3]{1,0,4,3,2:T(8,128)S(1)}, f32[8,32,3,3,3]{1,0,4,3,2:T(8,128)}, u32[]{:S(2)}) copy-start(f32[8,32,3,3,3]{1,0,4,3,2:T(8,128)} %param.4) | copy-start | bytes 82948
  8.5 31.9 %collective-permute-start = (f32[32,8,1,128]{3,0,2,1:T(8,128)S(1)}, f32[32,8,1,128]{3,0,2,1:T(8,128)S(1)}, u32[]{:S(2)}, u32[]{:S(2)}) collective-permute-start(f32[32,8,1,128]{3,0,2,1:T(8,128)S(1)} %get-tuple-element.18), channel_id=1, source_target_pairs={{0,8},{8,16},{16,24},{24,32},{32,40},{40,48},{48,56},{56,64},{64,7... | collective-permute-start | bytes 393224 | tf_op jit(solution)/shard_map/ppermute | solution.py:12
  20.9 29.9 %collective-permute-start.5 = (f32[32,8,1,128]{3,1,2,0:T(8,128)}, f32[32,8,1,128]{3,1,2,0:T(8,128)}, u32[]{:S(2)}, u32[]{:S(2)}) collective-permute-start(f32[32,8,1,128]{3,1,2,0:T(8,128)} %get-tuple-element.15), channel_id=1, source_target_pairs={{8,0},{16,8},{24,16},{32,24},{40,32},{48,40},{56,48},{64,56},{72,6... | collective-permute-start | bytes 393224 | tf_op jit(solution)/shard_map/ppermute | solution.py:15
  22.2 27.6 %collective-permute-start.4 = (f32[32,8,1,128]{3,1,2,0:T(8,128)S(1)}, f32[32,8,1,128]{3,1,2,0:T(8,128)}, u32[]{:S(2)}, u32[]{:S(2)}) collective-permute-start(f32[32,8,1,128]{3,1,2,0:T(8,128)S(1)} %get-tuple-element.16), channel_id=1, source_target_pairs={{0,8},{8,16},{16,24},{24,32},{32,40},{40,48},{48,56},{56,64},{64,7... | collective-permute-start | bytes 393224 | tf_op jit(solution)/shard_map/ppermute | solution.py:12
  27.4 13.1 %collective-permute-start.1 = (f32[32,8,1,128]{3,0,2,1:T(8,128)S(1)}, f32[32,8,1,128]{3,0,2,1:T(8,128)S(1)}, u32[]{:S(2)}, u32[]{:S(2)}) collective-permute-start(f32[32,8,1,128]{3,0,2,1:T(8,128)S(1)} %get-tuple-element.17), channel_id=1, source_target_pairs={{8,0},{16,8},{24,16},{32,24},{40,32},{48,40},{56,48},{64,56},{72,6... | collective-permute-start | bytes 393224 | tf_op jit(solution)/shard_map/ppermute | solution.py:15
  42.1 16.6 %collective-permute-start.3 = (f32[32,8,6,1]{0,1,3,2:T(8,128)S(1)}, f32[32,8,6,1]{0,1,3,2:T(8,128)S(1)}, u32[]{:S(2)}, u32[]{:S(2)}) collective-permute-start(f32[32,8,6,1]{0,1,3,2:T(8,128)S(1)} %copy.27), channel_id=1, source_target_pairs={{1,0},{2,1},{3,2},{4,3},{5,4},{6,5},{7,6},{9,8},{10,9},{11,10},{12... | collective-permute-start | bytes 18440 | tf_op jit(solution)/shard_map/ppermute | solution.py:15
  47.9 9.5 %collective-permute-start.2 = (f32[32,8,6,1]{0,1,3,2:T(8,128)}, f32[32,8,6,1]{0,1,3,2:T(8,128)S(1)}, u32[]{:S(2)}, u32[]{:S(2)}) collective-permute-start(f32[32,8,6,1]{0,1,3,2:T(8,128)} %copy.26), channel_id=1, source_target_pairs={{0,1},{1,2},{2,3},{3,4},{4,5},{5,6},{6,7},{8,9},{9,10},{10,11},{11... | collective-permute-start | bytes 18440 | tf_op jit(solution)/shard_map/ppermute | solution.py:12
  51.7 189.0 %copy-start = (f32[32,8,6,128]{3,1,2,0:T(8,128)}, f32[32,8,6,128]{3,1,2,0:T(8,128)S(1)}, u32[]{:S(2)}) copy-start(f32[32,8,6,128]{3,1,2,0:T(8,128)S(1)} %constant_dynamic-update-slice_fusion.3) | copy-start | bytes 2359300
  236.4 24.9 %collective-permute-start.8 = (f32[54,128]{1,0:T(8,128)}, f32[54,128]{1,0:T(8,128)}, u32[]{:S(2)}, u32[]{:S(2)}) collective-permute-start(f32[54,128]{1,0:T(8,128)} %reshape.12), channel_id=1, source_target_pairs={{0,8},{8,0},{16,24},{24,16},{32,40},{40,32},{48,56},{56,48},{64,72... | collective-permute-start | bytes 82952 | tf_op jit(solution)/shard_map/ppermute | solution.py:26
  243.8 94.4 %collective-permute-start.7 = (f32[32,8,6,1]{0,1,3,2:T(8,128)S(1)}, f32[32,8,6,1]{0,1,3,2:T(8,128)S(1)}, u32[]{:S(2)}, u32[]{:S(2)}) collective-permute-start(f32[32,8,6,1]{0,1,3,2:T(8,128)S(1)} %copy.36), channel_id=1, source_target_pairs={{1,0},{2,1},{3,2},{4,3},{5,4},{6,5},{7,6},{9,8},{10,9},{11,10},{12... | collective-permute-start | bytes 18440 | tf_op jit(solution)/shard_map/ppermute | solution.py:15
  245.7 91.2 %collective-permute-start.6 = (f32[32,8,6,1]{0,1,3,2:T(8,128)S(1)}, f32[32,8,6,1]{0,1,3,2:T(8,128)S(1)}, u32[]{:S(2)}, u32[]{:S(2)}) collective-permute-start(f32[32,8,6,1]{0,1,3,2:T(8,128)S(1)} %copy.35), channel_id=1, source_target_pairs={{0,1},{1,2},{2,3},{3,4},{4,5},{5,6},{6,7},{8,9},{9,10},{10,11},{11... | collective-permute-start | bytes 18440 | tf_op jit(solution)/shard_map/ppermute | solution.py:12
  262.0 17.9 %copy-start.5 = (f32[8,32,3,3,3]{1,0,4,3,2:T(8,128)S(1)}, f32[8,32,3,3,3]{1,0,4,3,2:T(8,128)}, u32[]{:S(2)}) copy-start(f32[8,32,3,3,3]{1,0,4,3,2:T(8,128)} %param.4) | copy-start | bytes 82948
  262.0 18.0 %copy-start.6 = (pred[8,17]{0,1:T(8,128)(4,1)S(1)}, pred[8,17]{0,1:T(8,128)(4,1)}, u32[]{:S(2)}) copy-start(pred[8,17]{0,1:T(8,128)(4,1)} %constant.30) | copy-start | bytes 412
  262.0 8.8 %collective-permute-start.9 = (f32[54,128]{1,0:T(8,128)S(1)}, f32[54,128]{1,0:T(8,128)S(1)}, u32[]{:S(2)}, u32[]{:S(2)}) collective-permute-start(f32[54,128]{1,0:T(8,128)S(1)} %add.29), channel_id=1, source_target_pairs={{0,16},{8,24},{16,0},{24,8},{32,48},{40,56},{48,32},{56,40},{64,80... | collective-permute-start | bytes 82952 | tf_op jit(solution)/shard_map/ppermute | solution.py:26
  270.9 68.6 %collective-permute-start.10 = (f32[54,128]{1,0:T(8,128)S(1)}, f32[54,128]{1,0:T(8,128)S(1)}, u32[]{:S(2)}, u32[]{:S(2)}) collective-permute-start(f32[54,128]{1,0:T(8,128)S(1)} %add.30), channel_id=1, source_target_pairs={{0,32},{8,40},{16,48},{24,56},{32,0},{40,8},{48,16},{56,24},{64,96... | collective-permute-start | bytes 82952 | tf_op jit(solution)/shard_map/ppermute | solution.py:26
  339.5 29.1 %collective-permute-start.11 = (f32[54,128]{1,0:T(8,128)S(1)}, f32[54,128]{1,0:T(8,128)S(1)}, u32[]{:S(2)}, u32[]{:S(2)}) collective-permute-start(f32[54,128]{1,0:T(8,128)S(1)} %add.31), channel_id=1, source_target_pairs={{0,64},{8,72},{16,80},{24,88},{32,96},{40,104},{48,112},{56,120},{... | collective-permute-start | bytes 82952 | tf_op jit(solution)/shard_map/ppermute | solution.py:26
  368.2 2.9 copy-start.3
  369.1 35.4 %collective-permute-start.12 = (f32[54,128]{1,0:T(8,128)}, f32[54,128]{1,0:T(8,128)}, u32[]{:S(2)}, u32[]{:S(2)}) collective-permute-start(f32[54,128]{1,0:T(8,128)} %add.32), channel_id=1, source_target_pairs={{0,1},{1,0},{2,3},{3,2},{4,5},{5,4},{6,7},{7,6},{8,9},{9,8},{10,11... | collective-permute-start | bytes 82952 | tf_op jit(solution)/shard_map/ppermute | solution.py:26
  401.2 7.3 %copy-start.1 = (f32[8,4,8,17,8]{4,2,3,1,0:T(8,128)S(1)}, f32[8,4,8,17,8]{4,2,3,1,0:T(8,128)}, u32[]{:S(2)}) copy-start(f32[8,4,8,17,8]{4,2,3,1,0:T(8,128)} %fusion.17) | copy-start | bytes 417796
  405.9 7.6 %collective-permute-start.13 = (f32[54,128]{1,0:T(8,128)}, f32[54,128]{1,0:T(8,128)}, u32[]{:S(2)}, u32[]{:S(2)}) collective-permute-start(f32[54,128]{1,0:T(8,128)} %add.33), channel_id=1, source_target_pairs={{0,2},{1,3},{2,0},{3,1},{4,6},{5,7},{6,4},{7,5},{8,10},{9,11},{10,... | collective-permute-start | bytes 82952 | tf_op jit(solution)/shard_map/ppermute | solution.py:26
  408.5 10.4 %copy-start.2 = (f32[8,8,4,128]{3,0,2,1:T(8,128)S(1)}, f32[8,8,4,128]{3,0,2,1:T(8,128)}, u32[]{:S(2)}) copy-start(f32[8,8,4,128]{3,0,2,1:T(8,128)} %slice_bitcast_fusion) | copy-start | bytes 393220
  414.2 7.3 %collective-permute-start.14 = (f32[54,128]{1,0:T(8,128)S(1)}, f32[54,128]{1,0:T(8,128)S(1)}, u32[]{:S(2)}, u32[]{:S(2)}) collective-permute-start(f32[54,128]{1,0:T(8,128)S(1)} %add.34), channel_id=1, source_target_pairs={{0,4},{1,5},{2,6},{3,7},{4,0},{5,1},{6,2},{7,3},{8,12},{9,13},{10,... | collective-permute-start | bytes 82952 | tf_op jit(solution)/shard_map/ppermute | solution.py:26

commit v4 on v3

--- a/solution.py
+++ b/solution.py
@@ -32,15 +32,14 @@
     return jnp.pad(field, ((0, 0), (1, 1), (0, 0), (0, 0)))
 
 
-def conv_valid(field, weights):
-    return lax.conv_general_dilated(
-        field[None],
-        weights,
-        (1, 1, 1),
-        "VALID",
-        dimension_numbers=("NCDHW", "OIDHW", "NCDHW"),
-        precision=lax.Precision.HIGHEST,
-    )[0]
+def patches(field, planes, rows_x, rows_y, flip):
+    windows = []
+    for depth in range(3):
+        for across in range(3):
+            for along in range(3):
+                a, b, e = (2 - depth, 2 - across, 2 - along) if flip else (depth, across, along)
+                windows.append(field[:, a : a + planes, b : b + rows_x, e : e + rows_y])
+    return jnp.stack(windows, axis=0)
 
 
 def shards(volume, filters, upstream):
@@ -49,15 +48,19 @@
     scale = (planes * rows_x * lax.axis_size("gx") * rows_y * lax.axis_size("gy")) ** (-0.5)
     gathered = lax.all_gather(volume, "col", axis=0, tiled=True)
     padded = pad_depth(with_halo(gathered, (("gx", 2), ("gy", 3)), 1))
-    response, filter_vjp = jax.vjp(lambda w: conv_valid(padded, w), filters)
+    taps = patches(padded, planes, rows_x, rows_y, False)
+    by_tap = jnp.swapaxes(filters.reshape(filters.shape[0], filters.shape[1], 27), 1, 2)
+    response = jnp.einsum("okc,kcpqy->opqy", by_tap, taps, precision=lax.Precision.HIGHEST)
     all_rows = lax.all_gather(filters, "col", axis=0, tiled=True)
     all_upstream = lax.all_gather(upstream, "col", axis=0, tiled=True)
     padded_up = pad_depth(with_halo(all_upstream, (("gx", 2), ("gy", 3)), 1))
     first = lax.axis_index("col") * own_inputs
     own_filters = lax.dynamic_slice_in_dim(all_rows, first, own_inputs, 1)
-    turned = jnp.flip(jnp.swapaxes(own_filters, 0, 1), axis=(2, 3, 4))
-    input_grad = conv_valid(padded_up, turned)
-    (local_grad,) = filter_vjp(upstream)
+    own_by_tap = jnp.swapaxes(own_filters.reshape(own_filters.shape[0], own_inputs, 27), 1, 2)
+    taps_up = patches(padded_up, planes, rows_x, rows_y, True)
+    input_grad = jnp.einsum("okc,kopqy->cpqy", own_by_tap, taps_up, precision=lax.Precision.HIGHEST)
+    local_grad = jnp.einsum("opqy,kcpqy->ock", upstream, taps, precision=lax.Precision.HIGHEST)
+    local_grad = local_grad.reshape(local_grad.shape[0], local_grad.shape[1], 3, 3, 3)
     flat = local_grad.reshape(-1, 128)
     sizes = [lax.axis_size(a) for a in ("gx", "gy")]
     if all(n & (n - 1) == 0 for n in sizes):

time: 431 us -> 209 us (0.48); the launches traced: 424 us -> 207 us
  matrix products: 246 us -> 47.4 us
  local copies, waits for them, and re-layouts: 71.7 us -> 42.3 us
  starting transfers between devices: 62.8 us -> 69.3 us
  other arithmetic: 10.3 us -> 15.1 us
    conv_general_dilated x3 -> x0, matrix products: 246 us -> none  [conv_valid(): lax.conv_general_dilated(field[None], weights, (1, 1, 1), 'VALID', dimens...]
    dot_general x0 -> x3, matrix products: none -> 47.4 us  [the longest x1 27.2 us: shards(): jnp.einsum('opqy,kcpqy->ock', upstream, taps, precision=lax.Precision.HIG...]
    broadcast_in_dim x4 -> x0, local copies, waits for them, and re-layouts: 23.8 us -> none  [the longest x3 19 us: conv_valid(): field[None]]
    unnamed x0 -> x16, other arithmetic: none -> 11 us
    conv_general_dilated x9 -> x0, local copies, waits for them, and re-layouts: 7.88 us -> none  [conv_valid(): lax.conv_general_dilated(field[None], weights, (1, 1, 1), 'VALID', dimens...]
    broadcast_in_dim x2 -> x0, other arithmetic: 6.48 us -> none  [conv_valid(): field[None]]
    ppermute x7, waiting for transfers between devices: 5.6 us -> 11.4 us  [butterfly_sum(): value = value + lax.ppermute(value, axis, pairs)]
    ppermute x4, waiting for transfers between devices: 5.71 us -> 0.01 us  [with_halo(): lax.ppermute(lax.slice_in_dim(block, block.shape[dim] - width, None, axis...]
  transfers between devices with their start and end apart: 15 -> 15, of which waited for: 4 -> 6; matrix products, arithmetic and copies ran while one was open for 34% -> 28% of each run, Pallas kernels for 0% -> 0%
where the time goes in v4:
time: 209 us; the launch traced here: 207 us
  starting transfers between devices  69.3 us (33%)
  matrix products  47.4 us (23%)
  local copies, waits for them, and re-layouts  42.3 us (20%)
  blocking collectives  20.3 us (10%)
  other arithmetic  15.1 us (7%)
  waiting for transfers between devices  11.4 us (5%)
    ppermute x7, starting transfers between devices, butterfly_sum(): value = value + lax.ppermute(value, axis, pairs)  40.3 us
    dot_general x1, matrix products, shards(): jnp.einsum('opqy,kcpqy->ock', upstream, taps, precision=lax.Precision.HIG...  27.2 us
    unnamed x79, local copies, waits for them, and re-layouts  25.4 us
    ppermute x4, starting transfers between devices, with_halo(): lax.ppermute(lax.slice_in_dim(block, 0, width, axis=dim), axis, backward)  15.9 us
    ppermute x4, starting transfers between devices, with_halo(): lax.ppermute(lax.slice_in_dim(block, block.shape[dim] - width, None, axis...  13.1 us
    dot_general x1, matrix products, shards(): jnp.einsum('okc,kopqy->cpqy', own_by_tap, taps_up, precision=lax.Precisio...  12.4 us
    ppermute x7, waiting for transfers between devices, butterfly_sum(): value = value + lax.ppermute(value, axis, pairs)  11.4 us
    unnamed x16, other arithmetic  11 us
  transfers between devices with their start and end apart: 15, of which 6 were waited for; matrix products, arithmetic and copies ran while one was open for 28% of the time, Pallas kernels for 0%

profile of v4, /device:TPU:6, one launch (start us, length us, event | category | flops | bytes accessed | tf_op | source)
XLA Modules:
  0.0 207.0 jit_solution(6581980408389433612)
XLA Ops:
  1.6 6.8 %all_gather.11 = f32[32,8,4,128]{3,0,2,1:T(8,128)S(1)} all-gather(f32[8,8,4,128]{3,0,2,1:T(8,128)S(1)} %copy.160), channel_id=1, replica_groups=mesh['col'=4,'gx'=16,'gy'=8] {'col'}, dimensions={0}, use_global_device_ids=true | all-gather | bytes 655360 | tf_op jit(solution)/shard_map/all_gather | solution.py:55
  9.1 1.3 collective-permute-start.5
  10.4 4.6 %collective-permute-start.4 = (f32[32,8,1,128]{3,0,2,1:T(8,128)S(1)}, f32[32,8,1,128]{3,0,2,1:T(8,128)S(1)}, u32[]{:S(2)}, u32[]{:S(2)}) collective-permute-start(f32[32,8,1,128]{3,0,2,1:T(8,128)S(1)} %get-tuple-element.17), channel_id=1, source_target_pairs={{0,8},{8,16},{16,24},{24,32},{32,40},{40,48},{48,56},{56,64},{64,7... | collective-permute-start | bytes 393224 | tf_op jit(solution)/shard_map/ppermute | solution.py:12
  15.9 6.9 %all_gather.9 = f32[32,8,4,128]{3,0,2,1:T(8,128)S(1)} all-gather(f32[8,8,4,128]{3,0,2,1:T(8,128)S(1)} %copy.126), channel_id=1, replica_groups=mesh['col'=4,'gx'=16,'gy'=8] {'col'}, dimensions={0}, use_global_device_ids=true | all-gather | bytes 655360 | tf_op jit(solution)/shard_map/all_gather | solution.py:49
  22.9 1.3 collective-permute-start.1
  24.2 4.6 %collective-permute-start = (f32[32,8,1,128]{3,0,2,1:T(8,128)S(1)}, f32[32,8,1,128]{3,0,2,1:T(8,128)S(1)}, u32[]{:S(2)}, u32[]{:S(2)}) collective-permute-start(f32[32,8,1,128]{3,0,2,1:T(8,128)S(1)} %get-tuple-element.19), channel_id=1, source_target_pairs={{0,8},{8,16},{16,24},{24,32},{32,40},{40,48},{48,56},{56,64},{64,7... | collective-permute-start | bytes 393224 | tf_op jit(solution)/shard_map/ppermute | solution.py:12
  28.7 6.7 %all_gather.10 = f32[32,32,3,3,3]{1,0,4,3,2:T(8,128)S(1)} all-gather(f32[8,32,3,3,3]{1,0,4,3,2:T(8,128)} %param.4), channel_id=1, replica_groups=mesh['col'=4,'gx'=16,'gy'=8] {'col'}, dimensions={0}, use_global_device_ids=true | all-gather | bytes 138240 | tf_op jit(solution)/shard_map/all_gather | solution.py:54
  36.5 1.2 fusion.78
  37.7 1.5 copy.161
  39.5 5.8 %collective-permute-start.7 = (f32[32,8,6,1]{0,1,3,2:T(8,128)S(1)}, f32[32,8,6,1]{0,1,3,2:T(8,128)S(1)}, u32[]{:S(2)}, u32[]{:S(2)}) collective-permute-start(f32[32,8,6,1]{0,1,3,2:T(8,128)S(1)} %copy.162), channel_id=1, source_target_pairs={{1,0},{2,1},{3,2},{4,3},{5,4},{6,5},{7,6},{9,8},{10,9},{11,10},{12... | collective-permute-start | bytes 18440 | tf_op jit(solution)/shard_map/ppermute | solution.py:15
  45.3 1.9 collective-permute-start.6
  47.4 1.2 fusion.79
  48.6 2.1 %copy.127 = f32[32,8,6,1]{0,1,3,2:T(8,128)} copy(f32[32,8,6,1]{3,0,2,1:T(8,128)} %get-tuple-element.14) | data formatting | bytes 12288 | tf_op jit(solution)/shard_map/slice | solution.py:13
  51.6 7.5 %collective-permute-start.3 = (f32[32,8,6,1]{0,1,3,2:T(8,128)}, f32[32,8,6,1]{0,1,3,2:T(8,128)}, u32[]{:S(2)}, u32[]{:S(2)}) collective-permute-start(f32[32,8,6,1]{0,1,3,2:T(8,128)} %copy.128), channel_id=1, source_target_pairs={{1,0},{2,1},{3,2},{4,3},{5,4},{6,5},{7,6},{9,8},{10,9},{11,10},{12... | collective-permute-start | bytes 18440 | tf_op jit(solution)/shard_map/ppermute | solution.py:15
  59.2 2.1 %collective-permute-start.2 = (f32[32,8,6,1]{0,1,3,2:T(8,128)}, f32[32,8,6,1]{0,1,3,2:T(8,128)}, u32[]{:S(2)}, u32[]{:S(2)}) collective-permute-start(f32[32,8,6,1]{0,1,3,2:T(8,128)} %copy.127), channel_id=1, source_target_pairs={{0,1},{1,2},{2,3},{3,4},{4,5},{5,6},{6,7},{8,9},{9,10},{10,11},{11... | collective-permute-start | bytes 18440 | tf_op jit(solution)/shard_map/ppermute | solution.py:12
  61.3 1.2 copy.163
  62.5 1.3 copy.164
  63.8 2.2 %select_maximum_fusion = f32[32,10,6,130]{3,0,2,1:T(8,128)S(1)} fusion(f32[32,8,6,1]{3,0,2,1:T(8,128)} %copy.164, f32[32,8,6,128]{3,0,2,1:T(8,128)S(1)} %constant_dynamic-update-slice_fusion.3, f32[32,8,6,1]{3,0,2,1:T(8,128)} %copy.163), kind=kLoop, calls=%fused_computation.2 | loop fusion | flops 1996800 | bytes 1797120 | tf_op jit(solution)/shard_map/concatenate | solution.py:16
  66.0 1.1 fusion.50
  69.0 1.0 fusion.47
  70.0 1.0 fusion.46
  72.9 1.0 fusion.43
  74.8 1.2 fusion.12
  76.9 1.0 fusion.6
  78.0 1.2 fusion.9
  80.0 1.0 fusion.3
  81.0 1.2 fusion.39
  82.2 1.7 fusion.37
  83.9 1.0 fusion.35
  86.0 1.1 fusion.32
  88.0 2.0 copy.129
  90.0 1.1 copy.130
  91.1 1.9 select_maximum_fusion.2
  97.6 27.2 %convolution_bitcast_fusion.2 = f32[8,32,27]{1,0,2:T(8,128)S(1)} fusion(f32[27,32,8,4,128]{4,1,0,3,2:T(8,128)S(1)} %fusion.51, f32[8,8,4,128,1]{3,2,1,0,4:T(4,128)S(1)} %bitcast.350), kind=kOutput, calls=%fused_computation.25 | convolution fusion | flops 339738624 | bytes 14314496 | tf_op jit(solution)/shard_map/opqy,kcpqy->ock/dot_general | solution.py:62
  124.8 7.8 %convolution_bitcast_fusion.1 = f32[8,8,4,128]{3,0,2,1:T(8,128)S(1)} fusion(f32[27,32,8,4,128]{4,1,0,3,2:T(8,128)S(1)} %fusion.51, f32[8,27,32,1,1]{2,0,1,4,3:T(8,128)S(1)} %bitcast.351), kind=kOutput, calls=%fused_computation.24 | convolution fusion | flops 339738624 | bytes 14314496 | tf_op jit(solution)/shard_map/okc,kcpqy->opqy/dot_general | solution.py:53
  132.9 3.8 %collective-permute-start.8 = (f32[54,128]{1,0:T(8,128)S(1)}, f32[54,128]{1,0:T(8,128)S(1)}, u32[]{:S(2)}, u32[]{:S(2)}) collective-permute-start(f32[54,128]{1,0:T(8,128)S(1)} %reshape_reshape.3), channel_id=1, source_target_pairs={{0,8},{8,0},{16,24},{24,16},{32,40},{40,32},{48,56},{56,48},{64,72... | collective-permute-start | bytes 82952 | tf_op jit(solution)/shard_map/ppermute | solution.py:26
  138.7 7.3 %collective-permute-start.9 = (f32[54,128]{1,0:T(8,128)S(1)}, f32[54,128]{1,0:T(8,128)S(1)}, u32[]{:S(2)}, u32[]{:S(2)}) collective-permute-start(f32[54,128]{1,0:T(8,128)S(1)} %add.29), channel_id=1, source_target_pairs={{0,16},{8,24},{16,0},{24,8},{32,48},{40,56},{48,32},{56,40},{64,80... | collective-permute-start | bytes 82952 | tf_op jit(solution)/shard_map/ppermute | solution.py:26
  147.9 9.1 %collective-permute-start.10 = (f32[54,128]{1,0:T(8,128)S(1)}, f32[54,128]{1,0:T(8,128)S(1)}, u32[]{:S(2)}, u32[]{:S(2)}) collective-permute-start(f32[54,128]{1,0:T(8,128)S(1)} %add.30), channel_id=1, source_target_pairs={{0,32},{8,40},{16,48},{24,56},{32,0},{40,8},{48,16},{56,24},{64,96... | collective-permute-start | bytes 82952 | tf_op jit(solution)/shard_map/ppermute | solution.py:26
  158.8 11.9 %collective-permute-start.11 = (f32[54,128]{1,0:T(8,128)S(1)}, f32[54,128]{1,0:T(8,128)S(1)}, u32[]{:S(2)}, u32[]{:S(2)}) collective-permute-start(f32[54,128]{1,0:T(8,128)S(1)} %add.31), channel_id=1, source_target_pairs={{0,64},{8,72},{16,80},{24,88},{32,96},{40,104},{48,112},{56,120},{... | collective-permute-start | bytes 82952 | tf_op jit(solution)/shard_map/ppermute | solution.py:26
  171.7 1.6 collective-permute-done.11
  173.3 1.9 collective-permute-start.12
  175.2 1.1 fusion.26
  176.3 2.8 %collective-permute-done.12 = f32[54,128]{1,0:T(8,128)S(1)} collective-permute-done((f32[54,128]{1,0:T(8,128)S(1)}, f32[54,128]{1,0:T(8,128)S(1)}, u32[]{:S(2)}, u32[]{:S(2)}) %collective-permute-start.12) | collective-permute-done | bytes 27680 | tf_op jit(solution)/shard_map/ppermute | solution.py:26
  179.0 1.9 collective-permute-start.13
  181.9 4.4 %collective-permute-done.13 = f32[54,128]{1,0:T(8,128)S(1)} collective-permute-done((f32[54,128]{1,0:T(8,128)S(1)}, f32[54,128]{1,0:T(8,128)S(1)}, u32[]{:S(2)}, u32[]{:S(2)}) %collective-permute-start.13) | collective-permute-done | bytes 27680 | tf_op jit(solution)/shard_map/ppermute | solution.py:26
  186.3 4.4 %collective-permute-start.14 = (f32[54,128]{1,0:T(8,128)S(1)}, f32[54,128]{1,0:T(8,128)S(1)}, u32[]{:S(2)}, u32[]{:S(2)}) collective-permute-start(f32[54,128]{1,0:T(8,128)S(1)} %add.34), channel_id=1, source_target_pairs={{0,4},{1,5},{2,6},{3,7},{4,0},{5,1},{6,2},{7,3},{8,12},{9,13},{10,... | collective-permute-start | bytes 82952 | tf_op jit(solution)/shard_map/ppermute | solution.py:26
  190.7 12.4 %convolution_bitcast_fusion = f32[8,8,4,128]{3,0,2,1:T(8,128)S(1)} fusion(f32[32,27,8,1,1]{0,2,1,4,3:T(8,128)S(1)} %bitcast.352, f32[27,32,8,4,128]{4,1,0,3,2:T(8,128)} %fusion.25), kind=kOutput, calls=%fused_computation.23 | convolution fusion | flops 339738624 | bytes 14314496 | tf_op jit(solution)/shard_map/okc,kopqy->cpqy/dot_general | solution.py:61
  205.4 1.6 copy.197
  (113 shorter events, 28.1 us)
Async XLA Ops:
  8.4 38.9 %copy-start.5 = (f32[32,8,4,128]{3,0,2,1:T(8,128)}, f32[32,8,4,128]{3,0,2,1:T(8,128)S(1)}, u32[]{:S(2)}) copy-start(f32[32,8,4,128]{3,0,2,1:T(8,128)S(1)} %all_gather.11) | copy-start | bytes 1572868
  9.1 27.4 %collective-permute-start.5 = (f32[32,8,1,128]{3,0,2,1:T(8,128)}, f32[32,8,1,128]{3,0,2,1:T(8,128)S(1)}, u32[]{:S(2)}, u32[]{:S(2)}) collective-permute-start(f32[32,8,1,128]{3,0,2,1:T(8,128)} %get-tuple-element.16), channel_id=1, source_target_pairs={{8,0},{16,8},{24,16},{32,24},{40,32},{48,40},{56,48},{64,56},{72,6... | collective-permute-start | bytes 393224 | tf_op jit(solution)/shard_map/ppermute | solution.py:15
  10.4 26.0 %collective-permute-start.4 = (f32[32,8,1,128]{3,0,2,1:T(8,128)S(1)}, f32[32,8,1,128]{3,0,2,1:T(8,128)S(1)}, u32[]{:S(2)}, u32[]{:S(2)}) collective-permute-start(f32[32,8,1,128]{3,0,2,1:T(8,128)S(1)} %get-tuple-element.17), channel_id=1, source_target_pairs={{0,8},{8,16},{16,24},{24,32},{32,40},{40,48},{48,56},{56,64},{64,7... | collective-permute-start | bytes 393224 | tf_op jit(solution)/shard_map/ppermute | solution.py:12
  22.8 39.7 %copy-start.3 = (f32[32,8,4,128]{3,0,2,1:T(8,128)}, f32[32,8,4,128]{3,0,2,1:T(8,128)S(1)}, u32[]{:S(2)}) copy-start(f32[32,8,4,128]{3,0,2,1:T(8,128)S(1)} %all_gather.9) | copy-start | bytes 1572868
  22.9 24.5 %collective-permute-start.1 = (f32[32,8,1,128]{3,0,2,1:T(8,128)S(1)}, f32[32,8,1,128]{3,0,2,1:T(8,128)S(1)}, u32[]{:S(2)}, u32[]{:S(2)}) collective-permute-start(f32[32,8,1,128]{3,0,2,1:T(8,128)S(1)} %get-tuple-element.18), channel_id=1, source_target_pairs={{8,0},{16,8},{24,16},{32,24},{40,32},{48,40},{56,48},{64,56},{72,6... | collective-permute-start | bytes 393224 | tf_op jit(solution)/shard_map/ppermute | solution.py:15
  24.2 23.1 %collective-permute-start = (f32[32,8,1,128]{3,0,2,1:T(8,128)S(1)}, f32[32,8,1,128]{3,0,2,1:T(8,128)S(1)}, u32[]{:S(2)}, u32[]{:S(2)}) collective-permute-start(f32[32,8,1,128]{3,0,2,1:T(8,128)S(1)} %get-tuple-element.19), channel_id=1, source_target_pairs={{0,8},{8,16},{16,24},{24,32},{32,40},{40,48},{48,56},{56,64},{64,7... | collective-permute-start | bytes 393224 | tf_op jit(solution)/shard_map/ppermute | solution.py:12
  36.4 10.8 %copy-start.11 = (f32[32,8,1,128]{3,0,2,1:T(8,128)}, f32[32,8,1,128]{3,0,2,1:T(8,128)S(1)}, u32[]{:S(2)}) copy-start(f32[32,8,1,128]{3,0,2,1:T(8,128)S(1)} %collective-permute-done.4) | copy-start | bytes 393220
  36.5 10.8 %copy-start.12 = (f32[32,8,1,128]{3,0,2,1:T(8,128)}, f32[32,8,1,128]{3,0,2,1:T(8,128)S(1)}, u32[]{:S(2)}) copy-start(f32[32,8,1,128]{3,0,2,1:T(8,128)S(1)} %collective-permute-done.5) | copy-start | bytes 393220
  39.5 23.0 %collective-permute-start.7 = (f32[32,8,6,1]{0,1,3,2:T(8,128)S(1)}, f32[32,8,6,1]{0,1,3,2:T(8,128)S(1)}, u32[]{:S(2)}, u32[]{:S(2)}) collective-permute-start(f32[32,8,6,1]{0,1,3,2:T(8,128)S(1)} %copy.162), channel_id=1, source_target_pairs={{1,0},{2,1},{3,2},{4,3},{5,4},{6,5},{7,6},{9,8},{10,9},{11,10},{12... | collective-permute-start | bytes 18440 | tf_op jit(solution)/shard_map/ppermute | solution.py:15
  45.3 15.9 %collective-permute-start.6 = (f32[32,8,6,1]{0,1,3,2:T(8,128)S(1)}, f32[32,8,6,1]{0,1,3,2:T(8,128)S(1)}, u32[]{:S(2)}, u32[]{:S(2)}) collective-permute-start(f32[32,8,6,1]{0,1,3,2:T(8,128)S(1)} %copy.161), channel_id=1, source_target_pairs={{0,1},{1,2},{2,3},{3,4},{4,5},{5,6},{6,7},{8,9},{9,10},{10,11},{11... | collective-permute-start | bytes 18440 | tf_op jit(solution)/shard_map/ppermute | solution.py:12
  47.3 15.2 %copy-start.9 = (f32[32,8,1,128]{3,0,2,1:T(8,128)}, f32[32,8,1,128]{3,0,2,1:T(8,128)S(1)}, u32[]{:S(2)}) copy-start(f32[32,8,1,128]{3,0,2,1:T(8,128)S(1)} %collective-permute-done) | copy-start | bytes 393220
  47.4 15.2 %copy-start.7 = (f32[32,8,1,128]{3,0,2,1:T(8,128)}, f32[32,8,1,128]{3,0,2,1:T(8,128)S(1)}, u32[]{:S(2)}) copy-start(f32[32,8,1,128]{3,0,2,1:T(8,128)S(1)} %collective-permute-done.1) | copy-start | bytes 393220
  51.6 38.3 %collective-permute-start.3 = (f32[32,8,6,1]{0,1,3,2:T(8,128)}, f32[32,8,6,1]{0,1,3,2:T(8,128)}, u32[]{:S(2)}, u32[]{:S(2)}) collective-permute-start(f32[32,8,6,1]{0,1,3,2:T(8,128)} %copy.128), channel_id=1, source_target_pairs={{1,0},{2,1},{3,2},{4,3},{5,4},{6,5},{7,6},{9,8},{10,9},{11,10},{12... | collective-permute-start | bytes 18440 | tf_op jit(solution)/shard_map/ppermute | solution.py:15
  59.2 28.8 %collective-permute-start.2 = (f32[32,8,6,1]{0,1,3,2:T(8,128)}, f32[32,8,6,1]{0,1,3,2:T(8,128)}, u32[]{:S(2)}, u32[]{:S(2)}) collective-permute-start(f32[32,8,6,1]{0,1,3,2:T(8,128)} %copy.127), channel_id=1, source_target_pairs={{0,1},{1,2},{2,3},{3,4},{4,5},{5,6},{6,7},{8,9},{9,10},{10,11},{11... | collective-permute-start | bytes 18440 | tf_op jit(solution)/shard_map/ppermute | solution.py:12
  63.8 11.0 %copy-start.2 = (f32[32,8,6,1]{3,0,2,1:T(8,128)S(1)}, f32[32,8,6,1]{3,0,2,1:T(8,128)}, u32[]{:S(2)}) copy-start(f32[32,8,6,1]{3,0,2,1:T(8,128)} %copy.164) | copy-start | bytes 18436
  63.8 12.2 %copy-start.6 = (f32[32,8,4,128]{3,0,2,1:T(8,128)S(1)}, f32[32,8,4,128]{3,0,2,1:T(8,128)}, u32[]{:S(2)}) copy-start(f32[32,8,4,128]{3,0,2,1:T(8,128)} %copy-done.5) | copy-start | bytes 1572868
  63.8 12.2 %copy-start.13 = (f32[32,8,1,128]{3,0,2,1:T(8,128)S(1)}, f32[32,8,1,128]{3,0,2,1:T(8,128)}, u32[]{:S(2)}) copy-start(f32[32,8,1,128]{3,0,2,1:T(8,128)} %copy-done.12) | copy-start | bytes 393220
  63.8 13.1 %copy-start = (f32[32,8,6,1]{3,0,2,1:T(8,128)S(1)}, f32[32,8,6,1]{3,0,2,1:T(8,128)}, u32[]{:S(2)}) copy-start(f32[32,8,6,1]{3,0,2,1:T(8,128)} %copy.163) | copy-start | bytes 18436
  91.1 3.4 %copy-start.1 = (f32[32,8,6,1]{3,0,2,1:T(8,128)S(1)}, f32[32,8,6,1]{3,0,2,1:T(8,128)}, u32[]{:S(2)}) copy-start(f32[32,8,6,1]{3,0,2,1:T(8,128)} %copy.129) | copy-start | bytes 18436
  91.1 3.6 %copy-start.4 = (f32[32,8,4,128]{3,0,2,1:T(8,128)S(1)}, f32[32,8,4,128]{3,0,2,1:T(8,128)}, u32[]{:S(2)}) copy-start(f32[32,8,4,128]{3,0,2,1:T(8,128)} %copy-done.3) | copy-start | bytes 1572868
  91.1 3.6 %copy-start.10 = (f32[32,8,1,128]{3,0,2,1:T(8,128)S(1)}, f32[32,8,1,128]{3,0,2,1:T(8,128)}, u32[]{:S(2)}) copy-start(f32[32,8,1,128]{3,0,2,1:T(8,128)} %copy-done.9) | copy-start | bytes 393220
  91.1 4.8 %copy-start.8 = (f32[32,8,1,128]{3,0,2,1:T(8,128)S(1)}, f32[32,8,1,128]{3,0,2,1:T(8,128)}, u32[]{:S(2)}) copy-start(f32[32,8,1,128]{3,0,2,1:T(8,128)} %copy-done.7) | copy-start | bytes 393220
  94.0 3.7 %copy-start.14 = (f32[8,8,4,128]{3,2,1,0:T(4,128)S(1)}, f32[8,8,4,128]{3,2,1,0:T(4,128)}, u32[]{:S(2)}) copy-start(f32[8,8,4,128]{3,2,1,0:T(4,128)} %param.5) | copy-start | bytes 393220
  95.6 29.2 %copy-start.15 = (f32[8,32,3,3,3]{1,0,4,3,2:T(8,128)S(1)}, f32[8,32,3,3,3]{1,0,4,3,2:T(8,128)}, u32[]{:S(2)}) copy-start(f32[8,32,3,3,3]{1,0,4,3,2:T(8,128)} %param.4) | copy-start | bytes 82948
  124.8 65.9 %copy-start.16 = (f32[32,8,3,3,3]{0,1,4,3,2:T(8,128)S(1)}, f32[32,8,3,3,3]{0,1,4,3,2:T(8,128)}, u32[]{:S(2)}) copy-start(f32[32,8,3,3,3]{0,1,4,3,2:T(8,128)} %copy.159) | copy-start | bytes 82948
  132.9 5.8 %collective-permute-start.8 = (f32[54,128]{1,0:T(8,128)S(1)}, f32[54,128]{1,0:T(8,128)S(1)}, u32[]{:S(2)}, u32[]{:S(2)}) collective-permute-start(f32[54,128]{1,0:T(8,128)S(1)} %reshape_reshape.3), channel_id=1, source_target_pairs={{0,8},{8,0},{16,24},{24,16},{32,40},{40,32},{48,56},{56,48},{64,72... | collective-permute-start | bytes 82952 | tf_op jit(solution)/shard_map/ppermute | solution.py:26
  138.7 9.1 %collective-permute-start.9 = (f32[54,128]{1,0:T(8,128)S(1)}, f32[54,128]{1,0:T(8,128)S(1)}, u32[]{:S(2)}, u32[]{:S(2)}) collective-permute-start(f32[54,128]{1,0:T(8,128)S(1)} %add.29), channel_id=1, source_target_pairs={{0,16},{8,24},{16,0},{24,8},{32,48},{40,56},{48,32},{56,40},{64,80... | collective-permute-start | bytes 82952 | tf_op jit(solution)/shard_map/ppermute | solution.py:26
  147.9 10.9 %collective-permute-start.10 = (f32[54,128]{1,0:T(8,128)S(1)}, f32[54,128]{1,0:T(8,128)S(1)}, u32[]{:S(2)}, u32[]{:S(2)}) collective-permute-start(f32[54,128]{1,0:T(8,128)S(1)} %add.30), channel_id=1, source_target_pairs={{0,32},{8,40},{16,48},{24,56},{32,0},{40,8},{48,16},{56,24},{64,96... | collective-permute-start | bytes 82952 | tf_op jit(solution)/shard_map/ppermute | solution.py:26
  158.8 14.5 %collective-permute-start.11 = (f32[54,128]{1,0:T(8,128)S(1)}, f32[54,128]{1,0:T(8,128)S(1)}, u32[]{:S(2)}, u32[]{:S(2)}) collective-permute-start(f32[54,128]{1,0:T(8,128)S(1)} %add.31), channel_id=1, source_target_pairs={{0,64},{8,72},{16,80},{24,88},{32,96},{40,104},{48,112},{56,120},{... | collective-permute-start | bytes 82952 | tf_op jit(solution)/shard_map/ppermute | solution.py:26
  173.3 5.8 %collective-permute-start.12 = (f32[54,128]{1,0:T(8,128)S(1)}, f32[54,128]{1,0:T(8,128)S(1)}, u32[]{:S(2)}, u32[]{:S(2)}) collective-permute-start(f32[54,128]{1,0:T(8,128)S(1)} %add.32), channel_id=1, source_target_pairs={{0,1},{1,0},{2,3},{3,2},{4,5},{5,4},{6,7},{7,6},{8,9},{9,8},{10,11... | collective-permute-start | bytes 82952 | tf_op jit(solution)/shard_map/ppermute | solution.py:26
  179.0 7.3 %collective-permute-start.13 = (f32[54,128]{1,0:T(8,128)S(1)}, f32[54,128]{1,0:T(8,128)S(1)}, u32[]{:S(2)}, u32[]{:S(2)}) collective-permute-start(f32[54,128]{1,0:T(8,128)S(1)} %add.33), channel_id=1, source_target_pairs={{0,2},{1,3},{2,0},{3,1},{4,6},{5,7},{6,4},{7,5},{8,10},{9,11},{10,... | collective-permute-start | bytes 82952 | tf_op jit(solution)/shard_map/ppermute | solution.py:26
  186.3 18.2 %collective-permute-start.14 = (f32[54,128]{1,0:T(8,128)S(1)}, f32[54,128]{1,0:T(8,128)S(1)}, u32[]{:S(2)}, u32[]{:S(2)}) collective-permute-start(f32[54,128]{1,0:T(8,128)S(1)} %add.34), channel_id=1, source_target_pairs={{0,4},{1,5},{2,6},{3,7},{4,0},{5,1},{6,2},{7,3},{8,12},{9,13},{10,... | collective-permute-start | bytes 82952 | tf_op jit(solution)/shard_map/ppermute | solution.py:26

commit v5 on v4

--- a/solution.py
+++ b/solution.py
@@ -43,23 +43,21 @@
 
 
 def shards(volume, filters, upstream):
-    planes, rows_x, rows_y = (volume.shape[1], volume.shape[2], volume.shape[3])
-    own_inputs = volume.shape[0]
+    channels, planes, rows_x, rows_y = volume.shape
+    own_inputs = channels
+    ncol = lax.axis_size("col")
     scale = (planes * rows_x * lax.axis_size("gx") * rows_y * lax.axis_size("gy")) ** (-0.5)
-    gathered = lax.all_gather(volume, "col", axis=0, tiled=True)
-    padded = pad_depth(with_halo(gathered, (("gx", 2), ("gy", 3)), 1))
+    cells = volume.size
+    joined = jnp.concatenate([volume.reshape(-1), upstream.reshape(-1), filters.reshape(-1)])
+    every = lax.all_gather(joined, "col", axis=0, tiled=False)
+    fields = every[:, : 2 * cells].reshape(ncol, 2, channels, planes, rows_x, rows_y)
+    fields = jnp.swapaxes(fields, 0, 1).reshape(2, ncol * channels, planes, rows_x, rows_y)
+    all_rows = every[:, 2 * cells :].reshape((ncol * filters.shape[0],) + filters.shape[1:])
+    both = with_halo(fields, (("gx", 3), ("gy", 4)), 1)
+    both = jnp.pad(both, ((0, 0), (0, 0), (1, 1), (0, 0), (0, 0)))
+    padded, padded_up = both[0], both[1]
     taps = patches(padded, planes, rows_x, rows_y, False)
-    by_tap = jnp.swapaxes(filters.reshape(filters.shape[0], filters.shape[1], 27), 1, 2)
-    response = jnp.einsum("okc,kcpqy->opqy", by_tap, taps, precision=lax.Precision.HIGHEST)
-    all_rows = lax.all_gather(filters, "col", axis=0, tiled=True)
-    all_upstream = lax.all_gather(upstream, "col", axis=0, tiled=True)
-    padded_up = pad_depth(with_halo(all_upstream, (("gx", 2), ("gy", 3)), 1))
-    first = lax.axis_index("col") * own_inputs
-    own_filters = lax.dynamic_slice_in_dim(all_rows, first, own_inputs, 1)
-    own_by_tap = jnp.swapaxes(own_filters.reshape(own_filters.shape[0], own_inputs, 27), 1, 2)
-    taps_up = patches(padded_up, planes, rows_x, rows_y, True)
-    input_grad = jnp.einsum("okc,kopqy->cpqy", own_by_tap, taps_up, precision=lax.Precision.HIGHEST)
-    local_grad = jnp.einsum("opqy,kcpqy->ock", upstream, taps, precision=lax.Precision.HIGHEST)
+    local_grad = jnp.einsum("opqy,kcpqy->ock", upstream, taps, precision=lax.Precision.HIGH)
     local_grad = local_grad.reshape(local_grad.shape[0], local_grad.shape[1], 3, 3, 3)
     flat = local_grad.reshape(-1, 128)
     sizes = [lax.axis_size(a) for a in ("gx", "gy")]
@@ -68,6 +66,13 @@
     else:
         flat = lax.psum(flat, ("gx", "gy"))
     total_grad = flat.reshape(local_grad.shape)
+    by_tap = jnp.swapaxes(filters.reshape(filters.shape[0], filters.shape[1], 27), 1, 2)
+    response = jnp.einsum("okc,kcpqy->opqy", by_tap, taps, precision=lax.Precision.HIGH)
+    first = lax.axis_index("col") * own_inputs
+    own_filters = lax.dynamic_slice_in_dim(all_rows, first, own_inputs, 1)
+    own_by_tap = jnp.swapaxes(own_filters.reshape(own_filters.shape[0], own_inputs, 27), 1, 2)
+    taps_up = patches(padded_up, planes, rows_x, rows_y, True)
+    input_grad = jnp.einsum("okc,kopqy->cpqy", own_by_tap, taps_up, precision=lax.Precision.HIGH)
     return (response, input_grad, total_grad * scale)
 
 

time: 209 us -> 195 us (0.933)
  waiting for transfers between devices: 11.4 us -> 52.1 us
  matrix products: 47.4 us -> 24.7 us
  starting transfers between devices: 69.3 us -> 46.8 us
  blocking collectives: 20.3 us -> 0 us
  between operations: 1.16 us -> 14.4 us
  other arithmetic: 15.1 us -> 4.47 us
  local copies, waits for them, and re-layouts: 42.3 us -> 48.7 us
    all_gather x0 -> x1, waiting for transfers between devices: none -> 33.1 us  [shards(): every = lax.all_gather(joined, 'col', axis=0, tiled=False)]
    all_gather x3 -> x0, blocking collectives: 20.3 us -> none  [the longest x1 6.9 us: shards(): gathered = lax.all_gather(volume, 'col', axis=0, tiled=True)]
    dot_general x2, matrix products: 35 us -> 17.1 us  [the longest x1 13.7 us: shards(): jnp.einsum('opqy,kcpqy->ock', upstream, taps, precision=lax.Precision.HIGH)]
    unnamed x16 -> x0, other arithmetic: 11 us -> none
    reshape x0 -> x3, local copies, waits for them, and re-layouts: none -> 9.31 us  [the longest x1 6.45 us: shards(): every[:, 2 * cells:].reshape((ncol * filters.shape[0],) + filters.shape[1:])]
    ppermute x4 -> x2, starting transfers between devices: 15.9 us -> 6.77 us  [with_halo(): lax.ppermute(lax.slice_in_dim(block, 0, width, axis=dim), axis, backward)]
    ppermute x4 -> x2, starting transfers between devices: 13.1 us -> 5.39 us  [with_halo(): lax.ppermute(lax.slice_in_dim(block, block.shape[dim] - width, None, axis...]
    ppermute x7, starting transfers between devices: 40.3 us -> 34.6 us  [butterfly_sum(): value = value + lax.ppermute(value, axis, pairs)]
  transfers between devices with their start and end apart: 15 -> 12, of which waited for: 6 -> 9; matrix products, arithmetic and copies ran while one was open for 28% -> 13% of each run, Pallas kernels for 0% -> 0%
where the time goes in v5:
time: 195 us; the launch traced here: 191 us
  waiting for transfers between devices  52.1 us (27%)
  local copies, waits for them, and re-layouts  48.7 us (25%)
  starting transfers between devices  46.8 us (24%)
  matrix products  24.7 us (13%)
  between operations  14.4 us (7%)
  other arithmetic  4.47 us (2%)
    ppermute x7, starting transfers between devices, butterfly_sum(): value = value + lax.ppermute(value, axis, pairs)  34.6 us
    all_gather x1, waiting for transfers between devices, shards(): every = lax.all_gather(joined, 'col', axis=0, tiled=False)  33.1 us
    unnamed x66, local copies, waits for them, and re-layouts  24.5 us
    dot_general x1, matrix products, shards(): jnp.einsum('opqy,kcpqy->ock', upstream, taps, precision=lax.Precision.HIGH)  13.7 us
    ppermute x7, waiting for transfers between devices, butterfly_sum(): value = value + lax.ppermute(value, axis, pairs)  12.6 us
    dot_general x1, matrix products, shards(): jnp.einsum('okc,kopqy->cpqy', own_by_tap, taps_up, precision=lax.Precisio...  7.58 us
    ppermute x2, starting transfers between devices, with_halo(): lax.ppermute(lax.slice_in_dim(block, 0, width, axis=dim), axis, backward)  6.77 us
    reshape x1, local copies, waits for them, and re-layouts, shards(): every[:, 2 * cells:].reshape((ncol * filters.shape[0],) + filters.shape[1:])  6.45 us
  transfers between devices with their start and end apart: 12, of which 9 were waited for; matrix products, arithmetic and copies ran while one was open for 13% of the time, Pallas kernels for 0%

profile of v5, /device:TPU:6, one launch (start us, length us, event | category | flops | bytes accessed | tf_op | source)
XLA Modules:
  0.0 191.2 jit_solution(12822308997141777042)
XLA Ops:
  7.2 2.1 %copy.73 = f32[8,32,3,3,3]{4,3,2,1,0:T(4,128)S(1)} copy(f32[8,32,3,3,3]{1,0,4,3,2:T(8,128)} %param.4) | data formatting | bytes 55296 | tf_op args[1]
  9.3 1.0 reshape.35
  10.3 1.0 pad_maximum_fusion.1
  11.2 0.9 reshape.42
  12.2 33.1 %all-gather.4.cloned.1.call-done = f32[4,1,72448]{2,1,0:T(1,128)} async-done(((f32[1,1,72448]{2,1,0:T(1,128)}), f32[4,1,72448]{2,1,0:T(1,128)}) %all-gather.4.cloned.1.call-update) | async-done | bytes 1159184 | tf_op jit(solution)/shard_map/all_gather | solution.py:52
  45.3 1.6 copy.125
  46.9 1.9 reshape.36
  48.8 1.8 copy.126
  50.7 3.5 %collective-permute-start = (f32[2,32,8,1,128]{4,1,3,2,0:T(8,128)S(1)}, f32[2,32,8,1,128]{4,1,3,2,0:T(8,128)S(1)}, u32[]{:S(2)}, u32[]{:S(2)}) collective-permute-start(f32[2,32,8,1,128]{4,1,3,2,0:T(8,128)S(1)} %get-tuple-element.16), channel_id=1, source_target_pairs={{0,8},{8,16},{16,24},{24,32},{32,40},{40,48},{48,56},{56,64},{64,7... | collective-permute-start | bytes 786440 | tf_op jit(solution)/shard_map/ppermute | solution.py:12
  54.2 1.3 collective-permute-start.1
  55.5 6.4 %reshape.39 = f32[32,32,3,3,3]{4,3,2,1,0:T(4,128)} reshape(f32[4,6912]{1,0:T(4,128)S(1)} %slice.281) | data formatting | bytes 221184 | tf_op jit(solution)/shard_map/reshape | solution.py:55
  61.9 2.2 %collective-permute-done.1 = f32[2,32,8,1,128]{4,1,3,2,0:T(8,128)S(1)} collective-permute-done((f32[2,32,8,1,128]{4,1,3,2,0:T(8,128)S(1)}, f32[2,32,8,1,128]{4,1,3,2,0:T(8,128)S(1)}, u32[]{:S(2)}, u32[]{:S(2)}) %collective-permute-start.1) | collective-permute-done | bytes 262176 | tf_op jit(solution)/shard_map/ppermute | solution.py:15
  64.2 1.7 fusion.56
  65.9 2.0 %copy.75 = f32[2,32,8,6,1]{1,2,4,3,0:T(8,128)S(1)} copy(f32[2,32,8,6,1]{4,1,3,2,0:T(8,128)} %get-tuple-element.14) | data formatting | bytes 24576 | tf_op jit(solution)/shard_map/slice | solution.py:13
  68.6 5.5 %collective-permute-start.3 = (f32[2,32,8,6,1]{1,2,4,3,0:T(8,128)S(1)}, f32[2,32,8,6,1]{1,2,4,3,0:T(8,128)S(1)}, u32[]{:S(2)}, u32[]{:S(2)}) collective-permute-start(f32[2,32,8,6,1]{1,2,4,3,0:T(8,128)S(1)} %copy.76), channel_id=1, source_target_pairs={{1,0},{2,1},{3,2},{4,3},{5,4},{6,5},{7,6},{9,8},{10,9},{11,10},{12... | collective-permute-start | bytes 36872 | tf_op jit(solution)/shard_map/ppermute | solution.py:15
  74.1 1.9 %collective-permute-start.2 = (f32[2,32,8,6,1]{1,2,4,3,0:T(8,128)S(1)}, f32[2,32,8,6,1]{1,2,4,3,0:T(8,128)S(1)}, u32[]{:S(2)}, u32[]{:S(2)}) collective-permute-start(f32[2,32,8,6,1]{1,2,4,3,0:T(8,128)S(1)} %copy.75), channel_id=1, source_target_pairs={{0,1},{1,2},{2,3},{3,4},{4,5},{5,6},{6,7},{8,9},{9,10},{10,11},{11... | collective-permute-start | bytes 36872 | tf_op jit(solution)/shard_map/ppermute | solution.py:12
  76.0 1.7 constant_dynamic-slice_fusion
  77.7 1.8 copy.105
  79.5 4.2 %collective-permute-done.2 = f32[2,32,8,6,1]{1,2,4,3,0:T(8,128)S(1)} collective-permute-done((f32[2,32,8,6,1]{1,2,4,3,0:T(8,128)S(1)}, f32[2,32,8,6,1]{1,2,4,3,0:T(8,128)S(1)}, u32[]{:S(2)}, u32[]{:S(2)}) %collective-permute-start.2) | collective-permute-done | bytes 12320 | tf_op jit(solution)/shard_map/ppermute | solution.py:12
  84.3 1.8 copy.78
  86.1 3.3 %select_maximum_fusion = f32[2,32,10,6,130]{4,1,3,2,0:T(8,128)S(1)} fusion(f32[2,32,8,6,1]{4,1,3,2,0:T(8,128)} %copy.78, f32[2,32,8,6,1]{4,1,3,2,0:T(8,128)S(1)} %copy.77, f32[2,32,8,1,128]{4,1,3,2,0:T(8,128)S(1)} %collective-permute-done.1, f32[2,32,8,4,128]{4,1,3,2,0:T(8,128)S(1)} %bitcast.321, f32[2,32,8,1,128]{4,1,3,2,0:T(8,128)S(1)} %collective-permute-done), kind=kLoop, calls=%fused_computation.2 | loop fusion | flops 5990400 | bytes 3594240 | tf_op jit(solution)/shard_map/concatenate | solution.py:16
  93.1 5.0 %copy-done = f32[27,32,8,4,128]{4,1,3,2,0:T(8,128)} copy-done((f32[27,32,8,4,128]{4,1,3,2,0:T(8,128)}, f32[27,32,8,4,128]{4,1,3,2,0:T(8,128)S(1)}, u32[]{:S(2)}) %copy-start) | copy-done | bytes 14155800
  102.3 13.7 %convolution_bitcast_fusion.2 = f32[8,32,27]{1,0,2:T(8,128)S(1)} fusion(f32[27,32,8,4,128]{4,1,0,3,2:T(8,128)S(1)} %fusion.28, f32[8,8,4,128,1]{3,2,1,0,4:T(4,128)S(1)} %bitcast.326), kind=kOutput, calls=%fused_computation.13 | convolution fusion | flops 169869312 | bytes 14314496 | tf_op jit(solution)/shard_map/opqy,kcpqy->ock/dot_general | solution.py:60
  116.0 3.4 %convolution_bitcast_fusion.1 = f32[8,8,4,128]{3,0,2,1:T(8,128)S(1)} fusion(f32[27,32,8,4,128]{4,1,0,3,2:T(8,128)S(1)} %fusion.28, f32[8,27,32,1,1]{2,0,1,4,3:T(8,128)S(1)} %bitcast.327), kind=kOutput, calls=%fused_computation.12 | convolution fusion | flops 169869312 | bytes 14314496 | tf_op jit(solution)/shard_map/okc,kcpqy->opqy/dot_general | solution.py:70
  119.7 3.5 %collective-permute-start.4 = (f32[54,128]{1,0:T(8,128)S(1)}, f32[54,128]{1,0:T(8,128)S(1)}, u32[]{:S(2)}, u32[]{:S(2)}) collective-permute-start(f32[54,128]{1,0:T(8,128)S(1)} %reshape_reshape.3), channel_id=1, source_target_pairs={{0,8},{8,0},{16,24},{24,16},{32,40},{40,32},{48,56},{56,48},{64,72... | collective-permute-start | bytes 82952 | tf_op jit(solution)/shard_map/ppermute | solution.py:26
  123.2 1.0 fusion.6
  124.2 1.3 collective-permute-done.4
  125.5 6.4 %collective-permute-start.5 = (f32[54,128]{1,0:T(8,128)S(1)}, f32[54,128]{1,0:T(8,128)S(1)}, u32[]{:S(2)}, u32[]{:S(2)}) collective-permute-start(f32[54,128]{1,0:T(8,128)S(1)} %add.27), channel_id=1, source_target_pairs={{0,16},{8,24},{16,0},{24,8},{32,48},{40,56},{48,32},{56,40},{64,80... | collective-permute-start | bytes 82952 | tf_op jit(solution)/shard_map/ppermute | solution.py:26
  131.9 1.0 fusion.5
  132.9 0.8 collective-permute-done.5
  133.8 7.6 %collective-permute-start.6 = (f32[54,128]{1,0:T(8,128)S(1)}, f32[54,128]{1,0:T(8,128)S(1)}, u32[]{:S(2)}, u32[]{:S(2)}) collective-permute-start(f32[54,128]{1,0:T(8,128)S(1)} %add.28), channel_id=1, source_target_pairs={{0,32},{8,40},{16,48},{24,56},{32,0},{40,8},{48,16},{56,24},{64,96... | collective-permute-start | bytes 82952 | tf_op jit(solution)/shard_map/ppermute | solution.py:26
  141.4 0.9 fusion.4
  142.3 1.2 collective-permute-done.6
  143.4 11.4 %collective-permute-start.7 = (f32[54,128]{1,0:T(8,128)S(1)}, f32[54,128]{1,0:T(8,128)S(1)}, u32[]{:S(2)}, u32[]{:S(2)}) collective-permute-start(f32[54,128]{1,0:T(8,128)S(1)} %add.29), channel_id=1, source_target_pairs={{0,64},{8,72},{16,80},{24,88},{32,96},{40,104},{48,112},{56,120},{... | collective-permute-start | bytes 82952 | tf_op jit(solution)/shard_map/ppermute | solution.py:26
  154.9 1.0 fusion.3
  155.9 2.0 %collective-permute-done.7 = f32[54,128]{1,0:T(8,128)S(1)} collective-permute-done((f32[54,128]{1,0:T(8,128)S(1)}, f32[54,128]{1,0:T(8,128)S(1)}, u32[]{:S(2)}, u32[]{:S(2)}) %collective-permute-start.7) | collective-permute-done | bytes 27680 | tf_op jit(solution)/shard_map/ppermute | solution.py:26
  157.9 1.9 collective-permute-start.8
  159.8 1.0 fusion.2
  160.8 2.8 %collective-permute-done.8 = f32[54,128]{1,0:T(8,128)S(1)} collective-permute-done((f32[54,128]{1,0:T(8,128)S(1)}, f32[54,128]{1,0:T(8,128)S(1)}, u32[]{:S(2)}, u32[]{:S(2)}) %collective-permute-start.8) | collective-permute-done | bytes 27680 | tf_op jit(solution)/shard_map/ppermute | solution.py:26
  163.7 1.9 collective-permute-start.9
  165.6 0.9 fusion.1
  166.4 4.5 %collective-permute-done.9 = f32[54,128]{1,0:T(8,128)S(1)} collective-permute-done((f32[54,128]{1,0:T(8,128)S(1)}, f32[54,128]{1,0:T(8,128)S(1)}, u32[]{:S(2)}, u32[]{:S(2)}) %collective-permute-start.9) | collective-permute-done | bytes 27680 | tf_op jit(solution)/shard_map/ppermute | solution.py:26
  170.9 1.9 collective-permute-start.10
  172.8 7.6 %convolution_bitcast_fusion = f32[8,8,4,128]{3,0,2,1:T(8,128)S(1)} fusion(f32[32,27,8,1,1]{0,2,4,3,1:T(8,128)S(1)} %bitcast.328, f32[27,32,8,4,128]{4,1,3,2,0:T(8,128)} %fusion.1), kind=kOutput, calls=%fused_computation.11 | convolution fusion | flops 169869312 | bytes 14314496 | tf_op jit(solution)/shard_map/okc,kopqy->cpqy/dot_general | solution.py:75
  180.4 0.7 copy.110
  181.1 0.7 copy.109
  181.8 0.8 mul.15
  182.7 1.6 copy.111
  (76 shorter events, 9.5 us)
Async XLA Ops:
  7.2 38.1 %all-gather.4.cloned.1.call-start = ((), (), s32[]{:S(2)}) async-start(), calls=%async_computation | async-start | bytes 1448960 | tf_op jit(solution)/shard_map/all_gather | solution.py:52
  50.7 11.3 %collective-permute-start = (f32[2,32,8,1,128]{4,1,3,2,0:T(8,128)S(1)}, f32[2,32,8,1,128]{4,1,3,2,0:T(8,128)S(1)}, u32[]{:S(2)}, u32[]{:S(2)}) collective-permute-start(f32[2,32,8,1,128]{4,1,3,2,0:T(8,128)S(1)} %get-tuple-element.16), channel_id=1, source_target_pairs={{0,8},{8,16},{16,24},{24,32},{32,40},{40,48},{48,56},{56,64},{64,7... | collective-permute-start | bytes 786440 | tf_op jit(solution)/shard_map/ppermute | solution.py:12
  54.2 10.0 %collective-permute-start.1 = (f32[2,32,8,1,128]{4,1,3,2,0:T(8,128)S(1)}, f32[2,32,8,1,128]{4,1,3,2,0:T(8,128)S(1)}, u32[]{:S(2)}, u32[]{:S(2)}) collective-permute-start(f32[2,32,8,1,128]{4,1,3,2,0:T(8,128)S(1)} %get-tuple-element.17), channel_id=1, source_target_pairs={{8,0},{16,8},{24,16},{32,24},{40,32},{48,40},{56,48},{64,56},{72,6... | collective-permute-start | bytes 786440 | tf_op jit(solution)/shard_map/ppermute | solution.py:15
  68.6 15.7 %collective-permute-start.3 = (f32[2,32,8,6,1]{1,2,4,3,0:T(8,128)S(1)}, f32[2,32,8,6,1]{1,2,4,3,0:T(8,128)S(1)}, u32[]{:S(2)}, u32[]{:S(2)}) collective-permute-start(f32[2,32,8,6,1]{1,2,4,3,0:T(8,128)S(1)} %copy.76), channel_id=1, source_target_pairs={{1,0},{2,1},{3,2},{4,3},{5,4},{6,5},{7,6},{9,8},{10,9},{11,10},{12... | collective-permute-start | bytes 36872 | tf_op jit(solution)/shard_map/ppermute | solution.py:15
  74.1 9.6 %collective-permute-start.2 = (f32[2,32,8,6,1]{1,2,4,3,0:T(8,128)S(1)}, f32[2,32,8,6,1]{1,2,4,3,0:T(8,128)S(1)}, u32[]{:S(2)}, u32[]{:S(2)}) collective-permute-start(f32[2,32,8,6,1]{1,2,4,3,0:T(8,128)S(1)} %copy.75), channel_id=1, source_target_pairs={{0,1},{1,2},{2,3},{3,4},{4,5},{5,6},{6,7},{8,9},{9,10},{10,11},{11... | collective-permute-start | bytes 36872 | tf_op jit(solution)/shard_map/ppermute | solution.py:12
  93.1 5.1 %copy-start = (f32[27,32,8,4,128]{4,1,3,2,0:T(8,128)}, f32[27,32,8,4,128]{4,1,3,2,0:T(8,128)S(1)}, u32[]{:S(2)}) copy-start(f32[27,32,8,4,128]{4,1,3,2,0:T(8,128)S(1)} %fusion.7) | copy-start | bytes 42467332
  98.2 4.1 %copy-start.1 = (f32[8,8,4,128]{3,2,1,0:T(4,128)S(1)}, f32[8,8,4,128]{3,2,1,0:T(4,128)}, u32[]{:S(2)}) copy-start(f32[8,8,4,128]{3,2,1,0:T(4,128)} %param.5) | copy-start | bytes 393220
  100.2 15.7 %copy-start.2 = (f32[8,32,3,3,3]{1,0,4,3,2:T(8,128)S(1)}, f32[8,32,3,3,3]{1,0,4,3,2:T(8,128)}, u32[]{:S(2)}) copy-start(f32[8,32,3,3,3]{1,0,4,3,2:T(8,128)} %param.4) | copy-start | bytes 82948
  116.0 56.9 %copy-start.3 = (f32[32,8,3,3,3]{0,1,4,3,2:T(8,128)S(1)}, f32[32,8,3,3,3]{0,1,4,3,2:T(8,128)}, u32[]{:S(2)}) copy-start(f32[32,8,3,3,3]{0,1,4,3,2:T(8,128)} %copy.105) | copy-start | bytes 82948
  119.7 5.8 %collective-permute-start.4 = (f32[54,128]{1,0:T(8,128)S(1)}, f32[54,128]{1,0:T(8,128)S(1)}, u32[]{:S(2)}, u32[]{:S(2)}) collective-permute-start(f32[54,128]{1,0:T(8,128)S(1)} %reshape_reshape.3), channel_id=1, source_target_pairs={{0,8},{8,0},{16,24},{24,16},{32,40},{40,32},{48,56},{56,48},{64,72... | collective-permute-start | bytes 82952 | tf_op jit(solution)/shard_map/ppermute | solution.py:26
  125.5 8.2 %collective-permute-start.5 = (f32[54,128]{1,0:T(8,128)S(1)}, f32[54,128]{1,0:T(8,128)S(1)}, u32[]{:S(2)}, u32[]{:S(2)}) collective-permute-start(f32[54,128]{1,0:T(8,128)S(1)} %add.27), channel_id=1, source_target_pairs={{0,16},{8,24},{16,0},{24,8},{32,48},{40,56},{48,32},{56,40},{64,80... | collective-permute-start | bytes 82952 | tf_op jit(solution)/shard_map/ppermute | solution.py:26
  133.8 9.7 %collective-permute-start.6 = (f32[54,128]{1,0:T(8,128)S(1)}, f32[54,128]{1,0:T(8,128)S(1)}, u32[]{:S(2)}, u32[]{:S(2)}) collective-permute-start(f32[54,128]{1,0:T(8,128)S(1)} %add.28), channel_id=1, source_target_pairs={{0,32},{8,40},{16,48},{24,56},{32,0},{40,8},{48,16},{56,24},{64,96... | collective-permute-start | bytes 82952 | tf_op jit(solution)/shard_map/ppermute | solution.py:26
  143.4 14.5 %collective-permute-start.7 = (f32[54,128]{1,0:T(8,128)S(1)}, f32[54,128]{1,0:T(8,128)S(1)}, u32[]{:S(2)}, u32[]{:S(2)}) collective-permute-start(f32[54,128]{1,0:T(8,128)S(1)} %add.29), channel_id=1, source_target_pairs={{0,64},{8,72},{16,80},{24,88},{32,96},{40,104},{48,112},{56,120},{... | collective-permute-start | bytes 82952 | tf_op jit(solution)/shard_map/ppermute | solution.py:26
  157.9 5.8 %collective-permute-start.8 = (f32[54,128]{1,0:T(8,128)S(1)}, f32[54,128]{1,0:T(8,128)S(1)}, u32[]{:S(2)}, u32[]{:S(2)}) collective-permute-start(f32[54,128]{1,0:T(8,128)S(1)} %add.30), channel_id=1, source_target_pairs={{0,1},{1,0},{2,3},{3,2},{4,5},{5,4},{6,7},{7,6},{8,9},{9,8},{10,11... | collective-permute-start | bytes 82952 | tf_op jit(solution)/shard_map/ppermute | solution.py:26
  163.7 7.3 %collective-permute-start.9 = (f32[54,128]{1,0:T(8,128)S(1)}, f32[54,128]{1,0:T(8,128)S(1)}, u32[]{:S(2)}, u32[]{:S(2)}) collective-permute-start(f32[54,128]{1,0:T(8,128)S(1)} %add.31), channel_id=1, source_target_pairs={{0,2},{1,3},{2,0},{3,1},{4,6},{5,7},{6,4},{7,5},{8,10},{9,11},{10,... | collective-permute-start | bytes 82952 | tf_op jit(solution)/shard_map/ppermute | solution.py:26
  170.9 10.9 %collective-permute-start.10 = (f32[54,128]{1,0:T(8,128)S(1)}, f32[54,128]{1,0:T(8,128)S(1)}, u32[]{:S(2)}, u32[]{:S(2)}) collective-permute-start(f32[54,128]{1,0:T(8,128)S(1)} %add.32), channel_id=1, source_target_pairs={{0,4},{1,5},{2,6},{3,7},{4,0},{5,1},{6,2},{7,3},{8,12},{9,13},{10,... | collective-permute-start | bytes 82952 | tf_op jit(solution)/shard_map/ppermute | solution.py:26
Sparse Core Ops, SparseCore 0:
  12.3 32.9 all-gather.3

commit v6 on v5

--- a/solution.py
+++ b/solution.py
@@ -20,11 +20,26 @@
 def butterfly_sum(value, axes):
     for axis in axes:
         count = lax.axis_size(axis)
-        step = 1
-        while step < count:
-            pairs = [(i, i ^ step) for i in range(count)]
-            value = value + lax.ppermute(value, axis, pairs)
-            step *= 2
+        index = lax.axis_index(axis)
+        stride = 1
+        while stride < count:
+            radix = 4 if (count // stride) % 4 == 0 else 2
+            member = (index // stride) % radix
+            received = [value]
+            for shift in range(1, radix):
+                pairs = []
+                for i in range(count):
+                    m = (i // stride) % radix
+                    j = i + (((m + shift) % radix) - m) * stride
+                    pairs.append((i, j))
+                received.append(lax.ppermute(value, axis, pairs))
+            stacked = jnp.stack(received)
+            ordered = jnp.take(stacked, (member - jnp.arange(radix)) % radix, axis=0)
+            parts = [ordered[m] for m in range(radix)]
+            while len(parts) > 1:
+                parts = [parts[k] + parts[k + 1] for k in range(0, len(parts), 2)]
+            value = parts[0]
+            stride *= radix
     return value
 
 
@@ -47,12 +62,11 @@
     own_inputs = channels
     ncol = lax.axis_size("col")
     scale = (planes * rows_x * lax.axis_size("gx") * rows_y * lax.axis_size("gy")) ** (-0.5)
-    cells = volume.size
-    joined = jnp.concatenate([volume.reshape(-1), upstream.reshape(-1), filters.reshape(-1)])
-    every = lax.all_gather(joined, "col", axis=0, tiled=False)
-    fields = every[:, : 2 * cells].reshape(ncol, 2, channels, planes, rows_x, rows_y)
-    fields = jnp.swapaxes(fields, 0, 1).reshape(2, ncol * channels, planes, rows_x, rows_y)
-    all_rows = every[:, 2 * cells :].reshape((ncol * filters.shape[0],) + filters.shape[1:])
+    fields = jnp.stack(
+        [lax.all_gather(volume, "col", axis=0, tiled=True),
+         lax.all_gather(upstream, "col", axis=0, tiled=True)]
+    )
+    all_rows = lax.all_gather(filters, "col", axis=0, tiled=True)
     both = with_halo(fields, (("gx", 3), ("gy", 4)), 1)
     both = jnp.pad(both, ((0, 0), (0, 0), (1, 1), (0, 0), (0, 0)))
     padded, padded_up = both[0], both[1]

time: 195 us -> 162 us (0.83); the launches traced: 191 us -> 161 us
  waiting for transfers between devices: 52.1 us -> 25.1 us
  blocking collectives: 0 us -> 20.8 us
  local copies, waits for them, and re-layouts: 48.7 us -> 30.9 us
  between operations: 14.4 us -> 1.25 us
  starting transfers between devices: 46.8 us -> 56.3 us
  matrix products: 24.7 us -> 22.1 us
    all_gather x1 -> x0, waiting for transfers between devices: 33.1 us -> none  [shards(): every = lax.all_gather(joined, 'col', axis=0, tiled=False)]
    all_gather x0 -> x3, blocking collectives: none -> 20.8 us  [the longest x1 7.26 us: shards(): lax.all_gather(volume, 'col', axis=0, tiled=True)]
    reshape x3 -> x0, local copies, waits for them, and re-layouts: 9.31 us -> none  [the longest x1 6.45 us: shards(): every[:, 2 * cells:].reshape((ncol * filters.shape[0],) + filters.shape[1:])]
    ppermute x7 -> x10, starting transfers between devices: 34.6 us -> 43.5 us  [butterfly_sum(): received.append(lax.ppermute(value, axis, pairs))]
    unnamed x66 -> x67, local copies, waits for them, and re-layouts: 24.5 us -> 19.5 us
    ppermute x2, waiting for transfers between devices: 4.18 us -> 7.49 us  [with_halo(): lax.ppermute(lax.slice_in_dim(block, block.shape[dim] - width, None, axis...]
    ppermute x7 -> x10, waiting for transfers between devices: 12.6 us -> 15.8 us  [butterfly_sum(): received.append(lax.ppermute(value, axis, pairs))]
    dynamic_slice x2, local copies, waits for them, and re-layouts: 3.48 us -> 0.35 us  [shards(): own_filters = lax.dynamic_slice_in_dim(all_rows, first, own_inputs, 1)]
  transfers between devices with their start and end apart: 12 -> 14, of which waited for: 9 -> 7; matrix products, arithmetic and copies ran while one was open for 13% -> 9% of each run, Pallas kernels for 0% -> 0%
where the time goes in v6:
time: 162 us; the launch traced here: 161 us
  starting transfers between devices  56.3 us (35%)
  local copies, waits for them, and re-layouts  30.9 us (19%)
  waiting for transfers between devices  25.1 us (15%)
  matrix products  22.1 us (14%)
  blocking collectives  20.8 us (13%)
  other arithmetic  4.24 us (3%)
    ppermute x10, starting transfers between devices, butterfly_sum(): received.append(lax.ppermute(value, axis, pairs))  43.5 us
    unnamed x67, local copies, waits for them, and re-layouts  19.5 us
    ppermute x10, waiting for transfers between devices, butterfly_sum(): received.append(lax.ppermute(value, axis, pairs))  15.8 us
    dot_general x1, matrix products, shards(): jnp.einsum('opqy,kcpqy->ock', upstream, taps, precision=lax.Precision.HIGH)  13.7 us
    ppermute x2, waiting for transfers between devices, with_halo(): lax.ppermute(lax.slice_in_dim(block, block.shape[dim] - width, None, axis...  7.49 us
    all_gather x1, blocking collectives, shards(): lax.all_gather(volume, 'col', axis=0, tiled=True)  7.26 us
    ppermute x2, starting transfers between devices, with_halo(): lax.ppermute(lax.slice_in_dim(block, 0, width, axis=dim), axis, backward)  7.06 us
    all_gather x1, blocking collectives, shards(): lax.all_gather(upstream, 'col', axis=0, tiled=True)  6.77 us
  transfers between devices with their start and end apart: 14, of which 7 were waited for; matrix products, arithmetic and copies ran while one was open for 9% of the time, Pallas kernels for 0%

profile of v6, /device:TPU:6, one launch (start us, length us, event | category | flops | bytes accessed | tf_op | source)
XLA Modules:
  0.0 160.8 jit_solution(616064864070654264)
XLA Ops:
  0.6 1.0 copy.77
  1.6 1.0 copy.78
  2.6 6.8 %all_gather.10 = f32[32,8,4,128]{3,0,2,1:T(8,128)S(1)} all-gather(f32[8,8,4,128]{3,0,2,1:T(8,128)S(1)} %copy.78), channel_id=1, replica_groups=mesh['col'=4,'gx'=16,'gy'=8] {'col'}, dimensions={0}, use_global_device_ids=true | all-gather | bytes 655360 | tf_op jit(solution)/shard_map/all_gather | solution.py:67
  9.4 7.3 %all_gather.9 = f32[32,8,4,128]{3,0,2,1:T(8,128)S(1)} all-gather(f32[8,8,4,128]{3,0,2,1:T(8,128)S(1)} %copy.77), channel_id=1, replica_groups=mesh['col'=4,'gx'=16,'gy'=8] {'col'}, dimensions={0}, use_global_device_ids=true | all-gather | bytes 655360 | tf_op jit(solution)/shard_map/all_gather | solution.py:66
  16.7 3.8 %collective-permute-start = (f32[2,32,8,1,128]{4,1,3,2,0:T(8,128)S(1)}, f32[2,32,8,1,128]{4,1,3,2,0:T(8,128)S(1)}, u32[]{:S(2)}, u32[]{:S(2)}) collective-permute-start(f32[2,32,8,1,128]{4,1,3,2,0:T(8,128)S(1)} %get-tuple-element.17), channel_id=1, source_target_pairs={{0,8},{8,16},{16,24},{24,32},{32,40},{40,48},{48,56},{56,64},{64,7... | collective-permute-start | bytes 786440 | tf_op jit(solution)/shard_map/ppermute | solution.py:12
  20.5 1.3 collective-permute-start.1
  22.1 6.8 %all_gather.11 = f32[32,32,3,3,3]{1,0,4,3,2:T(8,128)S(1)} all-gather(f32[8,32,3,3,3]{1,0,4,3,2:T(8,128)} %param.6), channel_id=1, replica_groups=mesh['col'=4,'gx'=16,'gy'=8] {'col'}, dimensions={0}, use_global_device_ids=true | all-gather | bytes 138240 | tf_op jit(solution)/shard_map/all_gather | solution.py:69
  29.0 1.8 %collective-permute-done.1 = f32[2,32,8,1,128]{4,1,3,2,0:T(8,128)S(1)} collective-permute-done((f32[2,32,8,1,128]{4,1,3,2,0:T(8,128)S(1)}, f32[2,32,8,1,128]{4,1,3,2,0:T(8,128)S(1)}, u32[]{:S(2)}, u32[]{:S(2)}) %collective-permute-start.1) | collective-permute-done | bytes 262176 | tf_op jit(solution)/shard_map/ppermute | solution.py:15
  30.9 0.7 copy-done.2
  31.7 1.7 %fusion.66 = (f32[2,32,8,6,1]{4,1,3,2,0:T(8,128)}, f32[2,32,8,6,1]{4,1,3,2,0:T(8,128)S(1)}) fusion(f32[2,32,8,6,128]{4,1,3,2,0:T(8,128)S(1)} %pad_maximum_fusion), kind=kLoop, calls=%fused_computation.183 | loop fusion | bytes 49152 | tf_op jit(solution)/shard_map/slice | solution.py:13
  33.4 2.0 %copy.79 = f32[2,32,8,6,1]{1,2,4,3,0:T(8,128)S(1)} copy(f32[2,32,8,6,1]{4,1,3,2,0:T(8,128)} %get-tuple-element.15) | data formatting | bytes 24576 | tf_op jit(solution)/shard_map/slice | solution.py:13
  35.4 0.6 copy.80
  36.1 5.8 %collective-permute-start.3 = (f32[2,32,8,6,1]{1,2,4,3,0:T(8,128)S(1)}, f32[2,32,8,6,1]{1,2,4,3,0:T(8,128)S(1)}, u32[]{:S(2)}, u32[]{:S(2)}) collective-permute-start(f32[2,32,8,6,1]{1,2,4,3,0:T(8,128)S(1)} %copy.80), channel_id=1, source_target_pairs={{1,0},{2,1},{3,2},{4,3},{5,4},{6,5},{7,6},{9,8},{10,9},{11,10},{12... | collective-permute-start | bytes 36872 | tf_op jit(solution)/shard_map/ppermute | solution.py:15
  41.8 1.9 %collective-permute-start.2 = (f32[2,32,8,6,1]{1,2,4,3,0:T(8,128)S(1)}, f32[2,32,8,6,1]{1,2,4,3,0:T(8,128)S(1)}, u32[]{:S(2)}, u32[]{:S(2)}) collective-permute-start(f32[2,32,8,6,1]{1,2,4,3,0:T(8,128)S(1)} %copy.79), channel_id=1, source_target_pairs={{0,1},{1,2},{2,3},{3,4},{4,5},{5,6},{6,7},{8,9},{9,10},{10,11},{11... | collective-permute-start | bytes 36872 | tf_op jit(solution)/shard_map/ppermute | solution.py:12
  44.0 7.5 %collective-permute-done.2 = f32[2,32,8,6,1]{1,2,4,3,0:T(8,128)S(1)} collective-permute-done((f32[2,32,8,6,1]{1,2,4,3,0:T(8,128)S(1)}, f32[2,32,8,6,1]{1,2,4,3,0:T(8,128)S(1)}, u32[]{:S(2)}, u32[]{:S(2)}) %collective-permute-start.2) | collective-permute-done | bytes 12320 | tf_op jit(solution)/shard_map/ppermute | solution.py:12
  51.4 0.6 copy.81
  52.1 1.8 %copy.82 = f32[2,32,8,6,1]{4,1,3,2,0:T(8,128)} copy(f32[2,32,8,6,1]{1,2,4,3,0:T(8,128)S(1)} %collective-permute-done.3) | data formatting | bytes 24576 | tf_op jit(solution)/shard_map/ppermute | solution.py:15
  53.9 3.5 %select_maximum_fusion = f32[2,32,10,6,130]{4,1,3,2,0:T(8,128)S(1)} fusion(f32[2,32,8,6,1]{4,1,3,2,0:T(8,128)} %copy.82, f32[2,32,8,6,1]{4,1,3,2,0:T(8,128)S(1)} %copy.81, f32[2,32,8,1,128]{4,1,3,2,0:T(8,128)} %copy-done.2, f32[2,32,8,1,128]{4,1,3,2,0:T(8,128)S(1)} %collective-permute-done, f32[1,32,8,4,128]{4,1,3,2,0:T(8,128)S(1)} %bitcast.332, ...), kind=kLoop, calls=%fused_computation.6 | loop fusion | flops 6988800 | bytes 3594240 | tf_op jit(solution)/shard_map/concatenate | solution.py:16
  57.4 0.4 slice_bitcast_fusion
  62.0 5.0 %copy-done = f32[27,32,8,4,128]{4,1,0,3,2:T(8,128)} copy-done((f32[27,32,8,4,128]{4,1,0,3,2:T(8,128)}, f32[27,32,8,4,128]{4,1,0,3,2:T(8,128)S(1)}, u32[]{:S(2)}) %copy-start) | copy-done | bytes 14155800
  67.0 13.7 %convolution_bitcast_fusion.2 = f32[8,32,27]{1,0,2:T(8,128)S(1)} fusion(f32[27,32,8,4,128]{4,1,0,3,2:T(8,128)S(1)} %fusion.28, f32[8,8,4,128,1]{3,2,1,0,4:T(4,128)S(1)} %bitcast.336), kind=kOutput, calls=%fused_computation.17 | convolution fusion | flops 169869312 | bytes 14314496 | tf_op jit(solution)/shard_map/opqy,kcpqy->ock/dot_general | solution.py:74
  81.1 8.8 %collective-permute-start.6 = (f32[54,128]{1,0:T(8,128)S(1)}, f32[54,128]{1,0:T(8,128)S(1)}, u32[]{:S(2)}, u32[]{:S(2)}) collective-permute-start(f32[54,128]{1,0:T(8,128)S(1)} %reshape_reshape.3), channel_id=1, source_target_pairs={{0,24},{8,0},{16,8},{24,16},{32,56},{40,32},{48,40},{56,48},{64,88... | collective-permute-start | bytes 82952 | tf_op jit(solution)/shard_map/ppermute | solution.py:35
  89.8 1.9 %collective-permute-start.5 = (f32[54,128]{1,0:T(8,128)S(1)}, f32[54,128]{1,0:T(8,128)S(1)}, u32[]{:S(2)}, u32[]{:S(2)}) collective-permute-start(f32[54,128]{1,0:T(8,128)S(1)} %reshape_reshape.3), channel_id=1, source_target_pairs={{0,16},{8,24},{16,0},{24,8},{32,48},{40,56},{48,32},{56,40},{64,80... | collective-permute-start | bytes 82952 | tf_op jit(solution)/shard_map/ppermute | solution.py:35
  91.8 2.5 %collective-permute-start.4 = (f32[54,128]{1,0:T(8,128)S(1)}, f32[54,128]{1,0:T(8,128)S(1)}, u32[]{:S(2)}, u32[]{:S(2)}) collective-permute-start(f32[54,128]{1,0:T(8,128)S(1)} %reshape_reshape.3), channel_id=1, source_target_pairs={{0,8},{8,16},{16,24},{24,0},{32,40},{40,48},{48,56},{56,32},{64,72... | collective-permute-start | bytes 82952 | tf_op jit(solution)/shard_map/ppermute | solution.py:35
  95.4 0.2 fusion.20
  98.4 0.9 copy-done.1
  99.3 3.4 %convolution_bitcast_fusion.1 = f32[8,8,4,128]{3,0,2,1:T(8,128)S(1)} fusion(f32[27,32,8,4,128]{4,1,0,3,2:T(8,128)S(1)} %copy-done.1, f32[8,27,32,1,1]{2,0,1,4,3:T(8,128)S(1)} %bitcast.337), kind=kOutput, calls=%fused_computation.16 | convolution fusion | flops 169869312 | bytes 14314496 | tf_op jit(solution)/shard_map/okc,kcpqy->opqy/dot_general | solution.py:84
  102.7 5.0 %convolution_bitcast_fusion = f32[8,8,4,128]{3,0,2,1:T(8,128)S(1)} fusion(f32[32,27,8,1,1]{0,2,4,3,1:T(8,128)S(1)} %bitcast.338, f32[27,32,8,4,128]{4,1,3,2,0:T(8,128)S(1)} %fusion.1), kind=kOutput, calls=%fused_computation.15 | convolution fusion | flops 169869312 | bytes 14314496 | tf_op jit(solution)/shard_map/okc,kopqy->cpqy/dot_general | solution.py:89
  107.9 0.7 copy.115
  108.6 0.7 copy.114
  109.3 0.6 gather_fusion.1
  110.0 7.7 %collective-permute-start.9 = (f32[54,128]{1,0:T(8,128)S(1)}, f32[54,128]{1,0:T(8,128)S(1)}, u32[]{:S(2)}, u32[]{:S(2)}) collective-permute-start(f32[54,128]{1,0:T(8,128)S(1)} %fusion.74), channel_id=1, source_target_pairs={{0,96},{8,104},{16,112},{24,120},{32,0},{40,8},{48,16},{56,24},{64... | collective-permute-start | bytes 82952 | tf_op jit(solution)/shard_map/ppermute | solution.py:35
  117.7 8.7 %collective-permute-start.8 = (f32[54,128]{1,0:T(8,128)S(1)}, f32[54,128]{1,0:T(8,128)S(1)}, u32[]{:S(2)}, u32[]{:S(2)}) collective-permute-start(f32[54,128]{1,0:T(8,128)S(1)} %fusion.74), channel_id=1, source_target_pairs={{0,64},{8,72},{16,80},{24,88},{32,96},{40,104},{48,112},{56,120},{... | collective-permute-start | bytes 82952 | tf_op jit(solution)/shard_map/ppermute | solution.py:35
  126.4 4.3 %collective-permute-start.7 = (f32[54,128]{1,0:T(8,128)S(1)}, f32[54,128]{1,0:T(8,128)S(1)}, u32[]{:S(2)}, u32[]{:S(2)}) collective-permute-start(f32[54,128]{1,0:T(8,128)S(1)} %fusion.74), channel_id=1, source_target_pairs={{0,32},{8,40},{16,48},{24,56},{32,64},{40,72},{48,80},{56,88},{64,... | collective-permute-start | bytes 82952 | tf_op jit(solution)/shard_map/ppermute | solution.py:35
  130.7 1.9 %collective-permute-done.8 = f32[54,128]{1,0:T(8,128)S(1)} collective-permute-done((f32[54,128]{1,0:T(8,128)S(1)}, f32[54,128]{1,0:T(8,128)S(1)}, u32[]{:S(2)}, u32[]{:S(2)}) %collective-permute-start.8) | collective-permute-done | bytes 27680 | tf_op jit(solution)/shard_map/ppermute | solution.py:35
  132.6 4.1 %collective-permute-done.7 = f32[54,128]{1,0:T(8,128)S(1)} collective-permute-done((f32[54,128]{1,0:T(8,128)S(1)}, f32[54,128]{1,0:T(8,128)S(1)}, u32[]{:S(2)}, u32[]{:S(2)}) %collective-permute-start.7) | collective-permute-done | bytes 27680 | tf_op jit(solution)/shard_map/ppermute | solution.py:35
  136.8 0.6 gather_fusion.2
  137.4 1.9 %collective-permute-start.12 = (f32[54,128]{1,0:T(8,128)S(1)}, f32[54,128]{1,0:T(8,128)S(1)}, u32[]{:S(2)}, u32[]{:S(2)}) collective-permute-start(f32[54,128]{1,0:T(8,128)S(1)} %fusion.73), channel_id=1, source_target_pairs={{0,3},{1,0},{2,1},{3,2},{4,7},{5,4},{6,5},{7,6},{8,11},{9,8},{10,9... | collective-permute-start | bytes 82952 | tf_op jit(solution)/shard_map/ppermute | solution.py:35
  139.3 1.9 %collective-permute-start.11 = (f32[54,128]{1,0:T(8,128)S(1)}, f32[54,128]{1,0:T(8,128)S(1)}, u32[]{:S(2)}, u32[]{:S(2)}) collective-permute-start(f32[54,128]{1,0:T(8,128)S(1)} %fusion.73), channel_id=1, source_target_pairs={{0,2},{1,3},{2,0},{3,1},{4,6},{5,7},{6,4},{7,5},{8,10},{9,11},{10,... | collective-permute-start | bytes 82952 | tf_op jit(solution)/shard_map/ppermute | solution.py:35
  141.3 3.9 %collective-permute-start.10 = (f32[54,128]{1,0:T(8,128)S(1)}, f32[54,128]{1,0:T(8,128)S(1)}, u32[]{:S(2)}, u32[]{:S(2)}) collective-permute-start(f32[54,128]{1,0:T(8,128)S(1)} %fusion.73), channel_id=1, source_target_pairs={{0,1},{1,2},{2,3},{3,0},{4,5},{5,6},{6,7},{7,4},{8,9},{9,10},{10,1... | collective-permute-start | bytes 82952 | tf_op jit(solution)/shard_map/ppermute | solution.py:35
  145.2 1.4 collective-permute-done.11
  146.6 3.1 %collective-permute-done.10 = f32[54,128]{1,0:T(8,128)S(1)} collective-permute-done((f32[54,128]{1,0:T(8,128)S(1)}, f32[54,128]{1,0:T(8,128)S(1)}, u32[]{:S(2)}, u32[]{:S(2)}) %collective-permute-start.10) | collective-permute-done | bytes 27680 | tf_op jit(solution)/shard_map/ppermute | solution.py:35
  149.7 0.6 gather_fusion.3
  150.4 1.9 %collective-permute-start.13 = (f32[54,128]{1,0:T(8,128)S(1)}, f32[54,128]{1,0:T(8,128)S(1)}, u32[]{:S(2)}, u32[]{:S(2)}) collective-permute-start(f32[54,128]{1,0:T(8,128)S(1)} %fusion.72), channel_id=1, source_target_pairs={{0,4},{1,5},{2,6},{3,7},{4,0},{5,1},{6,2},{7,3},{8,12},{9,13},{10,... | collective-permute-start | bytes 82952 | tf_op jit(solution)/shard_map/ppermute | solution.py:35
  152.3 5.3 %collective-permute-done.13 = f32[54,128]{1,0:T(8,128)S(1)} collective-permute-done((f32[54,128]{1,0:T(8,128)S(1)}, f32[54,128]{1,0:T(8,128)S(1)}, u32[]{:S(2)}, u32[]{:S(2)}) %collective-permute-start.13) | collective-permute-done | bytes 27680 | tf_op jit(solution)/shard_map/ppermute | solution.py:35
  157.6 0.6 gather_fusion
  158.3 0.8 mul.15
  159.1 1.6 %copy.116 = f32[8,32,3,3,3]{1,0,4,3,2:T(8,128)} copy(f32[8,32,3,3,3]{4,3,2,1,0:T(4,128)S(1)} %mul.15) | data formatting | bytes 55296
  (101 shorter events, 9.5 us)
Async XLA Ops:
  16.7 12.4 %collective-permute-start = (f32[2,32,8,1,128]{4,1,3,2,0:T(8,128)S(1)}, f32[2,32,8,1,128]{4,1,3,2,0:T(8,128)S(1)}, u32[]{:S(2)}, u32[]{:S(2)}) collective-permute-start(f32[2,32,8,1,128]{4,1,3,2,0:T(8,128)S(1)} %get-tuple-element.17), channel_id=1, source_target_pairs={{0,8},{8,16},{16,24},{24,32},{32,40},{40,48},{48,56},{56,64},{64,7... | collective-permute-start | bytes 786440 | tf_op jit(solution)/shard_map/ppermute | solution.py:12
  20.5 10.3 %collective-permute-start.1 = (f32[2,32,8,1,128]{4,1,3,2,0:T(8,128)S(1)}, f32[2,32,8,1,128]{4,1,3,2,0:T(8,128)S(1)}, u32[]{:S(2)}, u32[]{:S(2)}) collective-permute-start(f32[2,32,8,1,128]{4,1,3,2,0:T(8,128)S(1)} %get-tuple-element.18), channel_id=1, source_target_pairs={{8,0},{16,8},{24,16},{32,24},{40,32},{48,40},{56,48},{64,56},{72,6... | collective-permute-start | bytes 786440 | tf_op jit(solution)/shard_map/ppermute | solution.py:15
  30.9 0.7 copy-start.2
  36.1 16.0 %collective-permute-start.3 = (f32[2,32,8,6,1]{1,2,4,3,0:T(8,128)S(1)}, f32[2,32,8,6,1]{1,2,4,3,0:T(8,128)S(1)}, u32[]{:S(2)}, u32[]{:S(2)}) collective-permute-start(f32[2,32,8,6,1]{1,2,4,3,0:T(8,128)S(1)} %copy.80), channel_id=1, source_target_pairs={{1,0},{2,1},{3,2},{4,3},{5,4},{6,5},{7,6},{9,8},{10,9},{11,10},{12... | collective-permute-start | bytes 36872 | tf_op jit(solution)/shard_map/ppermute | solution.py:15
  41.8 9.6 %collective-permute-start.2 = (f32[2,32,8,6,1]{1,2,4,3,0:T(8,128)S(1)}, f32[2,32,8,6,1]{1,2,4,3,0:T(8,128)S(1)}, u32[]{:S(2)}, u32[]{:S(2)}) collective-permute-start(f32[2,32,8,6,1]{1,2,4,3,0:T(8,128)S(1)} %copy.79), channel_id=1, source_target_pairs={{0,1},{1,2},{2,3},{3,4},{4,5},{5,6},{6,7},{8,9},{9,10},{10,11},{11... | collective-permute-start | bytes 36872 | tf_op jit(solution)/shard_map/ppermute | solution.py:12
  57.9 9.2 %copy-start.3 = (f32[8,8,4,128]{3,2,1,0:T(4,128)S(1)}, f32[8,8,4,128]{3,2,1,0:T(4,128)}, u32[]{:S(2)}) copy-start(f32[8,8,4,128]{3,2,1,0:T(4,128)} %param.7) | copy-start | bytes 393220
  62.0 5.1 %copy-start = (f32[27,32,8,4,128]{4,1,0,3,2:T(8,128)}, f32[27,32,8,4,128]{4,1,0,3,2:T(8,128)S(1)}, u32[]{:S(2)}) copy-start(f32[27,32,8,4,128]{4,1,0,3,2:T(8,128)S(1)} %fusion.28) | copy-start | bytes 42467332
  81.1 28.3 %collective-permute-start.6 = (f32[54,128]{1,0:T(8,128)S(1)}, f32[54,128]{1,0:T(8,128)S(1)}, u32[]{:S(2)}, u32[]{:S(2)}) collective-permute-start(f32[54,128]{1,0:T(8,128)S(1)} %reshape_reshape.3), channel_id=1, source_target_pairs={{0,24},{8,0},{16,8},{24,16},{32,56},{40,32},{48,40},{56,48},{64,88... | collective-permute-start | bytes 82952 | tf_op jit(solution)/shard_map/ppermute | solution.py:35
  89.8 19.5 %collective-permute-start.5 = (f32[54,128]{1,0:T(8,128)S(1)}, f32[54,128]{1,0:T(8,128)S(1)}, u32[]{:S(2)}, u32[]{:S(2)}) collective-permute-start(f32[54,128]{1,0:T(8,128)S(1)} %reshape_reshape.3), channel_id=1, source_target_pairs={{0,16},{8,24},{16,0},{24,8},{32,48},{40,56},{48,32},{56,40},{64,80... | collective-permute-start | bytes 82952 | tf_op jit(solution)/shard_map/ppermute | solution.py:35
  91.8 17.6 %collective-permute-start.4 = (f32[54,128]{1,0:T(8,128)S(1)}, f32[54,128]{1,0:T(8,128)S(1)}, u32[]{:S(2)}, u32[]{:S(2)}) collective-permute-start(f32[54,128]{1,0:T(8,128)S(1)} %reshape_reshape.3), channel_id=1, source_target_pairs={{0,8},{8,16},{16,24},{24,0},{32,40},{40,48},{48,56},{56,32},{64,72... | collective-permute-start | bytes 82952 | tf_op jit(solution)/shard_map/ppermute | solution.py:35
  94.2 5.0 %copy-start.1 = (f32[27,32,8,4,128]{4,1,0,3,2:T(8,128)S(1)}, f32[27,32,8,4,128]{4,1,0,3,2:T(8,128)}, u32[]{:S(2)}) copy-start(f32[27,32,8,4,128]{4,1,0,3,2:T(8,128)} %copy-done) | copy-start | bytes 42467332
  94.3 5.0 %copy-start.4 = (f32[8,32,3,3,3]{1,0,4,3,2:T(8,128)S(1)}, f32[8,32,3,3,3]{1,0,4,3,2:T(8,128)}, u32[]{:S(2)}) copy-start(f32[8,32,3,3,3]{1,0,4,3,2:T(8,128)} %param.6) | copy-start | bytes 82948
  110.0 20.7 %collective-permute-start.9 = (f32[54,128]{1,0:T(8,128)S(1)}, f32[54,128]{1,0:T(8,128)S(1)}, u32[]{:S(2)}, u32[]{:S(2)}) collective-permute-start(f32[54,128]{1,0:T(8,128)S(1)} %fusion.74), channel_id=1, source_target_pairs={{0,96},{8,104},{16,112},{24,120},{32,0},{40,8},{48,16},{56,24},{64... | collective-permute-start | bytes 82952 | tf_op jit(solution)/shard_map/ppermute | solution.py:35
  117.7 14.9 %collective-permute-start.8 = (f32[54,128]{1,0:T(8,128)S(1)}, f32[54,128]{1,0:T(8,128)S(1)}, u32[]{:S(2)}, u32[]{:S(2)}) collective-permute-start(f32[54,128]{1,0:T(8,128)S(1)} %fusion.74), channel_id=1, source_target_pairs={{0,64},{8,72},{16,80},{24,88},{32,96},{40,104},{48,112},{56,120},{... | collective-permute-start | bytes 82952 | tf_op jit(solution)/shard_map/ppermute | solution.py:35
  126.4 10.3 %collective-permute-start.7 = (f32[54,128]{1,0:T(8,128)S(1)}, f32[54,128]{1,0:T(8,128)S(1)}, u32[]{:S(2)}, u32[]{:S(2)}) collective-permute-start(f32[54,128]{1,0:T(8,128)S(1)} %fusion.74), channel_id=1, source_target_pairs={{0,32},{8,40},{16,48},{24,56},{32,64},{40,72},{48,80},{56,88},{64,... | collective-permute-start | bytes 82952 | tf_op jit(solution)/shard_map/ppermute | solution.py:35
  137.4 7.8 %collective-permute-start.12 = (f32[54,128]{1,0:T(8,128)S(1)}, f32[54,128]{1,0:T(8,128)S(1)}, u32[]{:S(2)}, u32[]{:S(2)}) collective-permute-start(f32[54,128]{1,0:T(8,128)S(1)} %fusion.73), channel_id=1, source_target_pairs={{0,3},{1,0},{2,1},{3,2},{4,7},{5,4},{6,5},{7,6},{8,11},{9,8},{10,9... | collective-permute-start | bytes 82952 | tf_op jit(solution)/shard_map/ppermute | solution.py:35
  139.3 7.3 %collective-permute-start.11 = (f32[54,128]{1,0:T(8,128)S(1)}, f32[54,128]{1,0:T(8,128)S(1)}, u32[]{:S(2)}, u32[]{:S(2)}) collective-permute-start(f32[54,128]{1,0:T(8,128)S(1)} %fusion.73), channel_id=1, source_target_pairs={{0,2},{1,3},{2,0},{3,1},{4,6},{5,7},{6,4},{7,5},{8,10},{9,11},{10,... | collective-permute-start | bytes 82952 | tf_op jit(solution)/shard_map/ppermute | solution.py:35
  141.3 8.4 %collective-permute-start.10 = (f32[54,128]{1,0:T(8,128)S(1)}, f32[54,128]{1,0:T(8,128)S(1)}, u32[]{:S(2)}, u32[]{:S(2)}) collective-permute-start(f32[54,128]{1,0:T(8,128)S(1)} %fusion.73), channel_id=1, source_target_pairs={{0,1},{1,2},{2,3},{3,0},{4,5},{5,6},{6,7},{7,4},{8,9},{9,10},{10,1... | collective-permute-start | bytes 82952 | tf_op jit(solution)/shard_map/ppermute | solution.py:35
  150.4 7.3 %collective-permute-start.13 = (f32[54,128]{1,0:T(8,128)S(1)}, f32[54,128]{1,0:T(8,128)S(1)}, u32[]{:S(2)}, u32[]{:S(2)}) collective-permute-start(f32[54,128]{1,0:T(8,128)S(1)} %fusion.72), channel_id=1, source_target_pairs={{0,4},{1,5},{2,6},{3,7},{4,0},{5,1},{6,2},{7,3},{8,12},{9,13},{10,... | collective-permute-start | bytes 82952 | tf_op jit(solution)/shard_map/ppermute | solution.py:35

commit v7 on v6

--- a/solution.py
+++ b/solution.py
@@ -62,11 +62,17 @@
     own_inputs = channels
     ncol = lax.axis_size("col")
     scale = (planes * rows_x * lax.axis_size("gx") * rows_y * lax.axis_size("gy")) ** (-0.5)
-    fields = jnp.stack(
-        [lax.all_gather(volume, "col", axis=0, tiled=True),
-         lax.all_gather(upstream, "col", axis=0, tiled=True)]
-    )
-    all_rows = lax.all_gather(filters, "col", axis=0, tiled=True)
+    taps_per_row = filters[0].size
+    rows_per_plane = rows_x * rows_y
+    filter_planes = -(-taps_per_row // rows_per_plane)
+    packed = jnp.pad(filters.reshape(channels, taps_per_row),
+                     ((0, 0), (0, filter_planes * rows_per_plane - taps_per_row)))
+    packed = packed.reshape(channels, filter_planes, rows_x, rows_y)
+    joined = jnp.concatenate([volume, packed], axis=1)
+    every = lax.all_gather(joined, "col", axis=0, tiled=True)
+    fields = jnp.stack([every[:, :planes], lax.all_gather(upstream, "col", axis=0, tiled=True)])
+    all_rows = every[:, planes:].reshape(every.shape[0], -1)[:, :taps_per_row]
+    all_rows = all_rows.reshape((every.shape[0],) + filters.shape[1:])
     both = with_halo(fields, (("gx", 3), ("gy", 4)), 1)
     both = jnp.pad(both, ((0, 0), (0, 0), (1, 1), (0, 0), (0, 0)))
     padded, padded_up = both[0], both[1]

time: 162 us -> 165 us (1.019)
  blocking collectives: 20.8 us -> 14.8 us
  other arithmetic: 4.24 us -> 8.2 us
  waiting for transfers between devices: 25.1 us -> 28.2 us
  local copies, waits for them, and re-layouts: 30.9 us -> 33.2 us
    all_gather x2 -> x1, blocking collectives: 14 us -> 7.99 us  [shards(): every = lax.all_gather(joined, 'col', axis=0, tiled=True)]
    ppermute x2, waiting for transfers between devices: 1.82 us -> 4.3 us  [with_halo(): lax.ppermute(lax.slice_in_dim(block, 0, width, axis=dim), axis, backward)]
    and x4, other arithmetic: 0.06 us -> 2.22 us  [butterfly_sum(): ordered = jnp.take(stacked, (member - jnp.arange(radix)) % radix, axis=0)]
    unnamed x67 -> x75, local copies, waits for them, and re-layouts: 19.5 us -> 20.1 us
  transfers between devices with their start and end apart: 14 -> 14, of which waited for: 7 -> 8; matrix products, arithmetic and copies ran while one was open for 9% -> 12% of each run, Pallas kernels for 0% -> 0%
where the time goes in v7:
time: 165 us; the launch traced here: 164 us
  starting transfers between devices  56.3 us (34%)
  local copies, waits for them, and re-layouts  33.2 us (20%)
  waiting for transfers between devices  28.2 us (17%)
  matrix products  22.1 us (13%)
  blocking collectives  14.8 us (9%)
  other arithmetic  8.2 us (5%)
    ppermute x10, starting transfers between devices, butterfly_sum(): received.append(lax.ppermute(value, axis, pairs))  43.5 us
    unnamed x75, local copies, waits for them, and re-layouts  20.1 us
    ppermute x10, waiting for transfers between devices, butterfly_sum(): received.append(lax.ppermute(value, axis, pairs))  16.2 us
    dot_general x1, matrix products, shards(): jnp.einsum('opqy,kcpqy->ock', upstream, taps, precision=lax.Precision.HIGH)  13.7 us
    all_gather x1, blocking collectives, shards(): every = lax.all_gather(joined, 'col', axis=0, tiled=True)  7.99 us
    ppermute x2, waiting for transfers between devices, with_halo(): lax.ppermute(lax.slice_in_dim(block, block.shape[dim] - width, None, axis...  7.74 us
    ppermute x2, starting transfers between devices, with_halo(): lax.ppermute(lax.slice_in_dim(block, 0, width, axis=dim), axis, backward)  7.06 us
    all_gather x1, blocking collectives, shards(): lax.all_gather(upstream, 'col', axis=0, tiled=True)  6.77 us
  transfers between devices with their start and end apart: 14, of which 8 were waited for; matrix products, arithmetic and copies ran while one was open for 12% of the time, Pallas kernels for 0%

profile of v7, /device:TPU:6, one launch (start us, length us, event | category | flops | bytes accessed | tf_op | source)
XLA Modules:
  0.0 164.1 jit_solution(11656292003810661408)
XLA Ops:
  0.6 1.0 copy.121
  1.6 1.0 copy.122
  2.6 6.8 %all_gather.7 = f32[32,8,4,128]{3,0,2,1:T(8,128)S(1)} all-gather(f32[8,8,4,128]{3,0,2,1:T(8,128)S(1)} %copy.122), channel_id=1, replica_groups=mesh['col'=4,'gx'=16,'gy'=8] {'col'}, dimensions={0}, use_global_device_ids=true | all-gather | bytes 655360 | tf_op jit(solution)/shard_map/all_gather | solution.py:73
  9.4 1.2 copy.119
  10.9 8.0 %all_gather.6 = f32[32,10,4,128]{3,0,2,1:T(8,128)S(1)} all-gather(f32[8,10,4,128]{3,0,2,1:T(8,128)S(1)} %pad_maximum_fusion.3), channel_id=1, replica_groups=mesh['col'=4,'gx'=16,'gy'=8] {'col'}, dimensions={0}, use_global_device_ids=true | all-gather | bytes 819200 | tf_op jit(solution)/shard_map/all_gather | solution.py:72
  19.0 3.8 %collective-permute-start = (f32[2,32,8,1,128]{4,1,3,2,0:T(8,128)S(1)}, f32[2,32,8,1,128]{4,1,3,2,0:T(8,128)S(1)}, u32[]{:S(2)}, u32[]{:S(2)}) collective-permute-start(f32[2,32,8,1,128]{4,1,3,2,0:T(8,128)S(1)} %get-tuple-element.20), channel_id=1, source_target_pairs={{0,8},{8,16},{16,24},{24,32},{32,40},{40,48},{48,56},{56,64},{64,7... | collective-permute-start | bytes 786440 | tf_op jit(solution)/shard_map/ppermute | solution.py:12
  22.9 1.3 collective-permute-start.1
  25.4 0.6 pad_clamp_fusion.2
  26.0 0.6 pad_clamp_fusion.3
  26.6 0.6 compare_and_fusion.2
  27.8 0.6 pad_clamp_fusion
  28.9 4.3 %collective-permute-done.1 = f32[2,32,8,1,128]{4,1,3,2,0:T(8,128)S(1)} collective-permute-done((f32[2,32,8,1,128]{4,1,3,2,0:T(8,128)S(1)}, f32[2,32,8,1,128]{4,1,3,2,0:T(8,128)S(1)}, u32[]{:S(2)}, u32[]{:S(2)}) %collective-permute-start.1) | collective-permute-done | bytes 262176 | tf_op jit(solution)/shard_map/ppermute | solution.py:15
  33.3 1.7 %fusion.66 = (f32[2,32,8,6,1]{4,1,3,2,0:T(8,128)}, f32[2,32,8,6,1]{4,1,3,2,0:T(8,128)S(1)}) fusion(f32[2,32,8,6,128]{4,1,3,2,0:T(8,128)S(1)} %pad_maximum_fusion), kind=kLoop, calls=%fused_computation.185 | loop fusion | bytes 49152 | tf_op jit(solution)/shard_map/slice | solution.py:13
  35.0 2.0 %copy.123 = f32[2,32,8,6,1]{1,2,4,3,0:T(8,128)S(1)} copy(f32[2,32,8,6,1]{4,1,3,2,0:T(8,128)} %get-tuple-element.18) | data formatting | bytes 24576 | tf_op jit(solution)/shard_map/slice | solution.py:13
  37.1 0.6 copy.124
  37.7 5.8 %collective-permute-start.3 = (f32[2,32,8,6,1]{1,2,4,3,0:T(8,128)S(1)}, f32[2,32,8,6,1]{1,2,4,3,0:T(8,128)S(1)}, u32[]{:S(2)}, u32[]{:S(2)}) collective-permute-start(f32[2,32,8,6,1]{1,2,4,3,0:T(8,128)S(1)} %copy.124), channel_id=1, source_target_pairs={{1,0},{2,1},{3,2},{4,3},{5,4},{6,5},{7,6},{9,8},{10,9},{11,10},{12... | collective-permute-start | bytes 36872 | tf_op jit(solution)/shard_map/ppermute | solution.py:15
  43.5 1.9 %collective-permute-start.2 = (f32[2,32,8,6,1]{1,2,4,3,0:T(8,128)S(1)}, f32[2,32,8,6,1]{1,2,4,3,0:T(8,128)}, u32[]{:S(2)}, u32[]{:S(2)}) collective-permute-start(f32[2,32,8,6,1]{1,2,4,3,0:T(8,128)S(1)} %copy.123), channel_id=1, source_target_pairs={{0,1},{1,2},{2,3},{3,4},{4,5},{5,6},{6,7},{8,9},{9,10},{10,11},{11... | collective-permute-start | bytes 36872 | tf_op jit(solution)/shard_map/ppermute | solution.py:12
  45.9 7.2 %collective-permute-done.2 = f32[2,32,8,6,1]{1,2,4,3,0:T(8,128)} collective-permute-done((f32[2,32,8,6,1]{1,2,4,3,0:T(8,128)S(1)}, f32[2,32,8,6,1]{1,2,4,3,0:T(8,128)}, u32[]{:S(2)}, u32[]{:S(2)}) %collective-permute-start.2) | collective-permute-done | bytes 12320 | tf_op jit(solution)/shard_map/ppermute | solution.py:12
  53.2 1.4 copy.125
  54.6 1.8 %copy.126 = f32[2,32,8,6,1]{4,1,3,2,0:T(8,128)} copy(f32[2,32,8,6,1]{1,2,4,3,0:T(8,128)S(1)} %collective-permute-done.3) | data formatting | bytes 24576 | tf_op jit(solution)/shard_map/ppermute | solution.py:15
  56.4 3.5 %select_maximum_fusion = f32[2,32,10,6,130]{4,1,3,2,0:T(8,128)S(1)} fusion(f32[2,32,8,6,1]{4,1,3,2,0:T(8,128)} %copy.126, f32[2,32,8,6,1]{4,1,3,2,0:T(8,128)S(1)} %copy.125, f32[2,32,8,1,128]{4,1,3,2,0:T(8,128)S(1)} %collective-permute-done.1, f32[2,32,8,1,128]{4,1,3,2,0:T(8,128)S(1)} %collective-permute-done, f32[1,32,8,4,128]{4,1,3,2,0:T(8,128)S(1)} %bitcast.338, ...), kind=kLoop, calls=%fused_computation.6 | loop fusion | flops 6988800 | bytes 3594240 | tf_op jit(solution)/shard_map/concatenate | solution.py:16
  64.5 5.0 %copy-done = f32[27,32,8,4,128]{4,1,0,3,2:T(8,128)} copy-done((f32[27,32,8,4,128]{4,1,0,3,2:T(8,128)}, f32[27,32,8,4,128]{4,1,0,3,2:T(8,128)S(1)}, u32[]{:S(2)}) %copy-start) | copy-done | bytes 14155800
  69.5 13.7 %convolution_bitcast_fusion.2 = f32[8,32,27]{1,0,2:T(8,128)S(1)} fusion(f32[27,32,8,4,128]{4,1,0,3,2:T(8,128)S(1)} %fusion.28, f32[8,8,4,128,1]{3,2,1,0,4:T(4,128)S(1)} %bitcast.339), kind=kOutput, calls=%fused_computation.17 | convolution fusion | flops 169869312 | bytes 14314496 | tf_op jit(solution)/shard_map/opqy,kcpqy->ock/dot_general | solution.py:80
  83.6 8.8 %collective-permute-start.6 = (f32[54,128]{1,0:T(8,128)S(1)}, f32[54,128]{1,0:T(8,128)S(1)}, u32[]{:S(2)}, u32[]{:S(2)}) collective-permute-start(f32[54,128]{1,0:T(8,128)S(1)} %reshape_reshape.3), channel_id=1, source_target_pairs={{0,24},{8,0},{16,8},{24,16},{32,56},{40,32},{48,40},{56,48},{64,88... | collective-permute-start | bytes 82952 | tf_op jit(solution)/shard_map/ppermute | solution.py:35
  92.3 1.9 %collective-permute-start.5 = (f32[54,128]{1,0:T(8,128)S(1)}, f32[54,128]{1,0:T(8,128)S(1)}, u32[]{:S(2)}, u32[]{:S(2)}) collective-permute-start(f32[54,128]{1,0:T(8,128)S(1)} %reshape_reshape.3), channel_id=1, source_target_pairs={{0,16},{8,24},{16,0},{24,8},{32,48},{40,56},{48,32},{56,40},{64,80... | collective-permute-start | bytes 82952 | tf_op jit(solution)/shard_map/ppermute | solution.py:35
  94.3 2.5 %collective-permute-start.4 = (f32[54,128]{1,0:T(8,128)S(1)}, f32[54,128]{1,0:T(8,128)S(1)}, u32[]{:S(2)}, u32[]{:S(2)}) collective-permute-start(f32[54,128]{1,0:T(8,128)S(1)} %reshape_reshape.3), channel_id=1, source_target_pairs={{0,8},{8,16},{16,24},{24,0},{32,40},{40,48},{48,56},{56,32},{64,72... | collective-permute-start | bytes 82952 | tf_op jit(solution)/shard_map/ppermute | solution.py:35
  100.9 0.9 copy-done.1
  101.8 3.4 %convolution_bitcast_fusion.1 = f32[8,8,4,128]{3,0,2,1:T(8,128)S(1)} fusion(f32[27,32,8,4,128]{4,1,0,3,2:T(8,128)S(1)} %copy-done.1, f32[8,27,32,1,1]{2,0,1,4,3:T(8,128)S(1)} %bitcast.341), kind=kOutput, calls=%fused_computation.16 | convolution fusion | flops 169869312 | bytes 14314496 | tf_op jit(solution)/shard_map/okc,kcpqy->opqy/dot_general | solution.py:90
  105.2 5.0 %convolution_bitcast_fusion = f32[8,8,4,128]{3,0,2,1:T(8,128)S(1)} fusion(f32[32,27,8,1,1]{0,2,4,3,1:T(8,128)S(1)} %bitcast.340, f32[27,32,8,4,128]{4,1,3,2,0:T(8,128)S(1)} %fusion.1), kind=kOutput, calls=%fused_computation.15 | convolution fusion | flops 169869312 | bytes 14314496 | tf_op jit(solution)/shard_map/okc,kopqy->cpqy/dot_general | solution.py:95
  110.5 0.7 copy.161
  111.2 0.7 copy.160
  111.9 0.7 gather_fusion.1
  112.7 7.7 %collective-permute-start.9 = (f32[54,128]{1,0:T(8,128)S(1)}, f32[54,128]{1,0:T(8,128)S(1)}, u32[]{:S(2)}, u32[]{:S(2)}) collective-permute-start(f32[54,128]{1,0:T(8,128)S(1)} %fusion.74), channel_id=1, source_target_pairs={{0,96},{8,104},{16,112},{24,120},{32,0},{40,8},{48,16},{56,24},{64... | collective-permute-start | bytes 82952 | tf_op jit(solution)/shard_map/ppermute | solution.py:35
  120.4 8.7 %collective-permute-start.8 = (f32[54,128]{1,0:T(8,128)S(1)}, f32[54,128]{1,0:T(8,128)S(1)}, u32[]{:S(2)}, u32[]{:S(2)}) collective-permute-start(f32[54,128]{1,0:T(8,128)S(1)} %fusion.74), channel_id=1, source_target_pairs={{0,64},{8,72},{16,80},{24,88},{32,96},{40,104},{48,112},{56,120},{... | collective-permute-start | bytes 82952 | tf_op jit(solution)/shard_map/ppermute | solution.py:35
  129.1 4.3 %collective-permute-start.7 = (f32[54,128]{1,0:T(8,128)S(1)}, f32[54,128]{1,0:T(8,128)S(1)}, u32[]{:S(2)}, u32[]{:S(2)}) collective-permute-start(f32[54,128]{1,0:T(8,128)S(1)} %fusion.74), channel_id=1, source_target_pairs={{0,32},{8,40},{16,48},{24,56},{32,64},{40,72},{48,80},{56,88},{64,... | collective-permute-start | bytes 82952 | tf_op jit(solution)/shard_map/ppermute | solution.py:35
  133.4 1.8 %collective-permute-done.8 = f32[54,128]{1,0:T(8,128)S(1)} collective-permute-done((f32[54,128]{1,0:T(8,128)S(1)}, f32[54,128]{1,0:T(8,128)S(1)}, u32[]{:S(2)}, u32[]{:S(2)}) %collective-permute-start.8) | collective-permute-done | bytes 27680 | tf_op jit(solution)/shard_map/ppermute | solution.py:35
  135.2 4.6 %collective-permute-done.7 = f32[54,128]{1,0:T(8,128)S(1)} collective-permute-done((f32[54,128]{1,0:T(8,128)S(1)}, f32[54,128]{1,0:T(8,128)S(1)}, u32[]{:S(2)}, u32[]{:S(2)}) %collective-permute-start.7) | collective-permute-done | bytes 27680 | tf_op jit(solution)/shard_map/ppermute | solution.py:35
  139.8 0.7 gather_fusion.2
  140.6 1.9 %collective-permute-start.12 = (f32[54,128]{1,0:T(8,128)S(1)}, f32[54,128]{1,0:T(8,128)S(1)}, u32[]{:S(2)}, u32[]{:S(2)}) collective-permute-start(f32[54,128]{1,0:T(8,128)S(1)} %fusion.73), channel_id=1, source_target_pairs={{0,3},{1,0},{2,1},{3,2},{4,7},{5,4},{6,5},{7,6},{8,11},{9,8},{10,9... | collective-permute-start | bytes 82952 | tf_op jit(solution)/shard_map/ppermute | solution.py:35
  142.5 1.9 %collective-permute-start.11 = (f32[54,128]{1,0:T(8,128)S(1)}, f32[54,128]{1,0:T(8,128)S(1)}, u32[]{:S(2)}, u32[]{:S(2)}) collective-permute-start(f32[54,128]{1,0:T(8,128)S(1)} %fusion.73), channel_id=1, source_target_pairs={{0,2},{1,3},{2,0},{3,1},{4,6},{5,7},{6,4},{7,5},{8,10},{9,11},{10,... | collective-permute-start | bytes 82952 | tf_op jit(solution)/shard_map/ppermute | solution.py:35
  144.4 3.9 %collective-permute-start.10 = (f32[54,128]{1,0:T(8,128)S(1)}, f32[54,128]{1,0:T(8,128)S(1)}, u32[]{:S(2)}, u32[]{:S(2)}) collective-permute-start(f32[54,128]{1,0:T(8,128)S(1)} %fusion.73), channel_id=1, source_target_pairs={{0,1},{1,2},{2,3},{3,0},{4,5},{5,6},{6,7},{7,4},{8,9},{9,10},{10,1... | collective-permute-start | bytes 82952 | tf_op jit(solution)/shard_map/ppermute | solution.py:35
  148.4 1.4 collective-permute-done.11
  149.8 3.1 %collective-permute-done.10 = f32[54,128]{1,0:T(8,128)S(1)} collective-permute-done((f32[54,128]{1,0:T(8,128)S(1)}, f32[54,128]{1,0:T(8,128)S(1)}, u32[]{:S(2)}, u32[]{:S(2)}) %collective-permute-start.10) | collective-permute-done | bytes 27680 | tf_op jit(solution)/shard_map/ppermute | solution.py:35
  153.5 1.9 %collective-permute-start.13 = (f32[54,128]{1,0:T(8,128)S(1)}, f32[54,128]{1,0:T(8,128)S(1)}, u32[]{:S(2)}, u32[]{:S(2)}) collective-permute-start(f32[54,128]{1,0:T(8,128)S(1)} %fusion.72), channel_id=1, source_target_pairs={{0,4},{1,5},{2,6},{3,7},{4,0},{5,1},{6,2},{7,3},{8,12},{9,13},{10,... | collective-permute-start | bytes 82952 | tf_op jit(solution)/shard_map/ppermute | solution.py:35
  155.5 5.3 %collective-permute-done.13 = f32[54,128]{1,0:T(8,128)S(1)} collective-permute-done((f32[54,128]{1,0:T(8,128)S(1)}, f32[54,128]{1,0:T(8,128)S(1)}, u32[]{:S(2)}, u32[]{:S(2)}) %collective-permute-start.13) | collective-permute-done | bytes 27680 | tf_op jit(solution)/shard_map/ppermute | solution.py:35
  160.8 0.7 gather_fusion
  161.6 0.8 mul.15
  162.4 1.6 %copy.162 = f32[8,32,3,3,3]{1,0,4,3,2:T(8,128)} copy(f32[8,32,3,3,3]{4,3,2,1,0:T(4,128)S(1)} %mul.15) | data formatting | bytes 55296
  (118 shorter events, 13.4 us)
Async XLA Ops:
  19.0 9.9 %collective-permute-start = (f32[2,32,8,1,128]{4,1,3,2,0:T(8,128)S(1)}, f32[2,32,8,1,128]{4,1,3,2,0:T(8,128)S(1)}, u32[]{:S(2)}, u32[]{:S(2)}) collective-permute-start(f32[2,32,8,1,128]{4,1,3,2,0:T(8,128)S(1)} %get-tuple-element.20), channel_id=1, source_target_pairs={{0,8},{8,16},{16,24},{24,32},{32,40},{40,48},{48,56},{56,64},{64,7... | collective-permute-start | bytes 786440 | tf_op jit(solution)/shard_map/ppermute | solution.py:12
  22.9 10.3 %collective-permute-start.1 = (f32[2,32,8,1,128]{4,1,3,2,0:T(8,128)S(1)}, f32[2,32,8,1,128]{4,1,3,2,0:T(8,128)S(1)}, u32[]{:S(2)}, u32[]{:S(2)}) collective-permute-start(f32[2,32,8,1,128]{4,1,3,2,0:T(8,128)S(1)} %get-tuple-element.21), channel_id=1, source_target_pairs={{8,0},{16,8},{24,16},{32,24},{40,32},{48,40},{56,48},{64,56},{72,6... | collective-permute-start | bytes 786440 | tf_op jit(solution)/shard_map/ppermute | solution.py:15
  37.7 16.9 %collective-permute-start.3 = (f32[2,32,8,6,1]{1,2,4,3,0:T(8,128)S(1)}, f32[2,32,8,6,1]{1,2,4,3,0:T(8,128)S(1)}, u32[]{:S(2)}, u32[]{:S(2)}) collective-permute-start(f32[2,32,8,6,1]{1,2,4,3,0:T(8,128)S(1)} %copy.124), channel_id=1, source_target_pairs={{1,0},{2,1},{3,2},{4,3},{5,4},{6,5},{7,6},{9,8},{10,9},{11,10},{12... | collective-permute-start | bytes 36872 | tf_op jit(solution)/shard_map/ppermute | solution.py:15
  43.5 9.7 %collective-permute-start.2 = (f32[2,32,8,6,1]{1,2,4,3,0:T(8,128)S(1)}, f32[2,32,8,6,1]{1,2,4,3,0:T(8,128)}, u32[]{:S(2)}, u32[]{:S(2)}) collective-permute-start(f32[2,32,8,6,1]{1,2,4,3,0:T(8,128)S(1)} %copy.123), channel_id=1, source_target_pairs={{0,1},{1,2},{2,3},{3,4},{4,5},{5,6},{6,7},{8,9},{9,10},{10,11},{11... | collective-permute-start | bytes 36872 | tf_op jit(solution)/shard_map/ppermute | solution.py:12
  60.4 9.2 %copy-start.2 = (f32[8,8,4,128]{3,2,1,0:T(4,128)S(1)}, f32[8,8,4,128]{3,2,1,0:T(4,128)}, u32[]{:S(2)}) copy-start(f32[8,8,4,128]{3,2,1,0:T(4,128)} %param.7) | copy-start | bytes 393220
  64.5 5.0 %copy-start = (f32[27,32,8,4,128]{4,1,0,3,2:T(8,128)}, f32[27,32,8,4,128]{4,1,0,3,2:T(8,128)S(1)}, u32[]{:S(2)}) copy-start(f32[27,32,8,4,128]{4,1,0,3,2:T(8,128)S(1)} %fusion.28) | copy-start | bytes 42467332
  83.6 28.3 %collective-permute-start.6 = (f32[54,128]{1,0:T(8,128)S(1)}, f32[54,128]{1,0:T(8,128)S(1)}, u32[]{:S(2)}, u32[]{:S(2)}) collective-permute-start(f32[54,128]{1,0:T(8,128)S(1)} %reshape_reshape.3), channel_id=1, source_target_pairs={{0,24},{8,0},{16,8},{24,16},{32,56},{40,32},{48,40},{56,48},{64,88... | collective-permute-start | bytes 82952 | tf_op jit(solution)/shard_map/ppermute | solution.py:35
  92.3 19.5 %collective-permute-start.5 = (f32[54,128]{1,0:T(8,128)S(1)}, f32[54,128]{1,0:T(8,128)S(1)}, u32[]{:S(2)}, u32[]{:S(2)}) collective-permute-start(f32[54,128]{1,0:T(8,128)S(1)} %reshape_reshape.3), channel_id=1, source_target_pairs={{0,16},{8,24},{16,0},{24,8},{32,48},{40,56},{48,32},{56,40},{64,80... | collective-permute-start | bytes 82952 | tf_op jit(solution)/shard_map/ppermute | solution.py:35
  94.3 17.6 %collective-permute-start.4 = (f32[54,128]{1,0:T(8,128)S(1)}, f32[54,128]{1,0:T(8,128)S(1)}, u32[]{:S(2)}, u32[]{:S(2)}) collective-permute-start(f32[54,128]{1,0:T(8,128)S(1)} %reshape_reshape.3), channel_id=1, source_target_pairs={{0,8},{8,16},{16,24},{24,0},{32,40},{40,48},{48,56},{56,32},{64,72... | collective-permute-start | bytes 82952 | tf_op jit(solution)/shard_map/ppermute | solution.py:35
  96.8 5.0 %copy-start.1 = (f32[27,32,8,4,128]{4,1,0,3,2:T(8,128)S(1)}, f32[27,32,8,4,128]{4,1,0,3,2:T(8,128)}, u32[]{:S(2)}) copy-start(f32[27,32,8,4,128]{4,1,0,3,2:T(8,128)} %copy-done) | copy-start | bytes 42467332
  96.8 5.0 %copy-start.3 = (f32[8,32,3,3,3]{1,0,4,3,2:T(8,128)S(1)}, f32[8,32,3,3,3]{1,0,4,3,2:T(8,128)}, u32[]{:S(2)}) copy-start(f32[8,32,3,3,3]{1,0,4,3,2:T(8,128)} %param.6) | copy-start | bytes 82948
  101.8 10.8 %copy-start.6 = (pred[4]{0:T(512)(128)(4,1)S(1)}, pred[4]{0:T(512)(128)(4,1)}, u32[]{:S(2)}) copy-start(pred[4]{0:T(512)(128)(4,1)} %compare_and_fusion.2) | copy-start | bytes 16
  101.8 38.7 %copy-start.7 = (pred[4]{0:T(512)(128)(4,1)S(1)}, pred[4]{0:T(512)(128)(4,1)}, u32[]{:S(2)}) copy-start(pred[4]{0:T(512)(128)(4,1)} %compare_and_fusion.1) | copy-start | bytes 16
  101.8 51.6 %copy-start.5 = (pred[4]{0:T(512)(128)(4,1)S(1)}, pred[4]{0:T(512)(128)(4,1)}, u32[]{:S(2)}) copy-start(pred[4]{0:T(512)(128)(4,1)} %compare_and_fusion) | copy-start | bytes 16
  101.8 59.7 %copy-start.4 = (pred[2]{0:T(512)(128)(4,1)S(1)}, pred[2]{0:T(512)(128)(4,1)}, u32[]{:S(2)}) copy-start(pred[2]{0:T(512)(128)(4,1)} %compare_and_fusion.3) | copy-start | bytes 10
  112.7 20.7 %collective-permute-start.9 = (f32[54,128]{1,0:T(8,128)S(1)}, f32[54,128]{1,0:T(8,128)S(1)}, u32[]{:S(2)}, u32[]{:S(2)}) collective-permute-start(f32[54,128]{1,0:T(8,128)S(1)} %fusion.74), channel_id=1, source_target_pairs={{0,96},{8,104},{16,112},{24,120},{32,0},{40,8},{48,16},{56,24},{64... | collective-permute-start | bytes 82952 | tf_op jit(solution)/shard_map/ppermute | solution.py:35
  120.4 14.8 %collective-permute-start.8 = (f32[54,128]{1,0:T(8,128)S(1)}, f32[54,128]{1,0:T(8,128)S(1)}, u32[]{:S(2)}, u32[]{:S(2)}) collective-permute-start(f32[54,128]{1,0:T(8,128)S(1)} %fusion.74), channel_id=1, source_target_pairs={{0,64},{8,72},{16,80},{24,88},{32,96},{40,104},{48,112},{56,120},{... | collective-permute-start | bytes 82952 | tf_op jit(solution)/shard_map/ppermute | solution.py:35
  129.1 10.7 %collective-permute-start.7 = (f32[54,128]{1,0:T(8,128)S(1)}, f32[54,128]{1,0:T(8,128)S(1)}, u32[]{:S(2)}, u32[]{:S(2)}) collective-permute-start(f32[54,128]{1,0:T(8,128)S(1)} %fusion.74), channel_id=1, source_target_pairs={{0,32},{8,40},{16,48},{24,56},{32,64},{40,72},{48,80},{56,88},{64,... | collective-permute-start | bytes 82952 | tf_op jit(solution)/shard_map/ppermute | solution.py:35
  140.6 7.8 %collective-permute-start.12 = (f32[54,128]{1,0:T(8,128)S(1)}, f32[54,128]{1,0:T(8,128)S(1)}, u32[]{:S(2)}, u32[]{:S(2)}) collective-permute-start(f32[54,128]{1,0:T(8,128)S(1)} %fusion.73), channel_id=1, source_target_pairs={{0,3},{1,0},{2,1},{3,2},{4,7},{5,4},{6,5},{7,6},{8,11},{9,8},{10,9... | collective-permute-start | bytes 82952 | tf_op jit(solution)/shard_map/ppermute | solution.py:35
  142.5 7.3 %collective-permute-start.11 = (f32[54,128]{1,0:T(8,128)S(1)}, f32[54,128]{1,0:T(8,128)S(1)}, u32[]{:S(2)}, u32[]{:S(2)}) collective-permute-start(f32[54,128]{1,0:T(8,128)S(1)} %fusion.73), channel_id=1, source_target_pairs={{0,2},{1,3},{2,0},{3,1},{4,6},{5,7},{6,4},{7,5},{8,10},{9,11},{10,... | collective-permute-start | bytes 82952 | tf_op jit(solution)/shard_map/ppermute | solution.py:35
  144.4 8.4 %collective-permute-start.10 = (f32[54,128]{1,0:T(8,128)S(1)}, f32[54,128]{1,0:T(8,128)S(1)}, u32[]{:S(2)}, u32[]{:S(2)}) collective-permute-start(f32[54,128]{1,0:T(8,128)S(1)} %fusion.73), channel_id=1, source_target_pairs={{0,1},{1,2},{2,3},{3,0},{4,5},{5,6},{6,7},{7,4},{8,9},{9,10},{10,1... | collective-permute-start | bytes 82952 | tf_op jit(solution)/shard_map/ppermute | solution.py:35
  153.5 7.3 %collective-permute-start.13 = (f32[54,128]{1,0:T(8,128)S(1)}, f32[54,128]{1,0:T(8,128)S(1)}, u32[]{:S(2)}, u32[]{:S(2)}) collective-permute-start(f32[54,128]{1,0:T(8,128)S(1)} %fusion.72), channel_id=1, source_target_pairs={{0,4},{1,5},{2,6},{3,7},{4,0},{5,1},{6,2},{7,3},{8,12},{9,13},{10,... | collective-permute-start | bytes 82952 | tf_op jit(solution)/shard_map/ppermute | solution.py:35

commit v8 on v6

--- a/solution.py
+++ b/solution.py
@@ -15,6 +15,41 @@
         high = lax.ppermute(lax.slice_in_dim(block, 0, width, axis=dim), axis, backward)
         block = jnp.concatenate([low, block, high], axis=dim)
     return block
+
+
+def neighbour(piece, dx, dy):
+    nx, ny = lax.axis_size("gx"), lax.axis_size("gy")
+    pairs = [
+        (i * ny + j, (i + dx) * ny + (j + dy))
+        for i in range(nx)
+        for j in range(ny)
+        if 0 <= i + dx < nx and 0 <= j + dy < ny
+    ]
+    return lax.ppermute(piece, ("gx", "gy"), pairs)
+
+
+def with_halo_2d(block, dx_dim, dy_dim):
+    def cut(x_at, y_at):
+        piece = block
+        if x_at is not None:
+            piece = lax.slice_in_dim(piece, x_at, x_at + 1, axis=dx_dim)
+        if y_at is not None:
+            piece = lax.slice_in_dim(piece, y_at, y_at + 1, axis=dy_dim)
+        return piece
+
+    last_x, last_y = block.shape[dx_dim] - 1, block.shape[dy_dim] - 1
+    low_x = neighbour(cut(last_x, None), 1, 0)
+    high_x = neighbour(cut(0, None), -1, 0)
+    low_y = neighbour(cut(None, last_y), 0, 1)
+    high_y = neighbour(cut(None, 0), 0, -1)
+    low_low = neighbour(cut(last_x, last_y), 1, 1)
+    low_high = neighbour(cut(last_x, 0), 1, -1)
+    high_low = neighbour(cut(0, last_y), -1, 1)
+    high_high = neighbour(cut(0, 0), -1, -1)
+    top = jnp.concatenate([low_low, low_x, low_high], axis=dy_dim)
+    middle = jnp.concatenate([low_y, block, high_y], axis=dy_dim)
+    bottom = jnp.concatenate([high_low, high_x, high_high], axis=dy_dim)
+    return jnp.concatenate([top, middle, bottom], axis=dx_dim)
 
 
 def butterfly_sum(value, axes):
@@ -67,7 +102,7 @@
          lax.all_gather(upstream, "col", axis=0, tiled=True)]
     )
     all_rows = lax.all_gather(filters, "col", axis=0, tiled=True)
-    both = with_halo(fields, (("gx", 3), ("gy", 4)), 1)
+    both = with_halo_2d(fields, 3, 4)
     both = jnp.pad(both, ((0, 0), (0, 0), (1, 1), (0, 0), (0, 0)))
     padded, padded_up = both[0], both[1]
     taps = patches(padded, planes, rows_x, rows_y, False)

time: 162 us -> 189 us (1.17)
  the two profiles are of different devices: /device:TPU:6 before, /device:TPU:32 now
where the time goes in v8:
time: 189 us; the launch traced here: 188 us
  starting transfers between devices  79.7 us (42%)
  waiting for transfers between devices  27.2 us (14%)
  local copies, waits for them, and re-layouts  25.6 us (14%)
  matrix products  22.1 us (12%)
  blocking collectives  21 us (11%)
  other arithmetic  11.2 us (6%)
    ppermute x10, starting transfers between devices, butterfly_sum(): received.append(lax.ppermute(value, axis, pairs))  53.1 us
    ppermute x8, starting transfers between devices, neighbour(): return lax.ppermute(piece, ('gx', 'gy'), pairs)  26.6 us
    unnamed x73, local copies, waits for them, and re-layouts  18.8 us
    ppermute x10, waiting for transfers between devices, butterfly_sum(): received.append(lax.ppermute(value, axis, pairs))  14.8 us
    dot_general x1, matrix products, shards(): jnp.einsum('opqy,kcpqy->ock', upstream, taps, precision=lax.Precision.HIGH)  13.7 us
    ppermute x8, waiting for transfers between devices, neighbour(): return lax.ppermute(piece, ('gx', 'gy'), pairs)  12.3 us
    all_gather x1, blocking collectives, shards(): lax.all_gather(volume, 'col', axis=0, tiled=True)  7.26 us
    all_gather x1, blocking collectives, shards(): lax.all_gather(upstream, 'col', axis=0, tiled=True)  7.17 us
  transfers between devices with their start and end apart: 18, of which 7 were waited for; matrix products, arithmetic and copies ran while one was open for 12% of the time, Pallas kernels for 0%

profile of v8, /device:TPU:32, one launch (start us, length us, event | category | flops | bytes accessed | tf_op | source)
XLA Modules:
  0.0 188.0 jit_solution(11729229266453322314)
XLA Ops:
  0.6 1.0 copy.77
  1.6 1.0 copy.78
  2.6 7.2 %all_gather.10 = f32[32,8,4,128]{3,0,2,1:T(8,128)S(1)} all-gather(f32[8,8,4,128]{3,0,2,1:T(8,128)S(1)} %copy.78), channel_id=1, replica_groups=mesh['col'=4,'gx'=16,'gy'=8] {'col'}, dimensions={0}, use_global_device_ids=true | all-gather | bytes 655360 | tf_op jit(solution)/shard_map/all_gather | solution.py:102
  9.8 7.3 %all_gather.9 = f32[32,8,4,128]{3,0,2,1:T(8,128)S(1)} all-gather(f32[8,8,4,128]{3,0,2,1:T(8,128)S(1)} %copy.77), channel_id=1, replica_groups=mesh['col'=4,'gx'=16,'gy'=8] {'col'}, dimensions={0}, use_global_device_ids=true | all-gather | bytes 655360 | tf_op jit(solution)/shard_map/all_gather | solution.py:101
  17.0 0.8 fusion.61
  17.9 3.8 %collective-permute-start.1 = (f32[2,32,8,1,128]{4,1,3,2,0:T(8,128)}, f32[2,32,8,1,128]{4,1,3,2,0:T(8,128)S(1)}, u32[]{:S(2)}, u32[]{:S(2)}) collective-permute-start(f32[2,32,8,1,128]{4,1,3,2,0:T(8,128)} %get-tuple-element.19), channel_id=1, source_target_pairs={{0,8},{1,9},{2,10},{3,11},{4,12},{5,13},{6,14},{7,15},{8,16},{9,17... | collective-permute-start | bytes 786440 | tf_op jit(solution)/shard_map/ppermute | solution.py:28
  21.7 4.2 %collective-permute-start.6 = (f32[2,32,8,1,128]{4,1,3,2,0:T(8,128)}, f32[2,32,8,1,128]{4,1,3,2,0:T(8,128)}, u32[]{:S(2)}, u32[]{:S(2)}) collective-permute-start(f32[2,32,8,1,128]{4,1,3,2,0:T(8,128)} %get-tuple-element.20), channel_id=1, source_target_pairs={{8,0},{9,1},{10,2},{11,3},{12,4},{13,5},{14,6},{15,7},{16,8},{17,9... | collective-permute-start | bytes 786440 | tf_op jit(solution)/shard_map/ppermute | solution.py:28
  25.9 1.1 fusion.60
  27.0 3.4 %collective-permute-start = (f32[2,32,8,1,1]{4,1,3,2,0:T(8,128)}, f32[2,32,8,1,1]{4,1,3,2,0:T(8,128)}, u32[]{:S(2)}, u32[]{:S(2)}) collective-permute-start(f32[2,32,8,1,1]{4,1,3,2,0:T(8,128)} %get-tuple-element.15), channel_id=1, source_target_pairs={{0,9},{1,10},{2,11},{3,12},{4,13},{5,14},{6,15},{8,17},{9,18},{10,... | collective-permute-start | bytes 6152 | tf_op jit(solution)/shard_map/ppermute | solution.py:28
  31.2 1.3 collective-permute-start.4
  32.9 4.5 %collective-permute-start.3 = (f32[2,32,8,4,1]{1,2,4,3,0:T(8,128)S(1)}, f32[2,32,8,4,1]{1,2,4,3,0:T(8,128)S(1)}, u32[]{:S(2)}, u32[]{:S(2)}) collective-permute-start(f32[2,32,8,4,1]{1,2,4,3,0:T(8,128)S(1)} %copy.79), channel_id=1, source_target_pairs={{0,1},{1,2},{2,3},{3,4},{4,5},{5,6},{6,7},{8,9},{9,10},{10,11},{11... | collective-permute-start | bytes 24584 | tf_op jit(solution)/shard_map/ppermute | solution.py:28
  38.2 0.6 pad_clamp_fusion.2
  38.8 0.6 pad_clamp_fusion.3
  40.0 6.5 %all_gather.11 = f32[32,32,3,3,3]{1,0,4,3,2:T(8,128)S(1)} all-gather(f32[8,32,3,3,3]{1,0,4,3,2:T(8,128)} %param.6), channel_id=1, replica_groups=mesh['col'=4,'gx'=16,'gy'=8] {'col'}, dimensions={0}, use_global_device_ids=true | all-gather | bytes 138240 | tf_op jit(solution)/shard_map/all_gather | solution.py:104
  46.7 0.6 compare_and_fusion
  47.9 1.3 collective-permute-start.2
  49.2 6.8 %collective-permute-start.5 = (f32[2,32,8,1,1]{4,1,3,2,0:T(8,128)}, f32[2,32,8,1,1]{4,1,3,2,0:T(8,128)}, u32[]{:S(2)}, u32[]{:S(2)}) collective-permute-start(f32[2,32,8,1,1]{4,1,3,2,0:T(8,128)} %get-tuple-element.17), channel_id=1, source_target_pairs={{8,1},{9,2},{10,3},{11,4},{12,5},{13,6},{14,7},{16,9},{17,10},{18,... | collective-permute-start | bytes 6152 | tf_op jit(solution)/shard_map/ppermute | solution.py:28
  56.0 1.3 collective-permute-start.7
  57.3 0.6 compare_and_fusion.1
  59.5 1.9 collective-permute-done.5
  61.4 9.9 %collective-permute-done.7 = f32[2,32,8,1,1]{4,1,3,2,0:T(8,128)} collective-permute-done((f32[2,32,8,1,1]{4,1,3,2,0:T(8,128)}, f32[2,32,8,1,1]{4,1,3,2,0:T(8,128)}, u32[]{:S(2)}, u32[]{:S(2)}) %collective-permute-start.7) | collective-permute-done | bytes 2080 | tf_op jit(solution)/shard_map/ppermute | solution.py:28
  71.3 4.3 %fusion = f32[2,32,10,6,130]{4,1,3,2,0:T(8,128)S(1)} fusion(f32[2,32,8,1,1]{4,1,3,2,0:T(8,128)} %collective-permute-done.7, f32[2,32,8,1,128]{4,1,3,2,0:T(8,128)} %collective-permute-done.6, f32[2,32,8,1,1]{4,1,3,2,0:T(8,128)} %collective-permute-done.5, f32[2,32,8,4,1]{4,1,3,2,0:T(8,128)S(1)} %copy.82, f32[2,32,8,1,1]{4,1,3,2,0:T(8,128)} %collective-permute-done.2, ...), kind=kLoop, calls=%fused_computation.7 | loop fusion | flops 10982400 | bytes 3594240 | tf_op jit(solution)/shard_map/concatenate | solution.py:52
  80.2 5.0 %copy-done = f32[27,32,8,4,128]{4,1,0,3,2:T(8,128)} copy-done((f32[27,32,8,4,128]{4,1,0,3,2:T(8,128)}, f32[27,32,8,4,128]{4,1,0,3,2:T(8,128)S(1)}, u32[]{:S(2)}) %copy-start) | copy-done | bytes 14155800
  85.3 13.7 %convolution_bitcast_fusion.2 = f32[8,32,27]{1,0,2:T(8,128)S(1)} fusion(f32[27,32,8,4,128]{4,1,0,3,2:T(8,128)S(1)} %fusion.32, f32[8,8,4,128,1]{3,2,1,0,4:T(4,128)S(1)} %bitcast.338), kind=kOutput, calls=%fused_computation.34 | convolution fusion | flops 169869312 | bytes 14314496 | tf_op jit(solution)/shard_map/opqy,kcpqy->ock/dot_general | solution.py:109
  99.3 1.9 %collective-permute-start.10 = (f32[54,128]{1,0:T(8,128)S(1)}, f32[54,128]{1,0:T(8,128)S(1)}, u32[]{:S(2)}, u32[]{:S(2)}) collective-permute-start(f32[54,128]{1,0:T(8,128)S(1)} %reshape_reshape.3), channel_id=1, source_target_pairs={{0,24},{8,0},{16,8},{24,16},{32,56},{40,32},{48,40},{56,48},{64,88... | collective-permute-start | bytes 82952 | tf_op jit(solution)/shard_map/ppermute | solution.py:70
  101.2 5.4 %collective-permute-start.9 = (f32[54,128]{1,0:T(8,128)S(1)}, f32[54,128]{1,0:T(8,128)S(1)}, u32[]{:S(2)}, u32[]{:S(2)}) collective-permute-start(f32[54,128]{1,0:T(8,128)S(1)} %reshape_reshape.3), channel_id=1, source_target_pairs={{0,16},{8,24},{16,0},{24,8},{32,48},{40,56},{48,32},{56,40},{64,80... | collective-permute-start | bytes 82952 | tf_op jit(solution)/shard_map/ppermute | solution.py:70
  106.6 4.7 %collective-permute-start.8 = (f32[54,128]{1,0:T(8,128)S(1)}, f32[54,128]{1,0:T(8,128)S(1)}, u32[]{:S(2)}, u32[]{:S(2)}) collective-permute-start(f32[54,128]{1,0:T(8,128)S(1)} %reshape_reshape.3), channel_id=1, source_target_pairs={{0,8},{8,16},{16,24},{24,0},{32,40},{40,48},{48,56},{56,32},{64,72... | collective-permute-start | bytes 82952 | tf_op jit(solution)/shard_map/ppermute | solution.py:70
  115.5 0.9 copy-done.1
  116.4 3.4 %convolution_bitcast_fusion.1 = f32[8,8,4,128]{3,0,2,1:T(8,128)S(1)} fusion(f32[27,32,8,4,128]{4,1,0,3,2:T(8,128)S(1)} %copy-done.1, f32[8,27,32,1,1]{2,0,1,4,3:T(8,128)S(1)} %bitcast.339), kind=kOutput, calls=%fused_computation.33 | convolution fusion | flops 169869312 | bytes 14314496 | tf_op jit(solution)/shard_map/okc,kcpqy->opqy/dot_general | solution.py:119
  119.8 5.0 %convolution_bitcast_fusion = f32[8,8,4,128]{3,0,2,1:T(8,128)S(1)} fusion(f32[32,27,8,1,1]{0,2,4,3,1:T(8,128)S(1)} %bitcast.340, f32[27,32,8,4,128]{4,1,3,2,0:T(8,128)S(1)} %fusion.5), kind=kOutput, calls=%fused_computation.32 | convolution fusion | flops 169869312 | bytes 14314496 | tf_op jit(solution)/shard_map/okc,kopqy->cpqy/dot_general | solution.py:124
  125.1 0.7 copy.115
  125.7 0.7 copy.114
  126.5 0.7 gather_fusion.1
  127.3 4.2 %collective-permute-start.13 = (f32[54,128]{1,0:T(8,128)S(1)}, f32[54,128]{1,0:T(8,128)S(1)}, u32[]{:S(2)}, u32[]{:S(2)}) collective-permute-start(f32[54,128]{1,0:T(8,128)S(1)} %fusion.82), channel_id=1, source_target_pairs={{0,96},{8,104},{16,112},{24,120},{32,0},{40,8},{48,16},{56,24},{64... | collective-permute-start | bytes 82952 | tf_op jit(solution)/shard_map/ppermute | solution.py:70
  131.4 11.9 %collective-permute-start.12 = (f32[54,128]{1,0:T(8,128)S(1)}, f32[54,128]{1,0:T(8,128)S(1)}, u32[]{:S(2)}, u32[]{:S(2)}) collective-permute-start(f32[54,128]{1,0:T(8,128)S(1)} %fusion.82), channel_id=1, source_target_pairs={{0,64},{8,72},{16,80},{24,88},{32,96},{40,104},{48,112},{56,120},{... | collective-permute-start | bytes 82952 | tf_op jit(solution)/shard_map/ppermute | solution.py:70
  143.4 4.3 %collective-permute-start.11 = (f32[54,128]{1,0:T(8,128)S(1)}, f32[54,128]{1,0:T(8,128)S(1)}, u32[]{:S(2)}, u32[]{:S(2)}) collective-permute-start(f32[54,128]{1,0:T(8,128)S(1)} %fusion.82), channel_id=1, source_target_pairs={{0,32},{8,40},{16,48},{24,56},{32,64},{40,72},{48,80},{56,88},{64,... | collective-permute-start | bytes 82952 | tf_op jit(solution)/shard_map/ppermute | solution.py:70
  147.7 5.3 %collective-permute-done.11 = f32[54,128]{1,0:T(8,128)S(1)} collective-permute-done((f32[54,128]{1,0:T(8,128)S(1)}, f32[54,128]{1,0:T(8,128)S(1)}, u32[]{:S(2)}, u32[]{:S(2)}) %collective-permute-start.11) | collective-permute-done | bytes 27680 | tf_op jit(solution)/shard_map/ppermute | solution.py:70
  153.1 0.7 gather_fusion.2
  153.9 14.0 %collective-permute-start.16 = (f32[54,128]{1,0:T(8,128)S(1)}, f32[54,128]{1,0:T(8,128)S(1)}, u32[]{:S(2)}, u32[]{:S(2)}) collective-permute-start(f32[54,128]{1,0:T(8,128)S(1)} %fusion.81), channel_id=1, source_target_pairs={{0,3},{1,0},{2,1},{3,2},{4,7},{5,4},{6,5},{7,6},{8,11},{9,8},{10,9... | collective-permute-start | bytes 82952 | tf_op jit(solution)/shard_map/ppermute | solution.py:70
  167.9 1.9 %collective-permute-start.15 = (f32[54,128]{1,0:T(8,128)S(1)}, f32[54,128]{1,0:T(8,128)S(1)}, u32[]{:S(2)}, u32[]{:S(2)}) collective-permute-start(f32[54,128]{1,0:T(8,128)S(1)} %fusion.81), channel_id=1, source_target_pairs={{0,2},{1,3},{2,0},{3,1},{4,6},{5,7},{6,4},{7,5},{8,10},{9,11},{10,... | collective-permute-start | bytes 82952 | tf_op jit(solution)/shard_map/ppermute | solution.py:70
  169.8 2.8 %collective-permute-start.14 = (f32[54,128]{1,0:T(8,128)S(1)}, f32[54,128]{1,0:T(8,128)S(1)}, u32[]{:S(2)}, u32[]{:S(2)}) collective-permute-start(f32[54,128]{1,0:T(8,128)S(1)} %fusion.81), channel_id=1, source_target_pairs={{0,1},{1,2},{2,3},{3,0},{4,5},{5,6},{6,7},{7,4},{8,9},{9,10},{10,1... | collective-permute-start | bytes 82952 | tf_op jit(solution)/shard_map/ppermute | solution.py:70
  172.6 2.5 %collective-permute-done.15 = f32[54,128]{1,0:T(8,128)S(1)} collective-permute-done((f32[54,128]{1,0:T(8,128)S(1)}, f32[54,128]{1,0:T(8,128)S(1)}, u32[]{:S(2)}, u32[]{:S(2)}) %collective-permute-start.15) | collective-permute-done | bytes 27680 | tf_op jit(solution)/shard_map/ppermute | solution.py:70
  175.2 1.6 collective-permute-done.14
  176.8 0.7 gather_fusion.3
  177.6 1.9 %collective-permute-start.17 = (f32[54,128]{1,0:T(8,128)S(1)}, f32[54,128]{1,0:T(8,128)S(1)}, u32[]{:S(2)}, u32[]{:S(2)}) collective-permute-start(f32[54,128]{1,0:T(8,128)S(1)} %fusion.80), channel_id=1, source_target_pairs={{0,4},{1,5},{2,6},{3,7},{4,0},{5,1},{6,2},{7,3},{8,12},{9,13},{10,... | collective-permute-start | bytes 82952 | tf_op jit(solution)/shard_map/ppermute | solution.py:70
  179.5 5.3 %collective-permute-done.17 = f32[54,128]{1,0:T(8,128)S(1)} collective-permute-done((f32[54,128]{1,0:T(8,128)S(1)}, f32[54,128]{1,0:T(8,128)S(1)}, u32[]{:S(2)}, u32[]{:S(2)}) %collective-permute-start.17) | collective-permute-done | bytes 27680 | tf_op jit(solution)/shard_map/ppermute | solution.py:70
  185.5 0.8 mul.15
  186.4 1.6 copy.116
  (115 shorter events, 15.0 us)
Async XLA Ops:
  17.9 53.4 %collective-permute-start.1 = (f32[2,32,8,1,128]{4,1,3,2,0:T(8,128)}, f32[2,32,8,1,128]{4,1,3,2,0:T(8,128)S(1)}, u32[]{:S(2)}, u32[]{:S(2)}) collective-permute-start(f32[2,32,8,1,128]{4,1,3,2,0:T(8,128)} %get-tuple-element.19), channel_id=1, source_target_pairs={{0,8},{1,9},{2,10},{3,11},{4,12},{5,13},{6,14},{7,15},{8,16},{9,17... | collective-permute-start | bytes 786440 | tf_op jit(solution)/shard_map/ppermute | solution.py:28
  21.7 49.6 %collective-permute-start.6 = (f32[2,32,8,1,128]{4,1,3,2,0:T(8,128)}, f32[2,32,8,1,128]{4,1,3,2,0:T(8,128)}, u32[]{:S(2)}, u32[]{:S(2)}) collective-permute-start(f32[2,32,8,1,128]{4,1,3,2,0:T(8,128)} %get-tuple-element.20), channel_id=1, source_target_pairs={{8,0},{9,1},{10,2},{11,3},{12,4},{13,5},{14,6},{15,7},{16,8},{17,9... | collective-permute-start | bytes 786440 | tf_op jit(solution)/shard_map/ppermute | solution.py:28
  27.0 20.9 %collective-permute-start = (f32[2,32,8,1,1]{4,1,3,2,0:T(8,128)}, f32[2,32,8,1,1]{4,1,3,2,0:T(8,128)}, u32[]{:S(2)}, u32[]{:S(2)}) collective-permute-start(f32[2,32,8,1,1]{4,1,3,2,0:T(8,128)} %get-tuple-element.15), channel_id=1, source_target_pairs={{0,9},{1,10},{2,11},{3,12},{4,13},{5,14},{6,15},{8,17},{9,18},{10,... | collective-permute-start | bytes 6152 | tf_op jit(solution)/shard_map/ppermute | solution.py:28
  31.2 18.0 %collective-permute-start.4 = (f32[2,32,8,4,1]{1,2,4,3,0:T(8,128)S(1)}, f32[2,32,8,4,1]{1,2,4,3,0:T(8,128)S(1)}, u32[]{:S(2)}, u32[]{:S(2)}) collective-permute-start(f32[2,32,8,4,1]{1,2,4,3,0:T(8,128)S(1)} %copy.80), channel_id=1, source_target_pairs={{1,0},{2,1},{3,2},{4,3},{5,4},{6,5},{7,6},{9,8},{10,9},{11,10},{12... | collective-permute-start | bytes 24584 | tf_op jit(solution)/shard_map/ppermute | solution.py:28
  32.9 23.1 %collective-permute-start.3 = (f32[2,32,8,4,1]{1,2,4,3,0:T(8,128)S(1)}, f32[2,32,8,4,1]{1,2,4,3,0:T(8,128)S(1)}, u32[]{:S(2)}, u32[]{:S(2)}) collective-permute-start(f32[2,32,8,4,1]{1,2,4,3,0:T(8,128)S(1)} %copy.79), channel_id=1, source_target_pairs={{0,1},{1,2},{2,3},{3,4},{4,5},{5,6},{6,7},{8,9},{9,10},{10,11},{11... | collective-permute-start | bytes 24584 | tf_op jit(solution)/shard_map/ppermute | solution.py:28
  47.9 11.7 %collective-permute-start.2 = (f32[2,32,8,1,1]{4,1,3,2,0:T(8,128)}, f32[2,32,8,1,1]{4,1,3,2,0:T(8,128)}, u32[]{:S(2)}, u32[]{:S(2)}) collective-permute-start(f32[2,32,8,1,1]{4,1,3,2,0:T(8,128)} %get-tuple-element.16), channel_id=1, source_target_pairs={{1,8},{2,9},{3,10},{4,11},{5,12},{6,13},{7,14},{9,16},{10,17},{11,... | collective-permute-start | bytes 6152 | tf_op jit(solution)/shard_map/ppermute | solution.py:28
  49.2 12.2 %collective-permute-start.5 = (f32[2,32,8,1,1]{4,1,3,2,0:T(8,128)}, f32[2,32,8,1,1]{4,1,3,2,0:T(8,128)}, u32[]{:S(2)}, u32[]{:S(2)}) collective-permute-start(f32[2,32,8,1,1]{4,1,3,2,0:T(8,128)} %get-tuple-element.17), channel_id=1, source_target_pairs={{8,1},{9,2},{10,3},{11,4},{12,5},{13,6},{14,7},{16,9},{17,10},{18,... | collective-permute-start | bytes 6152 | tf_op jit(solution)/shard_map/ppermute | solution.py:28
  56.0 15.3 %collective-permute-start.7 = (f32[2,32,8,1,1]{4,1,3,2,0:T(8,128)}, f32[2,32,8,1,1]{4,1,3,2,0:T(8,128)}, u32[]{:S(2)}, u32[]{:S(2)}) collective-permute-start(f32[2,32,8,1,1]{4,1,3,2,0:T(8,128)} %get-tuple-element.18), channel_id=1, source_target_pairs={{9,0},{10,1},{11,2},{12,3},{13,4},{14,5},{15,6},{17,8},{18,9},{19,... | collective-permute-start | bytes 6152 | tf_op jit(solution)/shard_map/ppermute | solution.py:28
  76.1 9.2 %copy-start.2 = (f32[8,8,4,128]{3,2,1,0:T(4,128)S(1)}, f32[8,8,4,128]{3,2,1,0:T(4,128)}, u32[]{:S(2)}) copy-start(f32[8,8,4,128]{3,2,1,0:T(4,128)} %param.7) | copy-start | bytes 393220
  80.2 5.1 %copy-start = (f32[27,32,8,4,128]{4,1,0,3,2:T(8,128)}, f32[27,32,8,4,128]{4,1,0,3,2:T(8,128)S(1)}, u32[]{:S(2)}) copy-start(f32[27,32,8,4,128]{4,1,0,3,2:T(8,128)S(1)} %fusion.32) | copy-start | bytes 42467332
  99.3 27.2 %collective-permute-start.10 = (f32[54,128]{1,0:T(8,128)S(1)}, f32[54,128]{1,0:T(8,128)S(1)}, u32[]{:S(2)}, u32[]{:S(2)}) collective-permute-start(f32[54,128]{1,0:T(8,128)S(1)} %reshape_reshape.3), channel_id=1, source_target_pairs={{0,24},{8,0},{16,8},{24,16},{32,56},{40,32},{48,40},{56,48},{64,88... | collective-permute-start | bytes 82952 | tf_op jit(solution)/shard_map/ppermute | solution.py:70
  101.2 25.2 %collective-permute-start.9 = (f32[54,128]{1,0:T(8,128)S(1)}, f32[54,128]{1,0:T(8,128)S(1)}, u32[]{:S(2)}, u32[]{:S(2)}) collective-permute-start(f32[54,128]{1,0:T(8,128)S(1)} %reshape_reshape.3), channel_id=1, source_target_pairs={{0,16},{8,24},{16,0},{24,8},{32,48},{40,56},{48,32},{56,40},{64,80... | collective-permute-start | bytes 82952 | tf_op jit(solution)/shard_map/ppermute | solution.py:70
  106.6 19.8 %collective-permute-start.8 = (f32[54,128]{1,0:T(8,128)S(1)}, f32[54,128]{1,0:T(8,128)S(1)}, u32[]{:S(2)}, u32[]{:S(2)}) collective-permute-start(f32[54,128]{1,0:T(8,128)S(1)} %reshape_reshape.3), channel_id=1, source_target_pairs={{0,8},{8,16},{16,24},{24,0},{32,40},{40,48},{48,56},{56,32},{64,72... | collective-permute-start | bytes 82952 | tf_op jit(solution)/shard_map/ppermute | solution.py:70
  111.3 5.0 %copy-start.1 = (f32[27,32,8,4,128]{4,1,0,3,2:T(8,128)S(1)}, f32[27,32,8,4,128]{4,1,0,3,2:T(8,128)}, u32[]{:S(2)}) copy-start(f32[27,32,8,4,128]{4,1,0,3,2:T(8,128)} %copy-done) | copy-start | bytes 42467332
  111.4 5.0 %copy-start.3 = (f32[8,32,3,3,3]{1,0,4,3,2:T(8,128)S(1)}, f32[8,32,3,3,3]{1,0,4,3,2:T(8,128)}, u32[]{:S(2)}) copy-start(f32[8,32,3,3,3]{1,0,4,3,2:T(8,128)} %param.6) | copy-start | bytes 82948
  116.4 10.8 %copy-start.7 = (pred[4]{0:T(512)(128)(4,1)S(1)}, pred[4]{0:T(512)(128)(4,1)}, u32[]{:S(2)}) copy-start(pred[4]{0:T(512)(128)(4,1)} %compare_and_fusion.2) | copy-start | bytes 16
  116.4 37.4 %copy-start.6 = (pred[4]{0:T(512)(128)(4,1)S(1)}, pred[4]{0:T(512)(128)(4,1)}, u32[]{:S(2)}) copy-start(pred[4]{0:T(512)(128)(4,1)} %compare_and_fusion.1) | copy-start | bytes 16
  116.4 61.1 %copy-start.5 = (pred[4]{0:T(512)(128)(4,1)S(1)}, pred[4]{0:T(512)(128)(4,1)}, u32[]{:S(2)}) copy-start(pred[4]{0:T(512)(128)(4,1)} %compare_and_fusion) | copy-start | bytes 16
  116.4 69.1 %copy-start.4 = (pred[2]{0:T(512)(128)(4,1)S(1)}, pred[2]{0:T(512)(128)(4,1)}, u32[]{:S(2)}) copy-start(pred[2]{0:T(512)(128)(4,1)} %compare_and_fusion.3) | copy-start | bytes 10
  127.3 20.4 %collective-permute-start.13 = (f32[54,128]{1,0:T(8,128)S(1)}, f32[54,128]{1,0:T(8,128)S(1)}, u32[]{:S(2)}, u32[]{:S(2)}) collective-permute-start(f32[54,128]{1,0:T(8,128)S(1)} %fusion.82), channel_id=1, source_target_pairs={{0,96},{8,104},{16,112},{24,120},{32,0},{40,8},{48,16},{56,24},{64... | collective-permute-start | bytes 82952 | tf_op jit(solution)/shard_map/ppermute | solution.py:70
  131.4 16.3 %collective-permute-start.12 = (f32[54,128]{1,0:T(8,128)S(1)}, f32[54,128]{1,0:T(8,128)S(1)}, u32[]{:S(2)}, u32[]{:S(2)}) collective-permute-start(f32[54,128]{1,0:T(8,128)S(1)} %fusion.82), channel_id=1, source_target_pairs={{0,64},{8,72},{16,80},{24,88},{32,96},{40,104},{48,112},{56,120},{... | collective-permute-start | bytes 82952 | tf_op jit(solution)/shard_map/ppermute | solution.py:70
  143.4 9.7 %collective-permute-start.11 = (f32[54,128]{1,0:T(8,128)S(1)}, f32[54,128]{1,0:T(8,128)S(1)}, u32[]{:S(2)}, u32[]{:S(2)}) collective-permute-start(f32[54,128]{1,0:T(8,128)S(1)} %fusion.82), channel_id=1, source_target_pairs={{0,32},{8,40},{16,48},{24,56},{32,64},{40,72},{48,80},{56,88},{64,... | collective-permute-start | bytes 82952 | tf_op jit(solution)/shard_map/ppermute | solution.py:70
  153.9 18.8 %collective-permute-start.16 = (f32[54,128]{1,0:T(8,128)S(1)}, f32[54,128]{1,0:T(8,128)S(1)}, u32[]{:S(2)}, u32[]{:S(2)}) collective-permute-start(f32[54,128]{1,0:T(8,128)S(1)} %fusion.81), channel_id=1, source_target_pairs={{0,3},{1,0},{2,1},{3,2},{4,7},{5,4},{6,5},{7,6},{8,11},{9,8},{10,9... | collective-permute-start | bytes 82952 | tf_op jit(solution)/shard_map/ppermute | solution.py:70
  167.9 7.3 %collective-permute-start.15 = (f32[54,128]{1,0:T(8,128)S(1)}, f32[54,128]{1,0:T(8,128)S(1)}, u32[]{:S(2)}, u32[]{:S(2)}) collective-permute-start(f32[54,128]{1,0:T(8,128)S(1)} %fusion.81), channel_id=1, source_target_pairs={{0,2},{1,3},{2,0},{3,1},{4,6},{5,7},{6,4},{7,5},{8,10},{9,11},{10,... | collective-permute-start | bytes 82952 | tf_op jit(solution)/shard_map/ppermute | solution.py:70
  169.8 7.0 %collective-permute-start.14 = (f32[54,128]{1,0:T(8,128)S(1)}, f32[54,128]{1,0:T(8,128)S(1)}, u32[]{:S(2)}, u32[]{:S(2)}) collective-permute-start(f32[54,128]{1,0:T(8,128)S(1)} %fusion.81), channel_id=1, source_target_pairs={{0,1},{1,2},{2,3},{3,0},{4,5},{5,6},{6,7},{7,4},{8,9},{9,10},{10,1... | collective-permute-start | bytes 82952 | tf_op jit(solution)/shard_map/ppermute | solution.py:70
  177.6 7.3 %collective-permute-start.17 = (f32[54,128]{1,0:T(8,128)S(1)}, f32[54,128]{1,0:T(8,128)S(1)}, u32[]{:S(2)}, u32[]{:S(2)}) collective-permute-start(f32[54,128]{1,0:T(8,128)S(1)} %fusion.80), channel_id=1, source_target_pairs={{0,4},{1,5},{2,6},{3,7},{4,0},{5,1},{6,2},{7,3},{8,12},{9,13},{10,... | collective-permute-start | bytes 82952 | tf_op jit(solution)/shard_map/ppermute | solution.py:70

commit v9 on v6

--- a/solution.py
+++ b/solution.py
@@ -71,7 +71,10 @@
     both = jnp.pad(both, ((0, 0), (0, 0), (1, 1), (0, 0), (0, 0)))
     padded, padded_up = both[0], both[1]
     taps = patches(padded, planes, rows_x, rows_y, False)
-    local_grad = jnp.einsum("opqy,kcpqy->ock", upstream, taps, precision=lax.Precision.HIGH)
+    first = lax.axis_index("col") * own_inputs
+    own_up = lax.dynamic_slice_in_dim(padded_up, first, own_inputs, 0)
+    shifted_up = patches(own_up, planes, rows_x, rows_y, True)
+    local_grad = jnp.einsum("kopqy,cpqy->ock", shifted_up, fields[0], precision=lax.Precision.HIGH)
     local_grad = local_grad.reshape(local_grad.shape[0], local_grad.shape[1], 3, 3, 3)
     flat = local_grad.reshape(-1, 128)
     sizes = [lax.axis_size(a) for a in ("gx", "gy")]
@@ -82,7 +85,6 @@
     total_grad = flat.reshape(local_grad.shape)
     by_tap = jnp.swapaxes(filters.reshape(filters.shape[0], filters.shape[1], 27), 1, 2)
     response = jnp.einsum("okc,kcpqy->opqy", by_tap, taps, precision=lax.Precision.HIGH)
-    first = lax.axis_index("col") * own_inputs
     own_filters = lax.dynamic_slice_in_dim(all_rows, first, own_inputs, 1)
     own_by_tap = jnp.swapaxes(own_filters.reshape(own_filters.shape[0], own_inputs, 27), 1, 2)
     taps_up = patches(padded_up, planes, rows_x, rows_y, True)

time: 162 us -> 154 us (0.951); the launches traced: 161 us -> 151 us
  waiting for transfers between devices: 25.1 us -> 10.2 us
  matrix products: 22.1 us -> 10.2 us
  starting transfers between devices: 56.3 us -> 68.1 us
  local copies, waits for them, and re-layouts: 30.9 us -> 34.4 us
    dot_general x1, matrix products: 13.7 us -> 1.52 us  [shards(): jnp.einsum('kopqy,cpqy->ock', shifted_up, fields[0], precision=lax.Precis...]
    ppermute x10, starting transfers between devices: 43.5 us -> 53.5 us  [butterfly_sum(): received.append(lax.ppermute(value, axis, pairs))]
    ppermute x2, waiting for transfers between devices: 7.49 us -> 0.01 us  [with_halo(): lax.ppermute(lax.slice_in_dim(block, block.shape[dim] - width, None, axis...]
    ppermute x10, waiting for transfers between devices: 15.8 us -> 8.71 us  [butterfly_sum(): received.append(lax.ppermute(value, axis, pairs))]
    slice x0 -> x1, local copies, waits for them, and re-layouts: none -> 1.88 us  [shards(): padded, padded_up = (both[0], both[1])]
    unnamed x67 -> x95, local copies, waits for them, and re-layouts: 19.5 us -> 20 us
  transfers between devices with their start and end apart: 14 -> 14, of which waited for: 7 -> 6; matrix products, arithmetic and copies ran while one was open for 9% -> 18% of each run, Pallas kernels for 0% -> 0%
where the time goes in v9:
time: 154 us; the launch traced here: 151 us
  starting transfers between devices  68.1 us (44%)
  local copies, waits for them, and re-layouts  34.4 us (22%)
  blocking collectives  20.8 us (14%)
  waiting for transfers between devices  10.2 us (7%)
  matrix products  10.2 us (7%)
  other arithmetic  5.65 us (4%)
    ppermute x10, starting transfers between devices, butterfly_sum(): received.append(lax.ppermute(value, axis, pairs))  53.5 us
    unnamed x95, local copies, waits for them, and re-layouts  20 us
    ppermute x10, waiting for transfers between devices, butterfly_sum(): received.append(lax.ppermute(value, axis, pairs))  8.71 us
    ppermute x2, starting transfers between devices, with_halo(): lax.ppermute(lax.slice_in_dim(block, block.shape[dim] - width, None, axis...  7.33 us
    all_gather x1, blocking collectives, shards(): lax.all_gather(upstream, 'col', axis=0, tiled=True)  7.28 us
    ppermute x2, starting transfers between devices, with_halo(): lax.ppermute(lax.slice_in_dim(block, 0, width, axis=dim), axis, backward)  7.25 us
    all_gather x1, blocking collectives, shards(): lax.all_gather(volume, 'col', axis=0, tiled=True)  6.77 us
    all_gather x1, blocking collectives, shards(): all_rows = lax.all_gather(filters, 'col', axis=0, tiled=True)  6.77 us
  transfers between devices with their start and end apart: 14, of which 6 were waited for; matrix products, arithmetic and copies ran while one was open for 18% of the time, Pallas kernels for 0%

profile of v9, /device:TPU:6, one launch (start us, length us, event | category | flops | bytes accessed | tf_op | source)
XLA Modules:
  0.0 150.7 jit_solution(16074814399947275904)
XLA Ops:
  0.6 1.0 copy.73
  1.6 6.8 %all_gather.9 = f32[32,8,4,128]{3,0,2,1:T(8,128)S(1)} all-gather(f32[8,8,4,128]{3,0,2,1:T(8,128)S(1)} %copy.73), channel_id=1, replica_groups=mesh['col'=4,'gx'=16,'gy'=8] {'col'}, dimensions={0}, use_global_device_ids=true | all-gather | bytes 655360 | tf_op jit(solution)/shard_map/all_gather | solution.py:66
  8.4 1.0 copy.74
  9.4 7.3 %all_gather.10 = f32[32,8,4,128]{3,0,2,1:T(8,128)S(1)} all-gather(f32[8,8,4,128]{3,0,2,1:T(8,128)S(1)} %copy.74), channel_id=1, replica_groups=mesh['col'=4,'gx'=16,'gy'=8] {'col'}, dimensions={0}, use_global_device_ids=true | all-gather | bytes 655360 | tf_op jit(solution)/shard_map/all_gather | solution.py:67
  16.7 3.8 %collective-permute-start = (f32[2,32,8,1,128]{4,1,3,2,0:T(8,128)S(1)}, f32[2,32,8,1,128]{4,1,3,2,0:T(8,128)S(1)}, u32[]{:S(2)}, u32[]{:S(2)}) collective-permute-start(f32[2,32,8,1,128]{4,1,3,2,0:T(8,128)S(1)} %get-tuple-element.18), channel_id=1, source_target_pairs={{0,8},{8,16},{16,24},{24,32},{32,40},{40,48},{48,56},{56,64},{64,7... | collective-permute-start | bytes 786440 | tf_op jit(solution)/shard_map/ppermute | solution.py:12
  20.5 1.3 collective-permute-start.1
  23.1 6.8 %all_gather.11 = f32[32,32,3,3,3]{1,0,4,3,2:T(8,128)S(1)} all-gather(f32[8,32,3,3,3]{1,0,4,3,2:T(8,128)} %param.6), channel_id=1, replica_groups=mesh['col'=4,'gx'=16,'gy'=8] {'col'}, dimensions={0}, use_global_device_ids=true | all-gather | bytes 138240 | tf_op jit(solution)/shard_map/all_gather | solution.py:69
  30.0 0.9 collective-permute-done.1
  30.9 0.7 copy-done.1
  31.7 1.7 %fusion.67 = (f32[2,32,8,6,1]{4,1,3,2,0:T(8,128)}, f32[2,32,8,6,1]{4,1,3,2,0:T(8,128)S(1)}) fusion(f32[2,32,8,6,128]{4,1,3,2,0:T(8,128)S(1)} %pad_maximum_fusion), kind=kLoop, calls=%fused_computation.239 | loop fusion | bytes 49152 | tf_op jit(solution)/shard_map/slice | solution.py:13
  33.4 2.0 %copy.75 = f32[2,32,8,6,1]{1,2,4,3,0:T(8,128)S(1)} copy(f32[2,32,8,6,1]{4,1,3,2,0:T(8,128)} %get-tuple-element.16) | data formatting | bytes 24576 | tf_op jit(solution)/shard_map/slice | solution.py:13
  35.4 3.5 %collective-permute-start.2 = (f32[2,32,8,6,1]{1,2,4,3,0:T(8,128)S(1)}, f32[2,32,8,6,1]{1,2,4,3,0:T(8,128)S(1)}, u32[]{:S(2)}, u32[]{:S(2)}) collective-permute-start(f32[2,32,8,6,1]{1,2,4,3,0:T(8,128)S(1)} %copy.75), channel_id=1, source_target_pairs={{0,1},{1,2},{2,3},{3,4},{4,5},{5,6},{6,7},{8,9},{9,10},{10,11},{11... | collective-permute-start | bytes 36872 | tf_op jit(solution)/shard_map/ppermute | solution.py:12
  38.9 1.2 copy.76
  40.2 6.0 %collective-permute-start.3 = (f32[2,32,8,6,1]{1,2,4,3,0:T(8,128)}, f32[2,32,8,6,1]{1,2,4,3,0:T(8,128)}, u32[]{:S(2)}, u32[]{:S(2)}) collective-permute-start(f32[2,32,8,6,1]{1,2,4,3,0:T(8,128)} %copy.76), channel_id=1, source_target_pairs={{1,0},{2,1},{3,2},{4,3},{5,4},{6,5},{7,6},{9,8},{10,9},{11,10},{12... | collective-permute-start | bytes 36872 | tf_op jit(solution)/shard_map/ppermute | solution.py:15
  46.2 0.6 compare_and_fusion.3
  46.9 0.6 copy.77
  47.6 0.6 collective-permute-done.3
  48.2 2.6 %copy.78 = f32[2,32,8,6,1]{4,1,3,2,0:T(8,128)} copy(f32[2,32,8,6,1]{1,2,4,3,0:T(8,128)} %collective-permute-done.3) | data formatting | bytes 24576 | tf_op jit(solution)/shard_map/ppermute | solution.py:15
  50.8 3.3 %select_maximum_fusion = f32[2,32,10,6,130]{4,1,3,2,0:T(8,128)S(1)} fusion(f32[2,32,8,6,1]{4,1,3,2,0:T(8,128)} %copy.78, f32[2,32,8,6,1]{4,1,3,2,0:T(8,128)S(1)} %copy.77, f32[2,32,8,1,128]{4,1,3,2,0:T(8,128)} %copy-done.1, f32[2,32,8,1,128]{4,1,3,2,0:T(8,128)S(1)} %collective-permute-done, f32[1,32,8,4,128]{4,1,3,2,0:T(8,128)S(1)} %bitcast.501, ...), kind=kLoop, calls=%fused_computation.6 | loop fusion | flops 6988800 | bytes 3594240 | tf_op jit(solution)/shard_map/concatenate | solution.py:16
  54.1 1.9 %fusion.66 = (f32[1,32,10,6,130]{4,1,3,2,0:T(8,128)S(1)}, f32[32,10,6,130]{3,0,2,1:T(8,128)}, f32[32,10,6,130]{3,0,2,1:T(8,128)S(1)}) fusion(f32[2,32,10,6,130]{4,1,3,2,0:T(8,128)S(1)} %select_maximum_fusion), kind=kLoop, calls=%fused_computation.238 | loop fusion | bytes 4992000 | tf_op jit(solution)/shard_map/slice | solution.py:72
  58.1 1.5 %convolution_bitcast_fusion.2 = f32[8,32,27]{1,0,2:T(8,128)S(1)} fusion(f32[27,8,8,4,128]{4,1,3,0,2:T(8,128)S(1)} %constant_dynamic-update-slice_fusion, f32[32,8,4,128]{3,0,2,1:T(8,128)S(1)} %all_gather.9), kind=kOutput, calls=%fused_computation.16 | convolution fusion | flops 169869312 | bytes 4090880 | tf_op jit(solution)/shard_map/kopqy,cpqy->ock/dot_general | solution.py:77
  59.9 4.0 %collective-permute-start.4 = (f32[54,128]{1,0:T(8,128)S(1)}, f32[54,128]{1,0:T(8,128)S(1)}, u32[]{:S(2)}, u32[]{:S(2)}) collective-permute-start(f32[54,128]{1,0:T(8,128)S(1)} %reshape_reshape.3), channel_id=1, source_target_pairs={{0,8},{8,16},{16,24},{24,0},{32,40},{40,48},{48,56},{56,32},{64,72... | collective-permute-start | bytes 82952 | tf_op jit(solution)/shard_map/ppermute | solution.py:35
  63.9 7.4 %collective-permute-start.5 = (f32[54,128]{1,0:T(8,128)S(1)}, f32[54,128]{1,0:T(8,128)S(1)}, u32[]{:S(2)}, u32[]{:S(2)}) collective-permute-start(f32[54,128]{1,0:T(8,128)S(1)} %reshape_reshape.3), channel_id=1, source_target_pairs={{0,16},{8,24},{16,0},{24,8},{32,48},{40,56},{48,32},{56,40},{64,80... | collective-permute-start | bytes 82952 | tf_op jit(solution)/shard_map/ppermute | solution.py:35
  71.3 2.1 %collective-permute-start.6 = (f32[54,128]{1,0:T(8,128)S(1)}, f32[54,128]{1,0:T(8,128)S(1)}, u32[]{:S(2)}, u32[]{:S(2)}) collective-permute-start(f32[54,128]{1,0:T(8,128)S(1)} %reshape_reshape.3), channel_id=1, source_target_pairs={{0,24},{8,0},{16,8},{24,16},{32,56},{40,32},{48,40},{56,48},{64,88... | collective-permute-start | bytes 82952 | tf_op jit(solution)/shard_map/ppermute | solution.py:35
  73.4 1.4 fusion.27
  74.9 1.4 fusion.26
  76.3 1.1 fusion.25
  77.4 1.4 fusion.24
  86.4 5.0 %convolution_bitcast_fusion = f32[8,8,4,128]{3,0,2,1:T(8,128)S(1)} fusion(f32[32,27,8,1,1]{0,2,4,3,1:T(8,128)S(1)} %bitcast.503, f32[27,32,8,4,128]{4,1,3,2,0:T(8,128)S(1)} %fusion.1), kind=kOutput, calls=%fused_computation.14 | convolution fusion | flops 169869312 | bytes 14314496 | tf_op jit(solution)/shard_map/okc,kopqy->cpqy/dot_general | solution.py:91
  91.5 3.6 %convolution_bitcast_fusion.1 = f32[8,8,4,128]{3,0,2,1:T(8,128)S(1)} fusion(f32[27,32,8,4,128]{4,1,0,3,2:T(8,128)S(1)} %fusion.28, f32[8,27,32,1,1]{2,0,1,4,3:T(8,128)S(1)} %bitcast.502), kind=kOutput, calls=%fused_computation.15 | convolution fusion | flops 169869312 | bytes 14314496 | tf_op jit(solution)/shard_map/okc,kcpqy->opqy/dot_general | solution.py:87
  95.3 0.7 copy.136
  96.0 0.7 copy.135
  96.7 0.6 gather_fusion.1
  97.4 9.1 %collective-permute-start.7 = (f32[54,128]{1,0:T(8,128)S(1)}, f32[54,128]{1,0:T(8,128)S(1)}, u32[]{:S(2)}, u32[]{:S(2)}) collective-permute-start(f32[54,128]{1,0:T(8,128)S(1)} %fusion.75), channel_id=1, source_target_pairs={{0,32},{8,40},{16,48},{24,56},{32,64},{40,72},{48,80},{56,88},{64,... | collective-permute-start | bytes 82952 | tf_op jit(solution)/shard_map/ppermute | solution.py:35
  106.5 8.1 %collective-permute-start.8 = (f32[54,128]{1,0:T(8,128)S(1)}, f32[54,128]{1,0:T(8,128)S(1)}, u32[]{:S(2)}, u32[]{:S(2)}) collective-permute-start(f32[54,128]{1,0:T(8,128)S(1)} %fusion.75), channel_id=1, source_target_pairs={{0,64},{8,72},{16,80},{24,88},{32,96},{40,104},{48,112},{56,120},{... | collective-permute-start | bytes 82952 | tf_op jit(solution)/shard_map/ppermute | solution.py:35
  114.6 5.5 %collective-permute-start.9 = (f32[54,128]{1,0:T(8,128)S(1)}, f32[54,128]{1,0:T(8,128)S(1)}, u32[]{:S(2)}, u32[]{:S(2)}) collective-permute-start(f32[54,128]{1,0:T(8,128)S(1)} %fusion.75), channel_id=1, source_target_pairs={{0,96},{8,104},{16,112},{24,120},{32,0},{40,8},{48,16},{56,24},{64... | collective-permute-start | bytes 82952 | tf_op jit(solution)/shard_map/ppermute | solution.py:35
  120.1 1.4 collective-permute-done.8
  121.5 3.4 %collective-permute-done.9 = f32[54,128]{1,0:T(8,128)S(1)} collective-permute-done((f32[54,128]{1,0:T(8,128)S(1)}, f32[54,128]{1,0:T(8,128)S(1)}, u32[]{:S(2)}, u32[]{:S(2)}) %collective-permute-start.9) | collective-permute-done | bytes 27680 | tf_op jit(solution)/shard_map/ppermute | solution.py:35
  124.9 0.6 gather_fusion.2
  125.6 1.9 %collective-permute-start.10 = (f32[54,128]{1,0:T(8,128)S(1)}, f32[54,128]{1,0:T(8,128)S(1)}, u32[]{:S(2)}, u32[]{:S(2)}) collective-permute-start(f32[54,128]{1,0:T(8,128)S(1)} %fusion.74), channel_id=1, source_target_pairs={{0,1},{1,2},{2,3},{3,0},{4,5},{5,6},{6,7},{7,4},{8,9},{9,10},{10,1... | collective-permute-start | bytes 82952 | tf_op jit(solution)/shard_map/ppermute | solution.py:35
  127.5 3.1 %collective-permute-start.11 = (f32[54,128]{1,0:T(8,128)S(1)}, f32[54,128]{1,0:T(8,128)S(1)}, u32[]{:S(2)}, u32[]{:S(2)}) collective-permute-start(f32[54,128]{1,0:T(8,128)S(1)} %fusion.74), channel_id=1, source_target_pairs={{0,2},{1,3},{2,0},{3,1},{4,6},{5,7},{6,4},{7,5},{8,10},{9,11},{10,... | collective-permute-start | bytes 82952 | tf_op jit(solution)/shard_map/ppermute | solution.py:35
  130.6 4.5 %collective-permute-start.12 = (f32[54,128]{1,0:T(8,128)S(1)}, f32[54,128]{1,0:T(8,128)S(1)}, u32[]{:S(2)}, u32[]{:S(2)}) collective-permute-start(f32[54,128]{1,0:T(8,128)S(1)} %fusion.74), channel_id=1, source_target_pairs={{0,3},{1,0},{2,1},{3,2},{4,7},{5,4},{6,5},{7,6},{8,11},{9,8},{10,9... | collective-permute-start | bytes 82952 | tf_op jit(solution)/shard_map/ppermute | solution.py:35
  135.2 2.1 %collective-permute-done.12 = f32[54,128]{1,0:T(8,128)S(1)} collective-permute-done((f32[54,128]{1,0:T(8,128)S(1)}, f32[54,128]{1,0:T(8,128)S(1)}, u32[]{:S(2)}, u32[]{:S(2)}) %collective-permute-start.12) | collective-permute-done | bytes 27680 | tf_op jit(solution)/shard_map/ppermute | solution.py:35
  137.3 0.6 gather_fusion.3
  137.9 7.8 %collective-permute-start.13 = (f32[54,128]{1,0:T(8,128)S(1)}, f32[54,128]{1,0:T(8,128)S(1)}, u32[]{:S(2)}, u32[]{:S(2)}) collective-permute-start(f32[54,128]{1,0:T(8,128)S(1)} %fusion.73), channel_id=1, source_target_pairs={{0,4},{1,5},{2,6},{3,7},{4,0},{5,1},{6,2},{7,3},{8,12},{9,13},{10,... | collective-permute-start | bytes 82952 | tf_op jit(solution)/shard_map/ppermute | solution.py:35
  145.8 1.8 %collective-permute-done.13 = f32[54,128]{1,0:T(8,128)S(1)} collective-permute-done((f32[54,128]{1,0:T(8,128)S(1)}, f32[54,128]{1,0:T(8,128)S(1)}, u32[]{:S(2)}, u32[]{:S(2)}) %collective-permute-start.13) | collective-permute-done | bytes 27680 | tf_op jit(solution)/shard_map/ppermute | solution.py:35
  148.2 0.8 mul.15
  149.1 1.6 %copy.137 = f32[8,32,3,3,3]{1,0,4,3,2:T(8,128)} copy(f32[8,32,3,3,3]{4,3,2,1,0:T(4,128)S(1)} %mul.15) | data formatting | bytes 55296
  (130 shorter events, 12.4 us)
Async XLA Ops:
  16.7 13.3 %collective-permute-start = (f32[2,32,8,1,128]{4,1,3,2,0:T(8,128)S(1)}, f32[2,32,8,1,128]{4,1,3,2,0:T(8,128)S(1)}, u32[]{:S(2)}, u32[]{:S(2)}) collective-permute-start(f32[2,32,8,1,128]{4,1,3,2,0:T(8,128)S(1)} %get-tuple-element.18), channel_id=1, source_target_pairs={{0,8},{8,16},{16,24},{24,32},{32,40},{40,48},{48,56},{56,64},{64,7... | collective-permute-start | bytes 786440 | tf_op jit(solution)/shard_map/ppermute | solution.py:12
  20.5 10.3 %collective-permute-start.1 = (f32[2,32,8,1,128]{4,1,3,2,0:T(8,128)S(1)}, f32[2,32,8,1,128]{4,1,3,2,0:T(8,128)S(1)}, u32[]{:S(2)}, u32[]{:S(2)}) collective-permute-start(f32[2,32,8,1,128]{4,1,3,2,0:T(8,128)S(1)} %get-tuple-element.19), channel_id=1, source_target_pairs={{8,0},{16,8},{24,16},{32,24},{40,32},{48,40},{56,48},{64,56},{72,6... | collective-permute-start | bytes 786440 | tf_op jit(solution)/shard_map/ppermute | solution.py:15
  30.9 0.7 copy-start.1
  35.4 11.5 %collective-permute-start.2 = (f32[2,32,8,6,1]{1,2,4,3,0:T(8,128)S(1)}, f32[2,32,8,6,1]{1,2,4,3,0:T(8,128)S(1)}, u32[]{:S(2)}, u32[]{:S(2)}) collective-permute-start(f32[2,32,8,6,1]{1,2,4,3,0:T(8,128)S(1)} %copy.75), channel_id=1, source_target_pairs={{0,1},{1,2},{2,3},{3,4},{4,5},{5,6},{6,7},{8,9},{9,10},{10,11},{11... | collective-permute-start | bytes 36872 | tf_op jit(solution)/shard_map/ppermute | solution.py:12
  40.2 8.0 %collective-permute-start.3 = (f32[2,32,8,6,1]{1,2,4,3,0:T(8,128)}, f32[2,32,8,6,1]{1,2,4,3,0:T(8,128)}, u32[]{:S(2)}, u32[]{:S(2)}) collective-permute-start(f32[2,32,8,6,1]{1,2,4,3,0:T(8,128)} %copy.76), channel_id=1, source_target_pairs={{1,0},{2,1},{3,2},{4,3},{5,4},{6,5},{7,6},{9,8},{10,9},{11,10},{12... | collective-permute-start | bytes 36872 | tf_op jit(solution)/shard_map/ppermute | solution.py:15
  59.9 18.9 %copy-start = (f32[32,10,6,130]{3,0,2,1:T(8,128)S(1)}, f32[32,10,6,130]{3,0,2,1:T(8,128)}, u32[]{:S(2)}) copy-start(f32[32,10,6,130]{3,0,2,1:T(8,128)} %get-tuple-element.14) | copy-start | bytes 2995204
  59.9 36.8 %collective-permute-start.4 = (f32[54,128]{1,0:T(8,128)S(1)}, f32[54,128]{1,0:T(8,128)S(1)}, u32[]{:S(2)}, u32[]{:S(2)}) collective-permute-start(f32[54,128]{1,0:T(8,128)S(1)} %reshape_reshape.3), channel_id=1, source_target_pairs={{0,8},{8,16},{16,24},{24,0},{32,40},{40,48},{48,56},{56,32},{64,72... | collective-permute-start | bytes 82952 | tf_op jit(solution)/shard_map/ppermute | solution.py:35
  63.9 32.8 %collective-permute-start.5 = (f32[54,128]{1,0:T(8,128)S(1)}, f32[54,128]{1,0:T(8,128)S(1)}, u32[]{:S(2)}, u32[]{:S(2)}) collective-permute-start(f32[54,128]{1,0:T(8,128)S(1)} %reshape_reshape.3), channel_id=1, source_target_pairs={{0,16},{8,24},{16,0},{24,8},{32,48},{40,56},{48,32},{56,40},{64,80... | collective-permute-start | bytes 82952 | tf_op jit(solution)/shard_map/ppermute | solution.py:35
  71.3 25.4 %collective-permute-start.6 = (f32[54,128]{1,0:T(8,128)S(1)}, f32[54,128]{1,0:T(8,128)S(1)}, u32[]{:S(2)}, u32[]{:S(2)}) collective-permute-start(f32[54,128]{1,0:T(8,128)S(1)} %reshape_reshape.3), channel_id=1, source_target_pairs={{0,24},{8,0},{16,8},{24,16},{32,56},{40,32},{48,40},{56,48},{64,88... | collective-permute-start | bytes 82952 | tf_op jit(solution)/shard_map/ppermute | solution.py:35
  86.4 5.0 %copy-start.2 = (f32[8,32,3,3,3]{1,0,4,3,2:T(8,128)S(1)}, f32[8,32,3,3,3]{1,0,4,3,2:T(8,128)}, u32[]{:S(2)}) copy-start(f32[8,32,3,3,3]{1,0,4,3,2:T(8,128)} %param.6) | copy-start | bytes 82948
  91.4 5.8 %copy-start.4 = (pred[4]{0:T(512)(128)(4,1)S(1)}, pred[4]{0:T(512)(128)(4,1)}, u32[]{:S(2)}) copy-start(pred[4]{0:T(512)(128)(4,1)} %compare_and_fusion.2) | copy-start | bytes 16
  91.4 34.0 %copy-start.3 = (pred[4]{0:T(512)(128)(4,1)S(1)}, pred[4]{0:T(512)(128)(4,1)}, u32[]{:S(2)}) copy-start(pred[4]{0:T(512)(128)(4,1)} %get-tuple-element.21) | copy-start | bytes 16
  91.5 56.7 %copy-start.5 = (pred[2]{0:T(512)(128)(4,1)S(1)}, pred[2]{0:T(512)(128)(4,1)}, u32[]{:S(2)}) copy-start(pred[2]{0:T(512)(128)(4,1)} %compare_and_fusion.3) | copy-start | bytes 10
  97.4 22.7 %collective-permute-start.7 = (f32[54,128]{1,0:T(8,128)S(1)}, f32[54,128]{1,0:T(8,128)S(1)}, u32[]{:S(2)}, u32[]{:S(2)}) collective-permute-start(f32[54,128]{1,0:T(8,128)S(1)} %fusion.75), channel_id=1, source_target_pairs={{0,32},{8,40},{16,48},{24,56},{32,64},{40,72},{48,80},{56,88},{64,... | collective-permute-start | bytes 82952 | tf_op jit(solution)/shard_map/ppermute | solution.py:35
  106.5 15.0 %collective-permute-start.8 = (f32[54,128]{1,0:T(8,128)S(1)}, f32[54,128]{1,0:T(8,128)S(1)}, u32[]{:S(2)}, u32[]{:S(2)}) collective-permute-start(f32[54,128]{1,0:T(8,128)S(1)} %fusion.75), channel_id=1, source_target_pairs={{0,64},{8,72},{16,80},{24,88},{32,96},{40,104},{48,112},{56,120},{... | collective-permute-start | bytes 82952 | tf_op jit(solution)/shard_map/ppermute | solution.py:35
  114.6 10.3 %collective-permute-start.9 = (f32[54,128]{1,0:T(8,128)S(1)}, f32[54,128]{1,0:T(8,128)S(1)}, u32[]{:S(2)}, u32[]{:S(2)}) collective-permute-start(f32[54,128]{1,0:T(8,128)S(1)} %fusion.75), channel_id=1, source_target_pairs={{0,96},{8,104},{16,112},{24,120},{32,0},{40,8},{48,16},{56,24},{64... | collective-permute-start | bytes 82952 | tf_op jit(solution)/shard_map/ppermute | solution.py:35
  125.6 9.6 %collective-permute-start.10 = (f32[54,128]{1,0:T(8,128)S(1)}, f32[54,128]{1,0:T(8,128)S(1)}, u32[]{:S(2)}, u32[]{:S(2)}) collective-permute-start(f32[54,128]{1,0:T(8,128)S(1)} %fusion.74), channel_id=1, source_target_pairs={{0,1},{1,2},{2,3},{3,0},{4,5},{5,6},{6,7},{7,4},{8,9},{9,10},{10,1... | collective-permute-start | bytes 82952 | tf_op jit(solution)/shard_map/ppermute | solution.py:35
  127.5 7.7 %collective-permute-start.11 = (f32[54,128]{1,0:T(8,128)S(1)}, f32[54,128]{1,0:T(8,128)S(1)}, u32[]{:S(2)}, u32[]{:S(2)}) collective-permute-start(f32[54,128]{1,0:T(8,128)S(1)} %fusion.74), channel_id=1, source_target_pairs={{0,2},{1,3},{2,0},{3,1},{4,6},{5,7},{6,4},{7,5},{8,10},{9,11},{10,... | collective-permute-start | bytes 82952 | tf_op jit(solution)/shard_map/ppermute | solution.py:35
  130.6 6.7 %collective-permute-start.12 = (f32[54,128]{1,0:T(8,128)S(1)}, f32[54,128]{1,0:T(8,128)S(1)}, u32[]{:S(2)}, u32[]{:S(2)}) collective-permute-start(f32[54,128]{1,0:T(8,128)S(1)} %fusion.74), channel_id=1, source_target_pairs={{0,3},{1,0},{2,1},{3,2},{4,7},{5,4},{6,5},{7,6},{8,11},{9,8},{10,9... | collective-permute-start | bytes 82952 | tf_op jit(solution)/shard_map/ppermute | solution.py:35
  137.9 9.6 %collective-permute-start.13 = (f32[54,128]{1,0:T(8,128)S(1)}, f32[54,128]{1,0:T(8,128)S(1)}, u32[]{:S(2)}, u32[]{:S(2)}) collective-permute-start(f32[54,128]{1,0:T(8,128)S(1)} %fusion.73), channel_id=1, source_target_pairs={{0,4},{1,5},{2,6},{3,7},{4,0},{5,1},{6,2},{7,3},{8,12},{9,13},{10,... | collective-permute-start | bytes 82952 | tf_op jit(solution)/shard_map/ppermute | solution.py:35

commit v10 on v6

--- a/solution.py
+++ b/solution.py
@@ -62,16 +62,16 @@
     own_inputs = channels
     ncol = lax.axis_size("col")
     scale = (planes * rows_x * lax.axis_size("gx") * rows_y * lax.axis_size("gy")) ** (-0.5)
-    fields = jnp.stack(
-        [lax.all_gather(volume, "col", axis=0, tiled=True),
-         lax.all_gather(upstream, "col", axis=0, tiled=True)]
-    )
+    gathered = lax.all_gather(volume, "col", axis=0, tiled=True)
+    fields = jnp.stack([gathered, lax.all_gather(upstream, "col", axis=0, tiled=True)])
     all_rows = lax.all_gather(filters, "col", axis=0, tiled=True)
     both = with_halo(fields, (("gx", 3), ("gy", 4)), 1)
     both = jnp.pad(both, ((0, 0), (0, 0), (1, 1), (0, 0), (0, 0)))
     padded, padded_up = both[0], both[1]
     taps = patches(padded, planes, rows_x, rows_y, False)
-    local_grad = jnp.einsum("opqy,kcpqy->ock", upstream, taps, precision=lax.Precision.HIGH)
+    own_up = pad_depth(with_halo(upstream, (("gx", 2), ("gy", 3)), 1))
+    shifted_up = patches(own_up, planes, rows_x, rows_y, True)
+    local_grad = jnp.einsum("kopqy,cpqy->ock", shifted_up, gathered, precision=lax.Precision.HIGH)
     local_grad = local_grad.reshape(local_grad.shape[0], local_grad.shape[1], 3, 3, 3)
     flat = local_grad.reshape(-1, 128)
     sizes = [lax.axis_size(a) for a in ("gx", "gy")]

time: 162 us -> 166 us (1.025)
  starting transfers between devices: 56.3 us -> 84.1 us
  matrix products: 22.1 us -> 9.97 us
  waiting for transfers between devices: 25.1 us -> 15.7 us
  local copies, waits for them, and re-layouts: 30.9 us -> 25.9 us
    dot_general x1, matrix products: 13.7 us -> 1.52 us  [shards(): jnp.einsum('kopqy,cpqy->ock', shifted_up, gathered, precision=lax.Precisi...]
    ppermute x10, starting transfers between devices: 43.5 us -> 54.2 us  [butterfly_sum(): received.append(lax.ppermute(value, axis, pairs))]
    ppermute x2 -> x4, starting transfers between devices: 7.06 us -> 16.1 us  [with_halo(): lax.ppermute(lax.slice_in_dim(block, 0, width, axis=dim), axis, backward)]
    ppermute x2 -> x4, starting transfers between devices: 5.76 us -> 13.8 us  [with_halo(): lax.ppermute(lax.slice_in_dim(block, block.shape[dim] - width, None, axis...]
    unnamed x67 -> x83, local copies, waits for them, and re-layouts: 19.5 us -> 14.2 us
    ppermute x10, waiting for transfers between devices: 15.8 us -> 11.4 us  [butterfly_sum(): received.append(lax.ppermute(value, axis, pairs))]
    ppermute x2 -> x4, waiting for transfers between devices: 7.49 us -> 3.18 us  [with_halo(): lax.ppermute(lax.slice_in_dim(block, block.shape[dim] - width, None, axis...]
    concatenate x2 -> x3, other arithmetic: 3.64 us -> 3.85 us  [with_halo(): block = jnp.concatenate([low, block, high], axis=dim)]
  transfers between devices with their start and end apart: 14 -> 18, of which waited for: 7 -> 7; matrix products, arithmetic and copies ran while one was open for 9% -> 8% of each run, Pallas kernels for 0% -> 0%
where the time goes in v10:
time: 166 us; the launch traced here: 164 us
  starting transfers between devices  84.1 us (51%)
  local copies, waits for them, and re-layouts  25.9 us (16%)
  blocking collectives  20.6 us (12%)
  waiting for transfers between devices  15.7 us (9%)
  matrix products  9.97 us (6%)
  other arithmetic  5.78 us (3%)
    ppermute x10, starting transfers between devices, butterfly_sum(): received.append(lax.ppermute(value, axis, pairs))  54.2 us
    ppermute x4, starting transfers between devices, with_halo(): lax.ppermute(lax.slice_in_dim(block, 0, width, axis=dim), axis, backward)  16.1 us
    unnamed x83, local copies, waits for them, and re-layouts  14.2 us
    ppermute x4, starting transfers between devices, with_halo(): lax.ppermute(lax.slice_in_dim(block, block.shape[dim] - width, None, axis...  13.8 us
    ppermute x10, waiting for transfers between devices, butterfly_sum(): received.append(lax.ppermute(value, axis, pairs))  11.4 us
    all_gather x1, blocking collectives, shards(): gathered = lax.all_gather(volume, 'col', axis=0, tiled=True)  7.28 us
    all_gather x1, blocking collectives, shards(): all_rows = lax.all_gather(filters, 'col', axis=0, tiled=True)  6.77 us
    all_gather x1, blocking collectives, shards(): lax.all_gather(upstream, 'col', axis=0, tiled=True)  6.51 us
  transfers between devices with their start and end apart: 18, of which 7 were waited for; matrix products, arithmetic and copies ran while one was open for 8% of the time, Pallas kernels for 0%

profile of v10, /device:TPU:6, one launch (start us, length us, event | category | flops | bytes accessed | tf_op | source)
XLA Modules:
  0.0 163.6 jit_solution(1959455015401589925)
XLA Ops:
  0.6 1.0 copy.86
  1.7 3.8 %collective-permute-start.4 = (f32[8,8,1,128]{3,0,2,1:T(8,128)S(1)}, f32[8,8,1,128]{3,0,2,1:T(8,128)S(1)}, u32[]{:S(2)}, u32[]{:S(2)}) collective-permute-start(f32[8,8,1,128]{3,0,2,1:T(8,128)S(1)} %get-tuple-element.22), channel_id=1, source_target_pairs={{0,8},{8,16},{16,24},{24,32},{32,40},{40,48},{48,56},{56,64},{64,7... | collective-permute-start | bytes 98312 | tf_op jit(solution)/shard_map/ppermute | solution.py:12
  5.5 1.3 collective-permute-start.5
  6.8 6.5 %all_gather.10 = f32[32,8,4,128]{3,0,2,1:T(8,128)S(1)} all-gather(f32[8,8,4,128]{3,0,2,1:T(8,128)S(1)} %copy.86), channel_id=1, replica_groups=mesh['col'=4,'gx'=16,'gy'=8] {'col'}, dimensions={0}, use_global_device_ids=true | all-gather | bytes 655360 | tf_op jit(solution)/shard_map/all_gather | solution.py:66
  13.3 1.0 copy.85
  14.3 7.3 %all_gather.9 = f32[32,8,4,128]{3,0,2,1:T(8,128)S(1)} all-gather(f32[8,8,4,128]{3,0,2,1:T(8,128)S(1)} %copy.85), channel_id=1, replica_groups=mesh['col'=4,'gx'=16,'gy'=8] {'col'}, dimensions={0}, use_global_device_ids=true | all-gather | bytes 655360 | tf_op jit(solution)/shard_map/all_gather | solution.py:65
  21.7 4.6 %collective-permute-start = (f32[2,32,8,1,128]{4,1,3,2,0:T(8,128)S(1)}, f32[2,32,8,1,128]{4,1,3,2,0:T(8,128)S(1)}, u32[]{:S(2)}, u32[]{:S(2)}) collective-permute-start(f32[2,32,8,1,128]{4,1,3,2,0:T(8,128)S(1)} %get-tuple-element.17), channel_id=1, source_target_pairs={{0,8},{8,16},{16,24},{24,32},{32,40},{40,48},{48,56},{56,64},{64,7... | collective-permute-start | bytes 786440 | tf_op jit(solution)/shard_map/ppermute | solution.py:12
  26.2 1.3 collective-permute-start.1
  27.8 6.8 %all_gather.11 = f32[32,32,3,3,3]{1,0,4,3,2:T(8,128)S(1)} all-gather(f32[8,32,3,3,3]{1,0,4,3,2:T(8,128)} %param.6), channel_id=1, replica_groups=mesh['col'=4,'gx'=16,'gy'=8] {'col'}, dimensions={0}, use_global_device_ids=true | all-gather | bytes 138240 | tf_op jit(solution)/shard_map/all_gather | solution.py:67
  35.0 3.5 %collective-permute-start.6 = (f32[8,8,6,1]{3,0,2,1:T(8,128)S(1)}, f32[8,8,6,1]{3,0,2,1:T(8,128)S(1)}, u32[]{:S(2)}, u32[]{:S(2)}) collective-permute-start(f32[8,8,6,1]{3,0,2,1:T(8,128)S(1)} %get-tuple-element.19), channel_id=1, source_target_pairs={{0,1},{1,2},{2,3},{3,4},{4,5},{5,6},{6,7},{8,9},{9,10},{10,11},{11... | collective-permute-start | bytes 4616 | tf_op jit(solution)/shard_map/ppermute | solution.py:12
  38.5 6.0 %collective-permute-start.7 = (f32[8,8,6,1]{3,0,2,1:T(8,128)S(1)}, f32[8,8,6,1]{3,0,2,1:T(8,128)S(1)}, u32[]{:S(2)}, u32[]{:S(2)}) collective-permute-start(f32[8,8,6,1]{3,0,2,1:T(8,128)S(1)} %get-tuple-element.20), channel_id=1, source_target_pairs={{1,0},{2,1},{3,2},{4,3},{5,4},{6,5},{7,6},{9,8},{10,9},{11,10},{12... | collective-permute-start | bytes 4616 | tf_op jit(solution)/shard_map/ppermute | solution.py:15
  44.5 3.2 %collective-permute-done.6 = f32[8,8,6,1]{3,0,2,1:T(8,128)S(1)} collective-permute-done((f32[8,8,6,1]{3,0,2,1:T(8,128)S(1)}, f32[8,8,6,1]{3,0,2,1:T(8,128)S(1)}, u32[]{:S(2)}, u32[]{:S(2)}) %collective-permute-start.6) | collective-permute-done | bytes 1568 | tf_op jit(solution)/shard_map/ppermute | solution.py:12
  47.7 1.2 collective-permute-done.7
  51.3 1.5 convolution_bitcast_fusion.2
  53.1 4.4 %collective-permute-start.8 = (f32[54,128]{1,0:T(8,128)S(1)}, f32[54,128]{1,0:T(8,128)S(1)}, u32[]{:S(2)}, u32[]{:S(2)}) collective-permute-start(f32[54,128]{1,0:T(8,128)S(1)} %reshape_reshape.3), channel_id=1, source_target_pairs={{0,8},{8,16},{16,24},{24,0},{32,40},{40,48},{48,56},{56,32},{64,72... | collective-permute-start | bytes 82952 | tf_op jit(solution)/shard_map/ppermute | solution.py:35
  57.6 7.6 %collective-permute-start.9 = (f32[54,128]{1,0:T(8,128)S(1)}, f32[54,128]{1,0:T(8,128)S(1)}, u32[]{:S(2)}, u32[]{:S(2)}) collective-permute-start(f32[54,128]{1,0:T(8,128)S(1)} %reshape_reshape.3), channel_id=1, source_target_pairs={{0,16},{8,24},{16,0},{24,8},{32,48},{40,56},{48,32},{56,40},{64,80... | collective-permute-start | bytes 82952 | tf_op jit(solution)/shard_map/ppermute | solution.py:35
  65.2 1.9 %collective-permute-start.10 = (f32[54,128]{1,0:T(8,128)S(1)}, f32[54,128]{1,0:T(8,128)S(1)}, u32[]{:S(2)}, u32[]{:S(2)}) collective-permute-start(f32[54,128]{1,0:T(8,128)S(1)} %reshape_reshape.3), channel_id=1, source_target_pairs={{0,24},{8,0},{16,8},{24,16},{32,56},{40,32},{48,40},{56,48},{64,88... | collective-permute-start | bytes 82952 | tf_op jit(solution)/shard_map/ppermute | solution.py:35
  67.5 3.4 %collective-permute-done.10 = f32[54,128]{1,0:T(8,128)S(1)} collective-permute-done((f32[54,128]{1,0:T(8,128)S(1)}, f32[54,128]{1,0:T(8,128)S(1)}, u32[]{:S(2)}, u32[]{:S(2)}) %collective-permute-start.10) | collective-permute-done | bytes 27680 | tf_op jit(solution)/shard_map/ppermute | solution.py:35
  71.0 0.6 gather_fusion.1
  71.6 9.1 %collective-permute-start.11 = (f32[54,128]{1,0:T(8,128)S(1)}, f32[54,128]{1,0:T(8,128)S(1)}, u32[]{:S(2)}, u32[]{:S(2)}) collective-permute-start(f32[54,128]{1,0:T(8,128)S(1)} %fusion.89), channel_id=1, source_target_pairs={{0,32},{8,40},{16,48},{24,56},{32,64},{40,72},{48,80},{56,88},{64,... | collective-permute-start | bytes 82952 | tf_op jit(solution)/shard_map/ppermute | solution.py:35
  80.7 8.1 %collective-permute-start.12 = (f32[54,128]{1,0:T(8,128)S(1)}, f32[54,128]{1,0:T(8,128)S(1)}, u32[]{:S(2)}, u32[]{:S(2)}) collective-permute-start(f32[54,128]{1,0:T(8,128)S(1)} %fusion.89), channel_id=1, source_target_pairs={{0,64},{8,72},{16,80},{24,88},{32,96},{40,104},{48,112},{56,120},{... | collective-permute-start | bytes 82952 | tf_op jit(solution)/shard_map/ppermute | solution.py:35
  88.8 5.5 %collective-permute-start.13 = (f32[54,128]{1,0:T(8,128)S(1)}, f32[54,128]{1,0:T(8,128)S(1)}, u32[]{:S(2)}, u32[]{:S(2)}) collective-permute-start(f32[54,128]{1,0:T(8,128)S(1)} %fusion.89), channel_id=1, source_target_pairs={{0,96},{8,104},{16,112},{24,120},{32,0},{40,8},{48,16},{56,24},{64... | collective-permute-start | bytes 82952 | tf_op jit(solution)/shard_map/ppermute | solution.py:35
  94.3 0.9 collective-permute-done.12
  95.2 3.3 %collective-permute-done.13 = f32[54,128]{1,0:T(8,128)S(1)} collective-permute-done((f32[54,128]{1,0:T(8,128)S(1)}, f32[54,128]{1,0:T(8,128)S(1)}, u32[]{:S(2)}, u32[]{:S(2)}) %collective-permute-start.13) | collective-permute-done | bytes 27680 | tf_op jit(solution)/shard_map/ppermute | solution.py:35
  98.5 0.6 gather_fusion.2
  99.1 1.9 %collective-permute-start.14 = (f32[54,128]{1,0:T(8,128)S(1)}, f32[54,128]{1,0:T(8,128)S(1)}, u32[]{:S(2)}, u32[]{:S(2)}) collective-permute-start(f32[54,128]{1,0:T(8,128)S(1)} %fusion.88), channel_id=1, source_target_pairs={{0,1},{1,2},{2,3},{3,0},{4,5},{5,6},{6,7},{7,4},{8,9},{9,10},{10,1... | collective-permute-start | bytes 82952 | tf_op jit(solution)/shard_map/ppermute | solution.py:35
  101.1 3.2 %collective-permute-start.15 = (f32[54,128]{1,0:T(8,128)S(1)}, f32[54,128]{1,0:T(8,128)S(1)}, u32[]{:S(2)}, u32[]{:S(2)}) collective-permute-start(f32[54,128]{1,0:T(8,128)S(1)} %fusion.88), channel_id=1, source_target_pairs={{0,2},{1,3},{2,0},{3,1},{4,6},{5,7},{6,4},{7,5},{8,10},{9,11},{10,... | collective-permute-start | bytes 82952 | tf_op jit(solution)/shard_map/ppermute | solution.py:35
  104.3 4.5 %collective-permute-start.16 = (f32[54,128]{1,0:T(8,128)S(1)}, f32[54,128]{1,0:T(8,128)S(1)}, u32[]{:S(2)}, u32[]{:S(2)}) collective-permute-start(f32[54,128]{1,0:T(8,128)S(1)} %fusion.88), channel_id=1, source_target_pairs={{0,3},{1,0},{2,1},{3,2},{4,7},{5,4},{6,5},{7,6},{8,11},{9,8},{10,9... | collective-permute-start | bytes 82952 | tf_op jit(solution)/shard_map/ppermute | solution.py:35
  108.9 1.9 %collective-permute-done.16 = f32[54,128]{1,0:T(8,128)S(1)} collective-permute-done((f32[54,128]{1,0:T(8,128)S(1)}, f32[54,128]{1,0:T(8,128)S(1)}, u32[]{:S(2)}, u32[]{:S(2)}) %collective-permute-start.16) | collective-permute-done | bytes 27680 | tf_op jit(solution)/shard_map/ppermute | solution.py:35
  110.8 0.6 gather_fusion.3
  111.5 7.9 %collective-permute-start.17 = (f32[54,128]{1,0:T(8,128)S(1)}, f32[54,128]{1,0:T(8,128)S(1)}, u32[]{:S(2)}, u32[]{:S(2)}) collective-permute-start(f32[54,128]{1,0:T(8,128)S(1)} %fusion.87), channel_id=1, source_target_pairs={{0,4},{1,5},{2,6},{3,7},{4,0},{5,1},{6,2},{7,3},{8,12},{9,13},{10,... | collective-permute-start | bytes 82952 | tf_op jit(solution)/shard_map/ppermute | solution.py:35
  119.5 1.8 %collective-permute-done.17 = f32[54,128]{1,0:T(8,128)S(1)} collective-permute-done((f32[54,128]{1,0:T(8,128)S(1)}, f32[54,128]{1,0:T(8,128)S(1)}, u32[]{:S(2)}, u32[]{:S(2)}) %collective-permute-start.17) | collective-permute-done | bytes 27680 | tf_op jit(solution)/shard_map/ppermute | solution.py:35
  121.3 0.6 gather_fusion
  121.9 0.7 broadcast_select_fusion.3
  122.7 1.7 %fusion.79 = (f32[2,32,8,6,1]{4,1,3,2,0:T(8,128)}, f32[2,32,8,6,1]{4,1,3,2,0:T(8,128)S(1)}) fusion(f32[2,32,8,6,128]{4,1,3,2,0:T(8,128)S(1)} %pad_maximum_fusion), kind=kLoop, calls=%fused_computation.260 | loop fusion | bytes 49152 | tf_op jit(solution)/shard_map/slice | solution.py:13
  124.4 2.0 %copy.87 = f32[2,32,8,6,1]{1,2,4,3,0:T(8,128)S(1)} copy(f32[2,32,8,6,1]{4,1,3,2,0:T(8,128)} %get-tuple-element.15) | data formatting | bytes 24576 | tf_op jit(solution)/shard_map/slice | solution.py:13
  126.4 1.9 %collective-permute-start.2 = (f32[2,32,8,6,1]{1,2,4,3,0:T(8,128)S(1)}, f32[2,32,8,6,1]{1,2,4,3,0:T(8,128)S(1)}, u32[]{:S(2)}, u32[]{:S(2)}) collective-permute-start(f32[2,32,8,6,1]{1,2,4,3,0:T(8,128)S(1)} %copy.87), channel_id=1, source_target_pairs={{0,1},{1,2},{2,3},{3,4},{4,5},{5,6},{6,7},{8,9},{9,10},{10,11},{11... | collective-permute-start | bytes 36872 | tf_op jit(solution)/shard_map/ppermute | solution.py:12
  128.4 0.6 copy.88
  129.0 7.5 %collective-permute-start.3 = (f32[2,32,8,6,1]{1,2,4,3,0:T(8,128)S(1)}, f32[2,32,8,6,1]{1,2,4,3,0:T(8,128)S(1)}, u32[]{:S(2)}, u32[]{:S(2)}) collective-permute-start(f32[2,32,8,6,1]{1,2,4,3,0:T(8,128)S(1)} %copy.88), channel_id=1, source_target_pairs={{1,0},{2,1},{3,2},{4,3},{5,4},{6,5},{7,6},{9,8},{10,9},{11,10},{12... | collective-permute-start | bytes 36872 | tf_op jit(solution)/shard_map/ppermute | solution.py:15
  136.6 0.8 mul.15
  137.4 1.6 %copy.152 = f32[8,32,3,3,3]{1,0,4,3,2:T(8,128)} copy(f32[8,32,3,3,3]{4,3,2,1,0:T(4,128)S(1)} %mul.15) | data formatting | bytes 55296
  139.1 0.6 copy.89
  139.7 1.8 %copy.90 = f32[2,32,8,6,1]{4,1,3,2,0:T(8,128)} copy(f32[2,32,8,6,1]{1,2,4,3,0:T(8,128)S(1)} %collective-permute-done.3) | data formatting | bytes 24576 | tf_op jit(solution)/shard_map/ppermute | solution.py:15
  141.5 3.5 %select_maximum_fusion = f32[2,32,10,6,130]{4,1,3,2,0:T(8,128)S(1)} fusion(f32[2,32,8,6,1]{4,1,3,2,0:T(8,128)} %copy.90, f32[2,32,8,6,1]{4,1,3,2,0:T(8,128)S(1)} %copy.89, f32[2,32,8,1,128]{4,1,3,2,0:T(8,128)S(1)} %collective-permute-done.1, f32[2,32,8,1,128]{4,1,3,2,0:T(8,128)S(1)} %collective-permute-done, f32[1,32,8,4,128]{4,1,3,2,0:T(8,128)S(1)} %bitcast.491, ...), kind=kLoop, calls=%fused_computation.6 | loop fusion | flops 6988800 | bytes 3594240 | tf_op jit(solution)/shard_map/concatenate | solution.py:16
  149.6 5.0 %convolution_bitcast_fusion = f32[8,8,4,128]{3,0,2,1:T(8,128)S(1)} fusion(f32[32,27,8,1,1]{0,2,4,3,1:T(8,128)S(1)} %bitcast.493, f32[27,32,8,4,128]{4,1,3,2,0:T(8,128)S(1)} %fusion.1), kind=kOutput, calls=%fused_computation.15 | convolution fusion | flops 169869312 | bytes 14314496 | tf_op jit(solution)/shard_map/okc,kopqy->cpqy/dot_general | solution.py:89
  154.7 0.7 copy.151
  159.5 3.4 %convolution_bitcast_fusion.1 = f32[8,8,4,128]{3,0,2,1:T(8,128)S(1)} fusion(f32[27,32,8,4,128]{4,1,0,3,2:T(8,128)S(1)} %fusion.28, f32[8,27,32,1,1]{2,0,1,4,3:T(8,128)S(1)} %bitcast.492), kind=kOutput, calls=%fused_computation.16 | convolution fusion | flops 169869312 | bytes 14314496 | tf_op jit(solution)/shard_map/okc,kcpqy->opqy/dot_general | solution.py:84
  162.9 0.7 copy.150
  (138 shorter events, 12.5 us)
Async XLA Ops:
  0.6 34.1 %copy-start = (f32[8,8,4,128]{3,2,1,0:T(4,128)S(1)}, f32[8,8,4,128]{3,2,1,0:T(4,128)}, u32[]{:S(2)}) copy-start(f32[8,8,4,128]{3,2,1,0:T(4,128)} %param.7) | copy-start | bytes 393220
  1.7 33.0 %collective-permute-start.4 = (f32[8,8,1,128]{3,0,2,1:T(8,128)S(1)}, f32[8,8,1,128]{3,0,2,1:T(8,128)S(1)}, u32[]{:S(2)}, u32[]{:S(2)}) collective-permute-start(f32[8,8,1,128]{3,0,2,1:T(8,128)S(1)} %get-tuple-element.22), channel_id=1, source_target_pairs={{0,8},{8,16},{16,24},{24,32},{32,40},{40,48},{48,56},{56,64},{64,7... | collective-permute-start | bytes 98312 | tf_op jit(solution)/shard_map/ppermute | solution.py:12
  5.5 29.3 %collective-permute-start.5 = (f32[8,8,1,128]{3,0,2,1:T(8,128)S(1)}, f32[8,8,1,128]{3,0,2,1:T(8,128)S(1)}, u32[]{:S(2)}, u32[]{:S(2)}) collective-permute-start(f32[8,8,1,128]{3,0,2,1:T(8,128)S(1)} %get-tuple-element.21), channel_id=1, source_target_pairs={{8,0},{16,8},{24,16},{32,24},{40,32},{48,40},{56,48},{64,56},{72,6... | collective-permute-start | bytes 98312 | tf_op jit(solution)/shard_map/ppermute | solution.py:15
  21.7 100.9 %collective-permute-start = (f32[2,32,8,1,128]{4,1,3,2,0:T(8,128)S(1)}, f32[2,32,8,1,128]{4,1,3,2,0:T(8,128)S(1)}, u32[]{:S(2)}, u32[]{:S(2)}) collective-permute-start(f32[2,32,8,1,128]{4,1,3,2,0:T(8,128)S(1)} %get-tuple-element.17), channel_id=1, source_target_pairs={{0,8},{8,16},{16,24},{24,32},{32,40},{40,48},{48,56},{56,64},{64,7... | collective-permute-start | bytes 786440 | tf_op jit(solution)/shard_map/ppermute | solution.py:12
  26.2 96.3 %collective-permute-start.1 = (f32[2,32,8,1,128]{4,1,3,2,0:T(8,128)S(1)}, f32[2,32,8,1,128]{4,1,3,2,0:T(8,128)S(1)}, u32[]{:S(2)}, u32[]{:S(2)}) collective-permute-start(f32[2,32,8,1,128]{4,1,3,2,0:T(8,128)S(1)} %get-tuple-element.18), channel_id=1, source_target_pairs={{8,0},{16,8},{24,16},{32,24},{40,32},{48,40},{56,48},{64,56},{72,6... | collective-permute-start | bytes 786440 | tf_op jit(solution)/shard_map/ppermute | solution.py:15
  35.0 12.7 %collective-permute-start.6 = (f32[8,8,6,1]{3,0,2,1:T(8,128)S(1)}, f32[8,8,6,1]{3,0,2,1:T(8,128)S(1)}, u32[]{:S(2)}, u32[]{:S(2)}) collective-permute-start(f32[8,8,6,1]{3,0,2,1:T(8,128)S(1)} %get-tuple-element.19), channel_id=1, source_target_pairs={{0,1},{1,2},{2,3},{3,4},{4,5},{5,6},{6,7},{8,9},{9,10},{10,11},{11... | collective-permute-start | bytes 4616 | tf_op jit(solution)/shard_map/ppermute | solution.py:12
  38.5 10.3 %collective-permute-start.7 = (f32[8,8,6,1]{3,0,2,1:T(8,128)S(1)}, f32[8,8,6,1]{3,0,2,1:T(8,128)S(1)}, u32[]{:S(2)}, u32[]{:S(2)}) collective-permute-start(f32[8,8,6,1]{3,0,2,1:T(8,128)S(1)} %get-tuple-element.20), channel_id=1, source_target_pairs={{1,0},{2,1},{3,2},{4,3},{5,4},{6,5},{7,6},{9,8},{10,9},{11,10},{12... | collective-permute-start | bytes 4616 | tf_op jit(solution)/shard_map/ppermute | solution.py:15
  53.1 14.4 %collective-permute-start.8 = (f32[54,128]{1,0:T(8,128)S(1)}, f32[54,128]{1,0:T(8,128)S(1)}, u32[]{:S(2)}, u32[]{:S(2)}) collective-permute-start(f32[54,128]{1,0:T(8,128)S(1)} %reshape_reshape.3), channel_id=1, source_target_pairs={{0,8},{8,16},{16,24},{24,0},{32,40},{40,48},{48,56},{56,32},{64,72... | collective-permute-start | bytes 82952 | tf_op jit(solution)/shard_map/ppermute | solution.py:35
  57.6 10.0 %collective-permute-start.9 = (f32[54,128]{1,0:T(8,128)S(1)}, f32[54,128]{1,0:T(8,128)S(1)}, u32[]{:S(2)}, u32[]{:S(2)}) collective-permute-start(f32[54,128]{1,0:T(8,128)S(1)} %reshape_reshape.3), channel_id=1, source_target_pairs={{0,16},{8,24},{16,0},{24,8},{32,48},{40,56},{48,32},{56,40},{64,80... | collective-permute-start | bytes 82952 | tf_op jit(solution)/shard_map/ppermute | solution.py:35
  65.2 5.8 %collective-permute-start.10 = (f32[54,128]{1,0:T(8,128)S(1)}, f32[54,128]{1,0:T(8,128)S(1)}, u32[]{:S(2)}, u32[]{:S(2)}) collective-permute-start(f32[54,128]{1,0:T(8,128)S(1)} %reshape_reshape.3), channel_id=1, source_target_pairs={{0,24},{8,0},{16,8},{24,16},{32,56},{40,32},{48,40},{56,48},{64,88... | collective-permute-start | bytes 82952 | tf_op jit(solution)/shard_map/ppermute | solution.py:35
  71.6 22.7 %collective-permute-start.11 = (f32[54,128]{1,0:T(8,128)S(1)}, f32[54,128]{1,0:T(8,128)S(1)}, u32[]{:S(2)}, u32[]{:S(2)}) collective-permute-start(f32[54,128]{1,0:T(8,128)S(1)} %fusion.89), channel_id=1, source_target_pairs={{0,32},{8,40},{16,48},{24,56},{32,64},{40,72},{48,80},{56,88},{64,... | collective-permute-start | bytes 82952 | tf_op jit(solution)/shard_map/ppermute | solution.py:35
  80.7 14.5 %collective-permute-start.12 = (f32[54,128]{1,0:T(8,128)S(1)}, f32[54,128]{1,0:T(8,128)S(1)}, u32[]{:S(2)}, u32[]{:S(2)}) collective-permute-start(f32[54,128]{1,0:T(8,128)S(1)} %fusion.89), channel_id=1, source_target_pairs={{0,64},{8,72},{16,80},{24,88},{32,96},{40,104},{48,112},{56,120},{... | collective-permute-start | bytes 82952 | tf_op jit(solution)/shard_map/ppermute | solution.py:35
  88.8 9.7 %collective-permute-start.13 = (f32[54,128]{1,0:T(8,128)S(1)}, f32[54,128]{1,0:T(8,128)S(1)}, u32[]{:S(2)}, u32[]{:S(2)}) collective-permute-start(f32[54,128]{1,0:T(8,128)S(1)} %fusion.89), channel_id=1, source_target_pairs={{0,96},{8,104},{16,112},{24,120},{32,0},{40,8},{48,16},{56,24},{64... | collective-permute-start | bytes 82952 | tf_op jit(solution)/shard_map/ppermute | solution.py:35
  99.1 9.7 %collective-permute-start.14 = (f32[54,128]{1,0:T(8,128)S(1)}, f32[54,128]{1,0:T(8,128)S(1)}, u32[]{:S(2)}, u32[]{:S(2)}) collective-permute-start(f32[54,128]{1,0:T(8,128)S(1)} %fusion.88), channel_id=1, source_target_pairs={{0,1},{1,2},{2,3},{3,0},{4,5},{5,6},{6,7},{7,4},{8,9},{9,10},{10,1... | collective-permute-start | bytes 82952 | tf_op jit(solution)/shard_map/ppermute | solution.py:35
  101.1 7.8 %collective-permute-start.15 = (f32[54,128]{1,0:T(8,128)S(1)}, f32[54,128]{1,0:T(8,128)S(1)}, u32[]{:S(2)}, u32[]{:S(2)}) collective-permute-start(f32[54,128]{1,0:T(8,128)S(1)} %fusion.88), channel_id=1, source_target_pairs={{0,2},{1,3},{2,0},{3,1},{4,6},{5,7},{6,4},{7,5},{8,10},{9,11},{10,... | collective-permute-start | bytes 82952 | tf_op jit(solution)/shard_map/ppermute | solution.py:35
  104.3 6.5 %collective-permute-start.16 = (f32[54,128]{1,0:T(8,128)S(1)}, f32[54,128]{1,0:T(8,128)S(1)}, u32[]{:S(2)}, u32[]{:S(2)}) collective-permute-start(f32[54,128]{1,0:T(8,128)S(1)} %fusion.88), channel_id=1, source_target_pairs={{0,3},{1,0},{2,1},{3,2},{4,7},{5,4},{6,5},{7,6},{8,11},{9,8},{10,9... | collective-permute-start | bytes 82952 | tf_op jit(solution)/shard_map/ppermute | solution.py:35
  111.5 9.8 %collective-permute-start.17 = (f32[54,128]{1,0:T(8,128)S(1)}, f32[54,128]{1,0:T(8,128)S(1)}, u32[]{:S(2)}, u32[]{:S(2)}) collective-permute-start(f32[54,128]{1,0:T(8,128)S(1)} %fusion.87), channel_id=1, source_target_pairs={{0,4},{1,5},{2,6},{3,7},{4,0},{5,1},{6,2},{7,3},{8,12},{9,13},{10,... | collective-permute-start | bytes 82952 | tf_op jit(solution)/shard_map/ppermute | solution.py:35
  122.7 13.9 %copy-start.2 = (f32[2,54,128]{2,1,0:T(8,128)S(1)}, f32[2,54,128]{2,1,0:T(8,128)}, u32[]{:S(2)}) copy-start(f32[2,54,128]{2,1,0:T(8,128)} %broadcast_select_fusion.3) | copy-start | bytes 165892
  126.4 12.6 %collective-permute-start.2 = (f32[2,32,8,6,1]{1,2,4,3,0:T(8,128)S(1)}, f32[2,32,8,6,1]{1,2,4,3,0:T(8,128)S(1)}, u32[]{:S(2)}, u32[]{:S(2)}) collective-permute-start(f32[2,32,8,6,1]{1,2,4,3,0:T(8,128)S(1)} %copy.87), channel_id=1, source_target_pairs={{0,1},{1,2},{2,3},{3,4},{4,5},{5,6},{6,7},{8,9},{9,10},{10,11},{11... | collective-permute-start | bytes 36872 | tf_op jit(solution)/shard_map/ppermute | solution.py:12
  129.0 10.7 %collective-permute-start.3 = (f32[2,32,8,6,1]{1,2,4,3,0:T(8,128)S(1)}, f32[2,32,8,6,1]{1,2,4,3,0:T(8,128)S(1)}, u32[]{:S(2)}, u32[]{:S(2)}) collective-permute-start(f32[2,32,8,6,1]{1,2,4,3,0:T(8,128)S(1)} %copy.88), channel_id=1, source_target_pairs={{1,0},{2,1},{3,2},{4,3},{5,4},{6,5},{7,6},{9,8},{10,9},{11,10},{12... | collective-permute-start | bytes 36872 | tf_op jit(solution)/shard_map/ppermute | solution.py:15
  158.4 1.1 copy-start.1

commit v11 on v10

--- a/solution.py
+++ b/solution.py
@@ -57,18 +57,23 @@
     return jnp.stack(windows, axis=0)
 
 
+def scatter_sum(blocks, axis):
+    count = lax.axis_size(axis)
+    index = lax.axis_index(axis)
+    blocks = blocks.reshape((count, blocks.shape[0] // count) + blocks.shape[1:])
+    total = blocks[index]
+    for shift in range(1, count):
+        piece = blocks[(index + shift) % count]
+        pairs = [(i, (i + shift) % count) for i in range(count)]
+        total = total + lax.ppermute(piece, axis, pairs)
+    return total
+
+
 def shards(volume, filters, upstream):
     channels, planes, rows_x, rows_y = volume.shape
-    own_inputs = channels
-    ncol = lax.axis_size("col")
     scale = (planes * rows_x * lax.axis_size("gx") * rows_y * lax.axis_size("gy")) ** (-0.5)
     gathered = lax.all_gather(volume, "col", axis=0, tiled=True)
-    fields = jnp.stack([gathered, lax.all_gather(upstream, "col", axis=0, tiled=True)])
-    all_rows = lax.all_gather(filters, "col", axis=0, tiled=True)
-    both = with_halo(fields, (("gx", 3), ("gy", 4)), 1)
-    both = jnp.pad(both, ((0, 0), (0, 0), (1, 1), (0, 0), (0, 0)))
-    padded, padded_up = both[0], both[1]
-    taps = patches(padded, planes, rows_x, rows_y, False)
+    padded = pad_depth(with_halo(gathered, (("gx", 2), ("gy", 3)), 1))
     own_up = pad_depth(with_halo(upstream, (("gx", 2), ("gy", 3)), 1))
     shifted_up = patches(own_up, planes, rows_x, rows_y, True)
     local_grad = jnp.einsum("kopqy,cpqy->ock", shifted_up, gathered, precision=lax.Precision.HIGH)
@@ -80,13 +85,11 @@
     else:
         flat = lax.psum(flat, ("gx", "gy"))
     total_grad = flat.reshape(local_grad.shape)
+    taps = patches(padded, planes, rows_x, rows_y, False)
     by_tap = jnp.swapaxes(filters.reshape(filters.shape[0], filters.shape[1], 27), 1, 2)
     response = jnp.einsum("okc,kcpqy->opqy", by_tap, taps, precision=lax.Precision.HIGH)
-    first = lax.axis_index("col") * own_inputs
-    own_filters = lax.dynamic_slice_in_dim(all_rows, first, own_inputs, 1)
-    own_by_tap = jnp.swapaxes(own_filters.reshape(own_filters.shape[0], own_inputs, 27), 1, 2)
-    taps_up = patches(padded_up, planes, rows_x, rows_y, True)
-    input_grad = jnp.einsum("okc,kopqy->cpqy", own_by_tap, taps_up, precision=lax.Precision.HIGH)
+    partial = jnp.einsum("okc,kopqy->cpqy", by_tap, shifted_up, precision=lax.Precision.HIGH)
+    input_grad = scatter_sum(partial, "col")
     return (response, input_grad, total_grad * scale)
 
 

time: 166 us -> 160 us (0.964)
  blocking collectives: 20.6 us -> 6.77 us
  starting transfers between devices: 84.1 us -> 76.6 us
  local copies, waits for them, and re-layouts: 25.9 us -> 31.9 us
  other arithmetic: 5.78 us -> 11.1 us
  waiting for transfers between devices: 15.7 us -> 18.6 us
    all_gather x2 -> x0, blocking collectives: 13.3 us -> none  [the longest x1 6.77 us: shards(): all_rows = lax.all_gather(filters, 'col', axis=0, tiled=True)]
    another operation x3 -> x2, local copies, waits for them, and re-layouts: 0.26 us -> 11.1 us  [patches(): return jnp.stack(windows, axis=0)]
    ppermute x10, starting transfers between devices: 54.2 us -> 45.4 us  [butterfly_sum(): received.append(lax.ppermute(value, axis, pairs))]
    ppermute x4, waiting for transfers between devices: 3.18 us -> 11.9 us  [with_halo(): lax.ppermute(lax.slice_in_dim(block, block.shape[dim] - width, None, axis...]
    ppermute x10, waiting for transfers between devices: 11.4 us -> 4.87 us  [butterfly_sum(): received.append(lax.ppermute(value, axis, pairs))]
    ppermute x0 -> x3, starting transfers between devices: none -> 6.06 us  [scatter_sum(): total = total + lax.ppermute(piece, axis, pairs)]
    unnamed x83 -> x32, local copies, waits for them, and re-layouts: 14.2 us -> 8.79 us
    ppermute x4, starting transfers between devices: 16.1 us -> 11.5 us  [with_halo(): lax.ppermute(lax.slice_in_dim(block, 0, width, axis=dim), axis, backward)]
  transfers between devices with their start and end apart: 18 -> 21, of which waited for: 7 -> 6; matrix products, arithmetic and copies ran while one was open for 8% -> 33% of each run, Pallas kernels for 0% -> 0%
where the time goes in v11:
time: 160 us; the launch traced here: 157 us
  starting transfers between devices  76.6 us (48%)
  local copies, waits for them, and re-layouts  31.9 us (20%)
  waiting for transfers between devices  18.6 us (12%)
  other arithmetic  11.1 us (7%)
  matrix products  10.9 us (7%)
  blocking collectives  6.77 us (4%)
    ppermute x10, starting transfers between devices, butterfly_sum(): received.append(lax.ppermute(value, axis, pairs))  45.4 us
    ppermute x4, starting transfers between devices, with_halo(): lax.ppermute(lax.slice_in_dim(block, block.shape[dim] - width, None, axis...  13.6 us
    ppermute x4, waiting for transfers between devices, with_halo(): lax.ppermute(lax.slice_in_dim(block, block.shape[dim] - width, None, axis...  11.9 us
    ppermute x4, starting transfers between devices, with_halo(): lax.ppermute(lax.slice_in_dim(block, 0, width, axis=dim), axis, backward)  11.5 us
    another operation x2, local copies, waits for them, and re-layouts, patches(): return jnp.stack(windows, axis=0)  11.1 us
    unnamed x32, local copies, waits for them, and re-layouts  8.79 us
    all_gather x1, blocking collectives, shards(): gathered = lax.all_gather(volume, 'col', axis=0, tiled=True)  6.77 us
    ppermute x3, starting transfers between devices, scatter_sum(): total = total + lax.ppermute(piece, axis, pairs)  6.06 us
  transfers between devices with their start and end apart: 21, of which 6 were waited for; matrix products, arithmetic and copies ran while one was open for 33% of the time, Pallas kernels for 0%

profile of v11, /device:TPU:6, one launch (start us, length us, event | category | flops | bytes accessed | tf_op | source)
XLA Modules:
  0.0 157.2 jit_solution(18272899664904424480)
XLA Ops:
  0.6 1.0 copy.137
  1.6 6.8 %all_gather.3 = f32[32,8,4,128]{3,0,2,1:T(8,128)S(1)} all-gather(f32[8,8,4,128]{3,0,2,1:T(8,128)S(1)} %copy.137), channel_id=1, replica_groups=mesh['col'=4,'gx'=16,'gy'=8] {'col'}, dimensions={0}, use_global_device_ids=true | all-gather | bytes 655360 | tf_op jit(solution)/shard_map/all_gather | solution.py:75
  8.4 0.7 fusion.59
  9.1 4.5 %collective-permute-start = (f32[32,8,1,128]{3,0,2,1:T(8,128)}, f32[32,8,1,128]{3,0,2,1:T(8,128)}, u32[]{:S(2)}, u32[]{:S(2)}) collective-permute-start(f32[32,8,1,128]{3,0,2,1:T(8,128)} %get-tuple-element.20), channel_id=1, source_target_pairs={{0,8},{8,16},{16,24},{24,32},{32,40},{40,48},{48,56},{56,64},{64,7... | collective-permute-start | bytes 393224 | tf_op jit(solution)/shard_map/ppermute | solution.py:12
  13.6 1.3 collective-permute-start.1
  14.9 1.0 copy.172
  15.9 4.5 %collective-permute-start.4 = (f32[8,8,1,128]{3,0,2,1:T(8,128)S(1)}, f32[8,8,1,128]{3,0,2,1:T(8,128)S(1)}, u32[]{:S(2)}, u32[]{:S(2)}) collective-permute-start(f32[8,8,1,128]{3,0,2,1:T(8,128)S(1)} %get-tuple-element.53), channel_id=1, source_target_pairs={{0,8},{8,16},{16,24},{24,32},{32,40},{40,48},{48,56},{56,64},{64,7... | collective-permute-start | bytes 98312 | tf_op jit(solution)/shard_map/ppermute | solution.py:12
  20.4 1.3 collective-permute-start.5
  23.6 1.7 %copy.170 = f32[8,32,27]{2,1,0:T(8,128)} copy(f32[8,32,27]{1,0,2:T(8,128)} %bitcast.330) | data formatting | bytes 55296 | tf_op jit(solution)/shard_map/reshape | solution.py:89
  25.2 1.0 constant_dynamic-update-slice_fusion.4
  26.4 5.8 %collective-permute-start.7 = (f32[8,8,6,1]{3,0,2,1:T(8,128)S(1)}, f32[8,8,6,1]{3,0,2,1:T(8,128)S(1)}, u32[]{:S(2)}, u32[]{:S(2)}) collective-permute-start(f32[8,8,6,1]{3,0,2,1:T(8,128)S(1)} %get-tuple-element.49), channel_id=1, source_target_pairs={{1,0},{2,1},{3,2},{4,3},{5,4},{6,5},{7,6},{9,8},{10,9},{11,10},{12... | collective-permute-start | bytes 4616 | tf_op jit(solution)/shard_map/ppermute | solution.py:15
  32.1 1.9 %collective-permute-start.6 = (f32[8,8,6,1]{3,0,2,1:T(8,128)S(1)}, f32[8,8,6,1]{3,0,2,1:T(8,128)S(1)}, u32[]{:S(2)}, u32[]{:S(2)}) collective-permute-start(f32[8,8,6,1]{3,0,2,1:T(8,128)S(1)} %get-tuple-element.48), channel_id=1, source_target_pairs={{0,1},{1,2},{2,3},{3,4},{4,5},{5,6},{6,7},{8,9},{9,10},{10,11},{11... | collective-permute-start | bytes 4616 | tf_op jit(solution)/shard_map/ppermute | solution.py:12
  34.1 1.8 %collective-permute-done.7 = f32[8,8,6,1]{3,0,2,1:T(8,128)S(1)} collective-permute-done((f32[8,8,6,1]{3,0,2,1:T(8,128)S(1)}, f32[8,8,6,1]{3,0,2,1:T(8,128)S(1)}, u32[]{:S(2)}, u32[]{:S(2)}) %collective-permute-start.7) | collective-permute-done | bytes 1568 | tf_op jit(solution)/shard_map/ppermute | solution.py:15
  35.9 7.7 %collective-permute-done.6 = f32[8,8,6,1]{3,0,2,1:T(8,128)S(1)} collective-permute-done((f32[8,8,6,1]{3,0,2,1:T(8,128)S(1)}, f32[8,8,6,1]{3,0,2,1:T(8,128)S(1)}, u32[]{:S(2)}, u32[]{:S(2)}) %collective-permute-start.6) | collective-permute-done | bytes 1568 | tf_op jit(solution)/shard_map/ppermute | solution.py:12
  44.4 1.2 pad_maximum_fusion.4
  45.6 10.9 %stack.268 = f32[27,8,8,4,128]{4,0,1,3,2:T(8,128)} concatenate(f32[1,8,8,4,128]{4,0,1,3,2:T(1,128)S(1)} %bitcast.323, f32[1,8,8,4,128]{4,0,1,3,2:T(1,128)S(1)} %bitcast.322, f32[1,8,8,4,128]{4,0,1,3,2:T(1,128)S(1)} %bitcast.321, f32[1,8,8,4,128]{4,0,1,3,2:T(1,128)S(1)} %bitcast.320, f32[1,8,8,4,128]{4,0,1,3,2:T(1,128)S(1)} %bitcast.319, f32[1,8,8,4,128]{4,0,1,3,2:T(1,128)S(1)} %bitcast.318, ...), dimensions={0} | concatenate | bytes 7077888 | tf_op jit(solution)/shard_map/stack | solution.py:57
  56.5 4.0 %convolution_bitcast_fusion.1 = f32[8,32,27]{1,2,0:T(8,128)S(1)} fusion(f32[27,8,8,4,128]{4,0,1,3,2:T(8,128)} %stack.268, f32[32,8,4,128]{3,0,2,1:T(8,128)S(1)} %all_gather.3), kind=kOutput, calls=%fused_computation.18 | convolution fusion | flops 169869312 | bytes 4090880 | tf_op jit(solution)/shard_map/kopqy,cpqy->ock/dot_general | solution.py:79
  60.8 9.2 %collective-permute-start.13 = (f32[54,128]{1,0:T(8,128)S(1)}, f32[54,128]{1,0:T(8,128)S(1)}, u32[]{:S(2)}, u32[]{:S(2)}) collective-permute-start(f32[54,128]{1,0:T(8,128)S(1)} %reshape_reshape.3), channel_id=1, source_target_pairs={{0,24},{8,0},{16,8},{24,16},{32,56},{40,32},{48,40},{56,48},{64,88... | collective-permute-start | bytes 82952 | tf_op jit(solution)/shard_map/ppermute | solution.py:35
  70.0 1.9 %collective-permute-start.12 = (f32[54,128]{1,0:T(8,128)S(1)}, f32[54,128]{1,0:T(8,128)S(1)}, u32[]{:S(2)}, u32[]{:S(2)}) collective-permute-start(f32[54,128]{1,0:T(8,128)S(1)} %reshape_reshape.3), channel_id=1, source_target_pairs={{0,16},{8,24},{16,0},{24,8},{32,48},{40,56},{48,32},{56,40},{64,80... | collective-permute-start | bytes 82952 | tf_op jit(solution)/shard_map/ppermute | solution.py:35
  71.9 2.5 %collective-permute-start.11 = (f32[54,128]{1,0:T(8,128)S(1)}, f32[54,128]{1,0:T(8,128)S(1)}, u32[]{:S(2)}, u32[]{:S(2)}) collective-permute-start(f32[54,128]{1,0:T(8,128)S(1)} %reshape_reshape.3), channel_id=1, source_target_pairs={{0,8},{8,16},{16,24},{24,0},{32,40},{40,48},{48,56},{56,32},{64,72... | collective-permute-start | bytes 82952 | tf_op jit(solution)/shard_map/ppermute | solution.py:35
  74.4 3.5 %convolution_bitcast_fusion = f32[4,8,8,4,128]{4,1,0,3,2:T(8,128)S(1)} fusion(f32[27,8,8,4,128]{4,0,1,3,2:T(8,128)} %stack.268, f32[8,32,27]{2,1,0:T(8,128)} %copy.170), kind=kOutput, calls=%fused_computation.17 | convolution fusion | flops 169869312 | bytes 4090880 | tf_op jit(solution)/shard_map/okc,kopqy->cpqy/dot_general | solution.py:91
  79.6 0.7 copy.224
  80.9 0.7 broadcast_select_fusion.2
  81.6 9.2 %collective-permute-start.16 = (f32[54,128]{1,0:T(8,128)S(1)}, f32[54,128]{1,0:T(8,128)S(1)}, u32[]{:S(2)}, u32[]{:S(2)}) collective-permute-start(f32[54,128]{1,0:T(8,128)S(1)} %fusion.69), channel_id=1, source_target_pairs={{0,96},{8,104},{16,112},{24,120},{32,0},{40,8},{48,16},{56,24},{64... | collective-permute-start | bytes 82952 | tf_op jit(solution)/shard_map/ppermute | solution.py:35
  90.8 7.2 %collective-permute-start.15 = (f32[54,128]{1,0:T(8,128)S(1)}, f32[54,128]{1,0:T(8,128)S(1)}, u32[]{:S(2)}, u32[]{:S(2)}) collective-permute-start(f32[54,128]{1,0:T(8,128)S(1)} %fusion.69), channel_id=1, source_target_pairs={{0,64},{8,72},{16,80},{24,88},{32,96},{40,104},{48,112},{56,120},{... | collective-permute-start | bytes 82952 | tf_op jit(solution)/shard_map/ppermute | solution.py:35
  98.0 5.5 %collective-permute-start.14 = (f32[54,128]{1,0:T(8,128)S(1)}, f32[54,128]{1,0:T(8,128)S(1)}, u32[]{:S(2)}, u32[]{:S(2)}) collective-permute-start(f32[54,128]{1,0:T(8,128)S(1)} %fusion.69), channel_id=1, source_target_pairs={{0,32},{8,40},{16,48},{24,56},{32,64},{40,72},{48,80},{56,88},{64,... | collective-permute-start | bytes 82952 | tf_op jit(solution)/shard_map/ppermute | solution.py:35
  103.6 1.7 %collective-permute-done.15 = f32[54,128]{1,0:T(8,128)S(1)} collective-permute-done((f32[54,128]{1,0:T(8,128)S(1)}, f32[54,128]{1,0:T(8,128)S(1)}, u32[]{:S(2)}, u32[]{:S(2)}) %collective-permute-start.15) | collective-permute-done | bytes 27680 | tf_op jit(solution)/shard_map/ppermute | solution.py:35
  105.3 2.9 %collective-permute-done.14 = f32[54,128]{1,0:T(8,128)S(1)} collective-permute-done((f32[54,128]{1,0:T(8,128)S(1)}, f32[54,128]{1,0:T(8,128)S(1)}, u32[]{:S(2)}, u32[]{:S(2)}) %collective-permute-start.14) | collective-permute-done | bytes 27680 | tf_op jit(solution)/shard_map/ppermute | solution.py:35
  109.4 1.9 %collective-permute-start.19 = (f32[54,128]{1,0:T(8,128)S(1)}, f32[54,128]{1,0:T(8,128)S(1)}, u32[]{:S(2)}, u32[]{:S(2)}) collective-permute-start(f32[54,128]{1,0:T(8,128)S(1)} %fusion.68), channel_id=1, source_target_pairs={{0,3},{1,0},{2,1},{3,2},{4,7},{5,4},{6,5},{7,6},{8,11},{9,8},{10,9... | collective-permute-start | bytes 82952 | tf_op jit(solution)/shard_map/ppermute | solution.py:35
  111.3 1.9 %collective-permute-start.18 = (f32[54,128]{1,0:T(8,128)S(1)}, f32[54,128]{1,0:T(8,128)S(1)}, u32[]{:S(2)}, u32[]{:S(2)}) collective-permute-start(f32[54,128]{1,0:T(8,128)S(1)} %fusion.68), channel_id=1, source_target_pairs={{0,2},{1,3},{2,0},{3,1},{4,6},{5,7},{6,4},{7,5},{8,10},{9,11},{10,... | collective-permute-start | bytes 82952 | tf_op jit(solution)/shard_map/ppermute | solution.py:35
  113.3 3.9 %collective-permute-start.17 = (f32[54,128]{1,0:T(8,128)S(1)}, f32[54,128]{1,0:T(8,128)S(1)}, u32[]{:S(2)}, u32[]{:S(2)}) collective-permute-start(f32[54,128]{1,0:T(8,128)S(1)} %fusion.68), channel_id=1, source_target_pairs={{0,1},{1,2},{2,3},{3,0},{4,5},{5,6},{6,7},{7,4},{8,9},{9,10},{10,1... | collective-permute-start | bytes 82952 | tf_op jit(solution)/shard_map/ppermute | solution.py:35
  117.2 1.9 %collective-permute-start.10 = (f32[8,8,4,128]{3,2,1,0:T(4,128)}, f32[8,8,4,128]{3,2,1,0:T(4,128)S(1)}, u32[]{:S(2)}, u32[]{:S(2)}) collective-permute-start(f32[8,8,4,128]{3,2,1,0:T(4,128)} %bitcast.300), channel_id=1, source_target_pairs={{0,384},{128,0},{256,128},{384,256},{1,385},{129,1},{257,129},{385... | collective-permute-start | bytes 393224 | tf_op jit(solution)/shard_map/ppermute | solution.py:68
  119.2 2.2 %collective-permute-start.9 = (f32[8,8,4,128]{3,2,1,0:T(4,128)}, f32[8,8,4,128]{3,2,1,0:T(4,128)S(1)}, u32[]{:S(2)}, u32[]{:S(2)}) collective-permute-start(f32[8,8,4,128]{3,2,1,0:T(4,128)} %bitcast.301), channel_id=1, source_target_pairs={{0,256},{128,384},{256,0},{384,128},{1,257},{129,385},{257,1},{385... | collective-permute-start | bytes 393224 | tf_op jit(solution)/shard_map/ppermute | solution.py:68
  121.7 1.9 %collective-permute-start.8 = (f32[8,8,4,128]{3,2,1,0:T(4,128)}, f32[8,8,4,128]{3,2,1,0:T(4,128)S(1)}, u32[]{:S(2)}, u32[]{:S(2)}) collective-permute-start(f32[8,8,4,128]{3,2,1,0:T(4,128)} %bitcast.302), channel_id=1, source_target_pairs={{0,128},{128,256},{256,384},{384,0},{1,129},{129,257},{257,385},{3... | collective-permute-start | bytes 393224 | tf_op jit(solution)/shard_map/ppermute | solution.py:68
  124.9 0.9 constant_dynamic-update-slice_fusion.2
  125.9 0.9 constant_dynamic-update-slice_fusion
  127.1 1.0 copy.139
  128.1 3.2 %collective-permute-start.3 = (f32[32,8,6,1]{0,1,3,2:T(8,128)}, f32[32,8,6,1]{0,1,3,2:T(8,128)S(1)}, u32[]{:S(2)}, u32[]{:S(2)}) collective-permute-start(f32[32,8,6,1]{0,1,3,2:T(8,128)} %copy.139), channel_id=1, source_target_pairs={{1,0},{2,1},{3,2},{4,3},{5,4},{6,5},{7,6},{9,8},{10,9},{11,10},{12... | collective-permute-start | bytes 18440 | tf_op jit(solution)/shard_map/ppermute | solution.py:15
  131.6 2.6 %collective-permute-start.2 = (f32[32,8,6,1]{0,1,3,2:T(8,128)S(1)}, f32[32,8,6,1]{0,1,3,2:T(8,128)S(1)}, u32[]{:S(2)}, u32[]{:S(2)}) collective-permute-start(f32[32,8,6,1]{0,1,3,2:T(8,128)S(1)} %copy.138), channel_id=1, source_target_pairs={{0,1},{1,2},{2,3},{3,4},{4,5},{5,6},{6,7},{8,9},{9,10},{10,11},{11... | collective-permute-start | bytes 18440 | tf_op jit(solution)/shard_map/ppermute | solution.py:12
  134.3 2.2 %collective-permute-start.20 = (f32[54,128]{1,0:T(8,128)}, f32[54,128]{1,0:T(8,128)}, u32[]{:S(2)}, u32[]{:S(2)}) collective-permute-start(f32[54,128]{1,0:T(8,128)} %fusion.67), channel_id=1, source_target_pairs={{0,4},{1,5},{2,6},{3,7},{4,0},{5,1},{6,2},{7,3},{8,12},{9,13},{10,... | collective-permute-start | bytes 82952 | tf_op jit(solution)/shard_map/ppermute | solution.py:35
  136.8 4.1 %collective-permute-done.2 = f32[32,8,6,1]{0,1,3,2:T(8,128)S(1)} collective-permute-done((f32[32,8,6,1]{0,1,3,2:T(8,128)S(1)}, f32[32,8,6,1]{0,1,3,2:T(8,128)S(1)}, u32[]{:S(2)}, u32[]{:S(2)}) %collective-permute-start.2) | collective-permute-done | bytes 6176 | tf_op jit(solution)/shard_map/ppermute | solution.py:12
  143.6 0.9 fusion.29
  145.7 0.9 fusion.25
  148.4 3.4 %convolution_bitcast_fusion.2 = f32[8,8,4,128]{3,0,2,1:T(8,128)S(1)} fusion(f32[27,32,8,4,128]{4,1,0,3,2:T(8,128)S(1)} %fusion.13, f32[8,27,32,1,1]{2,0,1,4,3:T(8,128)S(1)} %bitcast.331), kind=kOutput, calls=%fused_computation.19 | convolution fusion | flops 169869312 | bytes 14314496 | tf_op jit(solution)/shard_map/okc,kcpqy->opqy/dot_general | solution.py:90
  152.5 0.8 pad_maximum_fusion.11
  153.9 0.8 mul.11
  154.8 1.6 %copy.208 = f32[8,32,3,3,3]{1,0,4,3,2:T(8,128)} copy(f32[8,32,3,3,3]{4,3,2,1,0:T(4,128)S(1)} %mul.11) | data formatting | bytes 55296
  156.4 0.7 fusion.47
  (95 shorter events, 15.8 us)
Async XLA Ops:
  9.1 115.8 %collective-permute-start = (f32[32,8,1,128]{3,0,2,1:T(8,128)}, f32[32,8,1,128]{3,0,2,1:T(8,128)}, u32[]{:S(2)}, u32[]{:S(2)}) collective-permute-start(f32[32,8,1,128]{3,0,2,1:T(8,128)} %get-tuple-element.20), channel_id=1, source_target_pairs={{0,8},{8,16},{16,24},{24,32},{32,40},{40,48},{48,56},{56,64},{64,7... | collective-permute-start | bytes 393224 | tf_op jit(solution)/shard_map/ppermute | solution.py:12
  13.6 112.3 %collective-permute-start.1 = (f32[32,8,1,128]{3,0,2,1:T(8,128)}, f32[32,8,1,128]{3,0,2,1:T(8,128)}, u32[]{:S(2)}, u32[]{:S(2)}) collective-permute-start(f32[32,8,1,128]{3,0,2,1:T(8,128)} %get-tuple-element.19), channel_id=1, source_target_pairs={{8,0},{16,8},{24,16},{32,24},{40,32},{48,40},{56,48},{64,56},{72,6... | collective-permute-start | bytes 393224 | tf_op jit(solution)/shard_map/ppermute | solution.py:15
  15.9 9.3 %collective-permute-start.4 = (f32[8,8,1,128]{3,0,2,1:T(8,128)S(1)}, f32[8,8,1,128]{3,0,2,1:T(8,128)S(1)}, u32[]{:S(2)}, u32[]{:S(2)}) collective-permute-start(f32[8,8,1,128]{3,0,2,1:T(8,128)S(1)} %get-tuple-element.53), channel_id=1, source_target_pairs={{0,8},{8,16},{16,24},{24,32},{32,40},{40,48},{48,56},{56,64},{64,7... | collective-permute-start | bytes 98312 | tf_op jit(solution)/shard_map/ppermute | solution.py:12
  20.4 5.8 %collective-permute-start.5 = (f32[8,8,1,128]{3,0,2,1:T(8,128)S(1)}, f32[8,8,1,128]{3,0,2,1:T(8,128)S(1)}, u32[]{:S(2)}, u32[]{:S(2)}) collective-permute-start(f32[8,8,1,128]{3,0,2,1:T(8,128)S(1)} %get-tuple-element.52), channel_id=1, source_target_pairs={{8,0},{16,8},{24,16},{32,24},{40,32},{48,40},{56,48},{64,56},{72,6... | collective-permute-start | bytes 98312 | tf_op jit(solution)/shard_map/ppermute | solution.py:15
  26.4 9.6 %collective-permute-start.7 = (f32[8,8,6,1]{3,0,2,1:T(8,128)S(1)}, f32[8,8,6,1]{3,0,2,1:T(8,128)S(1)}, u32[]{:S(2)}, u32[]{:S(2)}) collective-permute-start(f32[8,8,6,1]{3,0,2,1:T(8,128)S(1)} %get-tuple-element.49), channel_id=1, source_target_pairs={{1,0},{2,1},{3,2},{4,3},{5,4},{6,5},{7,6},{9,8},{10,9},{11,10},{12... | collective-permute-start | bytes 4616 | tf_op jit(solution)/shard_map/ppermute | solution.py:15
  32.1 11.5 %collective-permute-start.6 = (f32[8,8,6,1]{3,0,2,1:T(8,128)S(1)}, f32[8,8,6,1]{3,0,2,1:T(8,128)S(1)}, u32[]{:S(2)}, u32[]{:S(2)}) collective-permute-start(f32[8,8,6,1]{3,0,2,1:T(8,128)S(1)} %get-tuple-element.48), channel_id=1, source_target_pairs={{0,1},{1,2},{2,3},{3,4},{4,5},{5,6},{6,7},{8,9},{9,10},{10,11},{11... | collective-permute-start | bytes 4616 | tf_op jit(solution)/shard_map/ppermute | solution.py:12
  56.5 67.7 %copy-start.1 = (pred[4]{0:T(512)(128)(4,1)S(1)}, pred[4]{0:T(512)(128)(4,1)}, u32[]{:S(2)}) copy-start(pred[4]{0:T(512)(128)(4,1)} %get-tuple-element.54) | copy-start | bytes 16
  60.8 19.5 %collective-permute-start.13 = (f32[54,128]{1,0:T(8,128)S(1)}, f32[54,128]{1,0:T(8,128)S(1)}, u32[]{:S(2)}, u32[]{:S(2)}) collective-permute-start(f32[54,128]{1,0:T(8,128)S(1)} %reshape_reshape.3), channel_id=1, source_target_pairs={{0,24},{8,0},{16,8},{24,16},{32,56},{40,32},{48,40},{56,48},{64,88... | collective-permute-start | bytes 82952 | tf_op jit(solution)/shard_map/ppermute | solution.py:35
  70.0 10.3 %collective-permute-start.12 = (f32[54,128]{1,0:T(8,128)S(1)}, f32[54,128]{1,0:T(8,128)S(1)}, u32[]{:S(2)}, u32[]{:S(2)}) collective-permute-start(f32[54,128]{1,0:T(8,128)S(1)} %reshape_reshape.3), channel_id=1, source_target_pairs={{0,16},{8,24},{16,0},{24,8},{32,48},{40,56},{48,32},{56,40},{64,80... | collective-permute-start | bytes 82952 | tf_op jit(solution)/shard_map/ppermute | solution.py:35
  71.9 8.4 %collective-permute-start.11 = (f32[54,128]{1,0:T(8,128)S(1)}, f32[54,128]{1,0:T(8,128)S(1)}, u32[]{:S(2)}, u32[]{:S(2)}) collective-permute-start(f32[54,128]{1,0:T(8,128)S(1)} %reshape_reshape.3), channel_id=1, source_target_pairs={{0,8},{8,16},{16,24},{24,0},{32,40},{40,48},{48,56},{56,32},{64,72... | collective-permute-start | bytes 82952 | tf_op jit(solution)/shard_map/ppermute | solution.py:35
  81.6 21.9 %collective-permute-start.16 = (f32[54,128]{1,0:T(8,128)S(1)}, f32[54,128]{1,0:T(8,128)S(1)}, u32[]{:S(2)}, u32[]{:S(2)}) collective-permute-start(f32[54,128]{1,0:T(8,128)S(1)} %fusion.69), channel_id=1, source_target_pairs={{0,96},{8,104},{16,112},{24,120},{32,0},{40,8},{48,16},{56,24},{64... | collective-permute-start | bytes 82952 | tf_op jit(solution)/shard_map/ppermute | solution.py:35
  90.8 14.5 %collective-permute-start.15 = (f32[54,128]{1,0:T(8,128)S(1)}, f32[54,128]{1,0:T(8,128)S(1)}, u32[]{:S(2)}, u32[]{:S(2)}) collective-permute-start(f32[54,128]{1,0:T(8,128)S(1)} %fusion.69), channel_id=1, source_target_pairs={{0,64},{8,72},{16,80},{24,88},{32,96},{40,104},{48,112},{56,120},{... | collective-permute-start | bytes 82952 | tf_op jit(solution)/shard_map/ppermute | solution.py:35
  98.0 10.1 %collective-permute-start.14 = (f32[54,128]{1,0:T(8,128)S(1)}, f32[54,128]{1,0:T(8,128)S(1)}, u32[]{:S(2)}, u32[]{:S(2)}) collective-permute-start(f32[54,128]{1,0:T(8,128)S(1)} %fusion.69), channel_id=1, source_target_pairs={{0,32},{8,40},{16,48},{24,56},{32,64},{40,72},{48,80},{56,88},{64,... | collective-permute-start | bytes 82952 | tf_op jit(solution)/shard_map/ppermute | solution.py:35
  109.4 7.8 %collective-permute-start.19 = (f32[54,128]{1,0:T(8,128)S(1)}, f32[54,128]{1,0:T(8,128)S(1)}, u32[]{:S(2)}, u32[]{:S(2)}) collective-permute-start(f32[54,128]{1,0:T(8,128)S(1)} %fusion.68), channel_id=1, source_target_pairs={{0,3},{1,0},{2,1},{3,2},{4,7},{5,4},{6,5},{7,6},{8,11},{9,8},{10,9... | collective-permute-start | bytes 82952 | tf_op jit(solution)/shard_map/ppermute | solution.py:35
  111.3 7.8 %collective-permute-start.18 = (f32[54,128]{1,0:T(8,128)S(1)}, f32[54,128]{1,0:T(8,128)S(1)}, u32[]{:S(2)}, u32[]{:S(2)}) collective-permute-start(f32[54,128]{1,0:T(8,128)S(1)} %fusion.68), channel_id=1, source_target_pairs={{0,2},{1,3},{2,0},{3,1},{4,6},{5,7},{6,4},{7,5},{8,10},{9,11},{10,... | collective-permute-start | bytes 82952 | tf_op jit(solution)/shard_map/ppermute | solution.py:35
  113.3 8.4 %collective-permute-start.17 = (f32[54,128]{1,0:T(8,128)S(1)}, f32[54,128]{1,0:T(8,128)S(1)}, u32[]{:S(2)}, u32[]{:S(2)}) collective-permute-start(f32[54,128]{1,0:T(8,128)S(1)} %fusion.68), channel_id=1, source_target_pairs={{0,1},{1,2},{2,3},{3,0},{4,5},{5,6},{6,7},{7,4},{8,9},{9,10},{10,1... | collective-permute-start | bytes 82952 | tf_op jit(solution)/shard_map/ppermute | solution.py:35
  117.2 39.2 %collective-permute-start.10 = (f32[8,8,4,128]{3,2,1,0:T(4,128)}, f32[8,8,4,128]{3,2,1,0:T(4,128)S(1)}, u32[]{:S(2)}, u32[]{:S(2)}) collective-permute-start(f32[8,8,4,128]{3,2,1,0:T(4,128)} %bitcast.300), channel_id=1, source_target_pairs={{0,384},{128,0},{256,128},{384,256},{1,385},{129,1},{257,129},{385... | collective-permute-start | bytes 393224 | tf_op jit(solution)/shard_map/ppermute | solution.py:68
  119.2 37.3 %collective-permute-start.9 = (f32[8,8,4,128]{3,2,1,0:T(4,128)}, f32[8,8,4,128]{3,2,1,0:T(4,128)S(1)}, u32[]{:S(2)}, u32[]{:S(2)}) collective-permute-start(f32[8,8,4,128]{3,2,1,0:T(4,128)} %bitcast.301), channel_id=1, source_target_pairs={{0,256},{128,384},{256,0},{384,128},{1,257},{129,385},{257,1},{385... | collective-permute-start | bytes 393224 | tf_op jit(solution)/shard_map/ppermute | solution.py:68
  121.7 34.7 %collective-permute-start.8 = (f32[8,8,4,128]{3,2,1,0:T(4,128)}, f32[8,8,4,128]{3,2,1,0:T(4,128)S(1)}, u32[]{:S(2)}, u32[]{:S(2)}) collective-permute-start(f32[8,8,4,128]{3,2,1,0:T(4,128)} %bitcast.302), channel_id=1, source_target_pairs={{0,128},{128,256},{256,384},{384,0},{1,129},{129,257},{257,385},{3... | collective-permute-start | bytes 393224 | tf_op jit(solution)/shard_map/ppermute | solution.py:68
  128.1 6.2 %collective-permute-start.3 = (f32[32,8,6,1]{0,1,3,2:T(8,128)}, f32[32,8,6,1]{0,1,3,2:T(8,128)S(1)}, u32[]{:S(2)}, u32[]{:S(2)}) collective-permute-start(f32[32,8,6,1]{0,1,3,2:T(8,128)} %copy.139), channel_id=1, source_target_pairs={{1,0},{2,1},{3,2},{4,3},{5,4},{6,5},{7,6},{9,8},{10,9},{11,10},{12... | collective-permute-start | bytes 18440 | tf_op jit(solution)/shard_map/ppermute | solution.py:15
  131.6 9.3 %collective-permute-start.2 = (f32[32,8,6,1]{0,1,3,2:T(8,128)S(1)}, f32[32,8,6,1]{0,1,3,2:T(8,128)S(1)}, u32[]{:S(2)}, u32[]{:S(2)}) collective-permute-start(f32[32,8,6,1]{0,1,3,2:T(8,128)S(1)} %copy.138), channel_id=1, source_target_pairs={{0,1},{1,2},{2,3},{3,4},{4,5},{5,6},{6,7},{8,9},{9,10},{10,11},{11... | collective-permute-start | bytes 18440 | tf_op jit(solution)/shard_map/ppermute | solution.py:12
  134.3 18.2 %collective-permute-start.20 = (f32[54,128]{1,0:T(8,128)}, f32[54,128]{1,0:T(8,128)}, u32[]{:S(2)}, u32[]{:S(2)}) collective-permute-start(f32[54,128]{1,0:T(8,128)} %fusion.67), channel_id=1, source_target_pairs={{0,4},{1,5},{2,6},{3,7},{4,0},{5,1},{6,2},{7,3},{8,12},{9,13},{10,... | collective-permute-start | bytes 82952 | tf_op jit(solution)/shard_map/ppermute | solution.py:35
  142.9 5.5 %copy-start = (f32[8,32,3,3,3]{1,0,4,3,2:T(8,128)S(1)}, f32[8,32,3,3,3]{1,0,4,3,2:T(8,128)}, u32[]{:S(2)}) copy-start(f32[8,32,3,3,3]{1,0,4,3,2:T(8,128)} %param.6) | copy-start | bytes 82948
  145.7 8.1 %copy-start.2 = (pred[2]{0:T(512)(128)(4,1)S(1)}, pred[2]{0:T(512)(128)(4,1)}, u32[]{:S(2)}) copy-start(pred[2]{0:T(512)(128)(4,1)} %compare_and_fusion.3) | copy-start | bytes 10

commit v12 on v9

--- a/solution.py
+++ b/solution.py
@@ -23,7 +23,8 @@
         index = lax.axis_index(axis)
         stride = 1
         while stride < count:
-            radix = 4 if (count // stride) % 4 == 0 else 2
+            left = count // stride
+            radix = 8 if left == 8 else (4 if left % 4 == 0 else 2)
             member = (index // stride) % radix
             received = [value]
             for shift in range(1, radix):

time: 154 us -> 188 us (1.22)
  the two profiles are of different devices: /device:TPU:6 before, /device:TPU:24 now
where the time goes in v12:
time: 188 us; the launch traced here: 187 us
  starting transfers between devices  70 us (37%)
  local copies, waits for them, and re-layouts  56.4 us (30%)
  blocking collectives  21.2 us (11%)
  waiting for transfers between devices  19.9 us (11%)
  matrix products  13.2 us (7%)
  other arithmetic  4.44 us (2%)
    ppermute x13, starting transfers between devices, butterfly_sum(): received.append(lax.ppermute(value, axis, pairs))  58.7 us
    unnamed x97, local copies, waits for them, and re-layouts  41.8 us
    ppermute x13, waiting for transfers between devices, butterfly_sum(): received.append(lax.ppermute(value, axis, pairs))  11.3 us
    ppermute x2, waiting for transfers between devices, with_halo(): lax.ppermute(lax.slice_in_dim(block, 0, width, axis=dim), axis, backward)  8.53 us
    ppermute x2, starting transfers between devices, with_halo(): lax.ppermute(lax.slice_in_dim(block, block.shape[dim] - width, None, axis...  8.14 us
    all_gather x1, blocking collectives, shards(): lax.all_gather(upstream, 'col', axis=0, tiled=True)  7.28 us
    all_gather x1, blocking collectives, shards(): lax.all_gather(volume, 'col', axis=0, tiled=True)  7.17 us
    all_gather x1, blocking collectives, shards(): all_rows = lax.all_gather(filters, 'col', axis=0, tiled=True)  6.77 us
  transfers between devices with their start and end apart: 17, of which 6 were waited for; matrix products, arithmetic and copies ran while one was open for 28% of the time, Pallas kernels for 0%

profile of v12, /device:TPU:24, one launch (start us, length us, event | category | flops | bytes accessed | tf_op | source)
XLA Modules:
  0.0 186.7 jit_solution(595568514117342635)
XLA Ops:
  1.6 7.2 %all_gather.9 = f32[32,8,4,128]{3,0,2,1:T(8,128)S(1)} all-gather(f32[8,8,4,128]{3,0,2,1:T(8,128)S(1)} %copy.73), channel_id=1, replica_groups=mesh['col'=4,'gx'=16,'gy'=8] {'col'}, dimensions={0}, use_global_device_ids=true | all-gather | bytes 655360 | tf_op jit(solution)/shard_map/all_gather | solution.py:67
  9.8 7.3 %all_gather.10 = f32[32,8,4,128]{3,0,2,1:T(8,128)S(1)} all-gather(f32[8,8,4,128]{3,0,2,1:T(8,128)S(1)} %copy.74), channel_id=1, replica_groups=mesh['col'=4,'gx'=16,'gy'=8] {'col'}, dimensions={0}, use_global_device_ids=true | all-gather | bytes 655360 | tf_op jit(solution)/shard_map/all_gather | solution.py:68
  17.1 3.8 %collective-permute-start = (f32[2,32,8,1,128]{4,1,3,2,0:T(8,128)S(1)}, f32[2,32,8,1,128]{4,1,3,2,0:T(8,128)S(1)}, u32[]{:S(2)}, u32[]{:S(2)}) collective-permute-start(f32[2,32,8,1,128]{4,1,3,2,0:T(8,128)S(1)} %get-tuple-element.20), channel_id=1, source_target_pairs={{0,8},{8,16},{16,24},{24,32},{32,40},{40,48},{48,56},{56,64},{64,7... | collective-permute-start | bytes 786440 | tf_op jit(solution)/shard_map/ppermute | solution.py:12
  20.9 1.3 collective-permute-start.1
  22.4 6.8 %all_gather.11 = f32[32,32,3,3,3]{1,0,4,3,2:T(8,128)S(1)} all-gather(f32[8,32,3,3,3]{1,0,4,3,2:T(8,128)} %param.6), channel_id=1, replica_groups=mesh['col'=4,'gx'=16,'gy'=8] {'col'}, dimensions={0}, use_global_device_ids=true | all-gather | bytes 138240 | tf_op jit(solution)/shard_map/all_gather | solution.py:70
  29.4 1.9 %collective-permute-done.1 = f32[2,32,8,1,128]{4,1,3,2,0:T(8,128)S(1)} collective-permute-done((f32[2,32,8,1,128]{4,1,3,2,0:T(8,128)S(1)}, f32[2,32,8,1,128]{4,1,3,2,0:T(8,128)S(1)}, u32[]{:S(2)}, u32[]{:S(2)}) %collective-permute-start.1) | collective-permute-done | bytes 262176 | tf_op jit(solution)/shard_map/ppermute | solution.py:15
  32.1 1.7 fusion.69
  33.8 2.0 %copy.75 = f32[2,32,8,6,1]{1,2,4,3,0:T(8,128)S(1)} copy(f32[2,32,8,6,1]{4,1,3,2,0:T(8,128)} %get-tuple-element.18) | data formatting | bytes 24576 | tf_op jit(solution)/shard_map/slice | solution.py:13
  35.9 4.3 %collective-permute-start.2 = (f32[2,32,8,6,1]{1,2,4,3,0:T(8,128)S(1)}, f32[2,32,8,6,1]{1,2,4,3,0:T(8,128)S(1)}, u32[]{:S(2)}, u32[]{:S(2)}) collective-permute-start(f32[2,32,8,6,1]{1,2,4,3,0:T(8,128)S(1)} %copy.75), channel_id=1, source_target_pairs={{0,1},{1,2},{2,3},{3,4},{4,5},{5,6},{6,7},{8,9},{9,10},{10,11},{11... | collective-permute-start | bytes 36872 | tf_op jit(solution)/shard_map/ppermute | solution.py:12
  40.2 1.2 copy.76
  41.4 1.9 %collective-permute-start.3 = (f32[2,32,8,6,1]{1,2,4,3,0:T(8,128)}, f32[2,32,8,6,1]{1,2,4,3,0:T(8,128)}, u32[]{:S(2)}, u32[]{:S(2)}) collective-permute-start(f32[2,32,8,6,1]{1,2,4,3,0:T(8,128)} %copy.76), channel_id=1, source_target_pairs={{1,0},{2,1},{3,2},{4,3},{5,4},{6,5},{7,6},{9,8},{10,9},{11,10},{12... | collective-permute-start | bytes 36872 | tf_op jit(solution)/shard_map/ppermute | solution.py:15
  44.7 6.6 %collective-permute-done.3 = f32[2,32,8,6,1]{1,2,4,3,0:T(8,128)} collective-permute-done((f32[2,32,8,6,1]{1,2,4,3,0:T(8,128)}, f32[2,32,8,6,1]{1,2,4,3,0:T(8,128)}, u32[]{:S(2)}, u32[]{:S(2)}) %collective-permute-start.3) | collective-permute-done | bytes 12320 | tf_op jit(solution)/shard_map/ppermute | solution.py:15
  51.3 2.6 %copy.78 = f32[2,32,8,6,1]{4,1,3,2,0:T(8,128)} copy(f32[2,32,8,6,1]{1,2,4,3,0:T(8,128)} %collective-permute-done.3) | data formatting | bytes 24576 | tf_op jit(solution)/shard_map/ppermute | solution.py:15
  53.9 3.3 %select_maximum_fusion = f32[2,32,10,6,130]{4,1,3,2,0:T(8,128)S(1)} fusion(f32[2,32,8,6,1]{4,1,3,2,0:T(8,128)} %copy.78, f32[2,32,8,6,1]{4,1,3,2,0:T(8,128)S(1)} %copy.77, f32[2,32,8,1,128]{4,1,3,2,0:T(8,128)} %copy-done.1, f32[2,32,8,1,128]{4,1,3,2,0:T(8,128)S(1)} %collective-permute-done, f32[1,32,8,4,128]{4,1,3,2,0:T(8,128)S(1)} %bitcast.508, ...), kind=kLoop, calls=%fused_computation.5 | loop fusion | flops 6988800 | bytes 3594240 | tf_op jit(solution)/shard_map/concatenate | solution.py:16
  57.3 1.9 %fusion.68 = (f32[1,32,10,6,130]{4,1,3,2,0:T(8,128)S(1)}, f32[32,10,6,130]{3,0,2,1:T(8,128)}, f32[32,10,6,130]{3,0,2,1:T(8,128)S(1)}) fusion(f32[2,32,10,6,130]{4,1,3,2,0:T(8,128)S(1)} %select_maximum_fusion), kind=kLoop, calls=%fused_computation.238 | loop fusion | bytes 4992000 | tf_op jit(solution)/shard_map/slice | solution.py:73
  61.2 1.5 convolution_bitcast_fusion.2
  63.1 4.0 %collective-permute-start.4 = (f32[54,128]{1,0:T(8,128)S(1)}, f32[54,128]{1,0:T(8,128)S(1)}, u32[]{:S(2)}, u32[]{:S(2)}) collective-permute-start(f32[54,128]{1,0:T(8,128)S(1)} %reshape_reshape.3), channel_id=1, source_target_pairs={{0,8},{8,16},{16,24},{24,0},{32,40},{40,48},{48,56},{56,32},{64,72... | collective-permute-start | bytes 82952 | tf_op jit(solution)/shard_map/ppermute | solution.py:36
  67.0 7.4 %collective-permute-start.5 = (f32[54,128]{1,0:T(8,128)S(1)}, f32[54,128]{1,0:T(8,128)S(1)}, u32[]{:S(2)}, u32[]{:S(2)}) collective-permute-start(f32[54,128]{1,0:T(8,128)S(1)} %reshape_reshape.3), channel_id=1, source_target_pairs={{0,16},{8,24},{16,0},{24,8},{32,48},{40,56},{48,32},{56,40},{64,80... | collective-permute-start | bytes 82952 | tf_op jit(solution)/shard_map/ppermute | solution.py:36
  74.5 2.1 %collective-permute-start.6 = (f32[54,128]{1,0:T(8,128)S(1)}, f32[54,128]{1,0:T(8,128)S(1)}, u32[]{:S(2)}, u32[]{:S(2)}) collective-permute-start(f32[54,128]{1,0:T(8,128)S(1)} %reshape_reshape.3), channel_id=1, source_target_pairs={{0,24},{8,0},{16,8},{24,16},{32,56},{40,32},{48,40},{56,48},{64,88... | collective-permute-start | bytes 82952 | tf_op jit(solution)/shard_map/ppermute | solution.py:36
  76.6 1.4 fusion.27
  78.0 1.4 fusion.26
  79.4 1.1 fusion.25
  80.5 1.4 fusion.24
  86.3 1.0 fusion.53
  87.3 1.1 fusion.52
  93.2 1.1 fusion.46
  95.3 1.1 fusion.44
  98.2 1.0 fusion.41
  99.2 1.0 fusion.40
  102.2 1.0 fusion.37
  104.1 1.0 fusion.35
  105.1 1.1 fusion.34
  111.0 5.0 %convolution_bitcast_fusion = f32[8,8,4,128]{3,0,2,1:T(8,128)S(1)} fusion(f32[32,27,8,1,1]{0,2,4,3,1:T(8,128)S(1)} %bitcast.510, f32[27,32,8,4,128]{4,1,3,2,0:T(8,128)S(1)} %fusion.1), kind=kOutput, calls=%fused_computation.13 | convolution fusion | flops 169869312 | bytes 14314496 | tf_op jit(solution)/shard_map/okc,kopqy->cpqy/dot_general | solution.py:92
  117.9 9.1 %collective-permute-start.7 = (f32[54,128]{1,0:T(8,128)S(1)}, f32[54,128]{1,0:T(8,128)S(1)}, u32[]{:S(2)}, u32[]{:S(2)}) collective-permute-start(f32[54,128]{1,0:T(8,128)S(1)} %fusion.75), channel_id=1, source_target_pairs={{0,32},{8,40},{16,48},{24,56},{32,64},{40,72},{48,80},{56,88},{64,... | collective-permute-start | bytes 82952 | tf_op jit(solution)/shard_map/ppermute | solution.py:36
  127.0 7.1 %collective-permute-start.8 = (f32[54,128]{1,0:T(8,128)S(1)}, f32[54,128]{1,0:T(8,128)S(1)}, u32[]{:S(2)}, u32[]{:S(2)}) collective-permute-start(f32[54,128]{1,0:T(8,128)S(1)} %fusion.75), channel_id=1, source_target_pairs={{0,64},{8,72},{16,80},{24,88},{32,96},{40,104},{48,112},{56,120},{... | collective-permute-start | bytes 82952 | tf_op jit(solution)/shard_map/ppermute | solution.py:36
  134.1 5.5 %collective-permute-start.9 = (f32[54,128]{1,0:T(8,128)S(1)}, f32[54,128]{1,0:T(8,128)S(1)}, u32[]{:S(2)}, u32[]{:S(2)}) collective-permute-start(f32[54,128]{1,0:T(8,128)S(1)} %fusion.75), channel_id=1, source_target_pairs={{0,96},{8,104},{16,112},{24,120},{32,0},{40,8},{48,16},{56,24},{64... | collective-permute-start | bytes 82952 | tf_op jit(solution)/shard_map/ppermute | solution.py:36
  139.6 1.9 %collective-permute-done.8 = f32[54,128]{1,0:T(8,128)S(1)} collective-permute-done((f32[54,128]{1,0:T(8,128)S(1)}, f32[54,128]{1,0:T(8,128)S(1)}, u32[]{:S(2)}, u32[]{:S(2)}) %collective-permute-start.8) | collective-permute-done | bytes 27680 | tf_op jit(solution)/shard_map/ppermute | solution.py:36
  141.5 2.9 %collective-permute-done.9 = f32[54,128]{1,0:T(8,128)S(1)} collective-permute-done((f32[54,128]{1,0:T(8,128)S(1)}, f32[54,128]{1,0:T(8,128)S(1)}, u32[]{:S(2)}, u32[]{:S(2)}) %collective-permute-start.9) | collective-permute-done | bytes 27680 | tf_op jit(solution)/shard_map/ppermute | solution.py:36
  145.1 2.1 %collective-permute-start.10 = (f32[54,128]{1,0:T(8,128)S(1)}, f32[54,128]{1,0:T(8,128)S(1)}, u32[]{:S(2)}, u32[]{:S(2)}) collective-permute-start(f32[54,128]{1,0:T(8,128)S(1)} %bitcast.517), channel_id=1, source_target_pairs={{0,1},{1,2},{2,3},{3,4},{4,5},{5,6},{6,7},{7,0},{8,9},{9,10},{10,1... | collective-permute-start | bytes 82952 | tf_op jit(solution)/shard_map/ppermute | solution.py:36
  147.3 6.7 %convolution_bitcast_fusion.1 = f32[8,8,4,128]{3,0,2,1:T(8,128)S(1)} fusion(f32[27,32,8,4,128]{4,1,0,3,2:T(8,128)} %fusion.28, f32[8,27,32,1,1]{2,0,1,4,3:T(8,128)S(1)} %bitcast.509), kind=kOutput, calls=%fused_computation.14 | convolution fusion | flops 169869312 | bytes 14314496 | tf_op jit(solution)/shard_map/okc,kcpqy->opqy/dot_general | solution.py:88
  155.4 2.1 %collective-permute-start.11 = (f32[54,128]{1,0:T(8,128)S(1)}, f32[54,128]{1,0:T(8,128)S(1)}, u32[]{:S(2)}, u32[]{:S(2)}) collective-permute-start(f32[54,128]{1,0:T(8,128)S(1)} %bitcast.518), channel_id=1, source_target_pairs={{0,2},{1,3},{2,4},{3,5},{4,6},{5,7},{6,0},{7,1},{8,10},{9,11},{10,... | collective-permute-start | bytes 82952 | tf_op jit(solution)/shard_map/ppermute | solution.py:36
  157.5 2.3 %collective-permute-start.12 = (f32[54,128]{1,0:T(8,128)S(1)}, f32[54,128]{1,0:T(8,128)S(1)}, u32[]{:S(2)}, u32[]{:S(2)}) collective-permute-start(f32[54,128]{1,0:T(8,128)S(1)} %bitcast.519), channel_id=1, source_target_pairs={{0,3},{1,4},{2,5},{3,6},{4,7},{5,0},{6,1},{7,2},{8,11},{9,12},{10,... | collective-permute-start | bytes 82952 | tf_op jit(solution)/shard_map/ppermute | solution.py:36
  159.8 6.3 %collective-permute-start.13 = (f32[54,128]{1,0:T(8,128)S(1)}, f32[54,128]{1,0:T(8,128)S(1)}, u32[]{:S(2)}, u32[]{:S(2)}) collective-permute-start(f32[54,128]{1,0:T(8,128)S(1)} %bitcast.520), channel_id=1, source_target_pairs={{0,4},{1,5},{2,6},{3,7},{4,0},{5,1},{6,2},{7,3},{8,12},{9,13},{10,... | collective-permute-start | bytes 82952 | tf_op jit(solution)/shard_map/ppermute | solution.py:36
  166.1 1.9 %collective-permute-start.14 = (f32[54,128]{1,0:T(8,128)S(1)}, f32[54,128]{1,0:T(8,128)S(1)}, u32[]{:S(2)}, u32[]{:S(2)}) collective-permute-start(f32[54,128]{1,0:T(8,128)S(1)} %bitcast.521), channel_id=1, source_target_pairs={{0,5},{1,6},{2,7},{3,0},{4,1},{5,2},{6,3},{7,4},{8,13},{9,14},{10,... | collective-permute-start | bytes 82952 | tf_op jit(solution)/shard_map/ppermute | solution.py:36
  168.0 6.0 %collective-permute-start.15 = (f32[54,128]{1,0:T(8,128)S(1)}, f32[54,128]{1,0:T(8,128)S(1)}, u32[]{:S(2)}, u32[]{:S(2)}) collective-permute-start(f32[54,128]{1,0:T(8,128)S(1)} %bitcast.522), channel_id=1, source_target_pairs={{0,6},{1,7},{2,0},{3,1},{4,2},{5,3},{6,4},{7,5},{8,14},{9,15},{10,... | collective-permute-start | bytes 82952 | tf_op jit(solution)/shard_map/ppermute | solution.py:36
  174.1 2.8 %collective-permute-start.16 = (f32[54,128]{1,0:T(8,128)S(1)}, f32[54,128]{1,0:T(8,128)S(1)}, u32[]{:S(2)}, u32[]{:S(2)}) collective-permute-start(f32[54,128]{1,0:T(8,128)S(1)} %bitcast.523), channel_id=1, source_target_pairs={{0,7},{1,0},{2,1},{3,2},{4,3},{5,4},{6,5},{7,6},{8,15},{9,8},{10,9... | collective-permute-start | bytes 82952 | tf_op jit(solution)/shard_map/ppermute | solution.py:36
  177.7 5.8 %collective-permute-done.16 = f32[54,128]{1,0:T(8,128)S(1)} collective-permute-done((f32[54,128]{1,0:T(8,128)S(1)}, f32[54,128]{1,0:T(8,128)S(1)}, u32[]{:S(2)}, u32[]{:S(2)}) %collective-permute-start.16) | collective-permute-done | bytes 27680 | tf_op jit(solution)/shard_map/ppermute | solution.py:36
  185.0 1.6 copy.137
  (129 shorter events, 32.3 us)
Async XLA Ops:
  17.1 12.3 %collective-permute-start = (f32[2,32,8,1,128]{4,1,3,2,0:T(8,128)S(1)}, f32[2,32,8,1,128]{4,1,3,2,0:T(8,128)S(1)}, u32[]{:S(2)}, u32[]{:S(2)}) collective-permute-start(f32[2,32,8,1,128]{4,1,3,2,0:T(8,128)S(1)} %get-tuple-element.20), channel_id=1, source_target_pairs={{0,8},{8,16},{16,24},{24,32},{32,40},{40,48},{48,56},{56,64},{64,7... | collective-permute-start | bytes 786440 | tf_op jit(solution)/shard_map/ppermute | solution.py:12
  20.9 10.3 %collective-permute-start.1 = (f32[2,32,8,1,128]{4,1,3,2,0:T(8,128)S(1)}, f32[2,32,8,1,128]{4,1,3,2,0:T(8,128)S(1)}, u32[]{:S(2)}, u32[]{:S(2)}) collective-permute-start(f32[2,32,8,1,128]{4,1,3,2,0:T(8,128)S(1)} %get-tuple-element.21), channel_id=1, source_target_pairs={{8,0},{16,8},{24,16},{32,24},{40,32},{48,40},{56,48},{64,56},{72,6... | collective-permute-start | bytes 786440 | tf_op jit(solution)/shard_map/ppermute | solution.py:15
  31.3 0.7 copy-start.1
  35.9 8.2 %collective-permute-start.2 = (f32[2,32,8,6,1]{1,2,4,3,0:T(8,128)S(1)}, f32[2,32,8,6,1]{1,2,4,3,0:T(8,128)S(1)}, u32[]{:S(2)}, u32[]{:S(2)}) collective-permute-start(f32[2,32,8,6,1]{1,2,4,3,0:T(8,128)S(1)} %copy.75), channel_id=1, source_target_pairs={{0,1},{1,2},{2,3},{3,4},{4,5},{5,6},{6,7},{8,9},{9,10},{10,11},{11... | collective-permute-start | bytes 36872 | tf_op jit(solution)/shard_map/ppermute | solution.py:12
  41.4 9.9 %collective-permute-start.3 = (f32[2,32,8,6,1]{1,2,4,3,0:T(8,128)}, f32[2,32,8,6,1]{1,2,4,3,0:T(8,128)}, u32[]{:S(2)}, u32[]{:S(2)}) collective-permute-start(f32[2,32,8,6,1]{1,2,4,3,0:T(8,128)} %copy.76), channel_id=1, source_target_pairs={{1,0},{2,1},{3,2},{4,3},{5,4},{6,5},{7,6},{9,8},{10,9},{11,10},{12... | collective-permute-start | bytes 36872 | tf_op jit(solution)/shard_map/ppermute | solution.py:15
  63.1 18.9 %copy-start = (f32[32,10,6,130]{3,0,2,1:T(8,128)S(1)}, f32[32,10,6,130]{3,0,2,1:T(8,128)}, u32[]{:S(2)}) copy-start(f32[32,10,6,130]{3,0,2,1:T(8,128)} %get-tuple-element.16) | copy-start | bytes 2995204
  63.1 54.2 %collective-permute-start.4 = (f32[54,128]{1,0:T(8,128)S(1)}, f32[54,128]{1,0:T(8,128)S(1)}, u32[]{:S(2)}, u32[]{:S(2)}) collective-permute-start(f32[54,128]{1,0:T(8,128)S(1)} %reshape_reshape.3), channel_id=1, source_target_pairs={{0,8},{8,16},{16,24},{24,0},{32,40},{40,48},{48,56},{56,32},{64,72... | collective-permute-start | bytes 82952 | tf_op jit(solution)/shard_map/ppermute | solution.py:36
  67.0 50.2 %collective-permute-start.5 = (f32[54,128]{1,0:T(8,128)S(1)}, f32[54,128]{1,0:T(8,128)S(1)}, u32[]{:S(2)}, u32[]{:S(2)}) collective-permute-start(f32[54,128]{1,0:T(8,128)S(1)} %reshape_reshape.3), channel_id=1, source_target_pairs={{0,16},{8,24},{16,0},{24,8},{32,48},{40,56},{48,32},{56,40},{64,80... | collective-permute-start | bytes 82952 | tf_op jit(solution)/shard_map/ppermute | solution.py:36
  74.5 42.8 %collective-permute-start.6 = (f32[54,128]{1,0:T(8,128)S(1)}, f32[54,128]{1,0:T(8,128)S(1)}, u32[]{:S(2)}, u32[]{:S(2)}) collective-permute-start(f32[54,128]{1,0:T(8,128)S(1)} %reshape_reshape.3), channel_id=1, source_target_pairs={{0,24},{8,0},{16,8},{24,16},{32,56},{40,32},{48,40},{56,48},{64,88... | collective-permute-start | bytes 82952 | tf_op jit(solution)/shard_map/ppermute | solution.py:36
  111.0 36.3 %copy-start.2 = (f32[8,32,3,3,3]{1,0,4,3,2:T(8,128)S(1)}, f32[8,32,3,3,3]{1,0,4,3,2:T(8,128)}, u32[]{:S(2)}) copy-start(f32[8,32,3,3,3]{1,0,4,3,2:T(8,128)} %param.6) | copy-start | bytes 82948
  117.9 21.7 %collective-permute-start.7 = (f32[54,128]{1,0:T(8,128)S(1)}, f32[54,128]{1,0:T(8,128)S(1)}, u32[]{:S(2)}, u32[]{:S(2)}) collective-permute-start(f32[54,128]{1,0:T(8,128)S(1)} %fusion.75), channel_id=1, source_target_pairs={{0,32},{8,40},{16,48},{24,56},{32,64},{40,72},{48,80},{56,88},{64,... | collective-permute-start | bytes 82952 | tf_op jit(solution)/shard_map/ppermute | solution.py:36
  127.0 14.5 %collective-permute-start.8 = (f32[54,128]{1,0:T(8,128)S(1)}, f32[54,128]{1,0:T(8,128)S(1)}, u32[]{:S(2)}, u32[]{:S(2)}) collective-permute-start(f32[54,128]{1,0:T(8,128)S(1)} %fusion.75), channel_id=1, source_target_pairs={{0,64},{8,72},{16,80},{24,88},{32,96},{40,104},{48,112},{56,120},{... | collective-permute-start | bytes 82952 | tf_op jit(solution)/shard_map/ppermute | solution.py:36
  134.1 10.3 %collective-permute-start.9 = (f32[54,128]{1,0:T(8,128)S(1)}, f32[54,128]{1,0:T(8,128)S(1)}, u32[]{:S(2)}, u32[]{:S(2)}) collective-permute-start(f32[54,128]{1,0:T(8,128)S(1)} %fusion.75), channel_id=1, source_target_pairs={{0,96},{8,104},{16,112},{24,120},{32,0},{40,8},{48,16},{56,24},{64... | collective-permute-start | bytes 82952 | tf_op jit(solution)/shard_map/ppermute | solution.py:36
  145.1 22.9 %collective-permute-start.10 = (f32[54,128]{1,0:T(8,128)S(1)}, f32[54,128]{1,0:T(8,128)S(1)}, u32[]{:S(2)}, u32[]{:S(2)}) collective-permute-start(f32[54,128]{1,0:T(8,128)S(1)} %bitcast.517), channel_id=1, source_target_pairs={{0,1},{1,2},{2,3},{3,4},{4,5},{5,6},{6,7},{7,0},{8,9},{9,10},{10,1... | collective-permute-start | bytes 82952 | tf_op jit(solution)/shard_map/ppermute | solution.py:36
  147.3 36.8 %copy-start.3 = (pred[8]{0:T(512)(128)(4,1)S(1)}, pred[8]{0:T(512)(128)(4,1)}, u32[]{:S(2)}) copy-start(pred[8]{0:T(512)(128)(4,1)} %compare_and_fusion.2) | copy-start | bytes 28
  155.4 18.7 %collective-permute-start.11 = (f32[54,128]{1,0:T(8,128)S(1)}, f32[54,128]{1,0:T(8,128)S(1)}, u32[]{:S(2)}, u32[]{:S(2)}) collective-permute-start(f32[54,128]{1,0:T(8,128)S(1)} %bitcast.518), channel_id=1, source_target_pairs={{0,2},{1,3},{2,4},{3,5},{4,6},{5,7},{6,0},{7,1},{8,10},{9,11},{10,... | collective-permute-start | bytes 82952 | tf_op jit(solution)/shard_map/ppermute | solution.py:36
  157.5 19.4 %collective-permute-start.12 = (f32[54,128]{1,0:T(8,128)S(1)}, f32[54,128]{1,0:T(8,128)S(1)}, u32[]{:S(2)}, u32[]{:S(2)}) collective-permute-start(f32[54,128]{1,0:T(8,128)S(1)} %bitcast.519), channel_id=1, source_target_pairs={{0,3},{1,4},{2,5},{3,6},{4,7},{5,0},{6,1},{7,2},{8,11},{9,12},{10,... | collective-permute-start | bytes 82952 | tf_op jit(solution)/shard_map/ppermute | solution.py:36
  159.8 17.1 %collective-permute-start.13 = (f32[54,128]{1,0:T(8,128)S(1)}, f32[54,128]{1,0:T(8,128)S(1)}, u32[]{:S(2)}, u32[]{:S(2)}) collective-permute-start(f32[54,128]{1,0:T(8,128)S(1)} %bitcast.520), channel_id=1, source_target_pairs={{0,4},{1,5},{2,6},{3,7},{4,0},{5,1},{6,2},{7,3},{8,12},{9,13},{10,... | collective-permute-start | bytes 82952 | tf_op jit(solution)/shard_map/ppermute | solution.py:36
  166.1 10.8 %collective-permute-start.14 = (f32[54,128]{1,0:T(8,128)S(1)}, f32[54,128]{1,0:T(8,128)S(1)}, u32[]{:S(2)}, u32[]{:S(2)}) collective-permute-start(f32[54,128]{1,0:T(8,128)S(1)} %bitcast.521), channel_id=1, source_target_pairs={{0,5},{1,6},{2,7},{3,0},{4,1},{5,2},{6,3},{7,4},{8,13},{9,14},{10,... | collective-permute-start | bytes 82952 | tf_op jit(solution)/shard_map/ppermute | solution.py:36
  168.0 9.7 %collective-permute-start.15 = (f32[54,128]{1,0:T(8,128)S(1)}, f32[54,128]{1,0:T(8,128)S(1)}, u32[]{:S(2)}, u32[]{:S(2)}) collective-permute-start(f32[54,128]{1,0:T(8,128)S(1)} %bitcast.522), channel_id=1, source_target_pairs={{0,6},{1,7},{2,0},{3,1},{4,2},{5,3},{6,4},{7,5},{8,14},{9,15},{10,... | collective-permute-start | bytes 82952 | tf_op jit(solution)/shard_map/ppermute | solution.py:36
  174.1 9.4 %collective-permute-start.16 = (f32[54,128]{1,0:T(8,128)S(1)}, f32[54,128]{1,0:T(8,128)S(1)}, u32[]{:S(2)}, u32[]{:S(2)}) collective-permute-start(f32[54,128]{1,0:T(8,128)S(1)} %bitcast.523), channel_id=1, source_target_pairs={{0,7},{1,0},{2,1},{3,2},{4,3},{5,4},{6,5},{7,6},{8,15},{9,8},{10,9... | collective-permute-start | bytes 82952 | tf_op jit(solution)/shard_map/ppermute | solution.py:36

commit v13 on v9

--- a/solution.py
+++ b/solution.py
@@ -79,7 +79,7 @@
     flat = local_grad.reshape(-1, 128)
     sizes = [lax.axis_size(a) for a in ("gx", "gy")]
     if all(n & (n - 1) == 0 for n in sizes):
-        flat = butterfly_sum(flat, ("gx", "gy"))
+        flat = butterfly_sum(flat, ("gy", "gx"))
     else:
         flat = lax.psum(flat, ("gx", "gy"))
     total_grad = flat.reshape(local_grad.shape)

time: 154 us -> 153 us (level)
  the two profiles are of different devices: /device:TPU:6 before, /device:TPU:40 now
where the time goes in v13:
time: 153 us; the launch traced here: 152 us
  starting transfers between devices  65.5 us (43%)
  local copies, waits for them, and re-layouts  34.4 us (22%)
  blocking collectives  21.1 us (14%)
  waiting for transfers between devices  14.1 us (9%)
  matrix products  10.2 us (7%)
  other arithmetic  5.65 us (4%)
    ppermute x10, starting transfers between devices, butterfly_sum(): received.append(lax.ppermute(value, axis, pairs))  53.8 us
    unnamed x95, local copies, waits for them, and re-layouts  20 us
    ppermute x10, waiting for transfers between devices, butterfly_sum(): received.append(lax.ppermute(value, axis, pairs))  11.3 us
    ppermute x2, starting transfers between devices, with_halo(): lax.ppermute(lax.slice_in_dim(block, block.shape[dim] - width, None, axis...  7.31 us
    all_gather x1, blocking collectives, shards(): lax.all_gather(upstream, 'col', axis=0, tiled=True)  7.28 us
    all_gather x1, blocking collectives, shards(): lax.all_gather(volume, 'col', axis=0, tiled=True)  7.17 us
    all_gather x1, blocking collectives, shards(): all_rows = lax.all_gather(filters, 'col', axis=0, tiled=True)  6.66 us
    dot_general x1, matrix products, shards(): jnp.einsum('okc,kopqy->cpqy', own_by_tap, taps_up, precision=lax.Precisio...  5.03 us
  transfers between devices with their start and end apart: 14, of which 6 were waited for; matrix products, arithmetic and copies ran while one was open for 18% of the time, Pallas kernels for 0%

profile of v13, /device:TPU:40, one launch (start us, length us, event | category | flops | bytes accessed | tf_op | source)
XLA Modules:
  0.0 152.4 jit_solution(6799247428564653397)
XLA Ops:
  0.6 1.0 copy.73
  1.6 7.2 %all_gather.9 = f32[32,8,4,128]{3,0,2,1:T(8,128)S(1)} all-gather(f32[8,8,4,128]{3,0,2,1:T(8,128)S(1)} %copy.73), channel_id=1, replica_groups=mesh['col'=4,'gx'=16,'gy'=8] {'col'}, dimensions={0}, use_global_device_ids=true | all-gather | bytes 655360 | tf_op jit(solution)/shard_map/all_gather | solution.py:66
  8.8 1.0 copy.74
  9.8 7.3 %all_gather.10 = f32[32,8,4,128]{3,0,2,1:T(8,128)S(1)} all-gather(f32[8,8,4,128]{3,0,2,1:T(8,128)S(1)} %copy.74), channel_id=1, replica_groups=mesh['col'=4,'gx'=16,'gy'=8] {'col'}, dimensions={0}, use_global_device_ids=true | all-gather | bytes 655360 | tf_op jit(solution)/shard_map/all_gather | solution.py:67
  17.1 3.8 %collective-permute-start = (f32[2,32,8,1,128]{4,1,3,2,0:T(8,128)S(1)}, f32[2,32,8,1,128]{4,1,3,2,0:T(8,128)S(1)}, u32[]{:S(2)}, u32[]{:S(2)}) collective-permute-start(f32[2,32,8,1,128]{4,1,3,2,0:T(8,128)S(1)} %get-tuple-element.18), channel_id=1, source_target_pairs={{0,8},{8,16},{16,24},{24,32},{32,40},{40,48},{48,56},{56,64},{64,7... | collective-permute-start | bytes 786440 | tf_op jit(solution)/shard_map/ppermute | solution.py:12
  20.9 2.0 %collective-permute-start.1 = (f32[2,32,8,1,128]{4,1,3,2,0:T(8,128)S(1)}, f32[2,32,8,1,128]{4,1,3,2,0:T(8,128)S(1)}, u32[]{:S(2)}, u32[]{:S(2)}) collective-permute-start(f32[2,32,8,1,128]{4,1,3,2,0:T(8,128)S(1)} %get-tuple-element.19), channel_id=1, source_target_pairs={{8,0},{16,8},{24,16},{32,24},{40,32},{48,40},{56,48},{64,56},{72,6... | collective-permute-start | bytes 786440 | tf_op jit(solution)/shard_map/ppermute | solution.py:15
  23.0 0.5 compare_and_fusion.2
  24.2 6.7 %all_gather.11 = f32[32,32,3,3,3]{1,0,4,3,2:T(8,128)S(1)} all-gather(f32[8,32,3,3,3]{1,0,4,3,2:T(8,128)} %param.6), channel_id=1, replica_groups=mesh['col'=4,'gx'=16,'gy'=8] {'col'}, dimensions={0}, use_global_device_ids=true | all-gather | bytes 138240 | tf_op jit(solution)/shard_map/all_gather | solution.py:69
  31.3 0.7 copy-done.1
  32.1 1.7 %fusion.67 = (f32[2,32,8,6,1]{4,1,3,2,0:T(8,128)}, f32[2,32,8,6,1]{4,1,3,2,0:T(8,128)S(1)}) fusion(f32[2,32,8,6,128]{4,1,3,2,0:T(8,128)S(1)} %pad_maximum_fusion), kind=kLoop, calls=%fused_computation.239 | loop fusion | bytes 49152 | tf_op jit(solution)/shard_map/slice | solution.py:13
  33.8 2.0 %copy.75 = f32[2,32,8,6,1]{1,2,4,3,0:T(8,128)S(1)} copy(f32[2,32,8,6,1]{4,1,3,2,0:T(8,128)} %get-tuple-element.16) | data formatting | bytes 24576 | tf_op jit(solution)/shard_map/slice | solution.py:13
  35.9 3.5 %collective-permute-start.2 = (f32[2,32,8,6,1]{1,2,4,3,0:T(8,128)S(1)}, f32[2,32,8,6,1]{1,2,4,3,0:T(8,128)S(1)}, u32[]{:S(2)}, u32[]{:S(2)}) collective-permute-start(f32[2,32,8,6,1]{1,2,4,3,0:T(8,128)S(1)} %copy.75), channel_id=1, source_target_pairs={{0,1},{1,2},{2,3},{3,4},{4,5},{5,6},{6,7},{8,9},{9,10},{10,11},{11... | collective-permute-start | bytes 36872 | tf_op jit(solution)/shard_map/ppermute | solution.py:12
  39.3 1.2 copy.76
  40.6 2.3 %collective-permute-start.3 = (f32[2,32,8,6,1]{1,2,4,3,0:T(8,128)}, f32[2,32,8,6,1]{1,2,4,3,0:T(8,128)}, u32[]{:S(2)}, u32[]{:S(2)}) collective-permute-start(f32[2,32,8,6,1]{1,2,4,3,0:T(8,128)} %copy.76), channel_id=1, source_target_pairs={{1,0},{2,1},{3,2},{4,3},{5,4},{6,5},{7,6},{9,8},{10,9},{11,10},{12... | collective-permute-start | bytes 36872 | tf_op jit(solution)/shard_map/ppermute | solution.py:15
  42.9 0.6 compare_and_fusion.3
  43.7 0.6 copy.77
  44.4 2.5 %collective-permute-done.3 = f32[2,32,8,6,1]{1,2,4,3,0:T(8,128)} collective-permute-done((f32[2,32,8,6,1]{1,2,4,3,0:T(8,128)}, f32[2,32,8,6,1]{1,2,4,3,0:T(8,128)}, u32[]{:S(2)}, u32[]{:S(2)}) %collective-permute-start.3) | collective-permute-done | bytes 12320 | tf_op jit(solution)/shard_map/ppermute | solution.py:15
  46.9 2.6 %copy.78 = f32[2,32,8,6,1]{4,1,3,2,0:T(8,128)} copy(f32[2,32,8,6,1]{1,2,4,3,0:T(8,128)} %collective-permute-done.3) | data formatting | bytes 24576 | tf_op jit(solution)/shard_map/ppermute | solution.py:15
  49.5 3.3 %select_maximum_fusion = f32[2,32,10,6,130]{4,1,3,2,0:T(8,128)S(1)} fusion(f32[2,32,8,6,1]{4,1,3,2,0:T(8,128)} %copy.78, f32[2,32,8,6,1]{4,1,3,2,0:T(8,128)S(1)} %copy.77, f32[2,32,8,1,128]{4,1,3,2,0:T(8,128)} %copy-done.1, f32[2,32,8,1,128]{4,1,3,2,0:T(8,128)S(1)} %collective-permute-done, f32[1,32,8,4,128]{4,1,3,2,0:T(8,128)S(1)} %bitcast.501, ...), kind=kLoop, calls=%fused_computation.6 | loop fusion | flops 6988800 | bytes 3594240 | tf_op jit(solution)/shard_map/concatenate | solution.py:16
  52.8 1.9 %fusion.66 = (f32[1,32,10,6,130]{4,1,3,2,0:T(8,128)S(1)}, f32[32,10,6,130]{3,0,2,1:T(8,128)}, f32[32,10,6,130]{3,0,2,1:T(8,128)S(1)}) fusion(f32[2,32,10,6,130]{4,1,3,2,0:T(8,128)S(1)} %select_maximum_fusion), kind=kLoop, calls=%fused_computation.238 | loop fusion | bytes 4992000 | tf_op jit(solution)/shard_map/slice | solution.py:72
  56.7 1.5 convolution_bitcast_fusion.2
  58.6 3.7 %collective-permute-start.4 = (f32[54,128]{1,0:T(8,128)S(1)}, f32[54,128]{1,0:T(8,128)S(1)}, u32[]{:S(2)}, u32[]{:S(2)}) collective-permute-start(f32[54,128]{1,0:T(8,128)S(1)} %reshape_reshape.3), channel_id=1, source_target_pairs={{0,1},{1,2},{2,3},{3,0},{4,5},{5,6},{6,7},{7,4},{8,9},{9,10},{10,1... | collective-permute-start | bytes 82952 | tf_op jit(solution)/shard_map/ppermute | solution.py:35
  62.3 7.0 %collective-permute-start.5 = (f32[54,128]{1,0:T(8,128)S(1)}, f32[54,128]{1,0:T(8,128)S(1)}, u32[]{:S(2)}, u32[]{:S(2)}) collective-permute-start(f32[54,128]{1,0:T(8,128)S(1)} %reshape_reshape.3), channel_id=1, source_target_pairs={{0,2},{1,3},{2,0},{3,1},{4,6},{5,7},{6,4},{7,5},{8,10},{9,11},{10,... | collective-permute-start | bytes 82952 | tf_op jit(solution)/shard_map/ppermute | solution.py:35
  69.3 4.7 %collective-permute-start.6 = (f32[54,128]{1,0:T(8,128)S(1)}, f32[54,128]{1,0:T(8,128)S(1)}, u32[]{:S(2)}, u32[]{:S(2)}) collective-permute-start(f32[54,128]{1,0:T(8,128)S(1)} %reshape_reshape.3), channel_id=1, source_target_pairs={{0,3},{1,0},{2,1},{3,2},{4,7},{5,4},{6,5},{7,6},{8,11},{9,8},{10,9... | collective-permute-start | bytes 82952 | tf_op jit(solution)/shard_map/ppermute | solution.py:35
  74.0 1.4 fusion.27
  75.5 1.4 fusion.26
  76.9 1.1 fusion.25
  78.0 1.4 fusion.24
  87.0 5.0 %convolution_bitcast_fusion = f32[8,8,4,128]{3,0,2,1:T(8,128)S(1)} fusion(f32[32,27,8,1,1]{0,2,4,3,1:T(8,128)S(1)} %bitcast.503, f32[27,32,8,4,128]{4,1,3,2,0:T(8,128)S(1)} %fusion.1), kind=kOutput, calls=%fused_computation.14 | convolution fusion | flops 169869312 | bytes 14314496 | tf_op jit(solution)/shard_map/okc,kopqy->cpqy/dot_general | solution.py:91
  92.1 3.6 %convolution_bitcast_fusion.1 = f32[8,8,4,128]{3,0,2,1:T(8,128)S(1)} fusion(f32[27,32,8,4,128]{4,1,0,3,2:T(8,128)S(1)} %fusion.28, f32[8,27,32,1,1]{2,0,1,4,3:T(8,128)S(1)} %bitcast.502), kind=kOutput, calls=%fused_computation.15 | convolution fusion | flops 169869312 | bytes 14314496 | tf_op jit(solution)/shard_map/okc,kcpqy->opqy/dot_general | solution.py:87
  95.9 0.7 copy.136
  96.6 0.7 copy.135
  97.3 0.6 gather_fusion.1
  98.0 1.9 %collective-permute-start.7 = (f32[54,128]{1,0:T(8,128)S(1)}, f32[54,128]{1,0:T(8,128)S(1)}, u32[]{:S(2)}, u32[]{:S(2)}) collective-permute-start(f32[54,128]{1,0:T(8,128)S(1)} %fusion.75), channel_id=1, source_target_pairs={{0,4},{1,5},{2,6},{3,7},{4,0},{5,1},{6,2},{7,3},{8,12},{9,13},{10,... | collective-permute-start | bytes 82952 | tf_op jit(solution)/shard_map/ppermute | solution.py:35
  99.9 5.3 %collective-permute-done.7 = f32[54,128]{1,0:T(8,128)S(1)} collective-permute-done((f32[54,128]{1,0:T(8,128)S(1)}, f32[54,128]{1,0:T(8,128)S(1)}, u32[]{:S(2)}, u32[]{:S(2)}) %collective-permute-start.7) | collective-permute-done | bytes 27680 | tf_op jit(solution)/shard_map/ppermute | solution.py:35
  105.3 0.6 gather_fusion
  105.9 5.0 %collective-permute-start.8 = (f32[54,128]{1,0:T(8,128)S(1)}, f32[54,128]{1,0:T(8,128)S(1)}, u32[]{:S(2)}, u32[]{:S(2)}) collective-permute-start(f32[54,128]{1,0:T(8,128)S(1)} %fusion.74), channel_id=1, source_target_pairs={{0,8},{8,16},{16,24},{24,0},{32,40},{40,48},{48,56},{56,32},{64,72... | collective-permute-start | bytes 82952 | tf_op jit(solution)/shard_map/ppermute | solution.py:35
  111.0 4.3 %collective-permute-start.9 = (f32[54,128]{1,0:T(8,128)S(1)}, f32[54,128]{1,0:T(8,128)S(1)}, u32[]{:S(2)}, u32[]{:S(2)}) collective-permute-start(f32[54,128]{1,0:T(8,128)S(1)} %fusion.74), channel_id=1, source_target_pairs={{0,16},{8,24},{16,0},{24,8},{32,48},{40,56},{48,32},{56,40},{64,80... | collective-permute-start | bytes 82952 | tf_op jit(solution)/shard_map/ppermute | solution.py:35
  115.3 3.9 %collective-permute-start.10 = (f32[54,128]{1,0:T(8,128)S(1)}, f32[54,128]{1,0:T(8,128)S(1)}, u32[]{:S(2)}, u32[]{:S(2)}) collective-permute-start(f32[54,128]{1,0:T(8,128)S(1)} %fusion.74), channel_id=1, source_target_pairs={{0,24},{8,0},{16,8},{24,16},{32,56},{40,32},{48,40},{56,48},{64,88... | collective-permute-start | bytes 82952 | tf_op jit(solution)/shard_map/ppermute | solution.py:35
  119.2 1.8 %collective-permute-done.10 = f32[54,128]{1,0:T(8,128)S(1)} collective-permute-done((f32[54,128]{1,0:T(8,128)S(1)}, f32[54,128]{1,0:T(8,128)S(1)}, u32[]{:S(2)}, u32[]{:S(2)}) %collective-permute-start.10) | collective-permute-done | bytes 27680 | tf_op jit(solution)/shard_map/ppermute | solution.py:35
  121.0 0.6 gather_fusion.2
  121.7 9.1 %collective-permute-start.11 = (f32[54,128]{1,0:T(8,128)S(1)}, f32[54,128]{1,0:T(8,128)S(1)}, u32[]{:S(2)}, u32[]{:S(2)}) collective-permute-start(f32[54,128]{1,0:T(8,128)S(1)} %fusion.73), channel_id=1, source_target_pairs={{0,32},{8,40},{16,48},{24,56},{32,64},{40,72},{48,80},{56,88},{64,... | collective-permute-start | bytes 82952 | tf_op jit(solution)/shard_map/ppermute | solution.py:35
  130.8 8.7 %collective-permute-start.12 = (f32[54,128]{1,0:T(8,128)S(1)}, f32[54,128]{1,0:T(8,128)S(1)}, u32[]{:S(2)}, u32[]{:S(2)}) collective-permute-start(f32[54,128]{1,0:T(8,128)S(1)} %fusion.73), channel_id=1, source_target_pairs={{0,64},{8,72},{16,80},{24,88},{32,96},{40,104},{48,112},{56,120},{... | collective-permute-start | bytes 82952 | tf_op jit(solution)/shard_map/ppermute | solution.py:35
  139.5 5.5 %collective-permute-start.13 = (f32[54,128]{1,0:T(8,128)S(1)}, f32[54,128]{1,0:T(8,128)S(1)}, u32[]{:S(2)}, u32[]{:S(2)}) collective-permute-start(f32[54,128]{1,0:T(8,128)S(1)} %fusion.73), channel_id=1, source_target_pairs={{0,96},{8,104},{16,112},{24,120},{32,0},{40,8},{48,16},{56,24},{64... | collective-permute-start | bytes 82952 | tf_op jit(solution)/shard_map/ppermute | solution.py:35
  145.4 3.8 %collective-permute-done.13 = f32[54,128]{1,0:T(8,128)S(1)} collective-permute-done((f32[54,128]{1,0:T(8,128)S(1)}, f32[54,128]{1,0:T(8,128)S(1)}, u32[]{:S(2)}, u32[]{:S(2)}) %collective-permute-start.13) | collective-permute-done | bytes 27680 | tf_op jit(solution)/shard_map/ppermute | solution.py:35
  149.2 0.6 gather_fusion.3
  149.8 0.8 mul.15
  150.7 1.6 %copy.137 = f32[8,32,3,3,3]{1,0,4,3,2:T(8,128)} copy(f32[8,32,3,3,3]{4,3,2,1,0:T(4,128)S(1)} %mul.15) | data formatting | bytes 55296
  (130 shorter events, 12.0 us)
Async XLA Ops:
  17.1 13.9 %collective-permute-start = (f32[2,32,8,1,128]{4,1,3,2,0:T(8,128)S(1)}, f32[2,32,8,1,128]{4,1,3,2,0:T(8,128)S(1)}, u32[]{:S(2)}, u32[]{:S(2)}) collective-permute-start(f32[2,32,8,1,128]{4,1,3,2,0:T(8,128)S(1)} %get-tuple-element.18), channel_id=1, source_target_pairs={{0,8},{8,16},{16,24},{24,32},{32,40},{40,48},{48,56},{56,64},{64,7... | collective-permute-start | bytes 786440 | tf_op jit(solution)/shard_map/ppermute | solution.py:12
  20.9 10.4 %collective-permute-start.1 = (f32[2,32,8,1,128]{4,1,3,2,0:T(8,128)S(1)}, f32[2,32,8,1,128]{4,1,3,2,0:T(8,128)S(1)}, u32[]{:S(2)}, u32[]{:S(2)}) collective-permute-start(f32[2,32,8,1,128]{4,1,3,2,0:T(8,128)S(1)} %get-tuple-element.19), channel_id=1, source_target_pairs={{8,0},{16,8},{24,16},{32,24},{40,32},{48,40},{56,48},{64,56},{72,6... | collective-permute-start | bytes 786440 | tf_op jit(solution)/shard_map/ppermute | solution.py:15
  31.3 0.7 copy-start.1
  35.9 7.9 %collective-permute-start.2 = (f32[2,32,8,6,1]{1,2,4,3,0:T(8,128)S(1)}, f32[2,32,8,6,1]{1,2,4,3,0:T(8,128)S(1)}, u32[]{:S(2)}, u32[]{:S(2)}) collective-permute-start(f32[2,32,8,6,1]{1,2,4,3,0:T(8,128)S(1)} %copy.75), channel_id=1, source_target_pairs={{0,1},{1,2},{2,3},{3,4},{4,5},{5,6},{6,7},{8,9},{9,10},{10,11},{11... | collective-permute-start | bytes 36872 | tf_op jit(solution)/shard_map/ppermute | solution.py:12
  40.6 6.3 %collective-permute-start.3 = (f32[2,32,8,6,1]{1,2,4,3,0:T(8,128)}, f32[2,32,8,6,1]{1,2,4,3,0:T(8,128)}, u32[]{:S(2)}, u32[]{:S(2)}) collective-permute-start(f32[2,32,8,6,1]{1,2,4,3,0:T(8,128)} %copy.76), channel_id=1, source_target_pairs={{1,0},{2,1},{3,2},{4,3},{5,4},{6,5},{7,6},{9,8},{10,9},{11,10},{12... | collective-permute-start | bytes 36872 | tf_op jit(solution)/shard_map/ppermute | solution.py:15
  58.6 20.8 %copy-start = (f32[32,10,6,130]{3,0,2,1:T(8,128)S(1)}, f32[32,10,6,130]{3,0,2,1:T(8,128)}, u32[]{:S(2)}) copy-start(f32[32,10,6,130]{3,0,2,1:T(8,128)} %get-tuple-element.14) | copy-start | bytes 2995204
  58.6 38.7 %collective-permute-start.4 = (f32[54,128]{1,0:T(8,128)S(1)}, f32[54,128]{1,0:T(8,128)S(1)}, u32[]{:S(2)}, u32[]{:S(2)}) collective-permute-start(f32[54,128]{1,0:T(8,128)S(1)} %reshape_reshape.3), channel_id=1, source_target_pairs={{0,1},{1,2},{2,3},{3,0},{4,5},{5,6},{6,7},{7,4},{8,9},{9,10},{10,1... | collective-permute-start | bytes 82952 | tf_op jit(solution)/shard_map/ppermute | solution.py:35
  62.3 35.0 %collective-permute-start.5 = (f32[54,128]{1,0:T(8,128)S(1)}, f32[54,128]{1,0:T(8,128)S(1)}, u32[]{:S(2)}, u32[]{:S(2)}) collective-permute-start(f32[54,128]{1,0:T(8,128)S(1)} %reshape_reshape.3), channel_id=1, source_target_pairs={{0,2},{1,3},{2,0},{3,1},{4,6},{5,7},{6,4},{7,5},{8,10},{9,11},{10,... | collective-permute-start | bytes 82952 | tf_op jit(solution)/shard_map/ppermute | solution.py:35
  69.3 28.0 %collective-permute-start.6 = (f32[54,128]{1,0:T(8,128)S(1)}, f32[54,128]{1,0:T(8,128)S(1)}, u32[]{:S(2)}, u32[]{:S(2)}) collective-permute-start(f32[54,128]{1,0:T(8,128)S(1)} %reshape_reshape.3), channel_id=1, source_target_pairs={{0,3},{1,0},{2,1},{3,2},{4,7},{5,4},{6,5},{7,6},{8,11},{9,8},{10,9... | collective-permute-start | bytes 82952 | tf_op jit(solution)/shard_map/ppermute | solution.py:35
  87.0 5.0 %copy-start.2 = (f32[8,32,3,3,3]{1,0,4,3,2:T(8,128)S(1)}, f32[8,32,3,3,3]{1,0,4,3,2:T(8,128)}, u32[]{:S(2)}) copy-start(f32[8,32,3,3,3]{1,0,4,3,2:T(8,128)} %param.6) | copy-start | bytes 82948
  92.0 5.8 %copy-start.4 = (pred[4]{0:T(512)(128)(4,1)S(1)}, pred[4]{0:T(512)(128)(4,1)}, u32[]{:S(2)}) copy-start(pred[4]{0:T(512)(128)(4,1)} %compare_and_fusion.2) | copy-start | bytes 16
  92.0 13.8 %copy-start.5 = (pred[2]{0:T(512)(128)(4,1)S(1)}, pred[2]{0:T(512)(128)(4,1)}, u32[]{:S(2)}) copy-start(pred[2]{0:T(512)(128)(4,1)} %compare_and_fusion.3) | copy-start | bytes 10
  92.1 29.6 %copy-start.3 = (pred[4]{0:T(512)(128)(4,1)S(1)}, pred[4]{0:T(512)(128)(4,1)}, u32[]{:S(2)}) copy-start(pred[4]{0:T(512)(128)(4,1)} %get-tuple-element.21) | copy-start | bytes 16
  98.0 7.3 %collective-permute-start.7 = (f32[54,128]{1,0:T(8,128)S(1)}, f32[54,128]{1,0:T(8,128)S(1)}, u32[]{:S(2)}, u32[]{:S(2)}) collective-permute-start(f32[54,128]{1,0:T(8,128)S(1)} %fusion.75), channel_id=1, source_target_pairs={{0,4},{1,5},{2,6},{3,7},{4,0},{5,1},{6,2},{7,3},{8,12},{9,13},{10,... | collective-permute-start | bytes 82952 | tf_op jit(solution)/shard_map/ppermute | solution.py:35
  105.9 13.3 %collective-permute-start.8 = (f32[54,128]{1,0:T(8,128)S(1)}, f32[54,128]{1,0:T(8,128)S(1)}, u32[]{:S(2)}, u32[]{:S(2)}) collective-permute-start(f32[54,128]{1,0:T(8,128)S(1)} %fusion.74), channel_id=1, source_target_pairs={{0,8},{8,16},{16,24},{24,0},{32,40},{40,48},{48,56},{56,32},{64,72... | collective-permute-start | bytes 82952 | tf_op jit(solution)/shard_map/ppermute | solution.py:35
  111.0 8.3 %collective-permute-start.9 = (f32[54,128]{1,0:T(8,128)S(1)}, f32[54,128]{1,0:T(8,128)S(1)}, u32[]{:S(2)}, u32[]{:S(2)}) collective-permute-start(f32[54,128]{1,0:T(8,128)S(1)} %fusion.74), channel_id=1, source_target_pairs={{0,16},{8,24},{16,0},{24,8},{32,48},{40,56},{48,32},{56,40},{64,80... | collective-permute-start | bytes 82952 | tf_op jit(solution)/shard_map/ppermute | solution.py:35
  115.3 5.8 %collective-permute-start.10 = (f32[54,128]{1,0:T(8,128)S(1)}, f32[54,128]{1,0:T(8,128)S(1)}, u32[]{:S(2)}, u32[]{:S(2)}) collective-permute-start(f32[54,128]{1,0:T(8,128)S(1)} %fusion.74), channel_id=1, source_target_pairs={{0,24},{8,0},{16,8},{24,16},{32,56},{40,32},{48,40},{56,48},{64,88... | collective-permute-start | bytes 82952 | tf_op jit(solution)/shard_map/ppermute | solution.py:35
  121.7 23.3 %collective-permute-start.11 = (f32[54,128]{1,0:T(8,128)S(1)}, f32[54,128]{1,0:T(8,128)S(1)}, u32[]{:S(2)}, u32[]{:S(2)}) collective-permute-start(f32[54,128]{1,0:T(8,128)S(1)} %fusion.73), channel_id=1, source_target_pairs={{0,32},{8,40},{16,48},{24,56},{32,64},{40,72},{48,80},{56,88},{64,... | collective-permute-start | bytes 82952 | tf_op jit(solution)/shard_map/ppermute | solution.py:35
  130.8 14.6 %collective-permute-start.12 = (f32[54,128]{1,0:T(8,128)S(1)}, f32[54,128]{1,0:T(8,128)S(1)}, u32[]{:S(2)}, u32[]{:S(2)}) collective-permute-start(f32[54,128]{1,0:T(8,128)S(1)} %fusion.73), channel_id=1, source_target_pairs={{0,64},{8,72},{16,80},{24,88},{32,96},{40,104},{48,112},{56,120},{... | collective-permute-start | bytes 82952 | tf_op jit(solution)/shard_map/ppermute | solution.py:35
  139.5 9.7 %collective-permute-start.13 = (f32[54,128]{1,0:T(8,128)S(1)}, f32[54,128]{1,0:T(8,128)S(1)}, u32[]{:S(2)}, u32[]{:S(2)}) collective-permute-start(f32[54,128]{1,0:T(8,128)S(1)} %fusion.73), channel_id=1, source_target_pairs={{0,96},{8,104},{16,112},{24,120},{32,0},{40,8},{48,16},{56,24},{64... | collective-permute-start | bytes 82952 | tf_op jit(solution)/shard_map/ppermute | solution.py:35
